TPU v7x, 32 devices: a whole 2x2x4 slice. The times are simulated.
32 devices in a mesh: real: 4 (over x, core), space: 8 (over z, y).
Axes of the slice: x: 2, y: 2, z: 4, core: 2. Of those that a mesh axis runs over, the one named last changes fastest.
Arguments:
- perm_class: int32 [8, 16, 16, 128], P('space'), may hold values from 0 to 7
- class_values: float32 [8], replicated, may hold values from 0.3 to 10
- well_cells: int32 [64], P('real'), parts along dimension 0, may hold values from 0 to 262143
- well_rates: float32 [64], P('real'), parts along dimension 0, may hold values from 0.5 to 3
- guess: float32 [32, 16, 16, 128], P(('real', 'space')), parts along dimension 0, may hold values from -4 to 4
Outputs:
- pressure: float32 [32, 16, 16, 128], P(('real', 'space')), parts along dimension 0
- residual: float32 [32, 16, 16, 128], P(('real', 'space')), parts along dimension 0
There are 4 independent parts, one for each index of `real`. A program takes and returns all parts, laid end to end along the dimension named above; an argument that names none is the same for every part. Nothing has to cross between parts.
All inputs are finite; a program needn't handle non-finite values.
Results may differ from a plain program's by a relative error of at most 0.00015.
Values sent between devices are 32-bit elements; how exact they have to be, the bound alone decides.
No kernel may reach another device: no remote copies, remote signals or barrier semaphores. Data moves between devices by JAX's collectives and lax.ppermute only.
A program may use at most 128 MiB of HBM per device.

v0:
```python
import jax
import jax.numpy as jnp
from jax import lax
from jax.sharding import PartitionSpec as P

LEVELS = 3
SWEEPS = 2
CSWEEPS = 6


OMEGA = 0.8


def shifted(shard, axis, by):
    peers = lax.axis_size(axis)
    return lax.ppermute(shard, axis, [(i, (i + by) % peers) for i in range(peers)])


def exchange(fields, per_side):
    count_dev = lax.axis_size("space")
    plane_step = per_side * per_side
    if (2 * plane_step) % count_dev == 0:
        both_x = shifted(jnp.concatenate([fields[:, -1:], fields[:, :1]], axis=1), "space", plane_step)
        lower_x, upper_x = both_x[:, :1], both_x[:, 1:]
    else:
        lower_x = shifted(fields[:, -1:], "space", plane_step)
        upper_x = shifted(fields[:, :1], "space", -plane_step)
    lower_y = shifted(fields[:, :, -1:], "space", per_side)
    upper_y = shifted(fields[:, :, :1], "space", -per_side)
    lower_z = shifted(fields[:, :, :, -1:], "space", 1)
    upper_z = shifted(fields[:, :, :, :1], "space", -1)
    return [lower_x, upper_x, lower_y, upper_y, lower_z, upper_z]


def own_faces(values):
    return [values[-1:], values[:1], values[:, -1:], values[:, :1], values[:, :, -1:], values[:, :, :1]]


def exchange_mixed(fields, per_side):
    count_dev = lax.axis_size("space")
    plane_step = per_side * per_side
    outgoing = [own_faces(values) for values in fields]
    shifts = [plane_step, -plane_step, per_side, -per_side, 1, -1]
    flat = [jnp.concatenate([faces[d].reshape(-1) for faces in outgoing]) for d in range(6)]
    received = [None] * 6
    if (2 * plane_step) % count_dev == 0:
        both = shifted(jnp.concatenate([flat[0], flat[1]]), "space", plane_step)
        received[0], received[1] = both[: flat[0].shape[0]], both[flat[0].shape[0] :]
        rest = range(2, 6)
    else:
        rest = range(6)
    for d in rest:
        received[d] = shifted(flat[d], "space", shifts[d])
    result = [[None] * 6 for _ in fields]
    for d in range(6):
        offset = 0
        for number, faces in enumerate(outgoing):
            size = faces[d].size
            result[number][d] = received[d][offset : offset + size].reshape(faces[d].shape)
            offset += size
    return result


def gather_rows(block, per_side):
    count_dev = lax.axis_size("space")
    if count_dev > 16:
        return lax.all_gather(block[None], "space", axis=0, tiled=True)
    my_row = lax.axis_index("space")
    by_offset = jnp.stack([block] + [shifted(block, "space", k) for k in range(1, count_dev)])
    return jnp.take(by_offset, (my_row - jnp.arange(count_dev)) % count_dev, axis=0)


def pick(faces, number):
    return [face[number] for face in faces]


def with_faces(values, faces):
    lower_x, upper_x, lower_y, upper_y, lower_z, upper_z = faces
    return [
        jnp.concatenate([lower_x, values[:-1]], axis=0),
        jnp.concatenate([values[1:], upper_x], axis=0),
        jnp.concatenate([lower_y, values[:, :-1]], axis=1),
        jnp.concatenate([values[:, 1:], upper_y], axis=1),
        jnp.concatenate([lower_z, values[:, :, :-1]], axis=2),
        jnp.concatenate([values[:, :, 1:], upper_z], axis=2),
    ]


def rolled_faces(values, per_side):
    plane_step = per_side * per_side
    return [
        jnp.concatenate([jnp.roll(values[:, -1:], plane_step, axis=0), values[:, :-1]], axis=1),
        jnp.concatenate([values[:, 1:], jnp.roll(values[:, :1], -plane_step, axis=0)], axis=1),
        jnp.concatenate([jnp.roll(values[:, :, -1:], per_side, axis=0), values[:, :, :-1]], axis=2),
        jnp.concatenate([values[:, :, 1:], jnp.roll(values[:, :, :1], -per_side, axis=0)], axis=2),
        jnp.concatenate([jnp.roll(values[:, :, :, -1:], 1, axis=0), values[:, :, :, :-1]], axis=3),
        jnp.concatenate([values[:, :, :, 1:], jnp.roll(values[:, :, :, :1], -1, axis=0)], axis=3),
    ]


def coefficients(permeab, neighbors, scaling):
    face_coefs = [0.5 * (permeab + beside) for beside in neighbors]
    total_sum = face_coefs[0]
    for number in range(1, 6):
        total_sum = total_sum + face_coefs[number]
    return (face_coefs, scaling * total_sum)


def operate(values, neighbors, face_coefs, scaling):
    total_sum = face_coefs[0] * (values - neighbors[0])
    for number in range(1, 6):
        total_sum = total_sum + face_coefs[number] * (values - neighbors[number])
    return scaling * total_sum


def smooth(values, right_side, face_coefs, diagonal, scaling, neighbors):
    return values + OMEGA * (right_side - operate(values, neighbors, face_coefs, scaling)) / diagonal


def pair_mean(size, scale):
    rows = jnp.arange(size)[:, None] // 2
    cols = jnp.arange(size // 2)[None, :]
    return jnp.where(rows == cols, scale, 0.0).astype(jnp.float32)


def plane_mean(size_x, size_y):
    fine = jnp.arange(size_x * size_y)
    coarse_of = (fine // size_y // 2) * (size_y // 2) + (fine % size_y) // 2
    return jnp.where(
        jnp.arange(size_x * size_y // 4)[:, None] == coarse_of[None, :], 0.25, 0.0
    ).astype(jnp.float32)


def coarsen(values):
    size_x, size_y, size_z = values.shape
    along_z = jnp.dot(
        values.reshape(size_x * size_y, size_z),
        pair_mean(size_z, 0.5),
        precision=lax.Precision.HIGHEST,
    )
    both = jnp.dot(plane_mean(size_x, size_y), along_z, precision=lax.Precision.HIGHEST)
    return both.reshape(size_x // 2, size_y // 2, size_z // 2)


def refine(values):
    return jnp.repeat(jnp.repeat(jnp.repeat(values, 2, axis=0), 2, axis=1), 2, axis=2)


def coarsen_all(values):
    count_b, size_x, size_y, size_z = values.shape
    along_z = jnp.dot(
        values.reshape(count_b * size_x * size_y, size_z),
        pair_mean(size_z, 0.5),
        precision=lax.Precision.HIGHEST,
    ).reshape(count_b, size_x * size_y, size_z // 2)
    both = jnp.einsum(
        "pq,bqz->bpz", plane_mean(size_x, size_y), along_z, precision=lax.Precision.HIGHEST
    )
    return both.reshape(count_b, size_x // 2, size_y // 2, size_z // 2)


def refine_all(values):
    return jnp.repeat(jnp.repeat(jnp.repeat(values, 2, axis=1), 2, axis=2), 2, axis=3)


def refine_face(face):
    return jnp.repeat(jnp.repeat(face, 2, axis=0), 2, axis=1)


def refine_face_of(face):
    for axis in range(3):
        if face.shape[axis] != 1:
            face = jnp.repeat(face, 2, axis=axis)
    return face


def refined_faces(coarse_all, my_row, per_side):
    count_b = coarse_all.shape[0]

    def row(offset):
        return lax.dynamic_index_in_dim(coarse_all, (my_row + offset) % count_b, 0, keepdims=False)

    plane_step = per_side * per_side
    return [
        refine_face(row(-plane_step)[-1])[None],
        refine_face(row(plane_step)[0])[None],
        refine_face(row(-per_side)[:, -1])[:, None],
        refine_face(row(per_side)[:, 0])[:, None],
        refine_face(row(-1)[:, :, -1])[:, :, None],
        refine_face(row(1)[:, :, 0])[:, :, None],
    ]


def global_cycle(all_rhs, all_perm, first_level, per_side):
    perms = [all_perm]
    for number in range(LEVELS - first_level):
        perms.append(coarsen_all(perms[-1]))
    coefs = [
        coefficients(
            perms[number], rolled_faces(perms[number], per_side), 0.25 ** (first_level + number)
        )
        for number in range(LEVELS - first_level + 1)
    ]
    right_side = all_rhs
    stored = []
    rights = []
    for number in range(LEVELS - first_level):
        face_coefs, diagonal = coefs[number]
        scaling = 0.25 ** (first_level + number)
        values = OMEGA * right_side / diagonal
        for sweep_no in range(SWEEPS - 1):
            values = smooth(
                values, right_side, face_coefs, diagonal, scaling, rolled_faces(values, per_side)
            )
        leftover = right_side - operate(
            values, rolled_faces(values, per_side), face_coefs, scaling
        )
        stored.append(values)
        rights.append(right_side)
        right_side = coarsen_all(leftover)
    face_coefs, diagonal = coefs[LEVELS - first_level]
    scaling = 0.25**LEVELS
    correction = OMEGA * right_side / diagonal
    for sweep_no in range(CSWEEPS - 1):
        correction = smooth(
            correction, right_side, face_coefs, diagonal, scaling, rolled_faces(correction, per_side)
        )
    for number in reversed(range(LEVELS - first_level)):
        face_coefs, diagonal = coefs[number]
        scaling = 0.25 ** (first_level + number)
        values = stored[number] + refine_all(correction)
        for sweep_no in range(SWEEPS):
            values = smooth(
                values, rights[number], face_coefs, diagonal, scaling, rolled_faces(values, per_side)
            )
        correction = values
    return correction


def shards(perm_class, class_values, well_cells, well_rates, guess):
    count_dev = lax.axis_size("space")
    per_side = 2 + 2 * (count_dev // 64)
    my_row = lax.axis_index("space")
    block_no = (my_row + per_side * per_side + per_side + 1) % count_dev
    block_x = block_no // (per_side * per_side)
    block_y = block_no // per_side % per_side
    block_z = block_no % per_side
    classes = perm_class[0]
    width_x, width_y, width_z = classes.shape
    permeab = jnp.zeros(classes.shape, jnp.float32)
    for number in range(class_values.shape[0]):
        permeab = permeab + jnp.where(classes == number, class_values[number], 0.0)
    row_len = per_side * width_z
    plane = per_side * width_y * row_len
    glob_x = well_cells // plane
    glob_y = well_cells // row_len % (per_side * width_y)
    glob_z = well_cells % row_len
    onehot_x = jnp.where(
        (glob_x - block_x * width_x)[:, None] == jnp.arange(width_x)[None, :],
        well_rates[:, None],
        0.0,
    )
    onehot_y = jnp.where(
        (glob_y - block_y * width_y)[:, None] == jnp.arange(width_y)[None, :], 1.0, 0.0
    ).astype(jnp.float32)
    onehot_z = jnp.where(
        (glob_z - block_z * width_z)[:, None] == jnp.arange(width_z)[None, :], 1.0, 0.0
    ).astype(jnp.float32)
    source = jnp.einsum(
        "wi,wj,wk->ijk", onehot_x, onehot_y, onehot_z, precision=lax.Precision.HIGHEST
    )

    values = guess[0]
    coarse_perm = coarsen(permeab)
    first = exchange_mixed([permeab, values, coarse_perm], per_side)
    face_coefs, diagonal = coefficients(permeab, with_faces(permeab, first[0]), 1.0)
    values = smooth(values, source, face_coefs, diagonal, 1.0, with_faces(values, first[1]))
    for sweep_no in range(SWEEPS - 1):
        faces = pick(exchange(values[None], per_side), 0)
        values = smooth(values, source, face_coefs, diagonal, 1.0, with_faces(values, faces))
    stored_faces = pick(exchange(values[None], per_side), 0)
    leftover = source - operate(values, with_faces(values, stored_faces), face_coefs, 1.0)
    stored = values

    scaling = 0.25
    right_1 = coarsen(leftover)
    coefs_1, diagonal_1 = coefficients(coarse_perm, with_faces(coarse_perm, first[2]), scaling)
    values_1 = OMEGA * right_1 / diagonal_1
    for sweep_no in range(SWEEPS - 1):
        faces = pick(exchange(values_1[None], per_side), 0)
        values_1 = smooth(values_1, right_1, coefs_1, diagonal_1, scaling, with_faces(values_1, faces))
    stored_faces_1 = pick(exchange(values_1[None], per_side), 0)
    leftover_1 = right_1 - operate(values_1, with_faces(values_1, stored_faces_1), coefs_1, scaling)
    stored_1 = values_1

    gathered = gather_rows(jnp.stack([coarsen(coarse_perm), coarsen(leftover_1)]), per_side)
    correction_all = global_cycle(gathered[:, 1], gathered[:, 0], 2, per_side)

    correction = lax.dynamic_index_in_dim(correction_all, my_row, 0, keepdims=False)
    values_1 = stored_1 + refine(correction)
    faces = [
        mine + theirs
        for mine, theirs in zip(stored_faces_1, refined_faces(correction_all, my_row, per_side))
    ]
    values_1 = smooth(values_1, right_1, coefs_1, diagonal_1, scaling, with_faces(values_1, faces))
    for sweep_no in range(SWEEPS - 1):
        faces = pick(exchange(values_1[None], per_side), 0)
        values_1 = smooth(values_1, right_1, coefs_1, diagonal_1, scaling, with_faces(values_1, faces))
    coarse_faces = pick(exchange(values_1[None], per_side), 0)

    values = stored + refine(values_1)
    faces = [mine + refine_face_of(theirs) for mine, theirs in zip(stored_faces, coarse_faces)]
    values = smooth(values, source, face_coefs, diagonal, 1.0, with_faces(values, faces))
    for sweep_no in range(SWEEPS - 1):
        faces = pick(exchange(values[None], per_side), 0)
        values = smooth(values, source, face_coefs, diagonal, 1.0, with_faces(values, faces))
    faces = pick(exchange(values[None], per_side), 0)
    residual = source - operate(values, with_faces(values, faces), face_coefs, 1.0)
    return (values[None], residual[None])


def solution(mesh):
    return jax.shard_map(
        shards,
        mesh=mesh,
        in_specs=(
            P("space", None, None, None),
            P(),
            P("real"),
            P("real"),
            P(("real", "space"), None, None, None),
        ),
        out_specs=(P(("real", "space"), None, None, None), P(("real", "space"), None, None, None)),
        check_vma=False,
    )
```

profile of v0, /device:TPU:0, one launch (start us, length us, event | category | flops | bytes accessed | tf_op | source)
XLA Modules:
  0.0 202.7 jit_solution(9035012653961062568)
XLA Ops:
  2.0 5.9 %add_add_fusion = f32[1,16,16,128]{3,1,2,0:T(8,128)S(1)} fusion(s32[1,16,16,128]{3,2,1,0:T(8,128)} %param.5, f32[]{:T(128)} %bitcast.10, f32[]{:T(128)} %bitcast.9, f32[]{:T(128)} %bitcast.8, f32[]{:T(128)} %bitcast.7, f32[]{:T(128)} %bitcast.6, f32[]{:T(128)} %bitcast.5, f32[]{:T(128)} %bitcast.4, f32[]{:T(128)} %bitcast.3), kind=kLoop, calls=%fused_computation.142 | loop fusion | flops 753664 | bytes 262176 | tf_op jit(solution)/shard_map/add | solution.py:252
  9.0 4.1 %collective-permute-start = (f32[9216]{0:T(1024)S(1)}, f32[9216]{0:T(1024)S(1)}, u32[]{:S(2)}, u32[]{:S(2)}) collective-permute-start(f32[9216]{0:T(1024)S(1)} %constant_dynamic-update-slice_fusion.9), channel_id=1, source_target_pairs={{0,4},{1,5},{2,6},{3,7},{4,0},{5,1},{6,2},{7,3},{8,12},{9,13},{10,... | collective-permute-start | bytes 110600 | tf_op jit(solution)/shard_map/ppermute | solution.py:16
  13.1 5.0 %fusion.741 = f32[16,16,128]{2,0,1:T(8,128)S(1)} fusion(f32[]{:T(128)} %bitcast.10, f32[]{:T(128)} %bitcast.9, f32[]{:T(128)} %bitcast.8, f32[]{:T(128)} %bitcast.7, f32[]{:T(128)} %bitcast.6, f32[]{:T(128)} %bitcast.5, f32[]{:T(128)} %bitcast.4, f32[]{:T(128)} %bitcast.3, s32[1,16,16,128]{3,2,1,0:T(8,128)S(1)} %copy-done.1), kind=kLoop, calls=%fused_computation.1090 | loop fusion | flops 753664 | bytes 262176 | tf_op jit(solution)/shard_map/add | solution.py:252
  18.3 1.6 collective-permute-start.1
  20.0 2.2 %collective-permute-start.2 = (f32[4608]{0:T(1024)S(1)}, f32[4608]{0:T(1024)S(1)}, u32[]{:S(2)}, u32[]{:S(2)}) collective-permute-start(f32[4608]{0:T(1024)S(1)} %pad_maximum_fusion.23), channel_id=1, source_target_pairs={{0,6},{1,7},{2,0},{3,1},{4,2},{5,3},{6,4},{7,5},{8,14},{9,15},{10,... | collective-permute-start | bytes 55304 | tf_op jit(solution)/shard_map/ppermute | solution.py:16
  23.2 1.6 collective-permute-start.3
  25.4 3.3 %collective-permute-start.4 = (f32[576]{0:T(1024)S(1)}, f32[576]{0:T(1024)S(1)}, u32[]{:S(2)}, u32[]{:S(2)}) collective-permute-start(f32[576]{0:T(1024)S(1)} %pad_maximum_fusion.36), channel_id=1, source_target_pairs={{0,7},{1,0},{2,1},{3,2},{4,3},{5,4},{6,5},{7,6},{8,15},{9,8},{10,9... | collective-permute-start | bytes 6920 | tf_op jit(solution)/shard_map/ppermute | solution.py:16
  49.0 4.7 %collective-permute-start.9 = (f32[1,16,16,1]{3,2,1,0:T(8,128)S(1)}, f32[1,16,16,1]{3,2,1,0:T(8,128)S(1)}, u32[]{:S(2)}, u32[]{:S(2)}) collective-permute-start(f32[1,16,16,1]{3,2,1,0:T(8,128)S(1)} %get-tuple-element.112), channel_id=1, source_target_pairs={{0,7},{1,0},{2,1},{3,2},{4,3},{5,4},{6,5},{7,6},{8,15},{9,8},{10,9... | collective-permute-start | bytes 3080 | tf_op jit(solution)/shard_map/ppermute | solution.py:16
  54.8 3.8 %collective-permute-start.7 = (f32[1,16,1,128]{3,1,2,0:T(8,128)S(1)}, f32[1,16,1,128]{3,1,2,0:T(8,128)S(1)}, u32[]{:S(2)}, u32[]{:S(2)}) collective-permute-start(f32[1,16,1,128]{3,1,2,0:T(8,128)S(1)} %bitcast.736), channel_id=1, source_target_pairs={{0,6},{1,7},{2,0},{3,1},{4,2},{5,3},{6,4},{7,5},{8,14},{9,15},{10,... | collective-permute-start | bytes 24584 | tf_op jit(solution)/shard_map/ppermute | solution.py:16
  59.2 1.0 collective-permute-done.6
  60.8 4.7 %collective-permute-start.14 = (f32[1,16,16,1]{3,2,1,0:T(8,128)S(1)}, f32[1,16,16,1]{3,2,1,0:T(8,128)S(1)}, u32[]{:S(2)}, u32[]{:S(2)}) collective-permute-start(f32[1,16,16,1]{3,2,1,0:T(8,128)S(1)} %get-tuple-element.100), channel_id=1, source_target_pairs={{0,7},{1,0},{2,1},{3,2},{4,3},{5,4},{6,5},{7,6},{8,15},{9,8},{10,9... | collective-permute-start | bytes 3080 | tf_op jit(solution)/shard_map/ppermute | solution.py:16
  65.6 2.6 %collective-permute-start.11 = (f32[1,16,1,128]{3,1,2,0:T(8,128)S(1)}, f32[1,16,1,128]{3,1,2,0:T(8,128)S(1)}, u32[]{:S(2)}, u32[]{:S(2)}) collective-permute-start(f32[1,16,1,128]{3,1,2,0:T(8,128)S(1)} %bitcast.741), channel_id=1, source_target_pairs={{0,2},{1,3},{2,4},{3,5},{4,6},{5,7},{6,0},{7,1},{8,10},{9,11},{10,... | collective-permute-start | bytes 24584 | tf_op jit(solution)/shard_map/ppermute | solution.py:16
  68.2 1.2 collective-permute-start.12
  76.0 1.0 collective-permute-start.16
  77.0 2.9 %collective-permute-start.17 = (f32[1,8,1,64]{3,1,2,0:T(8,128)S(1)}, f32[1,8,1,64]{3,1,2,0:T(8,128)S(1)}, u32[]{:S(2)}, u32[]{:S(2)}) collective-permute-start(f32[1,8,1,64]{3,1,2,0:T(8,128)S(1)} %get-tuple-element.422), channel_id=1, source_target_pairs={{0,6},{1,7},{2,0},{3,1},{4,2},{5,3},{6,4},{7,5},{8,14},{9,15},{10,... | collective-permute-start | bytes 6152 | tf_op jit(solution)/shard_map/ppermute | solution.py:16
  79.9 0.9 collective-permute-start.18
  80.8 3.8 %collective-permute-start.19 = (f32[1,8,8,1]{3,1,2,0:T(8,128)S(1)}, f32[1,8,8,1]{3,1,2,0:T(8,128)S(1)}, u32[]{:S(2)}, u32[]{:S(2)}) collective-permute-start(f32[1,8,8,1]{3,1,2,0:T(8,128)S(1)} %get-tuple-element.423), channel_id=1, source_target_pairs={{0,7},{1,0},{2,1},{3,2},{4,3},{5,4},{6,5},{7,6},{8,15},{9,8},{10,9... | collective-permute-start | bytes 776 | tf_op jit(solution)/shard_map/ppermute | solution.py:16
  84.6 2.0 collective-permute-done.18
  87.8 1.1 collective-permute-start.20
  89.0 2.9 %collective-permute-start.22 = (f32[1,8,1,64]{3,1,2,0:T(8,128)S(1)}, f32[1,8,1,64]{3,1,2,0:T(8,128)S(1)}, u32[]{:S(2)}, u32[]{:S(2)}) collective-permute-start(f32[1,8,1,64]{3,1,2,0:T(8,128)S(1)} %get-tuple-element.400), channel_id=1, source_target_pairs={{0,6},{1,7},{2,0},{3,1},{4,2},{5,3},{6,4},{7,5},{8,14},{9,15},{10,... | collective-permute-start | bytes 6152 | tf_op jit(solution)/shard_map/ppermute | solution.py:16
  91.8 1.4 collective-permute-start.23
  93.2 3.4 %collective-permute-start.24 = (f32[1,8,8,1]{3,1,2,0:T(8,128)S(1)}, f32[1,8,8,1]{3,1,2,0:T(8,128)S(1)}, u32[]{:S(2)}, u32[]{:S(2)}) collective-permute-start(f32[1,8,8,1]{3,1,2,0:T(8,128)S(1)} %get-tuple-element.405), channel_id=1, source_target_pairs={{0,7},{1,0},{2,1},{3,2},{4,3},{5,4},{6,5},{7,6},{8,15},{9,8},{10,9... | collective-permute-start | bytes 776 | tf_op jit(solution)/shard_map/ppermute | solution.py:16
  96.6 1.9 collective-permute-done.23
  103.4 1.5 collective-permute-start.26
  105.2 3.5 %collective-permute-start.28 = (f32[2,4,4,32]{3,2,1,0:T(4,128)S(1)}, f32[2,4,4,32]{3,2,1,0:T(4,128)S(1)}, u32[]{:S(2)}, u32[]{:S(2)}) collective-permute-start(f32[2,4,4,32]{3,2,1,0:T(4,128)S(1)} %pad_maximum_fusion.26), channel_id=1, source_target_pairs={{0,4},{1,5},{2,6},{3,7},{4,0},{5,1},{6,2},{7,3},{8,12},{9,13},{10,... | collective-permute-start | bytes 12296 | tf_op jit(solution)/shard_map/ppermute | solution.py:16
  108.7 3.6 %collective-permute-start.29 = (f32[2,4,4,32]{3,2,1,0:T(4,128)S(1)}, f32[2,4,4,32]{3,2,1,0:T(4,128)S(1)}, u32[]{:S(2)}, u32[]{:S(2)}) collective-permute-start(f32[2,4,4,32]{3,2,1,0:T(4,128)S(1)} %pad_maximum_fusion.26), channel_id=1, source_target_pairs={{0,5},{1,6},{2,7},{3,0},{4,1},{5,2},{6,3},{7,4},{8,13},{9,14},{10,... | collective-permute-start | bytes 12296 | tf_op jit(solution)/shard_map/ppermute | solution.py:16
  112.4 1.5 collective-permute-start.31
  113.9 2.2 %collective-permute-done.30 = f32[2,4,4,32]{3,2,1,0:T(4,128)S(1)} collective-permute-done((f32[2,4,4,32]{3,2,1,0:T(4,128)S(1)}, f32[2,4,4,32]{3,2,1,0:T(4,128)S(1)}, u32[]{:S(2)}, u32[]{:S(2)}) %collective-permute-start.30) | collective-permute-done | bytes 4128 | tf_op jit(solution)/shard_map/ppermute | solution.py:16
  116.4 0.9 gather_fusion
  129.7 0.8 copy.1415
  133.2 0.8 copy.1422
  152.0 1.3 collective-permute-start.32
  153.3 0.8 collective-permute-start.35
  154.1 3.9 %collective-permute-start.36 = (f32[1,8,8,1]{3,1,2,0:T(8,128)S(1)}, f32[1,8,8,1]{3,1,2,0:T(8,128)S(1)}, u32[]{:S(2)}, u32[]{:S(2)}) collective-permute-start(f32[1,8,8,1]{3,1,2,0:T(8,128)S(1)} %get-tuple-element.267), channel_id=1, source_target_pairs={{0,7},{1,0},{2,1},{3,2},{4,3},{5,4},{6,5},{7,6},{8,15},{9,8},{10,9... | collective-permute-start | bytes 776 | tf_op jit(solution)/shard_map/ppermute | solution.py:16
  158.1 3.8 %collective-permute-start.34 = (f32[1,8,1,64]{3,1,2,0:T(8,128)S(1)}, f32[1,8,1,64]{3,1,2,0:T(8,128)S(1)}, u32[]{:S(2)}, u32[]{:S(2)}) collective-permute-start(f32[1,8,1,64]{3,1,2,0:T(8,128)S(1)} %get-tuple-element.269), channel_id=1, source_target_pairs={{0,6},{1,7},{2,0},{3,1},{4,2},{5,3},{6,4},{7,5},{8,14},{9,15},{10,... | collective-permute-start | bytes 6152 | tf_op jit(solution)/shard_map/ppermute | solution.py:16
  162.4 1.0 collective-permute-done.33
  164.9 1.6 collective-permute-start.41
  166.9 3.8 %collective-permute-start.39 = (f32[1,8,1,64]{3,1,2,0:T(8,128)S(1)}, f32[1,8,1,64]{3,1,2,0:T(8,128)S(1)}, u32[]{:S(2)}, u32[]{:S(2)}) collective-permute-start(f32[1,8,1,64]{3,1,2,0:T(8,128)S(1)} %get-tuple-element.251), channel_id=1, source_target_pairs={{0,6},{1,7},{2,0},{3,1},{4,2},{5,3},{6,4},{7,5},{8,14},{9,15},{10,... | collective-permute-start | bytes 6152 | tf_op jit(solution)/shard_map/ppermute | solution.py:16
  172.3 0.8 collective-permute-done.40
  174.6 1.6 collective-permute-done.38
  179.3 1.0 collective-permute-start.45
  180.3 3.8 %collective-permute-start.46 = (f32[1,16,16,1]{3,2,1,0:T(8,128)S(1)}, f32[1,16,16,1]{3,2,1,0:T(8,128)S(1)}, u32[]{:S(2)}, u32[]{:S(2)}) collective-permute-start(f32[1,16,16,1]{3,2,1,0:T(8,128)S(1)} %get-tuple-element.79), channel_id=1, source_target_pairs={{0,7},{1,0},{2,1},{3,2},{4,3},{5,4},{6,5},{7,6},{8,15},{9,8},{10,9... | collective-permute-start | bytes 3080 | tf_op jit(solution)/shard_map/ppermute | solution.py:16
  184.4 3.5 %collective-permute-start.44 = (f32[1,16,1,128]{3,1,2,0:T(8,128)S(1)}, f32[1,16,1,128]{3,1,2,0:T(8,128)S(1)}, u32[]{:S(2)}, u32[]{:S(2)}) collective-permute-start(f32[1,16,1,128]{3,1,2,0:T(8,128)S(1)} %bitcast.738), channel_id=1, source_target_pairs={{0,6},{1,7},{2,0},{3,1},{4,2},{5,3},{6,4},{7,5},{8,14},{9,15},{10,... | collective-permute-start | bytes 24584 | tf_op jit(solution)/shard_map/ppermute | solution.py:16
  188.7 0.9 collective-permute-done.43
  190.1 4.7 %collective-permute-start.51 = (f32[1,16,16,1]{3,1,2,0:T(8,128)S(1)}, f32[1,16,16,1]{3,1,2,0:T(8,128)S(1)}, u32[]{:S(2)}, u32[]{:S(2)}) collective-permute-start(f32[1,16,16,1]{3,1,2,0:T(8,128)S(1)} %get-tuple-element.67), channel_id=1, source_target_pairs={{0,7},{1,0},{2,1},{3,2},{4,3},{5,4},{6,5},{7,6},{8,15},{9,8},{10,9... | collective-permute-start | bytes 3080 | tf_op jit(solution)/shard_map/ppermute | solution.py:16
  195.7 2.6 %collective-permute-start.48 = (f32[1,16,1,128]{3,1,2,0:T(8,128)S(1)}, f32[1,16,1,128]{3,1,2,0:T(8,128)S(1)}, u32[]{:S(2)}, u32[]{:S(2)}) collective-permute-start(f32[1,16,1,128]{3,1,2,0:T(8,128)S(1)} %get-tuple-element.72), channel_id=1, source_target_pairs={{0,2},{1,3},{2,4},{3,5},{4,6},{5,7},{6,0},{7,1},{8,10},{9,11},{10,... | collective-permute-start | bytes 24584 | tf_op jit(solution)/shard_map/ppermute | solution.py:16
  198.2 1.3 collective-permute-start.49
  200.2 0.9 collective-permute-done.48
  (738 shorter events, 84.7 us)
Async XLA Ops:
  9.0 37.8 %collective-permute-start = (f32[9216]{0:T(1024)S(1)}, f32[9216]{0:T(1024)S(1)}, u32[]{:S(2)}, u32[]{:S(2)}) collective-permute-start(f32[9216]{0:T(1024)S(1)} %constant_dynamic-update-slice_fusion.9), channel_id=1, source_target_pairs={{0,4},{1,5},{2,6},{3,7},{4,0},{5,1},{6,2},{7,3},{8,12},{9,13},{10,... | collective-permute-start | bytes 110600 | tf_op jit(solution)/shard_map/ppermute | solution.py:16
  18.3 24.7 %collective-permute-start.1 = (f32[4608]{0:T(1024)S(1)}, f32[4608]{0:T(1024)S(1)}, u32[]{:S(2)}, u32[]{:S(2)}) collective-permute-start(f32[4608]{0:T(1024)S(1)} %pad_maximum_fusion.22), channel_id=1, source_target_pairs={{0,2},{1,3},{2,4},{3,5},{4,6},{5,7},{6,0},{7,1},{8,10},{9,11},{10,... | collective-permute-start | bytes 55304 | tf_op jit(solution)/shard_map/ppermute | solution.py:16
  20.0 23.6 %collective-permute-start.2 = (f32[4608]{0:T(1024)S(1)}, f32[4608]{0:T(1024)S(1)}, u32[]{:S(2)}, u32[]{:S(2)}) collective-permute-start(f32[4608]{0:T(1024)S(1)} %pad_maximum_fusion.23), channel_id=1, source_target_pairs={{0,6},{1,7},{2,0},{3,1},{4,2},{5,3},{6,4},{7,5},{8,14},{9,15},{10,... | collective-permute-start | bytes 55304 | tf_op jit(solution)/shard_map/ppermute | solution.py:16
  23.2 15.2 %collective-permute-start.3 = (f32[576]{0:T(1024)S(1)}, f32[576]{0:T(1024)S(1)}, u32[]{:S(2)}, u32[]{:S(2)}) collective-permute-start(f32[576]{0:T(1024)S(1)} %pad_maximum_fusion.35), channel_id=1, source_target_pairs={{0,1},{1,2},{2,3},{3,4},{4,5},{5,6},{6,7},{7,0},{8,9},{9,10},{10,1... | collective-permute-start | bytes 6920 | tf_op jit(solution)/shard_map/ppermute | solution.py:16
  25.4 13.0 %collective-permute-start.4 = (f32[576]{0:T(1024)S(1)}, f32[576]{0:T(1024)S(1)}, u32[]{:S(2)}, u32[]{:S(2)}) collective-permute-start(f32[576]{0:T(1024)S(1)} %pad_maximum_fusion.36), channel_id=1, source_target_pairs={{0,7},{1,0},{2,1},{3,2},{4,3},{5,4},{6,5},{7,6},{8,15},{9,8},{10,9... | collective-permute-start | bytes 6920 | tf_op jit(solution)/shard_map/ppermute | solution.py:16
  49.0 9.6 %collective-permute-start.8 = (f32[1,16,16,1]{3,2,1,0:T(8,128)S(1)}, f32[1,16,16,1]{3,2,1,0:T(8,128)S(1)}, u32[]{:S(2)}, u32[]{:S(2)}) collective-permute-start(f32[1,16,16,1]{3,2,1,0:T(8,128)S(1)} %get-tuple-element.113), channel_id=1, source_target_pairs={{0,1},{1,2},{2,3},{3,4},{4,5},{5,6},{6,7},{7,0},{8,9},{9,10},{10,1... | collective-permute-start | bytes 3080 | tf_op jit(solution)/shard_map/ppermute | solution.py:16
  49.0 9.8 %collective-permute-start.9 = (f32[1,16,16,1]{3,2,1,0:T(8,128)S(1)}, f32[1,16,16,1]{3,2,1,0:T(8,128)S(1)}, u32[]{:S(2)}, u32[]{:S(2)}) collective-permute-start(f32[1,16,16,1]{3,2,1,0:T(8,128)S(1)} %get-tuple-element.112), channel_id=1, source_target_pairs={{0,7},{1,0},{2,1},{3,2},{4,3},{5,4},{6,5},{7,6},{8,15},{9,8},{10,9... | collective-permute-start | bytes 3080 | tf_op jit(solution)/shard_map/ppermute | solution.py:16
  53.8 5.4 %collective-permute-start.5 = (f32[1,2,16,128]{3,2,1,0:T(8,128)S(1)}, f32[1,2,16,128]{3,2,1,0:T(8,128)S(1)}, u32[]{:S(2)}, u32[]{:S(2)}) collective-permute-start(f32[1,2,16,128]{3,2,1,0:T(8,128)S(1)} %pad_maximum_fusion.24), channel_id=1, source_target_pairs={{0,4},{1,5},{2,6},{3,7},{4,0},{5,1},{6,2},{7,3},{8,12},{9,13},{10,... | collective-permute-start | bytes 49160 | tf_op jit(solution)/shard_map/ppermute | solution.py:16
  54.8 5.4 %collective-permute-start.6 = (f32[1,16,1,128]{3,1,2,0:T(8,128)S(1)}, f32[1,16,1,128]{3,1,2,0:T(8,128)S(1)}, u32[]{:S(2)}, u32[]{:S(2)}) collective-permute-start(f32[1,16,1,128]{3,1,2,0:T(8,128)S(1)} %bitcast.737), channel_id=1, source_target_pairs={{0,2},{1,3},{2,4},{3,5},{4,6},{5,7},{6,0},{7,1},{8,10},{9,11},{10,... | collective-permute-start | bytes 24584 | tf_op jit(solution)/shard_map/ppermute | solution.py:16
  54.8 5.4 %collective-permute-start.7 = (f32[1,16,1,128]{3,1,2,0:T(8,128)S(1)}, f32[1,16,1,128]{3,1,2,0:T(8,128)S(1)}, u32[]{:S(2)}, u32[]{:S(2)}) collective-permute-start(f32[1,16,1,128]{3,1,2,0:T(8,128)S(1)} %bitcast.736), channel_id=1, source_target_pairs={{0,6},{1,7},{2,0},{3,1},{4,2},{5,3},{6,4},{7,5},{8,14},{9,15},{10,... | collective-permute-start | bytes 24584 | tf_op jit(solution)/shard_map/ppermute | solution.py:16
  60.8 8.7 %collective-permute-start.13 = (f32[1,16,16,1]{3,2,1,0:T(8,128)S(1)}, f32[1,16,16,1]{3,2,1,0:T(8,128)S(1)}, u32[]{:S(2)}, u32[]{:S(2)}) collective-permute-start(f32[1,16,16,1]{3,2,1,0:T(8,128)S(1)} %get-tuple-element.101), channel_id=1, source_target_pairs={{0,1},{1,2},{2,3},{3,4},{4,5},{5,6},{6,7},{7,0},{8,9},{9,10},{10,1... | collective-permute-start | bytes 3080 | tf_op jit(solution)/shard_map/ppermute | solution.py:16
  60.8 9.3 %collective-permute-start.14 = (f32[1,16,16,1]{3,2,1,0:T(8,128)S(1)}, f32[1,16,16,1]{3,2,1,0:T(8,128)S(1)}, u32[]{:S(2)}, u32[]{:S(2)}) collective-permute-start(f32[1,16,16,1]{3,2,1,0:T(8,128)S(1)} %get-tuple-element.100), channel_id=1, source_target_pairs={{0,7},{1,0},{2,1},{3,2},{4,3},{5,4},{6,5},{7,6},{8,15},{9,8},{10,9... | collective-permute-start | bytes 3080 | tf_op jit(solution)/shard_map/ppermute | solution.py:16
  65.5 5.3 %collective-permute-start.10 = (f32[1,2,16,128]{3,2,1,0:T(8,128)S(1)}, f32[1,2,16,128]{3,2,1,0:T(8,128)S(1)}, u32[]{:S(2)}, u32[]{:S(2)}) collective-permute-start(f32[1,2,16,128]{3,2,1,0:T(8,128)S(1)} %pad_maximum_fusion.25), channel_id=1, source_target_pairs={{0,4},{1,5},{2,6},{3,7},{4,0},{5,1},{6,2},{7,3},{8,12},{9,13},{10,... | collective-permute-start | bytes 49160 | tf_op jit(solution)/shard_map/ppermute | solution.py:16
  65.6 5.9 %collective-permute-start.11 = (f32[1,16,1,128]{3,1,2,0:T(8,128)S(1)}, f32[1,16,1,128]{3,1,2,0:T(8,128)S(1)}, u32[]{:S(2)}, u32[]{:S(2)}) collective-permute-start(f32[1,16,1,128]{3,1,2,0:T(8,128)S(1)} %bitcast.741), channel_id=1, source_target_pairs={{0,2},{1,3},{2,4},{3,5},{4,6},{5,7},{6,0},{7,1},{8,10},{9,11},{10,... | collective-permute-start | bytes 24584 | tf_op jit(solution)/shard_map/ppermute | solution.py:16
  76.0 11.3 %collective-permute-start.16 = (f32[1,8,1,64]{3,1,2,0:T(8,128)S(1)}, f32[1,8,1,64]{3,1,2,0:T(8,128)S(1)}, u32[]{:S(2)}, u32[]{:S(2)}) collective-permute-start(f32[1,8,1,64]{3,1,2,0:T(8,128)S(1)} %get-tuple-element.421), channel_id=1, source_target_pairs={{0,2},{1,3},{2,4},{3,5},{4,6},{5,7},{6,0},{7,1},{8,10},{9,11},{10,... | collective-permute-start | bytes 6152 | tf_op jit(solution)/shard_map/ppermute | solution.py:16
  77.0 10.4 %collective-permute-start.17 = (f32[1,8,1,64]{3,1,2,0:T(8,128)S(1)}, f32[1,8,1,64]{3,1,2,0:T(8,128)S(1)}, u32[]{:S(2)}, u32[]{:S(2)}) collective-permute-start(f32[1,8,1,64]{3,1,2,0:T(8,128)S(1)} %get-tuple-element.422), channel_id=1, source_target_pairs={{0,6},{1,7},{2,0},{3,1},{4,2},{5,3},{6,4},{7,5},{8,14},{9,15},{10,... | collective-permute-start | bytes 6152 | tf_op jit(solution)/shard_map/ppermute | solution.py:16
  79.9 7.5 %collective-permute-start.15 = (f32[1,2,8,64]{3,2,1,0:T(8,128)S(1)}, f32[1,2,8,64]{3,2,1,0:T(8,128)S(1)}, u32[]{:S(2)}, u32[]{:S(2)}) collective-permute-start(f32[1,2,8,64]{3,2,1,0:T(8,128)S(1)} %pad_maximum_fusion.29), channel_id=1, source_target_pairs={{0,4},{1,5},{2,6},{3,7},{4,0},{5,1},{6,2},{7,3},{8,12},{9,13},{10,... | collective-permute-start | bytes 12296 | tf_op jit(solution)/shard_map/ppermute | solution.py:16
  79.9 6.8 %collective-permute-start.18 = (f32[1,8,8,1]{3,1,2,0:T(8,128)S(1)}, f32[1,8,8,1]{3,1,2,0:T(8,128)S(1)}, u32[]{:S(2)}, u32[]{:S(2)}) collective-permute-start(f32[1,8,8,1]{3,1,2,0:T(8,128)S(1)} %get-tuple-element.424), channel_id=1, source_target_pairs={{0,1},{1,2},{2,3},{3,4},{4,5},{5,6},{6,7},{7,0},{8,9},{9,10},{10,1... | collective-permute-start | bytes 776 | tf_op jit(solution)/shard_map/ppermute | solution.py:16
  80.8 6.2 %collective-permute-start.19 = (f32[1,8,8,1]{3,1,2,0:T(8,128)S(1)}, f32[1,8,8,1]{3,1,2,0:T(8,128)S(1)}, u32[]{:S(2)}, u32[]{:S(2)}) collective-permute-start(f32[1,8,8,1]{3,1,2,0:T(8,128)S(1)} %get-tuple-element.423), channel_id=1, source_target_pairs={{0,7},{1,0},{2,1},{3,2},{4,3},{5,4},{6,5},{7,6},{8,15},{9,8},{10,9... | collective-permute-start | bytes 776 | tf_op jit(solution)/shard_map/ppermute | solution.py:16
  87.8 12.1 %collective-permute-start.21 = (f32[1,8,1,64]{3,1,2,0:T(8,128)S(1)}, f32[1,8,1,64]{3,1,2,0:T(8,128)S(1)}, u32[]{:S(2)}, u32[]{:S(2)}) collective-permute-start(f32[1,8,1,64]{3,1,2,0:T(8,128)S(1)} %get-tuple-element.399), channel_id=1, source_target_pairs={{0,2},{1,3},{2,4},{3,5},{4,6},{5,7},{6,0},{7,1},{8,10},{9,11},{10,... | collective-permute-start | bytes 6152 | tf_op jit(solution)/shard_map/ppermute | solution.py:16
  87.8 13.2 %collective-permute-start.20 = (f32[1,2,8,64]{3,2,1,0:T(8,128)S(1)}, f32[1,2,8,64]{3,2,1,0:T(8,128)S(1)}, u32[]{:S(2)}, u32[]{:S(2)}) collective-permute-start(f32[1,2,8,64]{3,2,1,0:T(8,128)S(1)} %pad_maximum_fusion.30), channel_id=1, source_target_pairs={{0,4},{1,5},{2,6},{3,7},{4,0},{5,1},{6,2},{7,3},{8,12},{9,13},{10,... | collective-permute-start | bytes 12296 | tf_op jit(solution)/shard_map/ppermute | solution.py:16
  89.0 11.5 %collective-permute-start.22 = (f32[1,8,1,64]{3,1,2,0:T(8,128)S(1)}, f32[1,8,1,64]{3,1,2,0:T(8,128)S(1)}, u32[]{:S(2)}, u32[]{:S(2)}) collective-permute-start(f32[1,8,1,64]{3,1,2,0:T(8,128)S(1)} %get-tuple-element.400), channel_id=1, source_target_pairs={{0,6},{1,7},{2,0},{3,1},{4,2},{5,3},{6,4},{7,5},{8,14},{9,15},{10,... | collective-permute-start | bytes 6152 | tf_op jit(solution)/shard_map/ppermute | solution.py:16
  91.8 6.6 %collective-permute-start.23 = (f32[1,8,8,1]{3,1,2,0:T(8,128)S(1)}, f32[1,8,8,1]{3,1,2,0:T(8,128)S(1)}, u32[]{:S(2)}, u32[]{:S(2)}) collective-permute-start(f32[1,8,8,1]{3,1,2,0:T(8,128)S(1)} %get-tuple-element.406), channel_id=1, source_target_pairs={{0,1},{1,2},{2,3},{3,4},{4,5},{5,6},{6,7},{7,0},{8,9},{9,10},{10,1... | collective-permute-start | bytes 776 | tf_op jit(solution)/shard_map/ppermute | solution.py:16
  93.2 6.0 %collective-permute-start.24 = (f32[1,8,8,1]{3,1,2,0:T(8,128)S(1)}, f32[1,8,8,1]{3,1,2,0:T(8,128)S(1)}, u32[]{:S(2)}, u32[]{:S(2)}) collective-permute-start(f32[1,8,8,1]{3,1,2,0:T(8,128)S(1)} %get-tuple-element.405), channel_id=1, source_target_pairs={{0,7},{1,0},{2,1},{3,2},{4,3},{5,4},{6,5},{7,6},{8,15},{9,8},{10,9... | collective-permute-start | bytes 776 | tf_op jit(solution)/shard_map/ppermute | solution.py:16
  103.3 9.0 %collective-permute-start.25 = (f32[2,4,4,32]{3,2,1,0:T(4,128)S(1)}, f32[2,4,4,32]{3,2,1,0:T(4,128)S(1)}, u32[]{:S(2)}, u32[]{:S(2)}) collective-permute-start(f32[2,4,4,32]{3,2,1,0:T(4,128)S(1)} %pad_maximum_fusion.26), channel_id=1, source_target_pairs={{0,1},{1,2},{2,3},{3,4},{4,5},{5,6},{6,7},{7,0},{8,9},{9,10},{10,1... | collective-permute-start | bytes 12296 | tf_op jit(solution)/shard_map/ppermute | solution.py:16
  103.4 9.0 %collective-permute-start.26 = (f32[2,4,4,32]{3,2,1,0:T(4,128)S(1)}, f32[2,4,4,32]{3,2,1,0:T(4,128)S(1)}, u32[]{:S(2)}, u32[]{:S(2)}) collective-permute-start(f32[2,4,4,32]{3,2,1,0:T(4,128)S(1)} %pad_maximum_fusion.26), channel_id=1, source_target_pairs={{0,2},{1,3},{2,4},{3,5},{4,6},{5,7},{6,0},{7,1},{8,10},{9,11},{10,... | collective-permute-start | bytes 12296 | tf_op jit(solution)/shard_map/ppermute | solution.py:16
  104.9 8.9 %collective-permute-start.27 = (f32[2,4,4,32]{3,2,1,0:T(4,128)S(1)}, f32[2,4,4,32]{3,2,1,0:T(4,128)S(1)}, u32[]{:S(2)}, u32[]{:S(2)}) collective-permute-start(f32[2,4,4,32]{3,2,1,0:T(4,128)S(1)} %pad_maximum_fusion.26), channel_id=1, source_target_pairs={{0,3},{1,4},{2,5},{3,6},{4,7},{5,0},{6,1},{7,2},{8,11},{9,12},{10,... | collective-permute-start | bytes 12296 | tf_op jit(solution)/shard_map/ppermute | solution.py:16
  105.2 8.6 %collective-permute-start.28 = (f32[2,4,4,32]{3,2,1,0:T(4,128)S(1)}, f32[2,4,4,32]{3,2,1,0:T(4,128)S(1)}, u32[]{:S(2)}, u32[]{:S(2)}) collective-permute-start(f32[2,4,4,32]{3,2,1,0:T(4,128)S(1)} %pad_maximum_fusion.26), channel_id=1, source_target_pairs={{0,4},{1,5},{2,6},{3,7},{4,0},{5,1},{6,2},{7,3},{8,12},{9,13},{10,... | collective-permute-start | bytes 12296 | tf_op jit(solution)/shard_map/ppermute | solution.py:16
  108.7 5.2 %collective-permute-start.29 = (f32[2,4,4,32]{3,2,1,0:T(4,128)S(1)}, f32[2,4,4,32]{3,2,1,0:T(4,128)S(1)}, u32[]{:S(2)}, u32[]{:S(2)}) collective-permute-start(f32[2,4,4,32]{3,2,1,0:T(4,128)S(1)} %pad_maximum_fusion.26), channel_id=1, source_target_pairs={{0,5},{1,6},{2,7},{3,0},{4,1},{5,2},{6,3},{7,4},{8,13},{9,14},{10,... | collective-permute-start | bytes 12296 | tf_op jit(solution)/shard_map/ppermute | solution.py:16
  152.0 10.4 %collective-permute-start.32 = (f32[1,2,8,64]{3,2,1,0:T(8,128)S(1)}, f32[1,2,8,64]{3,2,1,0:T(8,128)S(1)}, u32[]{:S(2)}, u32[]{:S(2)}) collective-permute-start(f32[1,2,8,64]{3,2,1,0:T(8,128)S(1)} %pad_maximum_fusion.33), channel_id=1, source_target_pairs={{0,4},{1,5},{2,6},{3,7},{4,0},{5,1},{6,2},{7,3},{8,12},{9,13},{10,... | collective-permute-start | bytes 12296 | tf_op jit(solution)/shard_map/ppermute | solution.py:16
  153.3 8.6 %collective-permute-start.35 = (f32[1,8,8,1]{3,1,2,0:T(8,128)S(1)}, f32[1,8,8,1]{3,1,2,0:T(8,128)S(1)}, u32[]{:S(2)}, u32[]{:S(2)}) collective-permute-start(f32[1,8,8,1]{3,1,2,0:T(8,128)S(1)} %get-tuple-element.268), channel_id=1, source_target_pairs={{0,1},{1,2},{2,3},{3,4},{4,5},{5,6},{6,7},{7,0},{8,9},{9,10},{10,1... | collective-permute-start | bytes 776 | tf_op jit(solution)/shard_map/ppermute | solution.py:16
  154.1 8.0 %collective-permute-start.36 = (f32[1,8,8,1]{3,1,2,0:T(8,128)S(1)}, f32[1,8,8,1]{3,1,2,0:T(8,128)S(1)}, u32[]{:S(2)}, u32[]{:S(2)}) collective-permute-start(f32[1,8,8,1]{3,1,2,0:T(8,128)S(1)} %get-tuple-element.267), channel_id=1, source_target_pairs={{0,7},{1,0},{2,1},{3,2},{4,3},{5,4},{6,5},{7,6},{8,15},{9,8},{10,9... | collective-permute-start | bytes 776 | tf_op jit(solution)/shard_map/ppermute | solution.py:16
  158.1 5.4 %collective-permute-start.33 = (f32[1,8,1,64]{3,1,2,0:T(8,128)S(1)}, f32[1,8,1,64]{3,1,2,0:T(8,128)S(1)}, u32[]{:S(2)}, u32[]{:S(2)}) collective-permute-start(f32[1,8,1,64]{3,1,2,0:T(8,128)S(1)} %get-tuple-element.270), channel_id=1, source_target_pairs={{0,2},{1,3},{2,4},{3,5},{4,6},{5,7},{6,0},{7,1},{8,10},{9,11},{10,... | collective-permute-start | bytes 6152 | tf_op jit(solution)/shard_map/ppermute | solution.py:16
  158.1 5.4 %collective-permute-start.34 = (f32[1,8,1,64]{3,1,2,0:T(8,128)S(1)}, f32[1,8,1,64]{3,1,2,0:T(8,128)S(1)}, u32[]{:S(2)}, u32[]{:S(2)}) collective-permute-start(f32[1,8,1,64]{3,1,2,0:T(8,128)S(1)} %get-tuple-element.269), channel_id=1, source_target_pairs={{0,6},{1,7},{2,0},{3,1},{4,2},{5,3},{6,4},{7,5},{8,14},{9,15},{10,... | collective-permute-start | bytes 6152 | tf_op jit(solution)/shard_map/ppermute | solution.py:16
  164.9 6.6 %collective-permute-start.41 = (f32[1,8,8,1]{3,1,2,0:T(8,128)S(1)}, f32[1,8,8,1]{3,1,2,0:T(8,128)S(1)}, u32[]{:S(2)}, u32[]{:S(2)}) collective-permute-start(f32[1,8,8,1]{3,1,2,0:T(8,128)S(1)} %get-tuple-element.249), channel_id=1, source_target_pairs={{0,7},{1,0},{2,1},{3,2},{4,3},{5,4},{6,5},{7,6},{8,15},{9,8},{10,9... | collective-permute-start | bytes 776 | tf_op jit(solution)/shard_map/ppermute | solution.py:16
  166.4 6.7 %collective-permute-start.40 = (f32[1,8,8,1]{3,1,2,0:T(8,128)S(1)}, f32[1,8,8,1]{3,1,2,0:T(8,128)S(1)}, u32[]{:S(2)}, u32[]{:S(2)}) collective-permute-start(f32[1,8,8,1]{3,1,2,0:T(8,128)S(1)} %get-tuple-element.250), channel_id=1, source_target_pairs={{0,1},{1,2},{2,3},{3,4},{4,5},{5,6},{6,7},{7,0},{8,9},{9,10},{10,1... | collective-permute-start | bytes 776 | tf_op jit(solution)/shard_map/ppermute | solution.py:16
  166.9 7.5 %collective-permute-start.39 = (f32[1,8,1,64]{3,1,2,0:T(8,128)S(1)}, f32[1,8,1,64]{3,1,2,0:T(8,128)S(1)}, u32[]{:S(2)}, u32[]{:S(2)}) collective-permute-start(f32[1,8,1,64]{3,1,2,0:T(8,128)S(1)} %get-tuple-element.251), channel_id=1, source_target_pairs={{0,6},{1,7},{2,0},{3,1},{4,2},{5,3},{6,4},{7,5},{8,14},{9,15},{10,... | collective-permute-start | bytes 6152 | tf_op jit(solution)/shard_map/ppermute | solution.py:16
  170.8 5.4 %collective-permute-start.38 = (f32[1,8,1,64]{3,1,2,0:T(8,128)S(1)}, f32[1,8,1,64]{3,1,2,0:T(8,128)S(1)}, u32[]{:S(2)}, u32[]{:S(2)}) collective-permute-start(f32[1,8,1,64]{3,1,2,0:T(8,128)S(1)} %get-tuple-element.252), channel_id=1, source_target_pairs={{0,2},{1,3},{2,4},{3,5},{4,6},{5,7},{6,0},{7,1},{8,10},{9,11},{10,... | collective-permute-start | bytes 6152 | tf_op jit(solution)/shard_map/ppermute | solution.py:16
  170.8 6.9 %collective-permute-start.37 = (f32[1,2,8,64]{3,1,2,0:T(2,128)S(1)}, f32[1,2,8,64]{3,1,2,0:T(2,128)S(1)}, u32[]{:S(2)}, u32[]{:S(2)}) collective-permute-start(f32[1,2,8,64]{3,1,2,0:T(2,128)S(1)} %pad_maximum_fusion.34), channel_id=1, source_target_pairs={{0,4},{1,5},{2,6},{3,7},{4,0},{5,1},{6,2},{7,3},{8,12},{9,13},{10,... | collective-permute-start | bytes 12296 | tf_op jit(solution)/shard_map/ppermute | solution.py:16
  179.3 8.7 %collective-permute-start.45 = (f32[1,16,16,1]{3,2,1,0:T(8,128)S(1)}, f32[1,16,16,1]{3,2,1,0:T(8,128)S(1)}, u32[]{:S(2)}, u32[]{:S(2)}) collective-permute-start(f32[1,16,16,1]{3,2,1,0:T(8,128)S(1)} %get-tuple-element.80), channel_id=1, source_target_pairs={{0,1},{1,2},{2,3},{3,4},{4,5},{5,6},{6,7},{7,0},{8,9},{9,10},{10,1... | collective-permute-start | bytes 3080 | tf_op jit(solution)/shard_map/ppermute | solution.py:16
  180.3 8.0 %collective-permute-start.46 = (f32[1,16,16,1]{3,2,1,0:T(8,128)S(1)}, f32[1,16,16,1]{3,2,1,0:T(8,128)S(1)}, u32[]{:S(2)}, u32[]{:S(2)}) collective-permute-start(f32[1,16,16,1]{3,2,1,0:T(8,128)S(1)} %get-tuple-element.79), channel_id=1, source_target_pairs={{0,7},{1,0},{2,1},{3,2},{4,3},{5,4},{6,5},{7,6},{8,15},{9,8},{10,9... | collective-permute-start | bytes 3080 | tf_op jit(solution)/shard_map/ppermute | solution.py:16
  184.0 4.6 %collective-permute-start.42 = (f32[1,2,16,128]{3,2,1,0:T(8,128)S(1)}, f32[1,2,16,128]{3,2,1,0:T(8,128)S(1)}, u32[]{:S(2)}, u32[]{:S(2)}) collective-permute-start(f32[1,2,16,128]{3,2,1,0:T(8,128)S(1)} %pad_maximum_fusion.27), channel_id=1, source_target_pairs={{0,4},{1,5},{2,6},{3,7},{4,0},{5,1},{6,2},{7,3},{8,12},{9,13},{10,... | collective-permute-start | bytes 49160 | tf_op jit(solution)/shard_map/ppermute | solution.py:16
  184.1 5.5 %collective-permute-start.43 = (f32[1,16,1,128]{3,1,2,0:T(8,128)S(1)}, f32[1,16,1,128]{3,1,2,0:T(8,128)S(1)}, u32[]{:S(2)}, u32[]{:S(2)}) collective-permute-start(f32[1,16,1,128]{3,1,2,0:T(8,128)S(1)} %bitcast.739), channel_id=1, source_target_pairs={{0,2},{1,3},{2,4},{3,5},{4,6},{5,7},{6,0},{7,1},{8,10},{9,11},{10,... | collective-permute-start | bytes 24584 | tf_op jit(solution)/shard_map/ppermute | solution.py:16
  184.4 5.2 %collective-permute-start.44 = (f32[1,16,1,128]{3,1,2,0:T(8,128)S(1)}, f32[1,16,1,128]{3,1,2,0:T(8,128)S(1)}, u32[]{:S(2)}, u32[]{:S(2)}) collective-permute-start(f32[1,16,1,128]{3,1,2,0:T(8,128)S(1)} %bitcast.738), channel_id=1, source_target_pairs={{0,6},{1,7},{2,0},{3,1},{4,2},{5,3},{6,4},{7,5},{8,14},{9,15},{10,... | collective-permute-start | bytes 24584 | tf_op jit(solution)/shard_map/ppermute | solution.py:16
  190.1 9.4 %collective-permute-start.50 = (f32[1,16,16,1]{3,1,2,0:T(8,128)S(1)}, f32[1,16,16,1]{3,1,2,0:T(8,128)S(1)}, u32[]{:S(2)}, u32[]{:S(2)}) collective-permute-start(f32[1,16,16,1]{3,1,2,0:T(8,128)S(1)} %get-tuple-element.68), channel_id=1, source_target_pairs={{0,1},{1,2},{2,3},{3,4},{4,5},{5,6},{6,7},{7,0},{8,9},{9,10},{10,1... | collective-permute-start | bytes 3080 | tf_op jit(solution)/shard_map/ppermute | solution.py:16
  190.1 9.7 %collective-permute-start.51 = (f32[1,16,16,1]{3,1,2,0:T(8,128)S(1)}, f32[1,16,16,1]{3,1,2,0:T(8,128)S(1)}, u32[]{:S(2)}, u32[]{:S(2)}) collective-permute-start(f32[1,16,16,1]{3,1,2,0:T(8,128)S(1)} %get-tuple-element.67), channel_id=1, source_target_pairs={{0,7},{1,0},{2,1},{3,2},{4,3},{5,4},{6,5},{7,6},{8,15},{9,8},{10,9... | collective-permute-start | bytes 3080 | tf_op jit(solution)/shard_map/ppermute | solution.py:16
  194.9 5.3 %collective-permute-start.47 = (f32[1,2,16,128]{3,1,2,0:T(2,128)S(1)}, f32[1,2,16,128]{3,1,2,0:T(2,128)S(1)}, u32[]{:S(2)}, u32[]{:S(2)}) collective-permute-start(f32[1,2,16,128]{3,1,2,0:T(2,128)S(1)} %pad_maximum_fusion.28), channel_id=1, source_target_pairs={{0,4},{1,5},{2,6},{3,7},{4,0},{5,1},{6,2},{7,3},{8,12},{9,13},{10,... | collective-permute-start | bytes 49160 | tf_op jit(solution)/shard_map/ppermute | solution.py:16
  195.7 5.4 %collective-permute-start.48 = (f32[1,16,1,128]{3,1,2,0:T(8,128)S(1)}, f32[1,16,1,128]{3,1,2,0:T(8,128)S(1)}, u32[]{:S(2)}, u32[]{:S(2)}) collective-permute-start(f32[1,16,1,128]{3,1,2,0:T(8,128)S(1)} %get-tuple-element.72), channel_id=1, source_target_pairs={{0,2},{1,3},{2,4},{3,5},{4,6},{5,7},{6,0},{7,1},{8,10},{9,11},{10,... | collective-permute-start | bytes 24584 | tf_op jit(solution)/shard_map/ppermute | solution.py:16
  (107 other events, 114.9 us)
where the time goes:
time: 204 us; the launch traced here: 203 us
  starting transfers between devices  91.6 us (45%)
  local copies, waits for them, and re-layouts  69.7 us (34%)
  other arithmetic  21.2 us (10%)
  waiting for transfers between devices  13.9 us (7%)
  matrix products  3.42 us (2%)
  between operations  3.03 us (1%)
    ppermute x52, starting transfers between devices, shifted(): lax.ppermute(shard, axis, [(i, (i + by) % peers) for i in range(peers)])  91.6 us
    unnamed x220, local copies, waits for them, and re-layouts  24.9 us
    ppermute x52, waiting for transfers between devices, shifted(): lax.ppermute(shard, axis, [(i, (i + by) % peers) for i in range(peers)])  13.9 us
    add x2, other arithmetic, shards(): permeab = permeab + jnp.where(classes == number, class_values[number], 0.0)  10.9 us
  transfers between devices with their start and end apart: 52, of which 13 were waited for; matrix products, arithmetic and copies ran while one was open for 15% of the time, Pallas kernels for 0%

commit v1 on v0

--- a/solution.py
+++ b/solution.py
@@ -271,10 +271,9 @@
     )
 
     values = guess[0]
-    coarse_perm = coarsen(permeab)
-    first = exchange_mixed([permeab, values, coarse_perm], per_side)
-    face_coefs, diagonal = coefficients(permeab, with_faces(permeab, first[0]), 1.0)
-    values = smooth(values, source, face_coefs, diagonal, 1.0, with_faces(values, first[1]))
+    first = exchange(jnp.stack([permeab, values]), per_side)
+    face_coefs, diagonal = coefficients(permeab, with_faces(permeab, pick(first, 0)), 1.0)
+    values = smooth(values, source, face_coefs, diagonal, 1.0, with_faces(values, pick(first, 1)))
     for sweep_no in range(SWEEPS - 1):
         faces = pick(exchange(values[None], per_side), 0)
         values = smooth(values, source, face_coefs, diagonal, 1.0, with_faces(values, faces))
@@ -282,34 +281,15 @@
     leftover = source - operate(values, with_faces(values, stored_faces), face_coefs, 1.0)
     stored = values
 
-    scaling = 0.25
-    right_1 = coarsen(leftover)
-    coefs_1, diagonal_1 = coefficients(coarse_perm, with_faces(coarse_perm, first[2]), scaling)
-    values_1 = OMEGA * right_1 / diagonal_1
-    for sweep_no in range(SWEEPS - 1):
-        faces = pick(exchange(values_1[None], per_side), 0)
-        values_1 = smooth(values_1, right_1, coefs_1, diagonal_1, scaling, with_faces(values_1, faces))
-    stored_faces_1 = pick(exchange(values_1[None], per_side), 0)
-    leftover_1 = right_1 - operate(values_1, with_faces(values_1, stored_faces_1), coefs_1, scaling)
-    stored_1 = values_1
-
-    gathered = gather_rows(jnp.stack([coarsen(coarse_perm), coarsen(leftover_1)]), per_side)
-    correction_all = global_cycle(gathered[:, 1], gathered[:, 0], 2, per_side)
+    gathered = gather_rows(jnp.stack([coarsen(permeab), coarsen(leftover)]), per_side)
+    correction_all = global_cycle(gathered[:, 1], gathered[:, 0], 1, per_side)
 
     correction = lax.dynamic_index_in_dim(correction_all, my_row, 0, keepdims=False)
-    values_1 = stored_1 + refine(correction)
+    values = stored + refine(correction)
     faces = [
         mine + theirs
-        for mine, theirs in zip(stored_faces_1, refined_faces(correction_all, my_row, per_side))
-    ]
-    values_1 = smooth(values_1, right_1, coefs_1, diagonal_1, scaling, with_faces(values_1, faces))
-    for sweep_no in range(SWEEPS - 1):
-        faces = pick(exchange(values_1[None], per_side), 0)
-        values_1 = smooth(values_1, right_1, coefs_1, diagonal_1, scaling, with_faces(values_1, faces))
-    coarse_faces = pick(exchange(values_1[None], per_side), 0)
-
-    values = stored + refine(values_1)
-    faces = [mine + refine_face_of(theirs) for mine, theirs in zip(stored_faces, coarse_faces)]
+        for mine, theirs in zip(stored_faces, refined_faces(correction_all, my_row, per_side))
+    ]
     values = smooth(values, source, face_coefs, diagonal, 1.0, with_faces(values, faces))
     for sweep_no in range(SWEEPS - 1):
         faces = pick(exchange(values[None], per_side), 0)

time: 204 us -> 214 us (1.049)
  starting transfers between devices: 91.6 us -> 63.2 us
  local copies, waits for them, and re-layouts: 69.7 us -> 85.4 us
  other arithmetic: 21.2 us -> 34.3 us
  matrix products: 3.42 us -> 12.4 us
    ppermute x52 -> x32, starting transfers between devices: 91.6 us -> 63.2 us  [shifted(): lax.ppermute(shard, axis, [(i, (i + by) % peers) for i in range(peers)])]
    unnamed x220 -> x181, local copies, waits for them, and re-layouts: 24.9 us -> 3.68 us
    concatenate x36 -> x16, local copies, waits for them, and re-layouts: 8.96 us -> 20.5 us  [the longest x4 5.73 us: rolled_faces(): jnp.concatenate([values[:, :, 1:], jnp.roll(values[:, :, :1], -per_side,...]
    add x9 -> x1, other arithmetic: 11 us -> 0.02 us  [shards(): values = stored + refine(correction)]
    dot_general x2 -> x4, matrix products: 0.63 us -> 7.96 us  [coarsen_all(): jnp.dot(values.reshape(count_b * size_x * size_y, size_z), pair_mean(size...]
    squeeze x0 -> x1, other arithmetic: none -> 6.28 us  [shards(): values = guess[0]]
    slice x8 -> x9, local copies, waits for them, and re-layouts: 0.37 us -> 6.1 us  [rolled_faces(): values[:, :, :, :-1]]
    slice x3 -> x10, local copies, waits for them, and re-layouts: 1.47 us -> 7.07 us  [rolled_faces(): values[:, :, :, 1:]]
  transfers between devices with their start and end apart: 52 -> 32, of which waited for: 13 -> 12; matrix products, arithmetic and copies ran while one was open for 15% -> 3% of each run, Pallas kernels for 0% -> 0%
where the time goes in v1:
time: 214 us; the launch traced here: 213 us
  local copies, waits for them, and re-layouts  85.4 us (40%)
  starting transfers between devices  63.2 us (30%)
  other arithmetic  34.3 us (16%)
  waiting for transfers between devices  13.9 us (6%)
  matrix products  12.4 us (6%)
  between operations  3.5 us (2%)
    ppermute x32, starting transfers between devices, shifted(): lax.ppermute(shard, axis, [(i, (i + by) % peers) for i in range(peers)])  63.2 us
    ppermute x32, waiting for transfers between devices, shifted(): lax.ppermute(shard, axis, [(i, (i + by) % peers) for i in range(peers)])  13.9 us
    dot_general x4, matrix products, coarsen_all(): jnp.dot(values.reshape(count_b * size_x * size_y, size_z), pair_mean(size...  7.96 us
    slice x10, local copies, waits for them, and re-layouts, rolled_faces(): values[:, :, :, 1:]  7.07 us
    add x14, other arithmetic, smooth(): values + OMEGA * (right_side - operate(values, neighbors, face_coefs, sca...  6.57 us
    squeeze x1, other arithmetic, shards(): values = guess[0]  6.28 us
    slice x9, local copies, waits for them, and re-layouts, rolled_faces(): values[:, :, :, :-1]  6.1 us
    concatenate x4, local copies, waits for them, and re-layouts, rolled_faces(): jnp.concatenate([values[:, :, 1:], jnp.roll(values[:, :, :1], -per_side,...  5.73 us
  transfers between devices with their start and end apart: 32, of which 12 were waited for; matrix products, arithmetic and copies ran while one was open for 3% of the time, Pallas kernels for 0%

profile of v1, /device:TPU:0, one launch (start us, length us, event | category | flops | bytes accessed | tf_op | source)
XLA Modules:
  0.0 212.6 jit_solution(18352670777439414417)
XLA Ops:
  0.6 1.6 fusion.708
  2.3 6.3 %copy_bitcast_fusion.3 = (f32[16,16,128]{2,0,1:T(8,128)S(1)}, f32[1,16,16,128]{3,1,2,0:T(8,128)S(1)}, f32[1,16,16,128]{3,1,2,0:T(8,128)S(1)}) fusion(f32[1,16,16,128]{3,2,1,0:T(8,128)} %param.9, f32[]{:T(128)} %bitcast.10, f32[]{:T(128)} %bitcast.9, f32[]{:T(128)} %bitcast.8, f32[]{:T(128)} %bitcast.7, f32[]{:T(128)} %bitcast.6, f32[]{:T(128)} %bitcast.5, ...), kind=kLoop, calls=%fused_computation.842 | loop fusion | flops 753664 | bytes 655392 | tf_op jit(solution)/shard_map/squeeze | solution.py:273
  8.6 4.1 %collective-permute-start = (f32[2,2,16,128]{3,1,2,0:T(2,128)S(1)}, f32[2,2,16,128]{3,1,2,0:T(2,128)S(1)}, u32[]{:S(2)}, u32[]{:S(2)}) collective-permute-start(f32[2,2,16,128]{3,1,2,0:T(2,128)S(1)} %fusion.350), channel_id=1, source_target_pairs={{0,4},{1,5},{2,6},{3,7},{4,0},{5,1},{6,2},{7,3},{8,12},{9,13},{10,... | collective-permute-start | bytes 98312 | tf_op jit(solution)/shard_map/ppermute | solution.py:16
  12.7 1.6 collective-permute-start.1
  14.3 2.2 %collective-permute-start.2 = (f32[2,16,1,128]{3,1,2,0:T(8,128)S(1)}, f32[2,16,1,128]{3,1,2,0:T(8,128)S(1)}, u32[]{:S(2)}, u32[]{:S(2)}) collective-permute-start(f32[2,16,1,128]{3,1,2,0:T(8,128)S(1)} %get-tuple-element.238), channel_id=1, source_target_pairs={{0,6},{1,7},{2,0},{3,1},{4,2},{5,3},{6,4},{7,5},{8,14},{9,15},{10,... | collective-permute-start | bytes 49160 | tf_op jit(solution)/shard_map/ppermute | solution.py:16
  16.7 1.6 collective-permute-start.3
  18.3 3.2 %collective-permute-start.4 = (f32[2,16,16,1]{3,1,2,0:T(8,128)S(1)}, f32[2,16,16,1]{3,1,2,0:T(8,128)S(1)}, u32[]{:S(2)}, u32[]{:S(2)}) collective-permute-start(f32[2,16,16,1]{3,1,2,0:T(8,128)S(1)} %get-tuple-element.236), channel_id=1, source_target_pairs={{0,7},{1,0},{2,1},{3,2},{4,3},{5,4},{6,5},{7,6},{8,15},{9,8},{10,9... | collective-permute-start | bytes 6152 | tf_op jit(solution)/shard_map/ppermute | solution.py:16
  23.8 4.8 %collective-permute-done.3 = f32[2,16,16,1]{3,1,2,0:T(8,128)S(1)} collective-permute-done((f32[2,16,16,1]{3,1,2,0:T(8,128)S(1)}, f32[2,16,16,1]{3,1,2,0:T(8,128)S(1)}, u32[]{:S(2)}, u32[]{:S(2)}) %collective-permute-start.3) | collective-permute-done | bytes 2080 | tf_op jit(solution)/shard_map/ppermute | solution.py:16
  28.6 2.2 %collective-permute-done.4 = f32[2,16,16,1]{3,1,2,0:T(8,128)S(1)} collective-permute-done((f32[2,16,16,1]{3,1,2,0:T(8,128)S(1)}, f32[2,16,16,1]{3,1,2,0:T(8,128)S(1)}, u32[]{:S(2)}, u32[]{:S(2)}) %collective-permute-start.4) | collective-permute-done | bytes 2080 | tf_op jit(solution)/shard_map/ppermute | solution.py:16
  33.7 4.4 %collective-permute-start.9 = (f32[1,16,16,1]{3,2,1,0:T(8,128)S(1)}, f32[1,16,16,1]{3,2,1,0:T(8,128)S(1)}, u32[]{:S(2)}, u32[]{:S(2)}) collective-permute-start(f32[1,16,16,1]{3,2,1,0:T(8,128)S(1)} %get-tuple-element.284), channel_id=1, source_target_pairs={{0,7},{1,0},{2,1},{3,2},{4,3},{5,4},{6,5},{7,6},{8,15},{9,8},{10,9... | collective-permute-start | bytes 3080 | tf_op jit(solution)/shard_map/ppermute | solution.py:16
  38.1 3.8 %collective-permute-start.7 = (f32[1,16,1,128]{3,1,2,0:T(8,128)S(1)}, f32[1,16,1,128]{3,1,2,0:T(8,128)S(1)}, u32[]{:S(2)}, u32[]{:S(2)}) collective-permute-start(f32[1,16,1,128]{3,1,2,0:T(8,128)S(1)} %bitcast.628), channel_id=1, source_target_pairs={{0,6},{1,7},{2,0},{3,1},{4,2},{5,3},{6,4},{7,5},{8,14},{9,15},{10,... | collective-permute-start | bytes 24584 | tf_op jit(solution)/shard_map/ppermute | solution.py:16
  45.5 4.1 %collective-permute-start.14 = (f32[1,16,16,1]{3,2,1,0:T(8,128)S(1)}, f32[1,16,16,1]{3,2,1,0:T(8,128)S(1)}, u32[]{:S(2)}, u32[]{:S(2)}) collective-permute-start(f32[1,16,16,1]{3,2,1,0:T(8,128)S(1)} %get-tuple-element.272), channel_id=1, source_target_pairs={{0,7},{1,0},{2,1},{3,2},{4,3},{5,4},{6,5},{7,6},{8,15},{9,8},{10,9... | collective-permute-start | bytes 3080 | tf_op jit(solution)/shard_map/ppermute | solution.py:16
  49.6 2.0 collective-permute-start.11
  51.6 1.9 collective-permute-start.12
  57.4 4.6 %collective-permute-start.17 = (f32[2,8,8,64]{3,2,1,0:T(8,128)S(1)}, f32[2,8,8,64]{3,2,1,0:T(8,128)S(1)}, u32[]{:S(2)}, u32[]{:S(2)}) collective-permute-start(f32[2,8,8,64]{3,2,1,0:T(8,128)S(1)} %pad_maximum_fusion.13), channel_id=1, source_target_pairs={{0,3},{1,4},{2,5},{3,6},{4,7},{5,0},{6,1},{7,2},{8,11},{9,12},{10,... | collective-permute-start | bytes 98312 | tf_op jit(solution)/shard_map/ppermute | solution.py:16
  61.9 2.9 %collective-permute-start.19 = (f32[2,8,8,64]{3,2,1,0:T(8,128)S(1)}, f32[2,8,8,64]{3,2,1,0:T(8,128)S(1)}, u32[]{:S(2)}, u32[]{:S(2)}) collective-permute-start(f32[2,8,8,64]{3,2,1,0:T(8,128)S(1)} %pad_maximum_fusion.13), channel_id=1, source_target_pairs={{0,5},{1,6},{2,7},{3,0},{4,1},{5,2},{6,3},{7,4},{8,13},{9,14},{10,... | collective-permute-start | bytes 98312 | tf_op jit(solution)/shard_map/ppermute | solution.py:16
  65.6 1.8 collective-permute-start.21
  92.6 4.6 %fusion.31 = f32[8,64,32]{1,2,0:T(8,128)S(1)} fusion(f32[8,7,8,64]{3,2,1,0:T(8,128)} %get-tuple-element.195, f32[4,1,8,64]{3,2,1,0:T(8,128)} %get-tuple-element.198, f32[4,1,8,64]{3,2,1,0:T(8,128)} %get-tuple-element.199, f32[4,1,8,64]{3,2,1,0:T(8,128)} %get-tuple-element.197, f32[4,1,8,64]{3,2,1,0:T(8,128)} %get-tuple-element.196, ...), kind=kOutput, calls=%fused_computation.60 | convolution fusion | flops 15568896 | bytes 2687232 | tf_op jit(solution)/shard_map/dot_general | solution.py:151
  103.1 1.8 fusion.163
  105.5 1.5 fusion.76
  113.1 1.7 copy.2007
  117.6 1.7 copy.2009
  119.3 1.7 copy.2001
  121.1 1.7 copy.1999
  122.8 1.5 copy.1998
  133.2 1.7 copy.2015
  138.1 1.7 copy.2017
  139.9 1.8 maximum_maximum_fusion.7
  141.7 1.7 copy.2014
  143.4 1.8 pad_maximum_fusion.8
  145.1 1.7 copy.2013
  146.9 1.8 maximum_maximum_fusion.6
  148.7 1.7 copy.2012
  150.4 1.8 pad_maximum_fusion.7
  152.1 1.7 copy.2011
  153.9 1.5 copy.2008
  155.4 1.5 copy.2010
  156.8 1.7 copy.2006
  158.5 1.7 copy.2005
  160.2 1.7 copy.2004
  161.9 1.7 copy.2003
  165.2 1.8 fusion.296
  187.4 1.7 collective-permute-start.25
  189.1 3.0 %collective-permute-start.26 = (f32[1,16,16,1]{3,2,1,0:T(8,128)S(1)}, f32[1,16,16,1]{3,2,1,0:T(8,128)S(1)}, u32[]{:S(2)}, u32[]{:S(2)}) collective-permute-start(f32[1,16,16,1]{3,2,1,0:T(8,128)S(1)} %get-tuple-element.254), channel_id=1, source_target_pairs={{0,7},{1,0},{2,1},{3,2},{4,3},{5,4},{6,5},{7,6},{8,15},{9,8},{10,9... | collective-permute-start | bytes 3080 | tf_op jit(solution)/shard_map/ppermute | solution.py:16
  192.2 3.8 %collective-permute-start.24 = (f32[1,16,1,128]{3,1,2,0:T(8,128)S(1)}, f32[1,16,1,128]{3,1,2,0:T(8,128)S(1)}, u32[]{:S(2)}, u32[]{:S(2)}) collective-permute-start(f32[1,16,1,128]{3,1,2,0:T(8,128)S(1)} %bitcast.627), channel_id=1, source_target_pairs={{0,6},{1,7},{2,0},{3,1},{4,2},{5,3},{6,4},{7,5},{8,14},{9,15},{10,... | collective-permute-start | bytes 24584 | tf_op jit(solution)/shard_map/ppermute | solution.py:16
  198.3 2.6 %collective-permute-start.27 = (f32[1,2,16,128]{3,1,2,0:T(2,128)S(1)}, f32[1,2,16,128]{3,1,2,0:T(2,128)S(1)}, u32[]{:S(2)}, u32[]{:S(2)}) collective-permute-start(f32[1,2,16,128]{3,1,2,0:T(2,128)S(1)} %pad_maximum_fusion.25), channel_id=1, source_target_pairs={{0,4},{1,5},{2,6},{3,7},{4,0},{5,1},{6,2},{7,3},{8,12},{9,13},{10,... | collective-permute-start | bytes 49160 | tf_op jit(solution)/shard_map/ppermute | solution.py:16
  202.1 3.5 %collective-permute-start.31 = (f32[1,16,16,1]{3,1,2,0:T(8,128)S(1)}, f32[1,16,16,1]{3,1,2,0:T(8,128)S(1)}, u32[]{:S(2)}, u32[]{:S(2)}) collective-permute-start(f32[1,16,16,1]{3,1,2,0:T(8,128)S(1)} %get-tuple-element.242), channel_id=1, source_target_pairs={{0,7},{1,0},{2,1},{3,2},{4,3},{5,4},{6,5},{7,6},{8,15},{9,8},{10,9... | collective-permute-start | bytes 3080 | tf_op jit(solution)/shard_map/ppermute | solution.py:16
  206.3 3.8 %collective-permute-start.29 = (f32[1,16,1,128]{3,1,2,0:T(8,128)S(1)}, f32[1,16,1,128]{3,1,2,0:T(8,128)S(1)}, u32[]{:S(2)}, u32[]{:S(2)}) collective-permute-start(f32[1,16,1,128]{3,1,2,0:T(8,128)S(1)} %get-tuple-element.246), channel_id=1, source_target_pairs={{0,6},{1,7},{2,0},{3,1},{4,2},{5,3},{6,4},{7,5},{8,14},{9,15},{10,... | collective-permute-start | bytes 24584 | tf_op jit(solution)/shard_map/ppermute | solution.py:16
  (566 shorter events, 92.2 us)
Async XLA Ops:
  8.6 23.7 %collective-permute-start = (f32[2,2,16,128]{3,1,2,0:T(2,128)S(1)}, f32[2,2,16,128]{3,1,2,0:T(2,128)S(1)}, u32[]{:S(2)}, u32[]{:S(2)}) collective-permute-start(f32[2,2,16,128]{3,1,2,0:T(2,128)S(1)} %fusion.350), channel_id=1, source_target_pairs={{0,4},{1,5},{2,6},{3,7},{4,0},{5,1},{6,2},{7,3},{8,12},{9,13},{10,... | collective-permute-start | bytes 98312 | tf_op jit(solution)/shard_map/ppermute | solution.py:16
  12.7 19.6 %collective-permute-start.1 = (f32[2,16,1,128]{3,1,2,0:T(8,128)S(1)}, f32[2,16,1,128]{3,1,2,0:T(8,128)S(1)}, u32[]{:S(2)}, u32[]{:S(2)}) collective-permute-start(f32[2,16,1,128]{3,1,2,0:T(8,128)S(1)} %get-tuple-element.239), channel_id=1, source_target_pairs={{0,2},{1,3},{2,4},{3,5},{4,6},{5,7},{6,0},{7,1},{8,10},{9,11},{10,... | collective-permute-start | bytes 49160 | tf_op jit(solution)/shard_map/ppermute | solution.py:16
  14.3 18.0 %collective-permute-start.2 = (f32[2,16,1,128]{3,1,2,0:T(8,128)S(1)}, f32[2,16,1,128]{3,1,2,0:T(8,128)S(1)}, u32[]{:S(2)}, u32[]{:S(2)}) collective-permute-start(f32[2,16,1,128]{3,1,2,0:T(8,128)S(1)} %get-tuple-element.238), channel_id=1, source_target_pairs={{0,6},{1,7},{2,0},{3,1},{4,2},{5,3},{6,4},{7,5},{8,14},{9,15},{10,... | collective-permute-start | bytes 49160 | tf_op jit(solution)/shard_map/ppermute | solution.py:16
  16.7 11.9 %collective-permute-start.3 = (f32[2,16,16,1]{3,1,2,0:T(8,128)S(1)}, f32[2,16,16,1]{3,1,2,0:T(8,128)S(1)}, u32[]{:S(2)}, u32[]{:S(2)}) collective-permute-start(f32[2,16,16,1]{3,1,2,0:T(8,128)S(1)} %get-tuple-element.237), channel_id=1, source_target_pairs={{0,1},{1,2},{2,3},{3,4},{4,5},{5,6},{6,7},{7,0},{8,9},{9,10},{10,1... | collective-permute-start | bytes 6152 | tf_op jit(solution)/shard_map/ppermute | solution.py:16
  18.3 12.5 %collective-permute-start.4 = (f32[2,16,16,1]{3,1,2,0:T(8,128)S(1)}, f32[2,16,16,1]{3,1,2,0:T(8,128)S(1)}, u32[]{:S(2)}, u32[]{:S(2)}) collective-permute-start(f32[2,16,16,1]{3,1,2,0:T(8,128)S(1)} %get-tuple-element.236), channel_id=1, source_target_pairs={{0,7},{1,0},{2,1},{3,2},{4,3},{5,4},{6,5},{7,6},{8,15},{9,8},{10,9... | collective-permute-start | bytes 6152 | tf_op jit(solution)/shard_map/ppermute | solution.py:16
  22.0 61.4 %copy-start.76 = (s32[64]{0:T(128)}, s32[64]{0:T(128)S(1)}, u32[]{:S(2)}) copy-start(s32[64]{0:T(128)S(1)} %get-tuple-element.463) | copy-start | bytes 772
  22.0 62.2 %copy-start.74 = (s32[64]{0:T(128)}, s32[64]{0:T(128)S(1)}, u32[]{:S(2)}) copy-start(s32[64]{0:T(128)S(1)} %get-tuple-element.464) | copy-start | bytes 772
  32.8 22.4 %copy-start = (f32[16,16,128]{2,0,1:T(8,128)}, f32[16,16,128]{2,0,1:T(8,128)S(1)}, u32[]{:S(2)}) copy-start(f32[16,16,128]{2,0,1:T(8,128)S(1)} %get-tuple-element.53) | copy-start | bytes 393220
  32.8 22.4 %copy-start.2 = (f32[16,16,128]{2,0,1:T(8,128)}, f32[16,16,128]{2,0,1:T(8,128)S(1)}, u32[]{:S(2)}) copy-start(f32[16,16,128]{2,0,1:T(8,128)S(1)} %get-tuple-element.54) | copy-start | bytes 393220
  32.8 22.4 %copy-start.4 = (f32[16,16,128]{2,0,1:T(8,128)}, f32[16,16,128]{2,0,1:T(8,128)S(1)}, u32[]{:S(2)}) copy-start(f32[16,16,128]{2,0,1:T(8,128)S(1)} %get-tuple-element.55) | copy-start | bytes 393220
  32.9 22.4 %copy-start.6 = (f32[16,16,128]{2,0,1:T(8,128)}, f32[16,16,128]{2,0,1:T(8,128)S(1)}, u32[]{:S(2)}) copy-start(f32[16,16,128]{2,0,1:T(8,128)S(1)} %get-tuple-element.56) | copy-start | bytes 393220
  32.9 22.4 %copy-start.8 = (f32[16,16,128]{2,0,1:T(8,128)}, f32[16,16,128]{2,0,1:T(8,128)S(1)}, u32[]{:S(2)}) copy-start(f32[16,16,128]{2,0,1:T(8,128)S(1)} %get-tuple-element.461) | copy-start | bytes 393220
  33.2 9.3 %collective-permute-start.5 = (f32[1,2,16,128]{3,2,1,0:T(8,128)S(1)}, f32[1,2,16,128]{3,2,1,0:T(8,128)S(1)}, u32[]{:S(2)}, u32[]{:S(2)}) collective-permute-start(f32[1,2,16,128]{3,2,1,0:T(8,128)S(1)} %pad_maximum_fusion.22), channel_id=1, source_target_pairs={{0,4},{1,5},{2,6},{3,7},{4,0},{5,1},{6,2},{7,3},{8,12},{9,13},{10,... | collective-permute-start | bytes 49160 | tf_op jit(solution)/shard_map/ppermute | solution.py:16
  33.3 8.7 %collective-permute-start.8 = (f32[1,16,16,1]{3,2,1,0:T(8,128)S(1)}, f32[1,16,16,1]{3,2,1,0:T(8,128)S(1)}, u32[]{:S(2)}, u32[]{:S(2)}) collective-permute-start(f32[1,16,16,1]{3,2,1,0:T(8,128)S(1)} %get-tuple-element.285), channel_id=1, source_target_pairs={{0,1},{1,2},{2,3},{3,4},{4,5},{5,6},{6,7},{7,0},{8,9},{9,10},{10,1... | collective-permute-start | bytes 3080 | tf_op jit(solution)/shard_map/ppermute | solution.py:16
  33.7 8.6 %collective-permute-start.9 = (f32[1,16,16,1]{3,2,1,0:T(8,128)S(1)}, f32[1,16,16,1]{3,2,1,0:T(8,128)S(1)}, u32[]{:S(2)}, u32[]{:S(2)}) collective-permute-start(f32[1,16,16,1]{3,2,1,0:T(8,128)S(1)} %get-tuple-element.284), channel_id=1, source_target_pairs={{0,7},{1,0},{2,1},{3,2},{4,3},{5,4},{6,5},{7,6},{8,15},{9,8},{10,9... | collective-permute-start | bytes 3080 | tf_op jit(solution)/shard_map/ppermute | solution.py:16
  38.1 5.5 %collective-permute-start.6 = (f32[1,16,1,128]{3,1,2,0:T(8,128)S(1)}, f32[1,16,1,128]{3,1,2,0:T(8,128)S(1)}, u32[]{:S(2)}, u32[]{:S(2)}) collective-permute-start(f32[1,16,1,128]{3,1,2,0:T(8,128)S(1)} %bitcast.630), channel_id=1, source_target_pairs={{0,2},{1,3},{2,4},{3,5},{4,6},{5,7},{6,0},{7,1},{8,10},{9,11},{10,... | collective-permute-start | bytes 24584 | tf_op jit(solution)/shard_map/ppermute | solution.py:16
  38.1 5.4 %collective-permute-start.7 = (f32[1,16,1,128]{3,1,2,0:T(8,128)S(1)}, f32[1,16,1,128]{3,1,2,0:T(8,128)S(1)}, u32[]{:S(2)}, u32[]{:S(2)}) collective-permute-start(f32[1,16,1,128]{3,1,2,0:T(8,128)S(1)} %bitcast.628), channel_id=1, source_target_pairs={{0,6},{1,7},{2,0},{3,1},{4,2},{5,3},{6,4},{7,5},{8,14},{9,15},{10,... | collective-permute-start | bytes 24584 | tf_op jit(solution)/shard_map/ppermute | solution.py:16
  44.1 10.1 %collective-permute-start.10 = (f32[1,2,16,128]{3,2,1,0:T(8,128)S(1)}, f32[1,2,16,128]{3,2,1,0:T(8,128)S(1)}, u32[]{:S(2)}, u32[]{:S(2)}) collective-permute-start(f32[1,2,16,128]{3,2,1,0:T(8,128)S(1)} %pad_maximum_fusion.23), channel_id=1, source_target_pairs={{0,4},{1,5},{2,6},{3,7},{4,0},{5,1},{6,2},{7,3},{8,12},{9,13},{10,... | collective-permute-start | bytes 49160 | tf_op jit(solution)/shard_map/ppermute | solution.py:16
  44.8 8.6 %collective-permute-start.13 = (f32[1,16,16,1]{3,2,1,0:T(8,128)S(1)}, f32[1,16,16,1]{3,2,1,0:T(8,128)S(1)}, u32[]{:S(2)}, u32[]{:S(2)}) collective-permute-start(f32[1,16,16,1]{3,2,1,0:T(8,128)S(1)} %get-tuple-element.273), channel_id=1, source_target_pairs={{0,1},{1,2},{2,3},{3,4},{4,5},{5,6},{6,7},{7,0},{8,9},{9,10},{10,1... | collective-permute-start | bytes 3080 | tf_op jit(solution)/shard_map/ppermute | solution.py:16
  45.5 8.4 %collective-permute-start.14 = (f32[1,16,16,1]{3,2,1,0:T(8,128)S(1)}, f32[1,16,16,1]{3,2,1,0:T(8,128)S(1)}, u32[]{:S(2)}, u32[]{:S(2)}) collective-permute-start(f32[1,16,16,1]{3,2,1,0:T(8,128)S(1)} %get-tuple-element.272), channel_id=1, source_target_pairs={{0,7},{1,0},{2,1},{3,2},{4,3},{5,4},{6,5},{7,6},{8,15},{9,8},{10,9... | collective-permute-start | bytes 3080 | tf_op jit(solution)/shard_map/ppermute | solution.py:16
  49.6 5.5 %collective-permute-start.11 = (f32[1,16,1,128]{3,1,2,0:T(8,128)S(1)}, f32[1,16,1,128]{3,1,2,0:T(8,128)S(1)}, u32[]{:S(2)}, u32[]{:S(2)}) collective-permute-start(f32[1,16,1,128]{3,1,2,0:T(8,128)S(1)} %bitcast.632), channel_id=1, source_target_pairs={{0,2},{1,3},{2,4},{3,5},{4,6},{5,7},{6,0},{7,1},{8,10},{9,11},{10,... | collective-permute-start | bytes 24584 | tf_op jit(solution)/shard_map/ppermute | solution.py:16
  51.6 3.7 %collective-permute-start.12 = (f32[1,16,1,128]{3,1,2,0:T(8,128)S(1)}, f32[1,16,1,128]{3,1,2,0:T(8,128)S(1)}, u32[]{:S(2)}, u32[]{:S(2)}) collective-permute-start(f32[1,16,1,128]{3,1,2,0:T(8,128)S(1)} %bitcast.631), channel_id=1, source_target_pairs={{0,6},{1,7},{2,0},{3,1},{4,2},{5,3},{6,4},{7,5},{8,14},{9,15},{10,... | collective-permute-start | bytes 24584 | tf_op jit(solution)/shard_map/ppermute | solution.py:16
  54.0 16.9 %copy-start.45 = (f32[16,16]{1,0:T(8,128)}, f32[16,16]{1,0:T(8,128)S(1)}, u32[]{:S(2)}) copy-start(f32[16,16]{1,0:T(8,128)S(1)} %reduce.3) | copy-start | bytes 3076
  54.2 16.7 %copy-start.54 = (f32[1,2,16,128]{3,2,1,0:T(8,128)}, f32[1,2,16,128]{3,2,1,0:T(8,128)S(1)}, u32[]{:S(2)}) copy-start(f32[1,2,16,128]{3,2,1,0:T(8,128)S(1)} %collective-permute-done.10) | copy-start | bytes 49156
  55.1 15.8 %copy-start.58 = (f32[1,16,1,128]{3,1,2,0:T(8,128)}, f32[1,16,1,128]{3,1,2,0:T(8,128)S(1)}, u32[]{:S(2)}) copy-start(f32[1,16,1,128]{3,1,2,0:T(8,128)S(1)} %collective-permute-done.11) | copy-start | bytes 24580
  55.2 15.7 %copy-start.60 = (f32[1,16,1,128]{3,1,2,0:T(8,128)}, f32[1,16,1,128]{3,1,2,0:T(8,128)S(1)}, u32[]{:S(2)}) copy-start(f32[1,16,1,128]{3,1,2,0:T(8,128)S(1)} %collective-permute-done.12) | copy-start | bytes 24580
  56.1 8.8 %collective-permute-start.15 = (f32[2,8,8,64]{3,2,1,0:T(8,128)S(1)}, f32[2,8,8,64]{3,2,1,0:T(8,128)S(1)}, u32[]{:S(2)}, u32[]{:S(2)}) collective-permute-start(f32[2,8,8,64]{3,2,1,0:T(8,128)S(1)} %pad_maximum_fusion.13), channel_id=1, source_target_pairs={{0,1},{1,2},{2,3},{3,4},{4,5},{5,6},{6,7},{7,0},{8,9},{9,10},{10,1... | collective-permute-start | bytes 98312 | tf_op jit(solution)/shard_map/ppermute | solution.py:16
  57.3 8.3 %collective-permute-start.16 = (f32[2,8,8,64]{3,2,1,0:T(8,128)S(1)}, f32[2,8,8,64]{3,2,1,0:T(8,128)S(1)}, u32[]{:S(2)}, u32[]{:S(2)}) collective-permute-start(f32[2,8,8,64]{3,2,1,0:T(8,128)S(1)} %pad_maximum_fusion.13), channel_id=1, source_target_pairs={{0,2},{1,3},{2,4},{3,5},{4,6},{5,7},{6,0},{7,1},{8,10},{9,11},{10,... | collective-permute-start | bytes 98312 | tf_op jit(solution)/shard_map/ppermute | solution.py:16
  57.4 10.1 %collective-permute-start.17 = (f32[2,8,8,64]{3,2,1,0:T(8,128)S(1)}, f32[2,8,8,64]{3,2,1,0:T(8,128)S(1)}, u32[]{:S(2)}, u32[]{:S(2)}) collective-permute-start(f32[2,8,8,64]{3,2,1,0:T(8,128)S(1)} %pad_maximum_fusion.13), channel_id=1, source_target_pairs={{0,3},{1,4},{2,5},{3,6},{4,7},{5,0},{6,1},{7,2},{8,11},{9,12},{10,... | collective-permute-start | bytes 98312 | tf_op jit(solution)/shard_map/ppermute | solution.py:16
  61.9 6.1 %collective-permute-start.18 = (f32[2,8,8,64]{3,2,1,0:T(8,128)S(1)}, f32[2,8,8,64]{3,2,1,0:T(8,128)S(1)}, u32[]{:S(2)}, u32[]{:S(2)}) collective-permute-start(f32[2,8,8,64]{3,2,1,0:T(8,128)S(1)} %pad_maximum_fusion.13), channel_id=1, source_target_pairs={{0,4},{1,5},{2,6},{3,7},{4,0},{5,1},{6,2},{7,3},{8,12},{9,13},{10,... | collective-permute-start | bytes 98312 | tf_op jit(solution)/shard_map/ppermute | solution.py:16
  61.9 6.1 %collective-permute-start.19 = (f32[2,8,8,64]{3,2,1,0:T(8,128)S(1)}, f32[2,8,8,64]{3,2,1,0:T(8,128)S(1)}, u32[]{:S(2)}, u32[]{:S(2)}) collective-permute-start(f32[2,8,8,64]{3,2,1,0:T(8,128)S(1)} %pad_maximum_fusion.13), channel_id=1, source_target_pairs={{0,5},{1,6},{2,7},{3,0},{4,1},{5,2},{6,3},{7,4},{8,13},{9,14},{10,... | collective-permute-start | bytes 98312 | tf_op jit(solution)/shard_map/ppermute | solution.py:16
  64.9 4.6 %collective-permute-start.20 = (f32[2,8,8,64]{3,2,1,0:T(8,128)S(1)}, f32[2,8,8,64]{3,2,1,0:T(8,128)S(1)}, u32[]{:S(2)}, u32[]{:S(2)}) collective-permute-start(f32[2,8,8,64]{3,2,1,0:T(8,128)S(1)} %pad_maximum_fusion.13), channel_id=1, source_target_pairs={{0,6},{1,7},{2,0},{3,1},{4,2},{5,3},{6,4},{7,5},{8,14},{9,15},{10,... | collective-permute-start | bytes 98312 | tf_op jit(solution)/shard_map/ppermute | solution.py:16
  65.6 4.6 %collective-permute-start.21 = (f32[2,8,8,64]{3,2,1,0:T(8,128)S(1)}, f32[2,8,8,64]{3,2,1,0:T(8,128)S(1)}, u32[]{:S(2)}, u32[]{:S(2)}) collective-permute-start(f32[2,8,8,64]{3,2,1,0:T(8,128)S(1)} %pad_maximum_fusion.13), channel_id=1, source_target_pairs={{0,7},{1,0},{2,1},{3,2},{4,3},{5,4},{6,5},{7,6},{8,15},{9,8},{10,9... | collective-permute-start | bytes 98312 | tf_op jit(solution)/shard_map/ppermute | solution.py:16
  85.0 16.9 %copy-start.22 = (f32[8,4,4,32]{0,3,2,1:T(8,128)}, f32[8,4,4,32]{0,3,2,1:T(8,128)S(1)}, u32[]{:S(2)}) copy-start(f32[8,4,4,32]{0,3,2,1:T(8,128)S(1)} %copy.1967) | copy-start | bytes 49156
  124.9 18.4 %copy-start.32 = (f32[2,4,1,32]{0,3,2,1:T(8,128)S(1)}, f32[2,4,1,32]{0,3,2,1:T(8,128)}, u32[]{:S(2)}) copy-start(f32[2,4,1,32]{0,3,2,1:T(8,128)} %get-tuple-element.142) | copy-start | bytes 3076
  143.4 21.9 %copy-start.30 = (f32[8,32,16]{1,2,0:T(8,128)S(1)}, f32[8,32,16]{1,2,0:T(8,128)}, u32[]{:S(2)}) copy-start(f32[8,32,16]{1,2,0:T(8,128)} %copy-done.29) | copy-start | bytes 49156
  145.1 20.1 %copy-start.33 = (f32[8,4,4,31]{3,2,1,0:T(4,128)S(1)}, f32[8,4,4,31]{3,2,1,0:T(4,128)}, u32[]{:S(2)}) copy-start(f32[8,4,4,31]{3,2,1,0:T(4,128)} %copy.2007) | copy-start | bytes 47620
  152.1 15.8 %copy-start.36 = (f32[8,2,2,15]{0,2,3,1:T(2,128)S(1)}, f32[8,2,2,15]{0,2,3,1:T(2,128)}, u32[]{:S(2)}) copy-start(f32[8,2,2,15]{0,2,3,1:T(2,128)} %get-tuple-element.414) | copy-start | bytes 5764
  186.1 11.2 %collective-permute-start.22 = (f32[1,2,16,128]{3,2,1,0:T(8,128)S(1)}, f32[1,2,16,128]{3,2,1,0:T(8,128)S(1)}, u32[]{:S(2)}, u32[]{:S(2)}) collective-permute-start(f32[1,2,16,128]{3,2,1,0:T(8,128)S(1)} %pad_maximum_fusion.24), channel_id=1, source_target_pairs={{0,4},{1,5},{2,6},{3,7},{4,0},{5,1},{6,2},{7,3},{8,12},{9,13},{10,... | collective-permute-start | bytes 49160 | tf_op jit(solution)/shard_map/ppermute | solution.py:16
  187.4 8.6 %collective-permute-start.25 = (f32[1,16,16,1]{3,2,1,0:T(8,128)S(1)}, f32[1,16,16,1]{3,2,1,0:T(8,128)S(1)}, u32[]{:S(2)}, u32[]{:S(2)}) collective-permute-start(f32[1,16,16,1]{3,2,1,0:T(8,128)S(1)} %get-tuple-element.255), channel_id=1, source_target_pairs={{0,1},{1,2},{2,3},{3,4},{4,5},{5,6},{6,7},{7,0},{8,9},{9,10},{10,1... | collective-permute-start | bytes 3080 | tf_op jit(solution)/shard_map/ppermute | solution.py:16
  189.1 7.9 %collective-permute-start.26 = (f32[1,16,16,1]{3,2,1,0:T(8,128)S(1)}, f32[1,16,16,1]{3,2,1,0:T(8,128)S(1)}, u32[]{:S(2)}, u32[]{:S(2)}) collective-permute-start(f32[1,16,16,1]{3,2,1,0:T(8,128)S(1)} %get-tuple-element.254), channel_id=1, source_target_pairs={{0,7},{1,0},{2,1},{3,2},{4,3},{5,4},{6,5},{7,6},{8,15},{9,8},{10,9... | collective-permute-start | bytes 3080 | tf_op jit(solution)/shard_map/ppermute | solution.py:16
  192.1 5.6 %collective-permute-start.23 = (f32[1,16,1,128]{3,1,2,0:T(8,128)S(1)}, f32[1,16,1,128]{3,1,2,0:T(8,128)S(1)}, u32[]{:S(2)}, u32[]{:S(2)}) collective-permute-start(f32[1,16,1,128]{3,1,2,0:T(8,128)S(1)} %bitcast.629), channel_id=1, source_target_pairs={{0,2},{1,3},{2,4},{3,5},{4,6},{5,7},{6,0},{7,1},{8,10},{9,11},{10,... | collective-permute-start | bytes 24584 | tf_op jit(solution)/shard_map/ppermute | solution.py:16
  192.2 5.5 %collective-permute-start.24 = (f32[1,16,1,128]{3,1,2,0:T(8,128)S(1)}, f32[1,16,1,128]{3,1,2,0:T(8,128)S(1)}, u32[]{:S(2)}, u32[]{:S(2)}) collective-permute-start(f32[1,16,1,128]{3,1,2,0:T(8,128)S(1)} %bitcast.627), channel_id=1, source_target_pairs={{0,6},{1,7},{2,0},{3,1},{4,2},{5,3},{6,4},{7,5},{8,14},{9,15},{10,... | collective-permute-start | bytes 24584 | tf_op jit(solution)/shard_map/ppermute | solution.py:16
  198.3 12.6 %collective-permute-start.27 = (f32[1,2,16,128]{3,1,2,0:T(2,128)S(1)}, f32[1,2,16,128]{3,1,2,0:T(2,128)S(1)}, u32[]{:S(2)}, u32[]{:S(2)}) collective-permute-start(f32[1,2,16,128]{3,1,2,0:T(2,128)S(1)} %pad_maximum_fusion.25), channel_id=1, source_target_pairs={{0,4},{1,5},{2,6},{3,7},{4,0},{5,1},{6,2},{7,3},{8,12},{9,13},{10,... | collective-permute-start | bytes 49160 | tf_op jit(solution)/shard_map/ppermute | solution.py:16
  200.9 9.3 %collective-permute-start.30 = (f32[1,16,16,1]{3,1,2,0:T(8,128)S(1)}, f32[1,16,16,1]{3,1,2,0:T(8,128)S(1)}, u32[]{:S(2)}, u32[]{:S(2)}) collective-permute-start(f32[1,16,16,1]{3,1,2,0:T(8,128)S(1)} %get-tuple-element.243), channel_id=1, source_target_pairs={{0,1},{1,2},{2,3},{3,4},{4,5},{5,6},{6,7},{7,0},{8,9},{9,10},{10,1... | collective-permute-start | bytes 3080 | tf_op jit(solution)/shard_map/ppermute | solution.py:16
  202.1 8.4 %collective-permute-start.31 = (f32[1,16,16,1]{3,1,2,0:T(8,128)S(1)}, f32[1,16,16,1]{3,1,2,0:T(8,128)S(1)}, u32[]{:S(2)}, u32[]{:S(2)}) collective-permute-start(f32[1,16,16,1]{3,1,2,0:T(8,128)S(1)} %get-tuple-element.242), channel_id=1, source_target_pairs={{0,7},{1,0},{2,1},{3,2},{4,3},{5,4},{6,5},{7,6},{8,15},{9,8},{10,9... | collective-permute-start | bytes 3080 | tf_op jit(solution)/shard_map/ppermute | solution.py:16
  206.3 5.4 %collective-permute-start.28 = (f32[1,16,1,128]{3,1,2,0:T(8,128)S(1)}, f32[1,16,1,128]{3,1,2,0:T(8,128)S(1)}, u32[]{:S(2)}, u32[]{:S(2)}) collective-permute-start(f32[1,16,1,128]{3,1,2,0:T(8,128)S(1)} %get-tuple-element.247), channel_id=1, source_target_pairs={{0,2},{1,3},{2,4},{3,5},{4,6},{5,7},{6,0},{7,1},{8,10},{9,11},{10,... | collective-permute-start | bytes 24584 | tf_op jit(solution)/shard_map/ppermute | solution.py:16
  206.3 5.4 %collective-permute-start.29 = (f32[1,16,1,128]{3,1,2,0:T(8,128)S(1)}, f32[1,16,1,128]{3,1,2,0:T(8,128)S(1)}, u32[]{:S(2)}, u32[]{:S(2)}) collective-permute-start(f32[1,16,1,128]{3,1,2,0:T(8,128)S(1)} %get-tuple-element.246), channel_id=1, source_target_pairs={{0,6},{1,7},{2,0},{3,1},{4,2},{5,3},{6,4},{7,5},{8,14},{9,15},{10,... | collective-permute-start | bytes 24584 | tf_op jit(solution)/shard_map/ppermute | solution.py:16
  (63 other events, 186.7 us)

commit v2 on v0

--- a/solution.py
+++ b/solution.py
@@ -16,41 +16,48 @@
     return lax.ppermute(shard, axis, [(i, (i + by) % peers) for i in range(peers)])
 
 
-def exchange(fields, per_side):
-    count_dev = lax.axis_size("space")
-    plane_step = per_side * per_side
-    if (2 * plane_step) % count_dev == 0:
-        both_x = shifted(jnp.concatenate([fields[:, -1:], fields[:, :1]], axis=1), "space", plane_step)
-        lower_x, upper_x = both_x[:, :1], both_x[:, 1:]
-    else:
-        lower_x = shifted(fields[:, -1:], "space", plane_step)
-        upper_x = shifted(fields[:, :1], "space", -plane_step)
-    lower_y = shifted(fields[:, :, -1:], "space", per_side)
-    upper_y = shifted(fields[:, :, :1], "space", -per_side)
-    lower_z = shifted(fields[:, :, :, -1:], "space", 1)
-    upper_z = shifted(fields[:, :, :, :1], "space", -1)
-    return [lower_x, upper_x, lower_y, upper_y, lower_z, upper_z]
-
-
 def own_faces(values):
     return [values[-1:], values[:1], values[:, -1:], values[:, :1], values[:, :, -1:], values[:, :, :1]]
 
 
+def send_faces(flat, shifts):
+    count_dev = lax.axis_size("space")
+    if count_dev > 16:
+        return [shifted(piece, "space", by) for piece, by in zip(flat, shifts)]
+    groups = {}
+    for number, by in enumerate(shifts):
+        groups.setdefault(by % count_dev, []).append(number)
+    width = max(sum(flat[n].shape[0] for n in members) for members in groups.values())
+    rows = []
+    for offset in range(count_dev):
+        members = groups.get(offset, [])
+        if members:
+            piece = jnp.concatenate([flat[n] for n in members])
+            rows.append(jnp.pad(piece, (0, width - piece.shape[0])))
+        else:
+            rows.append(jnp.zeros((width,), jnp.float32))
+    by_offset = jnp.stack(rows)
+    my_row = lax.axis_index("space")
+    lanes = jnp.arange(count_dev)
+    chunks = jnp.take(by_offset, (lanes - my_row) % count_dev, axis=0)
+    arrived = lax.all_to_all(chunks, "space", 0, 0, tiled=True)
+    arrived_by_offset = jnp.take(arrived, (my_row - lanes) % count_dev, axis=0)
+    result = [None] * len(flat)
+    for offset, members in groups.items():
+        start = 0
+        for n in members:
+            size = flat[n].shape[0]
+            result[n] = arrived_by_offset[offset, start : start + size]
+            start += size
+    return result
+
+
 def exchange_mixed(fields, per_side):
-    count_dev = lax.axis_size("space")
     plane_step = per_side * per_side
+    shifts = [plane_step, -plane_step, per_side, -per_side, 1, -1]
     outgoing = [own_faces(values) for values in fields]
-    shifts = [plane_step, -plane_step, per_side, -per_side, 1, -1]
     flat = [jnp.concatenate([faces[d].reshape(-1) for faces in outgoing]) for d in range(6)]
-    received = [None] * 6
-    if (2 * plane_step) % count_dev == 0:
-        both = shifted(jnp.concatenate([flat[0], flat[1]]), "space", plane_step)
-        received[0], received[1] = both[: flat[0].shape[0]], both[flat[0].shape[0] :]
-        rest = range(2, 6)
-    else:
-        rest = range(6)
-    for d in rest:
-        received[d] = shifted(flat[d], "space", shifts[d])
+    received = send_faces(flat, shifts)
     result = [[None] * 6 for _ in fields]
     for d in range(6):
         offset = 0
@@ -59,6 +66,11 @@
             result[number][d] = received[d][offset : offset + size].reshape(faces[d].shape)
             offset += size
     return result
+
+
+def exchange(fields, per_side):
+    per_field = exchange_mixed([fields[n] for n in range(fields.shape[0])], per_side)
+    return [jnp.stack([faces[d] for faces in per_field]) for d in range(6)]
 
 
 def gather_rows(block, per_side):

time: 204 us -> 222 us (1.088)
  waiting for transfers between devices: 13.9 us -> 59.4 us
  starting transfers between devices: 91.6 us -> 47.4 us
  local copies, waits for them, and re-layouts: 69.7 us -> 81.9 us
    ppermute x52 -> x7, starting transfers between devices: 91.6 us -> 10.2 us  [shifted(): lax.ppermute(shard, axis, [(i, (i + by) % peers) for i in range(peers)])]
    all_to_all x0 -> x9, waiting for transfers between devices: none -> 57.7 us  [send_faces(): arrived = lax.all_to_all(chunks, 'space', 0, 0, tiled=True)]
    all_to_all x0 -> x9, starting transfers between devices: none -> 37.2 us  [send_faces(): arrived = lax.all_to_all(chunks, 'space', 0, 0, tiled=True)]
    ppermute x52 -> x7, waiting for transfers between devices: 13.9 us -> 1.7 us  [shifted(): lax.ppermute(shard, axis, [(i, (i + by) % peers) for i in range(peers)])]
    gather x0 -> x18, local copies, waits for them, and re-layouts: none -> 10.6 us  [the longest x9 5.3 us: send_faces(): arrived_by_offset = jnp.take(arrived, (my_row - lanes) % count_dev, axis=0)]
    all_to_all x0 -> x9, local copies, waits for them, and re-layouts: none -> 6.81 us  [send_faces(): arrived = lax.all_to_all(chunks, 'space', 0, 0, tiled=True)]
    another operation x0 -> x52, local copies, waits for them, and re-layouts: none -> 6.44 us  [the longest x40 4.86 us: pick(): return [face[number] for face in faces]]
    concatenate x15 -> x1, local copies, waits for them, and re-layouts: 3.42 us -> 0.01 us  [send_faces(): piece = jnp.concatenate([flat[n] for n in members])]
  transfers between devices with their start and end apart: 52 -> 16, of which waited for: 13 -> 11; matrix products, arithmetic and copies ran while one was open for 15% -> 3% of each run, Pallas kernels for 0% -> 0%
where the time goes in v2:
time: 222 us; the launch traced here: 219 us
  local copies, waits for them, and re-layouts  81.9 us (37%)
  waiting for transfers between devices  59.4 us (27%)
  starting transfers between devices  47.4 us (21%)
  other arithmetic  22.9 us (10%)
  matrix products  4.18 us (2%)
  between operations  3.32 us (1%)
    all_to_all x9, waiting for transfers between devices, send_faces(): arrived = lax.all_to_all(chunks, 'space', 0, 0, tiled=True)  57.7 us
    all_to_all x9, starting transfers between devices, send_faces(): arrived = lax.all_to_all(chunks, 'space', 0, 0, tiled=True)  37.2 us
    unnamed x201, local copies, waits for them, and re-layouts  21.5 us
    add x2, other arithmetic, shards(): permeab = permeab + jnp.where(classes == number, class_values[number], 0.0)  11.4 us
    ppermute x7, starting transfers between devices, shifted(): lax.ppermute(shard, axis, [(i, (i + by) % peers) for i in range(peers)])  10.2 us
    all_to_all x9, local copies, waits for them, and re-layouts, send_faces(): arrived = lax.all_to_all(chunks, 'space', 0, 0, tiled=True)  6.81 us
    gather x9, local copies, waits for them, and re-layouts, send_faces(): arrived_by_offset = jnp.take(arrived, (my_row - lanes) % count_dev, axis=0)  5.3 us
    gather x9, local copies, waits for them, and re-layouts, send_faces(): chunks = jnp.take(by_offset, (lanes - my_row) % count_dev, axis=0)  5.29 us
  transfers between devices with their start and end apart: 16, of which 11 were waited for; matrix products, arithmetic and copies ran while one was open for 3% of the time, Pallas kernels for 0%

profile of v2, /device:TPU:0, one launch (start us, length us, event | category | flops | bytes accessed | tf_op | source)
XLA Modules:
  0.0 219.1 jit_solution(3945712265051390678)
XLA Ops:
  2.0 6.2 %add_add_fusion = f32[1,16,16,128]{3,1,2,0:T(8,128)S(1)} fusion(s32[1,16,16,128]{3,2,1,0:T(8,128)} %param.11, f32[]{:T(128)} %bitcast.10, f32[]{:T(128)} %bitcast.9, f32[]{:T(128)} %bitcast.8, f32[]{:T(128)} %bitcast.7, f32[]{:T(128)} %bitcast.6, f32[]{:T(128)} %bitcast.5, f32[]{:T(128)} %bitcast.4, f32[]{:T(128)} %bitcast.3), kind=kLoop, calls=%fused_computation.168 | loop fusion | flops 753664 | bytes 262176 | tf_op jit(solution)/shard_map/add | solution.py:264
  8.2 5.2 %fusion.676 = f32[16,16,128]{2,0,1:T(8,128)S(1)} fusion(f32[]{:T(128)} %bitcast.10, f32[]{:T(128)} %bitcast.9, f32[]{:T(128)} %bitcast.8, f32[]{:T(128)} %bitcast.7, f32[]{:T(128)} %bitcast.6, f32[]{:T(128)} %bitcast.5, f32[]{:T(128)} %bitcast.4, f32[]{:T(128)} %bitcast.3, s32[1,16,16,128]{3,2,1,0:T(8,128)S(1)} %copy-done.1), kind=kLoop, calls=%fused_computation.1097 | loop fusion | flops 753664 | bytes 262176 | tf_op jit(solution)/shard_map/add | solution.py:264
  18.0 1.0 copy.1218
  19.1 7.3 %all-to-all-start = ((f32[8,1,9216]{2,1,0:T(1,128)}), f32[8,1,9216]{2,1,0:T(1,128)S(1)}, u32[]{:S(2)}, u32[]{:S(2)}) async-start(f32[8,1,9216]{2,1,0:T(1,128)} %copy.1218), calls=%async_computation | async-start | bytes 589824 | tf_op jit(solution)/shard_map/all_to_all | solution.py:43
  32.7 3.3 %all-to-all-done = f32[8,1,9216]{2,1,0:T(1,128)S(1)} async-done(((f32[8,1,9216]{2,1,0:T(1,128)}), f32[8,1,9216]{2,1,0:T(1,128)S(1)}, u32[]{:S(2)}, u32[]{:S(2)}) %all-to-all-start) | async-done | bytes 294944 | tf_op jit(solution)/shard_map/all_to_all | solution.py:43
  36.8 0.7 slice_bitcast_fusion.29
  39.4 1.2 fusion.10
  40.9 0.9 slice_reduce_fusion.40
  41.7 0.8 slice_reduce_fusion.62
  44.4 0.8 copy.1227
  45.2 3.6 %all-to-all-start.1 = ((f32[8,1,4096]{2,1,0:T(1,128)}), f32[8,1,4096]{2,1,0:T(1,128)S(1)}, u32[]{:S(2)}, u32[]{:S(2)}) async-start(f32[8,1,4096]{2,1,0:T(1,128)} %copy.1227), calls=%async_computation.1 | async-start | bytes 262144 | tf_op jit(solution)/shard_map/all_to_all | solution.py:43
  49.7 6.5 %all-to-all-done.1 = f32[8,1,4096]{2,1,0:T(1,128)S(1)} async-done(((f32[8,1,4096]{2,1,0:T(1,128)}), f32[8,1,4096]{2,1,0:T(1,128)S(1)}, u32[]{:S(2)}, u32[]{:S(2)}) %all-to-all-start.1) | async-done | bytes 131104 | tf_op jit(solution)/shard_map/all_to_all | solution.py:43
  59.5 0.8 copy.1232
  60.3 3.4 %all-to-all-start.2 = ((f32[8,1,4096]{2,1,0:T(1,128)}), f32[8,1,4096]{2,1,0:T(1,128)S(1)}, u32[]{:S(2)}, u32[]{:S(2)}) async-start(f32[8,1,4096]{2,1,0:T(1,128)} %copy.1232), calls=%async_computation.2 | async-start | bytes 262144 | tf_op jit(solution)/shard_map/all_to_all | solution.py:43
  63.7 7.3 %all-to-all-done.2 = f32[8,1,4096]{2,1,0:T(1,128)S(1)} async-done(((f32[8,1,4096]{2,1,0:T(1,128)}), f32[8,1,4096]{2,1,0:T(1,128)S(1)}, u32[]{:S(2)}, u32[]{:S(2)}) %all-to-all-start.2) | async-done | bytes 131104 | tf_op jit(solution)/shard_map/all_to_all | solution.py:43
  78.0 3.3 %all-to-all-start.3 = ((f32[8,1,1024]{2,1,0:T(1,128)}), f32[8,1,1024]{2,1,0:T(1,128)S(1)}, u32[]{:S(2)}, u32[]{:S(2)}) async-start(f32[8,1,1024]{2,1,0:T(1,128)} %copy.1238), calls=%async_computation.3 | async-start | bytes 65536 | tf_op jit(solution)/shard_map/all_to_all | solution.py:43
  81.3 6.6 %all-to-all-done.3 = f32[8,1,1024]{2,1,0:T(1,128)S(1)} async-done(((f32[8,1,1024]{2,1,0:T(1,128)}), f32[8,1,1024]{2,1,0:T(1,128)S(1)}, u32[]{:S(2)}, u32[]{:S(2)}) %all-to-all-start.3) | async-done | bytes 32800 | tf_op jit(solution)/shard_map/all_to_all | solution.py:43
  91.5 3.3 %all-to-all-start.4 = ((f32[8,1,1024]{2,1,0:T(1,128)}), f32[8,1,1024]{2,1,0:T(1,128)S(1)}, u32[]{:S(2)}, u32[]{:S(2)}) async-start(f32[8,1,1024]{2,1,0:T(1,128)} %copy.1245), calls=%async_computation.4 | async-start | bytes 65536 | tf_op jit(solution)/shard_map/all_to_all | solution.py:43
  95.1 6.4 %all-to-all-done.4 = f32[8,1,1024]{2,1,0:T(1,128)S(1)} async-done(((f32[8,1,1024]{2,1,0:T(1,128)}), f32[8,1,1024]{2,1,0:T(1,128)S(1)}, u32[]{:S(2)}, u32[]{:S(2)}) %all-to-all-start.4) | async-done | bytes 32800 | tf_op jit(solution)/shard_map/all_to_all | solution.py:43
  104.7 0.7 collective-permute-start.1
  105.4 1.4 collective-permute-start.2
  106.8 3.1 %collective-permute-start.3 = (f32[2,4,4,32]{3,2,1,0:T(4,128)S(1)}, f32[2,4,4,32]{3,2,1,0:T(4,128)S(1)}, u32[]{:S(2)}, u32[]{:S(2)}) collective-permute-start(f32[2,4,4,32]{3,2,1,0:T(4,128)S(1)} %pad_maximum_fusion.28), channel_id=1, source_target_pairs={{0,4},{1,5},{2,6},{3,7},{4,0},{5,1},{6,2},{7,3},{8,12},{9,13},{10,... | collective-permute-start | bytes 12296 | tf_op jit(solution)/shard_map/ppermute | solution.py:16
  110.1 0.8 squeeze_stack_reshape_squeeze.195
  110.8 2.5 %collective-permute-start.5 = (f32[2,4,4,32]{3,2,1,0:T(4,128)S(1)}, f32[2,4,4,32]{3,2,1,0:T(4,128)S(1)}, u32[]{:S(2)}, u32[]{:S(2)}) collective-permute-start(f32[2,4,4,32]{3,2,1,0:T(4,128)S(1)} %pad_maximum_fusion.28), channel_id=1, source_target_pairs={{0,6},{1,7},{2,0},{3,1},{4,2},{5,3},{6,4},{7,5},{8,14},{9,15},{10,... | collective-permute-start | bytes 12296 | tf_op jit(solution)/shard_map/ppermute | solution.py:16
  113.4 2.0 collective-permute-start.6
  115.6 1.6 collective-permute-done.6
  117.1 0.7 gather_fusion
  119.4 0.7 fusion.583
  120.1 0.7 fusion.584
  127.1 0.7 fusion.655
  129.1 0.7 fusion.653
  129.8 0.7 fusion.654
  137.3 0.7 copy-done.10
  138.1 0.7 copy-done.5
  151.1 0.7 copy-done.11
  154.7 6.0 %all-to-all-start.5 = ((f32[8,1,1024]{2,1,0:T(1,128)}), f32[8,1,1024]{2,1,0:T(1,128)S(1)}, u32[]{:S(2)}, u32[]{:S(2)}) async-start(f32[8,1,1024]{2,1,0:T(1,128)} %copy.1316), calls=%async_computation.5 | async-start | bytes 65536 | tf_op jit(solution)/shard_map/all_to_all | solution.py:43
  160.7 6.7 %all-to-all-done.5 = f32[8,1,1024]{2,1,0:T(1,128)S(1)} async-done(((f32[8,1,1024]{2,1,0:T(1,128)}), f32[8,1,1024]{2,1,0:T(1,128)S(1)}, u32[]{:S(2)}, u32[]{:S(2)}) %all-to-all-start.5) | async-done | bytes 32800 | tf_op jit(solution)/shard_map/all_to_all | solution.py:43
  171.9 3.6 %all-to-all-start.6 = ((f32[8,1,1024]{2,1,0:T(1,128)}), f32[8,1,1024]{2,1,0:T(1,128)S(1)}, u32[]{:S(2)}, u32[]{:S(2)}) async-start(f32[8,1,1024]{2,1,0:T(1,128)} %copy.1322), calls=%async_computation.6 | async-start | bytes 65536 | tf_op jit(solution)/shard_map/all_to_all | solution.py:43
  175.5 6.4 %all-to-all-done.6 = f32[8,1,1024]{2,1,0:T(1,128)S(1)} async-done(((f32[8,1,1024]{2,1,0:T(1,128)}), f32[8,1,1024]{2,1,0:T(1,128)S(1)}, u32[]{:S(2)}, u32[]{:S(2)}) %all-to-all-start.6) | async-done | bytes 32800 | tf_op jit(solution)/shard_map/all_to_all | solution.py:43
  187.0 0.9 fusion.510
  189.9 0.8 copy.1339
  190.7 3.4 %all-to-all-start.7 = ((f32[8,1,4096]{2,1,0:T(1,128)}), f32[8,1,4096]{2,1,0:T(1,128)S(1)}, u32[]{:S(2)}, u32[]{:S(2)}) async-start(f32[8,1,4096]{2,1,0:T(1,128)} %copy.1339), calls=%async_computation.7 | async-start | bytes 262144 | tf_op jit(solution)/shard_map/all_to_all | solution.py:43
  194.1 7.4 %all-to-all-done.7 = f32[8,1,4096]{2,1,0:T(1,128)S(1)} async-done(((f32[8,1,4096]{2,1,0:T(1,128)}), f32[8,1,4096]{2,1,0:T(1,128)S(1)}, u32[]{:S(2)}, u32[]{:S(2)}) %all-to-all-start.7) | async-done | bytes 131104 | tf_op jit(solution)/shard_map/all_to_all | solution.py:43
  203.3 0.7 copy.1347
  205.4 0.8 copy.1344
  206.2 3.4 %all-to-all-start.8 = ((f32[8,1,4096]{2,1,0:T(1,128)}), f32[8,1,4096]{2,1,0:T(1,128)S(1)}, u32[]{:S(2)}, u32[]{:S(2)}) async-start(f32[8,1,4096]{2,1,0:T(1,128)} %copy.1344), calls=%async_computation.8 | async-start | bytes 262144 | tf_op jit(solution)/shard_map/all_to_all | solution.py:43
  209.6 7.3 %all-to-all-done.8 = f32[8,1,4096]{2,1,0:T(1,128)S(1)} async-done(((f32[8,1,4096]{2,1,0:T(1,128)}), f32[8,1,4096]{2,1,0:T(1,128)S(1)}, u32[]{:S(2)}, u32[]{:S(2)}) %all-to-all-start.8) | async-done | bytes 131104 | tf_op jit(solution)/shard_map/all_to_all | solution.py:43
  218.4 0.7 copy.1348
  (745 shorter events, 80.9 us)
Async XLA Ops:
  0.6 12.8 %copy-start.78 = (s32[128]{0:T(128)}, s32[128]{0:T(128)S(1)}, u32[]{:S(2)}) copy-start(s32[128]{0:T(128)S(1)} %and_select_fusion.13) | copy-start | bytes 1540
  1.3 12.5 %copy-start.76 = (s32[256]{0:T(256)}, s32[256]{0:T(256)S(1)}, u32[]{:S(2)}) copy-start(s32[256]{0:T(256)S(1)} %fusion.466) | copy-start | bytes 3076
  2.0 6.2 %copy-start.1 = (s32[1,16,16,128]{3,2,1,0:T(8,128)S(1)}, s32[1,16,16,128]{3,2,1,0:T(8,128)}, u32[]{:S(2)}) copy-start(s32[1,16,16,128]{3,2,1,0:T(8,128)} %param.11) | copy-start | bytes 393220
  13.8 0.9 copy-start
  15.1 75.7 %copy-start.38 = (pred[8]{0:T(512)(128)(4,1)}, pred[8]{0:T(512)(128)(4,1)S(1)}, u32[]{:S(2)}) copy-start(pred[8]{0:T(512)(128)(4,1)S(1)} %compare_and_fusion.1) | copy-start | bytes 28
  19.1 16.9 %all-to-all-start = ((f32[8,1,9216]{2,1,0:T(1,128)}), f32[8,1,9216]{2,1,0:T(1,128)S(1)}, u32[]{:S(2)}, u32[]{:S(2)}) async-start(f32[8,1,9216]{2,1,0:T(1,128)} %copy.1218), calls=%async_computation | async-start | bytes 589824 | tf_op jit(solution)/shard_map/all_to_all | solution.py:43
  27.8 1.9 copy-start.87
  27.9 4.0 %copy-start.81 = (s32[64]{0:T(128)}, s32[64]{0:T(128)S(1)}, u32[]{:S(2)}) copy-start(s32[64]{0:T(128)S(1)} %get-tuple-element.494) | copy-start | bytes 772
  27.9 8.2 %copy-start.57 = (s32[1024]{0:T(1024)}, s32[1024]{0:T(1024)S(1)}, u32[]{:S(2)}) copy-start(s32[1024]{0:T(1024)S(1)} %pad_clamp_fusion.1) | copy-start | bytes 12292
  36.8 1.5 copy-start.2
  45.2 11.0 %all-to-all-start.1 = ((f32[8,1,4096]{2,1,0:T(1,128)}), f32[8,1,4096]{2,1,0:T(1,128)S(1)}, u32[]{:S(2)}, u32[]{:S(2)}) async-start(f32[8,1,4096]{2,1,0:T(1,128)} %copy.1227), calls=%async_computation.1 | async-start | bytes 262144 | tf_op jit(solution)/shard_map/all_to_all | solution.py:43
  49.7 6.6 %copy-start.58 = (s32[1024]{0:T(1024)S(1)}, s32[1024]{0:T(1024)}, u32[]{:S(2)}) copy-start(s32[1024]{0:T(1024)} %copy-done.57) | copy-start | bytes 12292
  60.3 10.7 %all-to-all-start.2 = ((f32[8,1,4096]{2,1,0:T(1,128)}), f32[8,1,4096]{2,1,0:T(1,128)S(1)}, u32[]{:S(2)}, u32[]{:S(2)}) async-start(f32[8,1,4096]{2,1,0:T(1,128)} %copy.1232), calls=%async_computation.2 | async-start | bytes 262144 | tf_op jit(solution)/shard_map/all_to_all | solution.py:43
  71.8 2.0 copy-start.16
  71.8 2.0 copy-start.18
  78.0 9.9 %all-to-all-start.3 = ((f32[8,1,1024]{2,1,0:T(1,128)}), f32[8,1,1024]{2,1,0:T(1,128)S(1)}, u32[]{:S(2)}, u32[]{:S(2)}) async-start(f32[8,1,1024]{2,1,0:T(1,128)} %copy.1238), calls=%async_computation.3 | async-start | bytes 65536 | tf_op jit(solution)/shard_map/all_to_all | solution.py:43
  91.5 9.9 %all-to-all-start.4 = ((f32[8,1,1024]{2,1,0:T(1,128)}), f32[8,1,1024]{2,1,0:T(1,128)S(1)}, u32[]{:S(2)}, u32[]{:S(2)}) async-start(f32[8,1,1024]{2,1,0:T(1,128)} %copy.1245), calls=%async_computation.4 | async-start | bytes 65536 | tf_op jit(solution)/shard_map/all_to_all | solution.py:43
  104.2 6.6 %collective-permute-start = (f32[2,4,4,32]{3,2,1,0:T(4,128)S(1)}, f32[2,4,4,32]{3,2,1,0:T(4,128)S(1)}, u32[]{:S(2)}, u32[]{:S(2)}) collective-permute-start(f32[2,4,4,32]{3,2,1,0:T(4,128)S(1)} %pad_maximum_fusion.28), channel_id=1, source_target_pairs={{0,1},{1,2},{2,3},{3,4},{4,5},{5,6},{6,7},{7,0},{8,9},{9,10},{10,1... | collective-permute-start | bytes 12296 | tf_op jit(solution)/shard_map/ppermute | solution.py:16
  104.7 8.6 %collective-permute-start.1 = (f32[2,4,4,32]{3,2,1,0:T(4,128)S(1)}, f32[2,4,4,32]{3,2,1,0:T(4,128)S(1)}, u32[]{:S(2)}, u32[]{:S(2)}) collective-permute-start(f32[2,4,4,32]{3,2,1,0:T(4,128)S(1)} %pad_maximum_fusion.28), channel_id=1, source_target_pairs={{0,2},{1,3},{2,4},{3,5},{4,6},{5,7},{6,0},{7,1},{8,10},{9,11},{10,... | collective-permute-start | bytes 12296 | tf_op jit(solution)/shard_map/ppermute | solution.py:16
  105.4 9.9 %collective-permute-start.2 = (f32[2,4,4,32]{3,2,1,0:T(4,128)S(1)}, f32[2,4,4,32]{3,2,1,0:T(4,128)S(1)}, u32[]{:S(2)}, u32[]{:S(2)}) collective-permute-start(f32[2,4,4,32]{3,2,1,0:T(4,128)S(1)} %pad_maximum_fusion.28), channel_id=1, source_target_pairs={{0,3},{1,4},{2,5},{3,6},{4,7},{5,0},{6,1},{7,2},{8,11},{9,12},{10,... | collective-permute-start | bytes 12296 | tf_op jit(solution)/shard_map/ppermute | solution.py:16
  106.8 8.6 %collective-permute-start.3 = (f32[2,4,4,32]{3,2,1,0:T(4,128)S(1)}, f32[2,4,4,32]{3,2,1,0:T(4,128)S(1)}, u32[]{:S(2)}, u32[]{:S(2)}) collective-permute-start(f32[2,4,4,32]{3,2,1,0:T(4,128)S(1)} %pad_maximum_fusion.28), channel_id=1, source_target_pairs={{0,4},{1,5},{2,6},{3,7},{4,0},{5,1},{6,2},{7,3},{8,12},{9,13},{10,... | collective-permute-start | bytes 12296 | tf_op jit(solution)/shard_map/ppermute | solution.py:16
  109.9 5.5 %collective-permute-start.4 = (f32[2,4,4,32]{3,2,1,0:T(4,128)S(1)}, f32[2,4,4,32]{3,2,1,0:T(4,128)S(1)}, u32[]{:S(2)}, u32[]{:S(2)}) collective-permute-start(f32[2,4,4,32]{3,2,1,0:T(4,128)S(1)} %pad_maximum_fusion.28), channel_id=1, source_target_pairs={{0,5},{1,6},{2,7},{3,0},{4,1},{5,2},{6,3},{7,4},{8,13},{9,14},{10,... | collective-permute-start | bytes 12296 | tf_op jit(solution)/shard_map/ppermute | solution.py:16
  110.8 4.7 %collective-permute-start.5 = (f32[2,4,4,32]{3,2,1,0:T(4,128)S(1)}, f32[2,4,4,32]{3,2,1,0:T(4,128)S(1)}, u32[]{:S(2)}, u32[]{:S(2)}) collective-permute-start(f32[2,4,4,32]{3,2,1,0:T(4,128)S(1)} %pad_maximum_fusion.28), channel_id=1, source_target_pairs={{0,6},{1,7},{2,0},{3,1},{4,2},{5,3},{6,4},{7,5},{8,14},{9,15},{10,... | collective-permute-start | bytes 12296 | tf_op jit(solution)/shard_map/ppermute | solution.py:16
  113.4 3.7 %collective-permute-start.6 = (f32[2,4,4,32]{3,2,1,0:T(4,128)S(1)}, f32[2,4,4,32]{3,2,1,0:T(4,128)S(1)}, u32[]{:S(2)}, u32[]{:S(2)}) collective-permute-start(f32[2,4,4,32]{3,2,1,0:T(4,128)S(1)} %pad_maximum_fusion.28), channel_id=1, source_target_pairs={{0,7},{1,0},{2,1},{3,2},{4,3},{5,4},{6,5},{7,6},{8,15},{9,8},{10,9... | collective-permute-start | bytes 12296 | tf_op jit(solution)/shard_map/ppermute | solution.py:16
  130.5 2.0 copy-start.8
  137.2 0.8 copy-start.10
  137.2 0.8 copy-start.52
  137.2 0.8 copy-start.53
  137.2 0.8 copy-start.9
  137.2 0.8 copy-start.50
  137.2 0.8 copy-start.51
  138.0 0.8 copy-start.5
  138.0 0.9 copy-start.6
  138.1 0.9 copy-start.3
  138.1 0.9 copy-start.4
  138.1 0.8 copy-start.84
  139.0 0.9 copy-start.30
  139.0 0.9 copy-start.31
  139.0 0.9 copy-start.32
  139.0 0.9 copy-start.33
  139.0 0.9 copy-start.34
  139.0 0.9 copy-start.35
  139.6 0.8 copy-start.29
  154.7 12.6 %all-to-all-start.5 = ((f32[8,1,1024]{2,1,0:T(1,128)}), f32[8,1,1024]{2,1,0:T(1,128)S(1)}, u32[]{:S(2)}, u32[]{:S(2)}) async-start(f32[8,1,1024]{2,1,0:T(1,128)} %copy.1316), calls=%async_computation.5 | async-start | bytes 65536 | tf_op jit(solution)/shard_map/all_to_all | solution.py:43
  160.7 6.7 %copy-start.59 = (s32[1024]{0:T(1024)S(1)}, s32[1024]{0:T(1024)}, u32[]{:S(2)}) copy-start(s32[1024]{0:T(1024)} %copy-done.57) | copy-start | bytes 12292
  171.9 10.0 %all-to-all-start.6 = ((f32[8,1,1024]{2,1,0:T(1,128)}), f32[8,1,1024]{2,1,0:T(1,128)S(1)}, u32[]{:S(2)}, u32[]{:S(2)}) async-start(f32[8,1,1024]{2,1,0:T(1,128)} %copy.1322), calls=%async_computation.6 | async-start | bytes 65536 | tf_op jit(solution)/shard_map/all_to_all | solution.py:43
  190.7 10.8 %all-to-all-start.7 = ((f32[8,1,4096]{2,1,0:T(1,128)}), f32[8,1,4096]{2,1,0:T(1,128)S(1)}, u32[]{:S(2)}, u32[]{:S(2)}) async-start(f32[8,1,4096]{2,1,0:T(1,128)} %copy.1339), calls=%async_computation.7 | async-start | bytes 262144 | tf_op jit(solution)/shard_map/all_to_all | solution.py:43
  206.2 10.7 %all-to-all-start.8 = ((f32[8,1,4096]{2,1,0:T(1,128)}), f32[8,1,4096]{2,1,0:T(1,128)S(1)}, u32[]{:S(2)}, u32[]{:S(2)}) async-start(f32[8,1,4096]{2,1,0:T(1,128)} %copy.1344), calls=%async_computation.8 | async-start | bytes 262144 | tf_op jit(solution)/shard_map/all_to_all | solution.py:43
  (57 other events, 39.1 us)

commit v3 on v0

--- a/solution.py
+++ b/solution.py
@@ -191,17 +191,98 @@
     ]
 
 
+def neighbour_rows(count_b, size_x, size_y, per_side):
+    count_r = count_b * size_x * size_y
+    index = jnp.arange(count_r)
+    row = index // (size_x * size_y)
+    at_x = index // size_y % size_x
+    at_y = index % size_y
+    plane_step = per_side * per_side
+    picks = []
+    for axis_no, (size, step) in enumerate(((size_x, plane_step), (size_y, per_side))):
+        coord = at_x if axis_no == 0 else at_y
+        for sign in (-1, 1):
+            edge = size - 1 if sign > 0 else 0
+            moved = jnp.where(coord == edge, size - 1 - edge, coord + sign)
+            new_row = jnp.where(coord == edge, (row + sign * step) % count_b, row)
+            if axis_no == 0:
+                picks.append((new_row * size_x + moved) * size_y + at_y)
+            else:
+                picks.append((new_row * size_x + at_x) * size_y + moved)
+    for sign in (-1, 1):
+        picks.append((((row + sign) % count_b) * size_x + at_x) * size_y + at_y)
+    target = jnp.concatenate(picks)
+    return jnp.where(target[:, None] == index[None, :], 1.0, 0.0).astype(jnp.float32)
+
+
+def lane_shift(size_z, sign):
+    lanes_in = jnp.arange(size_z)[:, None]
+    lanes_out = jnp.arange(size_z)[None, :]
+    inner = jnp.where(lanes_in == lanes_out + sign, 1.0, 0.0)
+    edge_in, edge_out = (size_z - 1, 0) if sign < 0 else (0, size_z - 1)
+    wrap = jnp.where((lanes_in == edge_in) & (lanes_out == edge_out), 1.0, 0.0)
+    return jnp.concatenate([inner, wrap]).astype(jnp.float32)
+
+
+def flat_faces(values, picker, lower_z, upper_z):
+    count_r = values.shape[0]
+    rows = jnp.dot(picker, values, precision=lax.Precision.HIGHEST)
+    lower = jnp.dot(
+        jnp.concatenate([values, rows[4 * count_r : 5 * count_r]], axis=1),
+        lower_z,
+        precision=lax.Precision.HIGHEST,
+    )
+    upper = jnp.dot(
+        jnp.concatenate([values, rows[5 * count_r :]], axis=1),
+        upper_z,
+        precision=lax.Precision.HIGHEST,
+    )
+    return [rows[k * count_r : (k + 1) * count_r] for k in range(4)] + [lower, upper]
+
+
+def row_mean(count_b, size_x, size_y):
+    index = jnp.arange(count_b * size_x * size_y)
+    row = index // (size_x * size_y)
+    coarse_of = (row * (size_x // 2) + index // size_y % size_x // 2) * (size_y // 2) + index % size_y // 2
+    return jnp.where(
+        jnp.arange(count_b * size_x * size_y // 4)[:, None] == coarse_of[None, :], 0.25, 0.0
+    ).astype(jnp.float32)
+
+
 def global_cycle(all_rhs, all_perm, first_level, per_side):
-    perms = [all_perm]
+    count_b, size_x, size_y, size_z = all_rhs.shape
+    shapes = [(size_x >> n, size_y >> n, size_z >> n) for n in range(LEVELS - first_level + 1)]
+    pickers = [neighbour_rows(count_b, sx, sy, per_side) for sx, sy, sz in shapes]
+    shifts = [(lane_shift(sz, -1), lane_shift(sz, 1)) for sx, sy, sz in shapes]
+    means = [(row_mean(count_b, sx, sy), pair_mean(sz, 0.5)) for sx, sy, sz in shapes[:-1]]
+
+    def faces(values, number):
+        return flat_faces(values, pickers[number], *shifts[number])
+
+    def down(values, number):
+        rows, lanes = means[number]
+        return jnp.dot(
+            rows,
+            jnp.dot(values, lanes, precision=lax.Precision.HIGHEST),
+            precision=lax.Precision.HIGHEST,
+        )
+
+    def up(values, number):
+        rows, lanes = means[number]
+        return jnp.dot(
+            rows.T * 4.0,
+            jnp.dot(values, lanes.T * 2.0, precision=lax.Precision.HIGHEST),
+            precision=lax.Precision.HIGHEST,
+        )
+
+    perms = [all_perm.reshape(-1, size_z)]
     for number in range(LEVELS - first_level):
-        perms.append(coarsen_all(perms[-1]))
+        perms.append(down(perms[-1], number))
     coefs = [
-        coefficients(
-            perms[number], rolled_faces(perms[number], per_side), 0.25 ** (first_level + number)
-        )
+        coefficients(perms[number], faces(perms[number], number), 0.25 ** (first_level + number))
         for number in range(LEVELS - first_level + 1)
     ]
-    right_side = all_rhs
+    right_side = all_rhs.reshape(-1, size_z)
     stored = []
     rights = []
     for number in range(LEVELS - first_level):
@@ -209,32 +290,29 @@
         scaling = 0.25 ** (first_level + number)
         values = OMEGA * right_side / diagonal
         for sweep_no in range(SWEEPS - 1):
-            values = smooth(
-                values, right_side, face_coefs, diagonal, scaling, rolled_faces(values, per_side)
-            )
-        leftover = right_side - operate(
-            values, rolled_faces(values, per_side), face_coefs, scaling
-        )
+            values = smooth(values, right_side, face_coefs, diagonal, scaling, faces(values, number))
+        leftover = right_side - operate(values, faces(values, number), face_coefs, scaling)
         stored.append(values)
         rights.append(right_side)
-        right_side = coarsen_all(leftover)
-    face_coefs, diagonal = coefs[LEVELS - first_level]
+        right_side = down(leftover, number)
+    last = LEVELS - first_level
+    face_coefs, diagonal = coefs[last]
     scaling = 0.25**LEVELS
     correction = OMEGA * right_side / diagonal
     for sweep_no in range(CSWEEPS - 1):
         correction = smooth(
-            correction, right_side, face_coefs, diagonal, scaling, rolled_faces(correction, per_side)
+            correction, right_side, face_coefs, diagonal, scaling, faces(correction, last)
         )
     for number in reversed(range(LEVELS - first_level)):
         face_coefs, diagonal = coefs[number]
         scaling = 0.25 ** (first_level + number)
-        values = stored[number] + refine_all(correction)
+        values = stored[number] + up(correction, number)
         for sweep_no in range(SWEEPS):
             values = smooth(
-                values, rights[number], face_coefs, diagonal, scaling, rolled_faces(values, per_side)
+                values, rights[number], face_coefs, diagonal, scaling, faces(values, number)
             )
         correction = values
-    return correction
+    return correction.reshape(count_b, size_x, size_y, size_z)
 
 
 def shards(perm_class, class_values, well_cells, well_rates, guess):

time: 204 us -> 196 us (0.961)
  local copies, waits for them, and re-layouts: 69.7 us -> 41.7 us
  matrix products: 3.42 us -> 16.3 us
  other arithmetic: 21.2 us -> 25.5 us
  waiting for transfers between devices: 13.9 us -> 16.5 us
    unnamed x220 -> x110, local copies, waits for them, and re-layouts: 24.9 us -> 10.6 us
    dot_general x4 -> x39, matrix products: 0.95 us -> 13.2 us  [the longest x11 7.99 us: flat_faces(): rows = jnp.dot(picker, values, precision=lax.Precision.HIGHEST)]
    slice x90 -> x11, local copies, waits for them, and re-layouts: 12.3 us -> 0.68 us  [the longest x9 0.57 us: flat_faces(): rows[5 * count_r:]]
    unnamed x1 -> x7, other arithmetic: 0.01 us -> 6.38 us
    concatenate x10 -> x1, local copies, waits for them, and re-layouts: 4.21 us -> 0.66 us  [neighbour_rows(): target = jnp.concatenate(picks)]
    ppermute x52, waiting for transfers between devices: 13.9 us -> 16.5 us  [shifted(): lax.ppermute(shard, axis, [(i, (i + by) % peers) for i in range(peers)])]
    add x17 -> x9, other arithmetic: 3.66 us -> 1.3 us  [smooth(): values + OMEGA * (right_side - operate(values, neighbors, face_coefs, sca...]
  transfers between devices with their start and end apart: 52 -> 52, of which waited for: 13 -> 15; matrix products, arithmetic and copies ran while one was open for 15% -> 21% of each run, Pallas kernels for 0% -> 0%
where the time goes in v3:
time: 196 us; the launch traced here: 195 us
  starting transfers between devices  92.2 us (47%)
  local copies, waits for them, and re-layouts  41.7 us (21%)
  other arithmetic  25.5 us (13%)
  waiting for transfers between devices  16.5 us (8%)
  matrix products  16.3 us (8%)
  between operations  2.66 us (1%)
    ppermute x52, starting transfers between devices, shifted(): lax.ppermute(shard, axis, [(i, (i + by) % peers) for i in range(peers)])  92.2 us
    ppermute x52, waiting for transfers between devices, shifted(): lax.ppermute(shard, axis, [(i, (i + by) % peers) for i in range(peers)])  16.5 us
    add x2, other arithmetic, shards(): permeab = permeab + jnp.where(classes == number, class_values[number], 0.0)  11.1 us
    unnamed x110, local copies, waits for them, and re-layouts  10.6 us
    dot_general x11, matrix products, flat_faces(): rows = jnp.dot(picker, values, precision=lax.Precision.HIGHEST)  7.99 us
    unnamed x7, other arithmetic  6.38 us
    reshape x16, local copies, waits for them, and re-layouts, exchange_mixed(): received[d][offset:offset + size].reshape(faces[d].shape)  4.13 us
  transfers between devices with their start and end apart: 52, of which 15 were waited for; matrix products, arithmetic and copies ran while one was open for 21% of the time, Pallas kernels for 0%

profile of v3, /device:TPU:0, one launch (start us, length us, event | category | flops | bytes accessed | tf_op | source)
XLA Modules:
  0.0 194.9 jit_solution(15121632068676084605)
XLA Ops:
  2.0 6.0 %add_add_fusion = f32[1,16,16,128]{3,1,2,0:T(8,128)S(1)} fusion(s32[1,16,16,128]{3,2,1,0:T(8,128)} %param.5, f32[]{:T(128)} %bitcast.10, f32[]{:T(128)} %bitcast.9, f32[]{:T(128)} %bitcast.8, f32[]{:T(128)} %bitcast.7, f32[]{:T(128)} %bitcast.6, f32[]{:T(128)} %bitcast.5, f32[]{:T(128)} %bitcast.4, f32[]{:T(128)} %bitcast.3), kind=kLoop, calls=%fused_computation.285 | loop fusion | flops 753664 | bytes 262176 | tf_op jit(solution)/shard_map/add | solution.py:330
  8.0 1.3 constant_dynamic-update-slice_fusion.9
  10.9 4.1 %collective-permute-start = (f32[9216]{0:T(1024)S(1)}, f32[9216]{0:T(1024)S(1)}, u32[]{:S(2)}, u32[]{:S(2)}) collective-permute-start(f32[9216]{0:T(1024)S(1)} %constant_dynamic-update-slice_fusion.10), channel_id=1, source_target_pairs={{0,4},{1,5},{2,6},{3,7},{4,0},{5,1},{6,2},{7,3},{8,12},{9,13},{10,... | collective-permute-start | bytes 110600 | tf_op jit(solution)/shard_map/ppermute | solution.py:16
  15.0 5.1 %fusion.838 = f32[16,16,128]{2,0,1:T(8,128)S(1)} fusion(f32[]{:T(128)} %bitcast.10, f32[]{:T(128)} %bitcast.9, f32[]{:T(128)} %bitcast.8, f32[]{:T(128)} %bitcast.7, f32[]{:T(128)} %bitcast.6, f32[]{:T(128)} %bitcast.5, f32[]{:T(128)} %bitcast.4, f32[]{:T(128)} %bitcast.3, s32[1,16,16,128]{3,2,1,0:T(8,128)S(1)} %copy-done.1), kind=kLoop, calls=%fused_computation.1265 | loop fusion | flops 753664 | bytes 262176 | tf_op jit(solution)/shard_map/add | solution.py:330
  20.2 1.6 collective-permute-start.1
  21.9 2.2 %collective-permute-start.2 = (f32[4608]{0:T(1024)S(1)}, f32[4608]{0:T(1024)S(1)}, u32[]{:S(2)}, u32[]{:S(2)}) collective-permute-start(f32[4608]{0:T(1024)S(1)} %pad_maximum_fusion.35), channel_id=1, source_target_pairs={{0,6},{1,7},{2,0},{3,1},{4,2},{5,3},{6,4},{7,5},{8,14},{9,15},{10,... | collective-permute-start | bytes 55304 | tf_op jit(solution)/shard_map/ppermute | solution.py:16
  25.2 1.6 collective-permute-start.3
  27.3 3.3 %collective-permute-start.4 = (f32[576]{0:T(1024)S(1)}, f32[576]{0:T(1024)S(1)}, u32[]{:S(2)}, u32[]{:S(2)}) collective-permute-start(f32[576]{0:T(1024)S(1)} %pad_maximum_fusion.82), channel_id=1, source_target_pairs={{0,7},{1,0},{2,1},{3,2},{4,3},{5,4},{6,5},{7,6},{8,15},{9,8},{10,9... | collective-permute-start | bytes 6920 | tf_op jit(solution)/shard_map/ppermute | solution.py:16
  35.1 1.3 constant_dynamic-update-slice_fusion.17
  36.4 1.3 constant_dynamic-update-slice_fusion.16
  37.6 1.3 constant_dynamic-update-slice_fusion.15
  38.9 1.3 constant_dynamic-update-slice_fusion.14
  40.2 1.3 constant_dynamic-update-slice_fusion.13
  61.1 4.7 %collective-permute-start.9 = (f32[1,16,16,1]{3,2,1,0:T(8,128)S(1)}, f32[1,16,16,1]{3,2,1,0:T(8,128)S(1)}, u32[]{:S(2)}, u32[]{:S(2)}) collective-permute-start(f32[1,16,16,1]{3,2,1,0:T(8,128)S(1)} %get-tuple-element.100), channel_id=1, source_target_pairs={{0,7},{1,0},{2,1},{3,2},{4,3},{5,4},{6,5},{7,6},{8,15},{9,8},{10,9... | collective-permute-start | bytes 3080 | tf_op jit(solution)/shard_map/ppermute | solution.py:16
  66.8 3.8 %collective-permute-start.7 = (f32[1,16,1,128]{3,1,2,0:T(8,128)S(1)}, f32[1,16,1,128]{3,1,2,0:T(8,128)S(1)}, u32[]{:S(2)}, u32[]{:S(2)}) collective-permute-start(f32[1,16,1,128]{3,1,2,0:T(8,128)S(1)} %bitcast.662), channel_id=1, source_target_pairs={{0,6},{1,7},{2,0},{3,1},{4,2},{5,3},{6,4},{7,5},{8,14},{9,15},{10,... | collective-permute-start | bytes 24584 | tf_op jit(solution)/shard_map/ppermute | solution.py:16
  72.9 4.7 %collective-permute-start.14 = (f32[1,16,16,1]{3,2,1,0:T(8,128)S(1)}, f32[1,16,16,1]{3,2,1,0:T(8,128)S(1)}, u32[]{:S(2)}, u32[]{:S(2)}) collective-permute-start(f32[1,16,16,1]{3,2,1,0:T(8,128)S(1)} %get-tuple-element.88), channel_id=1, source_target_pairs={{0,7},{1,0},{2,1},{3,2},{4,3},{5,4},{6,5},{7,6},{8,15},{9,8},{10,9... | collective-permute-start | bytes 3080 | tf_op jit(solution)/shard_map/ppermute | solution.py:16
  77.6 2.6 %collective-permute-start.11 = (f32[1,16,1,128]{3,1,2,0:T(8,128)S(1)}, f32[1,16,1,128]{3,1,2,0:T(8,128)S(1)}, u32[]{:S(2)}, u32[]{:S(2)}) collective-permute-start(f32[1,16,1,128]{3,1,2,0:T(8,128)S(1)} %bitcast.667), channel_id=1, source_target_pairs={{0,2},{1,3},{2,4},{3,5},{4,6},{5,7},{6,0},{7,1},{8,10},{9,11},{10,... | collective-permute-start | bytes 24584 | tf_op jit(solution)/shard_map/ppermute | solution.py:16
  80.3 1.2 collective-permute-start.12
  88.5 2.9 %collective-permute-start.17 = (f32[1,8,1,64]{3,1,2,0:T(8,128)S(1)}, f32[1,8,1,64]{3,1,2,0:T(8,128)S(1)}, u32[]{:S(2)}, u32[]{:S(2)}) collective-permute-start(f32[1,8,1,64]{3,1,2,0:T(8,128)S(1)} %get-tuple-element.222), channel_id=1, source_target_pairs={{0,6},{1,7},{2,0},{3,1},{4,2},{5,3},{6,4},{7,5},{8,14},{9,15},{10,... | collective-permute-start | bytes 6152 | tf_op jit(solution)/shard_map/ppermute | solution.py:16
  92.4 3.8 %collective-permute-start.19 = (f32[1,8,8,1]{3,1,2,0:T(8,128)S(1)}, f32[1,8,8,1]{3,1,2,0:T(8,128)S(1)}, u32[]{:S(2)}, u32[]{:S(2)}) collective-permute-start(f32[1,8,8,1]{3,1,2,0:T(8,128)S(1)} %get-tuple-element.223), channel_id=1, source_target_pairs={{0,7},{1,0},{2,1},{3,2},{4,3},{5,4},{6,5},{7,6},{8,15},{9,8},{10,9... | collective-permute-start | bytes 776 | tf_op jit(solution)/shard_map/ppermute | solution.py:16
  96.2 1.9 collective-permute-done.18
  99.3 1.3 collective-permute-start.20
  100.5 2.9 %collective-permute-start.22 = (f32[1,8,1,64]{3,1,2,0:T(8,128)S(1)}, f32[1,8,1,64]{3,1,2,0:T(8,128)S(1)}, u32[]{:S(2)}, u32[]{:S(2)}) collective-permute-start(f32[1,8,1,64]{3,1,2,0:T(8,128)S(1)} %get-tuple-element.200), channel_id=1, source_target_pairs={{0,6},{1,7},{2,0},{3,1},{4,2},{5,3},{6,4},{7,5},{8,14},{9,15},{10,... | collective-permute-start | bytes 6152 | tf_op jit(solution)/shard_map/ppermute | solution.py:16
  103.4 1.4 collective-permute-start.23
  104.8 3.3 %collective-permute-start.24 = (f32[1,8,8,1]{3,1,2,0:T(8,128)S(1)}, f32[1,8,8,1]{3,1,2,0:T(8,128)S(1)}, u32[]{:S(2)}, u32[]{:S(2)}) collective-permute-start(f32[1,8,8,1]{3,1,2,0:T(8,128)S(1)} %get-tuple-element.205), channel_id=1, source_target_pairs={{0,7},{1,0},{2,1},{3,2},{4,3},{5,4},{6,5},{7,6},{8,15},{9,8},{10,9... | collective-permute-start | bytes 776 | tf_op jit(solution)/shard_map/ppermute | solution.py:16
  108.1 1.9 collective-permute-done.23
  112.6 1.3 collective-permute-start.26
  114.5 3.4 %collective-permute-start.28 = (f32[2,4,4,32]{3,2,1,0:T(4,128)S(1)}, f32[2,4,4,32]{3,2,1,0:T(4,128)S(1)}, u32[]{:S(2)}, u32[]{:S(2)}) collective-permute-start(f32[2,4,4,32]{3,2,1,0:T(4,128)S(1)} %pad_maximum_fusion.62), channel_id=1, source_target_pairs={{0,4},{1,5},{2,6},{3,7},{4,0},{5,1},{6,2},{7,3},{8,12},{9,13},{10,... | collective-permute-start | bytes 12296 | tf_op jit(solution)/shard_map/ppermute | solution.py:16
  117.9 3.7 %collective-permute-start.29 = (f32[2,4,4,32]{3,2,1,0:T(4,128)S(1)}, f32[2,4,4,32]{3,2,1,0:T(4,128)S(1)}, u32[]{:S(2)}, u32[]{:S(2)}) collective-permute-start(f32[2,4,4,32]{3,2,1,0:T(4,128)S(1)} %pad_maximum_fusion.62), channel_id=1, source_target_pairs={{0,5},{1,6},{2,7},{3,0},{4,1},{5,2},{6,3},{7,4},{8,13},{9,14},{10,... | collective-permute-start | bytes 12296 | tf_op jit(solution)/shard_map/ppermute | solution.py:16
  121.6 1.5 collective-permute-start.31
  123.1 2.2 %collective-permute-done.30 = f32[2,4,4,32]{3,2,1,0:T(4,128)S(1)} collective-permute-done((f32[2,4,4,32]{3,2,1,0:T(4,128)S(1)}, f32[2,4,4,32]{3,2,1,0:T(4,128)S(1)}, u32[]{:S(2)}, u32[]{:S(2)}) %collective-permute-start.30) | collective-permute-done | bytes 4128 | tf_op jit(solution)/shard_map/ppermute | solution.py:16
  126.7 1.3 fusion.90
  128.5 1.2 fusion.88
  139.2 1.2 fusion.84
  146.0 1.3 collective-permute-start.32
  148.1 4.0 %collective-permute-start.36 = (f32[1,8,8,1]{3,1,2,0:T(8,128)S(1)}, f32[1,8,8,1]{3,1,2,0:T(8,128)S(1)}, u32[]{:S(2)}, u32[]{:S(2)}) collective-permute-start(f32[1,8,8,1]{3,1,2,0:T(8,128)S(1)} %get-tuple-element.175), channel_id=1, source_target_pairs={{0,7},{1,0},{2,1},{3,2},{4,3},{5,4},{6,5},{7,6},{8,15},{9,8},{10,9... | collective-permute-start | bytes 776 | tf_op jit(solution)/shard_map/ppermute | solution.py:16
  152.1 3.8 %collective-permute-start.34 = (f32[1,8,1,64]{3,1,2,0:T(8,128)S(1)}, f32[1,8,1,64]{3,1,2,0:T(8,128)S(1)}, u32[]{:S(2)}, u32[]{:S(2)}) collective-permute-start(f32[1,8,1,64]{3,1,2,0:T(8,128)S(1)} %get-tuple-element.177), channel_id=1, source_target_pairs={{0,6},{1,7},{2,0},{3,1},{4,2},{5,3},{6,4},{7,5},{8,14},{9,15},{10,... | collective-permute-start | bytes 6152 | tf_op jit(solution)/shard_map/ppermute | solution.py:16
  158.9 1.5 collective-permute-start.41
  161.0 3.8 %collective-permute-start.39 = (f32[1,8,1,64]{3,1,2,0:T(8,128)S(1)}, f32[1,8,1,64]{3,1,2,0:T(8,128)S(1)}, u32[]{:S(2)}, u32[]{:S(2)}) collective-permute-start(f32[1,8,1,64]{3,1,2,0:T(8,128)S(1)} %get-tuple-element.159), channel_id=1, source_target_pairs={{0,6},{1,7},{2,0},{3,1},{4,2},{5,3},{6,4},{7,5},{8,14},{9,15},{10,... | collective-permute-start | bytes 6152 | tf_op jit(solution)/shard_map/ppermute | solution.py:16
  165.7 1.3 collective-permute-done.40
  167.9 2.4 %collective-permute-done.38 = f32[1,8,1,64]{3,1,2,0:T(8,128)S(1)} collective-permute-done((f32[1,8,1,64]{3,1,2,0:T(8,128)S(1)}, f32[1,8,1,64]{3,1,2,0:T(8,128)S(1)}, u32[]{:S(2)}, u32[]{:S(2)}) %collective-permute-start.38) | collective-permute-done | bytes 2080 | tf_op jit(solution)/shard_map/ppermute | solution.py:16
  171.4 1.7 collective-permute-start.45
  173.1 3.1 %collective-permute-start.46 = (f32[1,16,16,1]{3,2,1,0:T(8,128)S(1)}, f32[1,16,16,1]{3,2,1,0:T(8,128)S(1)}, u32[]{:S(2)}, u32[]{:S(2)}) collective-permute-start(f32[1,16,16,1]{3,2,1,0:T(8,128)S(1)} %get-tuple-element.68), channel_id=1, source_target_pairs={{0,7},{1,0},{2,1},{3,2},{4,3},{5,4},{6,5},{7,6},{8,15},{9,8},{10,9... | collective-permute-start | bytes 3080 | tf_op jit(solution)/shard_map/ppermute | solution.py:16
  176.2 1.6 collective-permute-start.43
  177.8 2.3 %collective-permute-start.44 = (f32[1,16,1,128]{3,1,2,0:T(8,128)S(1)}, f32[1,16,1,128]{3,1,2,0:T(8,128)S(1)}, u32[]{:S(2)}, u32[]{:S(2)}) collective-permute-start(f32[1,16,1,128]{3,1,2,0:T(8,128)S(1)} %bitcast.664), channel_id=1, source_target_pairs={{0,6},{1,7},{2,0},{3,1},{4,2},{5,3},{6,4},{7,5},{8,14},{9,15},{10,... | collective-permute-start | bytes 24584 | tf_op jit(solution)/shard_map/ppermute | solution.py:16
  182.4 4.6 %collective-permute-start.51 = (f32[1,16,16,1]{3,1,2,0:T(8,128)S(1)}, f32[1,16,16,1]{3,1,2,0:T(8,128)S(1)}, u32[]{:S(2)}, u32[]{:S(2)}) collective-permute-start(f32[1,16,16,1]{3,1,2,0:T(8,128)S(1)} %get-tuple-element.56), channel_id=1, source_target_pairs={{0,7},{1,0},{2,1},{3,2},{4,3},{5,4},{6,5},{7,6},{8,15},{9,8},{10,9... | collective-permute-start | bytes 3080 | tf_op jit(solution)/shard_map/ppermute | solution.py:16
  187.8 2.6 %collective-permute-start.48 = (f32[1,16,1,128]{3,1,2,0:T(8,128)S(1)}, f32[1,16,1,128]{3,1,2,0:T(8,128)S(1)}, u32[]{:S(2)}, u32[]{:S(2)}) collective-permute-start(f32[1,16,1,128]{3,1,2,0:T(8,128)S(1)} %get-tuple-element.61), channel_id=1, source_target_pairs={{0,2},{1,3},{2,4},{3,5},{4,6},{5,7},{6,0},{7,1},{8,10},{9,11},{10,... | collective-permute-start | bytes 24584 | tf_op jit(solution)/shard_map/ppermute | solution.py:16
  190.4 1.3 collective-permute-start.49
  (570 shorter events, 73.3 us)
Async XLA Ops:
  10.9 48.0 %collective-permute-start = (f32[9216]{0:T(1024)S(1)}, f32[9216]{0:T(1024)S(1)}, u32[]{:S(2)}, u32[]{:S(2)}) collective-permute-start(f32[9216]{0:T(1024)S(1)} %constant_dynamic-update-slice_fusion.10), channel_id=1, source_target_pairs={{0,4},{1,5},{2,6},{3,7},{4,0},{5,1},{6,2},{7,3},{8,12},{9,13},{10,... | collective-permute-start | bytes 110600 | tf_op jit(solution)/shard_map/ppermute | solution.py:16
  20.2 34.8 %collective-permute-start.1 = (f32[4608]{0:T(1024)S(1)}, f32[4608]{0:T(1024)S(1)}, u32[]{:S(2)}, u32[]{:S(2)}) collective-permute-start(f32[4608]{0:T(1024)S(1)} %pad_maximum_fusion.34), channel_id=1, source_target_pairs={{0,2},{1,3},{2,4},{3,5},{4,6},{5,7},{6,0},{7,1},{8,10},{9,11},{10,... | collective-permute-start | bytes 55304 | tf_op jit(solution)/shard_map/ppermute | solution.py:16
  21.9 33.7 %collective-permute-start.2 = (f32[4608]{0:T(1024)S(1)}, f32[4608]{0:T(1024)S(1)}, u32[]{:S(2)}, u32[]{:S(2)}) collective-permute-start(f32[4608]{0:T(1024)S(1)} %pad_maximum_fusion.35), channel_id=1, source_target_pairs={{0,6},{1,7},{2,0},{3,1},{4,2},{5,3},{6,4},{7,5},{8,14},{9,15},{10,... | collective-permute-start | bytes 55304 | tf_op jit(solution)/shard_map/ppermute | solution.py:16
  25.2 24.1 %collective-permute-start.3 = (f32[576]{0:T(1024)S(1)}, f32[576]{0:T(1024)S(1)}, u32[]{:S(2)}, u32[]{:S(2)}) collective-permute-start(f32[576]{0:T(1024)S(1)} %pad_maximum_fusion.81), channel_id=1, source_target_pairs={{0,1},{1,2},{2,3},{3,4},{4,5},{5,6},{6,7},{7,0},{8,9},{9,10},{10,1... | collective-permute-start | bytes 6920 | tf_op jit(solution)/shard_map/ppermute | solution.py:16
  27.3 22.0 %collective-permute-start.4 = (f32[576]{0:T(1024)S(1)}, f32[576]{0:T(1024)S(1)}, u32[]{:S(2)}, u32[]{:S(2)}) collective-permute-start(f32[576]{0:T(1024)S(1)} %pad_maximum_fusion.82), channel_id=1, source_target_pairs={{0,7},{1,0},{2,1},{3,2},{4,3},{5,4},{6,5},{7,6},{8,15},{9,8},{10,9... | collective-permute-start | bytes 6920 | tf_op jit(solution)/shard_map/ppermute | solution.py:16
  61.0 9.6 %collective-permute-start.8 = (f32[1,16,16,1]{3,2,1,0:T(8,128)S(1)}, f32[1,16,16,1]{3,2,1,0:T(8,128)S(1)}, u32[]{:S(2)}, u32[]{:S(2)}) collective-permute-start(f32[1,16,16,1]{3,2,1,0:T(8,128)S(1)} %get-tuple-element.101), channel_id=1, source_target_pairs={{0,1},{1,2},{2,3},{3,4},{4,5},{5,6},{6,7},{7,0},{8,9},{9,10},{10,1... | collective-permute-start | bytes 3080 | tf_op jit(solution)/shard_map/ppermute | solution.py:16
  61.1 9.8 %collective-permute-start.9 = (f32[1,16,16,1]{3,2,1,0:T(8,128)S(1)}, f32[1,16,16,1]{3,2,1,0:T(8,128)S(1)}, u32[]{:S(2)}, u32[]{:S(2)}) collective-permute-start(f32[1,16,16,1]{3,2,1,0:T(8,128)S(1)} %get-tuple-element.100), channel_id=1, source_target_pairs={{0,7},{1,0},{2,1},{3,2},{4,3},{5,4},{6,5},{7,6},{8,15},{9,8},{10,9... | collective-permute-start | bytes 3080 | tf_op jit(solution)/shard_map/ppermute | solution.py:16
  65.8 5.4 %collective-permute-start.5 = (f32[1,2,16,128]{3,2,1,0:T(8,128)S(1)}, f32[1,2,16,128]{3,2,1,0:T(8,128)S(1)}, u32[]{:S(2)}, u32[]{:S(2)}) collective-permute-start(f32[1,2,16,128]{3,2,1,0:T(8,128)S(1)} %pad_maximum_fusion.60), channel_id=1, source_target_pairs={{0,4},{1,5},{2,6},{3,7},{4,0},{5,1},{6,2},{7,3},{8,12},{9,13},{10,... | collective-permute-start | bytes 49160 | tf_op jit(solution)/shard_map/ppermute | solution.py:16
  66.8 5.4 %collective-permute-start.6 = (f32[1,16,1,128]{3,1,2,0:T(8,128)S(1)}, f32[1,16,1,128]{3,1,2,0:T(8,128)S(1)}, u32[]{:S(2)}, u32[]{:S(2)}) collective-permute-start(f32[1,16,1,128]{3,1,2,0:T(8,128)S(1)} %bitcast.663), channel_id=1, source_target_pairs={{0,2},{1,3},{2,4},{3,5},{4,6},{5,7},{6,0},{7,1},{8,10},{9,11},{10,... | collective-permute-start | bytes 24584 | tf_op jit(solution)/shard_map/ppermute | solution.py:16
  66.8 5.4 %collective-permute-start.7 = (f32[1,16,1,128]{3,1,2,0:T(8,128)S(1)}, f32[1,16,1,128]{3,1,2,0:T(8,128)S(1)}, u32[]{:S(2)}, u32[]{:S(2)}) collective-permute-start(f32[1,16,1,128]{3,1,2,0:T(8,128)S(1)} %bitcast.662), channel_id=1, source_target_pairs={{0,6},{1,7},{2,0},{3,1},{4,2},{5,3},{6,4},{7,5},{8,14},{9,15},{10,... | collective-permute-start | bytes 24584 | tf_op jit(solution)/shard_map/ppermute | solution.py:16
  72.8 8.7 %collective-permute-start.13 = (f32[1,16,16,1]{3,2,1,0:T(8,128)S(1)}, f32[1,16,16,1]{3,2,1,0:T(8,128)S(1)}, u32[]{:S(2)}, u32[]{:S(2)}) collective-permute-start(f32[1,16,16,1]{3,2,1,0:T(8,128)S(1)} %get-tuple-element.89), channel_id=1, source_target_pairs={{0,1},{1,2},{2,3},{3,4},{4,5},{5,6},{6,7},{7,0},{8,9},{9,10},{10,1... | collective-permute-start | bytes 3080 | tf_op jit(solution)/shard_map/ppermute | solution.py:16
  72.9 8.9 %collective-permute-start.14 = (f32[1,16,16,1]{3,2,1,0:T(8,128)S(1)}, f32[1,16,16,1]{3,2,1,0:T(8,128)S(1)}, u32[]{:S(2)}, u32[]{:S(2)}) collective-permute-start(f32[1,16,16,1]{3,2,1,0:T(8,128)S(1)} %get-tuple-element.88), channel_id=1, source_target_pairs={{0,7},{1,0},{2,1},{3,2},{4,3},{5,4},{6,5},{7,6},{8,15},{9,8},{10,9... | collective-permute-start | bytes 3080 | tf_op jit(solution)/shard_map/ppermute | solution.py:16
  77.6 4.6 %collective-permute-start.10 = (f32[1,2,16,128]{3,2,1,0:T(8,128)S(1)}, f32[1,2,16,128]{3,2,1,0:T(8,128)S(1)}, u32[]{:S(2)}, u32[]{:S(2)}) collective-permute-start(f32[1,2,16,128]{3,2,1,0:T(8,128)S(1)} %pad_maximum_fusion.61), channel_id=1, source_target_pairs={{0,4},{1,5},{2,6},{3,7},{4,0},{5,1},{6,2},{7,3},{8,12},{9,13},{10,... | collective-permute-start | bytes 49160 | tf_op jit(solution)/shard_map/ppermute | solution.py:16
  77.6 5.5 %collective-permute-start.11 = (f32[1,16,1,128]{3,1,2,0:T(8,128)S(1)}, f32[1,16,1,128]{3,1,2,0:T(8,128)S(1)}, u32[]{:S(2)}, u32[]{:S(2)}) collective-permute-start(f32[1,16,1,128]{3,1,2,0:T(8,128)S(1)} %bitcast.667), channel_id=1, source_target_pairs={{0,2},{1,3},{2,4},{3,5},{4,6},{5,7},{6,0},{7,1},{8,10},{9,11},{10,... | collective-permute-start | bytes 24584 | tf_op jit(solution)/shard_map/ppermute | solution.py:16
  87.6 11.2 %collective-permute-start.16 = (f32[1,8,1,64]{3,1,2,0:T(8,128)S(1)}, f32[1,8,1,64]{3,1,2,0:T(8,128)S(1)}, u32[]{:S(2)}, u32[]{:S(2)}) collective-permute-start(f32[1,8,1,64]{3,1,2,0:T(8,128)S(1)} %get-tuple-element.221), channel_id=1, source_target_pairs={{0,2},{1,3},{2,4},{3,5},{4,6},{5,7},{6,0},{7,1},{8,10},{9,11},{10,... | collective-permute-start | bytes 6152 | tf_op jit(solution)/shard_map/ppermute | solution.py:16
  88.5 10.2 %collective-permute-start.17 = (f32[1,8,1,64]{3,1,2,0:T(8,128)S(1)}, f32[1,8,1,64]{3,1,2,0:T(8,128)S(1)}, u32[]{:S(2)}, u32[]{:S(2)}) collective-permute-start(f32[1,8,1,64]{3,1,2,0:T(8,128)S(1)} %get-tuple-element.222), channel_id=1, source_target_pairs={{0,6},{1,7},{2,0},{3,1},{4,2},{5,3},{6,4},{7,5},{8,14},{9,15},{10,... | collective-permute-start | bytes 6152 | tf_op jit(solution)/shard_map/ppermute | solution.py:16
  91.5 7.3 %collective-permute-start.15 = (f32[1,2,8,64]{3,2,1,0:T(8,128)S(1)}, f32[1,2,8,64]{3,2,1,0:T(8,128)S(1)}, u32[]{:S(2)}, u32[]{:S(2)}) collective-permute-start(f32[1,2,8,64]{3,2,1,0:T(8,128)S(1)} %pad_maximum_fusion.75), channel_id=1, source_target_pairs={{0,4},{1,5},{2,6},{3,7},{4,0},{5,1},{6,2},{7,3},{8,12},{9,13},{10,... | collective-permute-start | bytes 12296 | tf_op jit(solution)/shard_map/ppermute | solution.py:16
  91.5 6.6 %collective-permute-start.18 = (f32[1,8,8,1]{3,1,2,0:T(8,128)S(1)}, f32[1,8,8,1]{3,1,2,0:T(8,128)S(1)}, u32[]{:S(2)}, u32[]{:S(2)}) collective-permute-start(f32[1,8,8,1]{3,1,2,0:T(8,128)S(1)} %get-tuple-element.224), channel_id=1, source_target_pairs={{0,1},{1,2},{2,3},{3,4},{4,5},{5,6},{6,7},{7,0},{8,9},{9,10},{10,1... | collective-permute-start | bytes 776 | tf_op jit(solution)/shard_map/ppermute | solution.py:16
  92.4 6.0 %collective-permute-start.19 = (f32[1,8,8,1]{3,1,2,0:T(8,128)S(1)}, f32[1,8,8,1]{3,1,2,0:T(8,128)S(1)}, u32[]{:S(2)}, u32[]{:S(2)}) collective-permute-start(f32[1,8,8,1]{3,1,2,0:T(8,128)S(1)} %get-tuple-element.223), channel_id=1, source_target_pairs={{0,7},{1,0},{2,1},{3,2},{4,3},{5,4},{6,5},{7,6},{8,15},{9,8},{10,9... | collective-permute-start | bytes 776 | tf_op jit(solution)/shard_map/ppermute | solution.py:16
  99.2 11.2 %collective-permute-start.21 = (f32[1,8,1,64]{3,1,2,0:T(8,128)S(1)}, f32[1,8,1,64]{3,1,2,0:T(8,128)S(1)}, u32[]{:S(2)}, u32[]{:S(2)}) collective-permute-start(f32[1,8,1,64]{3,1,2,0:T(8,128)S(1)} %get-tuple-element.199), channel_id=1, source_target_pairs={{0,2},{1,3},{2,4},{3,5},{4,6},{5,7},{6,0},{7,1},{8,10},{9,11},{10,... | collective-permute-start | bytes 6152 | tf_op jit(solution)/shard_map/ppermute | solution.py:16
  99.3 11.2 %collective-permute-start.20 = (f32[1,2,8,64]{3,2,1,0:T(8,128)S(1)}, f32[1,2,8,64]{3,2,1,0:T(8,128)S(1)}, u32[]{:S(2)}, u32[]{:S(2)}) collective-permute-start(f32[1,2,8,64]{3,2,1,0:T(8,128)S(1)} %pad_maximum_fusion.76), channel_id=1, source_target_pairs={{0,4},{1,5},{2,6},{3,7},{4,0},{5,1},{6,2},{7,3},{8,12},{9,13},{10,... | collective-permute-start | bytes 12296 | tf_op jit(solution)/shard_map/ppermute | solution.py:16
  100.5 9.9 %collective-permute-start.22 = (f32[1,8,1,64]{3,1,2,0:T(8,128)S(1)}, f32[1,8,1,64]{3,1,2,0:T(8,128)S(1)}, u32[]{:S(2)}, u32[]{:S(2)}) collective-permute-start(f32[1,8,1,64]{3,1,2,0:T(8,128)S(1)} %get-tuple-element.200), channel_id=1, source_target_pairs={{0,6},{1,7},{2,0},{3,1},{4,2},{5,3},{6,4},{7,5},{8,14},{9,15},{10,... | collective-permute-start | bytes 6152 | tf_op jit(solution)/shard_map/ppermute | solution.py:16
  103.4 6.6 %collective-permute-start.23 = (f32[1,8,8,1]{3,1,2,0:T(8,128)S(1)}, f32[1,8,8,1]{3,1,2,0:T(8,128)S(1)}, u32[]{:S(2)}, u32[]{:S(2)}) collective-permute-start(f32[1,8,8,1]{3,1,2,0:T(8,128)S(1)} %get-tuple-element.206), channel_id=1, source_target_pairs={{0,1},{1,2},{2,3},{3,4},{4,5},{5,6},{6,7},{7,0},{8,9},{9,10},{10,1... | collective-permute-start | bytes 776 | tf_op jit(solution)/shard_map/ppermute | solution.py:16
  104.8 5.4 %collective-permute-start.24 = (f32[1,8,8,1]{3,1,2,0:T(8,128)S(1)}, f32[1,8,8,1]{3,1,2,0:T(8,128)S(1)}, u32[]{:S(2)}, u32[]{:S(2)}) collective-permute-start(f32[1,8,8,1]{3,1,2,0:T(8,128)S(1)} %get-tuple-element.205), channel_id=1, source_target_pairs={{0,7},{1,0},{2,1},{3,2},{4,3},{5,4},{6,5},{7,6},{8,15},{9,8},{10,9... | collective-permute-start | bytes 776 | tf_op jit(solution)/shard_map/ppermute | solution.py:16
  112.1 9.5 %collective-permute-start.25 = (f32[2,4,4,32]{3,2,1,0:T(4,128)S(1)}, f32[2,4,4,32]{3,2,1,0:T(4,128)S(1)}, u32[]{:S(2)}, u32[]{:S(2)}) collective-permute-start(f32[2,4,4,32]{3,2,1,0:T(4,128)S(1)} %pad_maximum_fusion.62), channel_id=1, source_target_pairs={{0,1},{1,2},{2,3},{3,4},{4,5},{5,6},{6,7},{7,0},{8,9},{9,10},{10,1... | collective-permute-start | bytes 12296 | tf_op jit(solution)/shard_map/ppermute | solution.py:16
  112.6 9.0 %collective-permute-start.26 = (f32[2,4,4,32]{3,2,1,0:T(4,128)S(1)}, f32[2,4,4,32]{3,2,1,0:T(4,128)S(1)}, u32[]{:S(2)}, u32[]{:S(2)}) collective-permute-start(f32[2,4,4,32]{3,2,1,0:T(4,128)S(1)} %pad_maximum_fusion.62), channel_id=1, source_target_pairs={{0,2},{1,3},{2,4},{3,5},{4,6},{5,7},{6,0},{7,1},{8,10},{9,11},{10,... | collective-permute-start | bytes 12296 | tf_op jit(solution)/shard_map/ppermute | solution.py:16
  113.9 9.2 %collective-permute-start.27 = (f32[2,4,4,32]{3,2,1,0:T(4,128)S(1)}, f32[2,4,4,32]{3,2,1,0:T(4,128)S(1)}, u32[]{:S(2)}, u32[]{:S(2)}) collective-permute-start(f32[2,4,4,32]{3,2,1,0:T(4,128)S(1)} %pad_maximum_fusion.62), channel_id=1, source_target_pairs={{0,3},{1,4},{2,5},{3,6},{4,7},{5,0},{6,1},{7,2},{8,11},{9,12},{10,... | collective-permute-start | bytes 12296 | tf_op jit(solution)/shard_map/ppermute | solution.py:16
  114.5 8.6 %collective-permute-start.28 = (f32[2,4,4,32]{3,2,1,0:T(4,128)S(1)}, f32[2,4,4,32]{3,2,1,0:T(4,128)S(1)}, u32[]{:S(2)}, u32[]{:S(2)}) collective-permute-start(f32[2,4,4,32]{3,2,1,0:T(4,128)S(1)} %pad_maximum_fusion.62), channel_id=1, source_target_pairs={{0,4},{1,5},{2,6},{3,7},{4,0},{5,1},{6,2},{7,3},{8,12},{9,13},{10,... | collective-permute-start | bytes 12296 | tf_op jit(solution)/shard_map/ppermute | solution.py:16
  117.9 5.2 %collective-permute-start.29 = (f32[2,4,4,32]{3,2,1,0:T(4,128)S(1)}, f32[2,4,4,32]{3,2,1,0:T(4,128)S(1)}, u32[]{:S(2)}, u32[]{:S(2)}) collective-permute-start(f32[2,4,4,32]{3,2,1,0:T(4,128)S(1)} %pad_maximum_fusion.62), channel_id=1, source_target_pairs={{0,5},{1,6},{2,7},{3,0},{4,1},{5,2},{6,3},{7,4},{8,13},{9,14},{10,... | collective-permute-start | bytes 12296 | tf_op jit(solution)/shard_map/ppermute | solution.py:16
  121.6 4.0 %collective-permute-start.31 = (f32[2,4,4,32]{3,2,1,0:T(4,128)S(1)}, f32[2,4,4,32]{3,2,1,0:T(4,128)S(1)}, u32[]{:S(2)}, u32[]{:S(2)}) collective-permute-start(f32[2,4,4,32]{3,2,1,0:T(4,128)S(1)} %pad_maximum_fusion.62), channel_id=1, source_target_pairs={{0,7},{1,0},{2,1},{3,2},{4,3},{5,4},{6,5},{7,6},{8,15},{9,8},{10,9... | collective-permute-start | bytes 12296 | tf_op jit(solution)/shard_map/ppermute | solution.py:16
  146.0 10.4 %collective-permute-start.32 = (f32[1,2,8,64]{3,2,1,0:T(8,128)S(1)}, f32[1,2,8,64]{3,2,1,0:T(8,128)S(1)}, u32[]{:S(2)}, u32[]{:S(2)}) collective-permute-start(f32[1,2,8,64]{3,2,1,0:T(8,128)S(1)} %pad_maximum_fusion.79), channel_id=1, source_target_pairs={{0,4},{1,5},{2,6},{3,7},{4,0},{5,1},{6,2},{7,3},{8,12},{9,13},{10,... | collective-permute-start | bytes 12296 | tf_op jit(solution)/shard_map/ppermute | solution.py:16
  147.4 8.6 %collective-permute-start.35 = (f32[1,8,8,1]{3,1,2,0:T(8,128)S(1)}, f32[1,8,8,1]{3,1,2,0:T(8,128)S(1)}, u32[]{:S(2)}, u32[]{:S(2)}) collective-permute-start(f32[1,8,8,1]{3,1,2,0:T(8,128)S(1)} %get-tuple-element.176), channel_id=1, source_target_pairs={{0,1},{1,2},{2,3},{3,4},{4,5},{5,6},{6,7},{7,0},{8,9},{9,10},{10,1... | collective-permute-start | bytes 776 | tf_op jit(solution)/shard_map/ppermute | solution.py:16
  148.1 8.1 %collective-permute-start.36 = (f32[1,8,8,1]{3,1,2,0:T(8,128)S(1)}, f32[1,8,8,1]{3,1,2,0:T(8,128)S(1)}, u32[]{:S(2)}, u32[]{:S(2)}) collective-permute-start(f32[1,8,8,1]{3,1,2,0:T(8,128)S(1)} %get-tuple-element.175), channel_id=1, source_target_pairs={{0,7},{1,0},{2,1},{3,2},{4,3},{5,4},{6,5},{7,6},{8,15},{9,8},{10,9... | collective-permute-start | bytes 776 | tf_op jit(solution)/shard_map/ppermute | solution.py:16
  152.1 5.4 %collective-permute-start.33 = (f32[1,8,1,64]{3,1,2,0:T(8,128)S(1)}, f32[1,8,1,64]{3,1,2,0:T(8,128)S(1)}, u32[]{:S(2)}, u32[]{:S(2)}) collective-permute-start(f32[1,8,1,64]{3,1,2,0:T(8,128)S(1)} %get-tuple-element.178), channel_id=1, source_target_pairs={{0,2},{1,3},{2,4},{3,5},{4,6},{5,7},{6,0},{7,1},{8,10},{9,11},{10,... | collective-permute-start | bytes 6152 | tf_op jit(solution)/shard_map/ppermute | solution.py:16
  152.1 5.4 %collective-permute-start.34 = (f32[1,8,1,64]{3,1,2,0:T(8,128)S(1)}, f32[1,8,1,64]{3,1,2,0:T(8,128)S(1)}, u32[]{:S(2)}, u32[]{:S(2)}) collective-permute-start(f32[1,8,1,64]{3,1,2,0:T(8,128)S(1)} %get-tuple-element.177), channel_id=1, source_target_pairs={{0,6},{1,7},{2,0},{3,1},{4,2},{5,3},{6,4},{7,5},{8,14},{9,15},{10,... | collective-permute-start | bytes 6152 | tf_op jit(solution)/shard_map/ppermute | solution.py:16
  158.9 6.6 %collective-permute-start.41 = (f32[1,8,8,1]{3,1,2,0:T(8,128)S(1)}, f32[1,8,8,1]{3,1,2,0:T(8,128)S(1)}, u32[]{:S(2)}, u32[]{:S(2)}) collective-permute-start(f32[1,8,8,1]{3,1,2,0:T(8,128)S(1)} %get-tuple-element.157), channel_id=1, source_target_pairs={{0,7},{1,0},{2,1},{3,2},{4,3},{5,4},{6,5},{7,6},{8,15},{9,8},{10,9... | collective-permute-start | bytes 776 | tf_op jit(solution)/shard_map/ppermute | solution.py:16
  160.4 6.6 %collective-permute-start.40 = (f32[1,8,8,1]{3,1,2,0:T(8,128)S(1)}, f32[1,8,8,1]{3,1,2,0:T(8,128)S(1)}, u32[]{:S(2)}, u32[]{:S(2)}) collective-permute-start(f32[1,8,8,1]{3,1,2,0:T(8,128)S(1)} %get-tuple-element.158), channel_id=1, source_target_pairs={{0,1},{1,2},{2,3},{3,4},{4,5},{5,6},{6,7},{7,0},{8,9},{9,10},{10,1... | collective-permute-start | bytes 776 | tf_op jit(solution)/shard_map/ppermute | solution.py:16
  161.0 6.7 %collective-permute-start.39 = (f32[1,8,1,64]{3,1,2,0:T(8,128)S(1)}, f32[1,8,1,64]{3,1,2,0:T(8,128)S(1)}, u32[]{:S(2)}, u32[]{:S(2)}) collective-permute-start(f32[1,8,1,64]{3,1,2,0:T(8,128)S(1)} %get-tuple-element.159), channel_id=1, source_target_pairs={{0,6},{1,7},{2,0},{3,1},{4,2},{5,3},{6,4},{7,5},{8,14},{9,15},{10,... | collective-permute-start | bytes 6152 | tf_op jit(solution)/shard_map/ppermute | solution.py:16
  164.8 5.5 %collective-permute-start.38 = (f32[1,8,1,64]{3,1,2,0:T(8,128)S(1)}, f32[1,8,1,64]{3,1,2,0:T(8,128)S(1)}, u32[]{:S(2)}, u32[]{:S(2)}) collective-permute-start(f32[1,8,1,64]{3,1,2,0:T(8,128)S(1)} %get-tuple-element.160), channel_id=1, source_target_pairs={{0,2},{1,3},{2,4},{3,5},{4,6},{5,7},{6,0},{7,1},{8,10},{9,11},{10,... | collective-permute-start | bytes 6152 | tf_op jit(solution)/shard_map/ppermute | solution.py:16
  164.8 5.7 %collective-permute-start.37 = (f32[1,2,8,64]{3,1,2,0:T(2,128)S(1)}, f32[1,2,8,64]{3,1,2,0:T(2,128)S(1)}, u32[]{:S(2)}, u32[]{:S(2)}) collective-permute-start(f32[1,2,8,64]{3,1,2,0:T(2,128)S(1)} %pad_maximum_fusion.80), channel_id=1, source_target_pairs={{0,4},{1,5},{2,6},{3,7},{4,0},{5,1},{6,2},{7,3},{8,12},{9,13},{10,... | collective-permute-start | bytes 12296 | tf_op jit(solution)/shard_map/ppermute | solution.py:16
  171.4 8.7 %collective-permute-start.45 = (f32[1,16,16,1]{3,2,1,0:T(8,128)S(1)}, f32[1,16,16,1]{3,2,1,0:T(8,128)S(1)}, u32[]{:S(2)}, u32[]{:S(2)}) collective-permute-start(f32[1,16,16,1]{3,2,1,0:T(8,128)S(1)} %get-tuple-element.69), channel_id=1, source_target_pairs={{0,1},{1,2},{2,3},{3,4},{4,5},{5,6},{6,7},{7,0},{8,9},{9,10},{10,1... | collective-permute-start | bytes 3080 | tf_op jit(solution)/shard_map/ppermute | solution.py:16
  173.1 7.3 %collective-permute-start.46 = (f32[1,16,16,1]{3,2,1,0:T(8,128)S(1)}, f32[1,16,16,1]{3,2,1,0:T(8,128)S(1)}, u32[]{:S(2)}, u32[]{:S(2)}) collective-permute-start(f32[1,16,16,1]{3,2,1,0:T(8,128)S(1)} %get-tuple-element.68), channel_id=1, source_target_pairs={{0,7},{1,0},{2,1},{3,2},{4,3},{5,4},{6,5},{7,6},{8,15},{9,8},{10,9... | collective-permute-start | bytes 3080 | tf_op jit(solution)/shard_map/ppermute | solution.py:16
  176.2 4.6 %collective-permute-start.42 = (f32[1,2,16,128]{3,2,1,0:T(8,128)S(1)}, f32[1,2,16,128]{3,2,1,0:T(8,128)S(1)}, u32[]{:S(2)}, u32[]{:S(2)}) collective-permute-start(f32[1,2,16,128]{3,2,1,0:T(8,128)S(1)} %pad_maximum_fusion.63), channel_id=1, source_target_pairs={{0,4},{1,5},{2,6},{3,7},{4,0},{5,1},{6,2},{7,3},{8,12},{9,13},{10,... | collective-permute-start | bytes 49160 | tf_op jit(solution)/shard_map/ppermute | solution.py:16
  176.2 5.5 %collective-permute-start.43 = (f32[1,16,1,128]{3,1,2,0:T(8,128)S(1)}, f32[1,16,1,128]{3,1,2,0:T(8,128)S(1)}, u32[]{:S(2)}, u32[]{:S(2)}) collective-permute-start(f32[1,16,1,128]{3,1,2,0:T(8,128)S(1)} %bitcast.665), channel_id=1, source_target_pairs={{0,2},{1,3},{2,4},{3,5},{4,6},{5,7},{6,0},{7,1},{8,10},{9,11},{10,... | collective-permute-start | bytes 24584 | tf_op jit(solution)/shard_map/ppermute | solution.py:16
  182.2 9.4 %collective-permute-start.50 = (f32[1,16,16,1]{3,1,2,0:T(8,128)S(1)}, f32[1,16,16,1]{3,1,2,0:T(8,128)S(1)}, u32[]{:S(2)}, u32[]{:S(2)}) collective-permute-start(f32[1,16,16,1]{3,1,2,0:T(8,128)S(1)} %get-tuple-element.57), channel_id=1, source_target_pairs={{0,1},{1,2},{2,3},{3,4},{4,5},{5,6},{6,7},{7,0},{8,9},{9,10},{10,1... | collective-permute-start | bytes 3080 | tf_op jit(solution)/shard_map/ppermute | solution.py:16
  182.4 9.6 %collective-permute-start.51 = (f32[1,16,16,1]{3,1,2,0:T(8,128)S(1)}, f32[1,16,16,1]{3,1,2,0:T(8,128)S(1)}, u32[]{:S(2)}, u32[]{:S(2)}) collective-permute-start(f32[1,16,16,1]{3,1,2,0:T(8,128)S(1)} %get-tuple-element.56), channel_id=1, source_target_pairs={{0,7},{1,0},{2,1},{3,2},{4,3},{5,4},{6,5},{7,6},{8,15},{9,8},{10,9... | collective-permute-start | bytes 3080 | tf_op jit(solution)/shard_map/ppermute | solution.py:16
  187.0 5.3 %collective-permute-start.47 = (f32[1,2,16,128]{3,1,2,0:T(2,128)S(1)}, f32[1,2,16,128]{3,1,2,0:T(2,128)S(1)}, u32[]{:S(2)}, u32[]{:S(2)}) collective-permute-start(f32[1,2,16,128]{3,1,2,0:T(2,128)S(1)} %pad_maximum_fusion.64), channel_id=1, source_target_pairs={{0,4},{1,5},{2,6},{3,7},{4,0},{5,1},{6,2},{7,3},{8,12},{9,13},{10,... | collective-permute-start | bytes 49160 | tf_op jit(solution)/shard_map/ppermute | solution.py:16
  187.8 5.4 %collective-permute-start.48 = (f32[1,16,1,128]{3,1,2,0:T(8,128)S(1)}, f32[1,16,1,128]{3,1,2,0:T(8,128)S(1)}, u32[]{:S(2)}, u32[]{:S(2)}) collective-permute-start(f32[1,16,1,128]{3,1,2,0:T(8,128)S(1)} %get-tuple-element.61), channel_id=1, source_target_pairs={{0,2},{1,3},{2,4},{3,5},{4,6},{5,7},{6,0},{7,1},{8,10},{9,11},{10,... | collective-permute-start | bytes 24584 | tf_op jit(solution)/shard_map/ppermute | solution.py:16
  (52 other events, 72.9 us)

commit v4 on v3

--- a/solution.py
+++ b/solution.py
@@ -61,6 +61,39 @@
     return result
 
 
+def exchange_with_coarse(fields, coarse, per_side):
+    count_dev = lax.axis_size("space")
+    plane_step = per_side * per_side
+    size_x, size_y, size_z = fields.shape[1:]
+    half_x, half_y, half_z = coarse.shape
+
+    def padded(face):
+        pads = [(0, full - part) if part != 1 else (0, 0) for full, part in zip((size_x, size_y, size_z), face.shape)]
+        return jnp.pad(face, pads)[None]
+
+    def message(number):
+        pieces = [fields[:, -1:], fields[:, :1], fields[:, :, -1:], fields[:, :, :1], fields[:, :, :, -1:], fields[:, :, :, :1]]
+        return jnp.concatenate([pieces[number], padded(own_faces(coarse)[number])], axis=0)
+
+    shifts = [plane_step, -plane_step, per_side, -per_side, 1, -1]
+    received = [None] * 6
+    if (2 * plane_step) % count_dev == 0:
+        both = shifted(jnp.concatenate([message(0), message(1)], axis=1), "space", plane_step)
+        received[0], received[1] = both[:, :1], both[:, 1:]
+        rest = range(2, 6)
+    else:
+        rest = range(6)
+    for number in rest:
+        received[number] = shifted(message(number), "space", shifts[number])
+    count = fields.shape[0]
+    field_faces = [face[:count] for face in received]
+    coarse_faces = []
+    for number, face in enumerate(received):
+        shape = own_faces(coarse)[number].shape
+        coarse_faces.append(face[count, : shape[0], : shape[1], : shape[2]])
+    return field_faces, coarse_faces
+
+
 def gather_rows(block, per_side):
     count_dev = lax.axis_size("space")
     if count_dev > 16:
@@ -225,18 +258,16 @@
 
 
 def flat_faces(values, picker, lower_z, upper_z):
-    count_r = values.shape[0]
+    count_r, size_z = values.shape
     rows = jnp.dot(picker, values, precision=lax.Precision.HIGHEST)
-    lower = jnp.dot(
-        jnp.concatenate([values, rows[4 * count_r : 5 * count_r]], axis=1),
-        lower_z,
-        precision=lax.Precision.HIGHEST,
-    )
-    upper = jnp.dot(
-        jnp.concatenate([values, rows[5 * count_r :]], axis=1),
-        upper_z,
-        precision=lax.Precision.HIGHEST,
-    )
+
+    def along_z(shift, wrapped):
+        return jnp.dot(values, shift[:size_z], precision=lax.Precision.HIGHEST) + jnp.dot(
+            wrapped, shift[size_z:], precision=lax.Precision.HIGHEST
+        )
+
+    lower = along_z(lower_z, rows[4 * count_r : 5 * count_r])
+    upper = along_z(upper_z, rows[5 * count_r :])
     return [rows[k * count_r : (k + 1) * count_r] for k in range(4)] + [lower, upper]
 
 
@@ -350,9 +381,9 @@
 
     values = guess[0]
     coarse_perm = coarsen(permeab)
-    first = exchange_mixed([permeab, values, coarse_perm], per_side)
-    face_coefs, diagonal = coefficients(permeab, with_faces(permeab, first[0]), 1.0)
-    values = smooth(values, source, face_coefs, diagonal, 1.0, with_faces(values, first[1]))
+    first, coarse_first = exchange_with_coarse(jnp.stack([permeab, values]), coarse_perm, per_side)
+    face_coefs, diagonal = coefficients(permeab, with_faces(permeab, pick(first, 0)), 1.0)
+    values = smooth(values, source, face_coefs, diagonal, 1.0, with_faces(values, pick(first, 1)))
     for sweep_no in range(SWEEPS - 1):
         faces = pick(exchange(values[None], per_side), 0)
         values = smooth(values, source, face_coefs, diagonal, 1.0, with_faces(values, faces))
@@ -362,7 +393,7 @@
 
     scaling = 0.25
     right_1 = coarsen(leftover)
-    coefs_1, diagonal_1 = coefficients(coarse_perm, with_faces(coarse_perm, first[2]), scaling)
+    coefs_1, diagonal_1 = coefficients(coarse_perm, with_faces(coarse_perm, coarse_first), scaling)
     values_1 = OMEGA * right_1 / diagonal_1
     for sweep_no in range(SWEEPS - 1):
         faces = pick(exchange(values_1[None], per_side), 0)

time: 196 us -> 195 us (level)
  waiting for transfers between devices: 16.5 us -> 55.5 us
  starting transfers between devices: 92.2 us -> 64.2 us
  other arithmetic: 25.5 us -> 17.1 us
  local copies, waits for them, and re-layouts: 41.7 us -> 36.2 us
  matrix products: 16.3 us -> 18.3 us
    ppermute x52, waiting for transfers between devices: 16.5 us -> 55.5 us  [shifted(): lax.ppermute(shard, axis, [(i, (i + by) % peers) for i in range(peers)])]
    ppermute x52, starting transfers between devices: 92.2 us -> 64.2 us  [shifted(): lax.ppermute(shard, axis, [(i, (i + by) % peers) for i in range(peers)])]
    add x2 -> x0, other arithmetic: 11.1 us -> none  [shards(): permeab = permeab + jnp.where(classes == number, class_values[number], 0.0)]
    unnamed x7, other arithmetic: 6.38 us -> 0.1 us
    squeeze x0 -> x1, other arithmetic: none -> 6.21 us  [shards(): values = guess[0]]
    dot_general x22 -> x44, matrix products: 4.19 us -> 10.1 us  [the longest x22 5.67 us: along_z(): jnp.dot(wrapped, shift[size_z:], precision=lax.Precision.HIGHEST)]
    reshape x28 -> x0, local copies, waits for them, and re-layouts: 4.93 us -> none  [the longest x16 4.13 us: exchange_mixed(): received[d][offset:offset + size].reshape(faces[d].shape)]
    dot_general x11, matrix products: 7.99 us -> 4.73 us  [flat_faces(): rows = jnp.dot(picker, values, precision=lax.Precision.HIGHEST)]
  transfers between devices with their start and end apart: 52 -> 52, of which waited for: 15 -> 20; matrix products, arithmetic and copies ran while one was open for 21% -> 13% of each run, Pallas kernels for 0% -> 0%
where the time goes in v4:
time: 195 us; the launch traced here: 194 us
  starting transfers between devices  64.2 us (33%)
  waiting for transfers between devices  55.5 us (28%)
  local copies, waits for them, and re-layouts  36.2 us (19%)
  matrix products  18.3 us (9%)
  other arithmetic  17.1 us (9%)
  between operations  2.61 us (1%)
    ppermute x52, starting transfers between devices, shifted(): lax.ppermute(shard, axis, [(i, (i + by) % peers) for i in range(peers)])  64.2 us
    ppermute x52, waiting for transfers between devices, shifted(): lax.ppermute(shard, axis, [(i, (i + by) % peers) for i in range(peers)])  55.5 us
    unnamed x98, local copies, waits for them, and re-layouts  11.7 us
    squeeze x1, other arithmetic, shards(): values = guess[0]  6.21 us
    dot_general x22, matrix products, along_z(): jnp.dot(wrapped, shift[size_z:], precision=lax.Precision.HIGHEST)  5.67 us
    dot_general x11, matrix products, flat_faces(): rows = jnp.dot(picker, values, precision=lax.Precision.HIGHEST)  4.73 us
    dot_general x22, matrix products, along_z(): jnp.dot(values, shift[:size_z], precision=lax.Precision.HIGHEST)  4.42 us
    squeeze x18, local copies, waits for them, and re-layouts, pick(): return [face[number] for face in faces]  4.4 us
  transfers between devices with their start and end apart: 52, of which 20 were waited for; matrix products, arithmetic and copies ran while one was open for 13% of the time, Pallas kernels for 0%

profile of v4, /device:TPU:0, one launch (start us, length us, event | category | flops | bytes accessed | tf_op | source)
XLA Modules:
  0.0 194.0 jit_solution(6323714802833328255)
XLA Ops:
  2.0 6.2 %copy_bitcast_fusion.3 = (f32[16,16,128]{2,0,1:T(8,128)S(1)}, f32[1,16,16,128]{3,1,2,0:T(8,128)S(1)}, f32[1,16,16,128]{3,1,2,0:T(8,128)S(1)}) fusion(f32[1,16,16,128]{3,2,1,0:T(8,128)} %param.9, f32[]{:T(128)} %bitcast.10, f32[]{:T(128)} %bitcast.9, f32[]{:T(128)} %bitcast.8, f32[]{:T(128)} %bitcast.7, f32[]{:T(128)} %bitcast.6, f32[]{:T(128)} %bitcast.5, ...), kind=kLoop, calls=%fused_computation.1494 | loop fusion | flops 753664 | bytes 655392 | tf_op jit(solution)/shard_map/squeeze | solution.py:382
  9.5 5.1 %collective-permute-start.2 = (f32[3,16,1,128]{3,1,2,0:T(8,128)}, f32[3,16,1,128]{3,1,2,0:T(8,128)}, u32[]{:S(2)}, u32[]{:S(2)}) collective-permute-start(f32[3,16,1,128]{3,1,2,0:T(8,128)} %get-tuple-element.55), channel_id=1, source_target_pairs={{0,6},{1,7},{2,0},{3,1},{4,2},{5,3},{6,4},{7,5},{8,14},{9,15},{10,... | collective-permute-start | bytes 73736 | tf_op jit(solution)/shard_map/ppermute | solution.py:16
  15.3 1.0 collective-permute-start
  16.8 1.6 collective-permute-start.3
  18.7 3.3 %collective-permute-start.4 = (f32[3,16,16,1]{3,1,2,0:T(8,128)S(1)}, f32[3,16,16,1]{3,1,2,0:T(8,128)S(1)}, u32[]{:S(2)}, u32[]{:S(2)}) collective-permute-start(f32[3,16,16,1]{3,1,2,0:T(8,128)S(1)} %fusion.114), channel_id=1, source_target_pairs={{0,7},{1,0},{2,1},{3,2},{4,3},{5,4},{6,5},{7,6},{8,15},{9,8},{10,9... | collective-permute-start | bytes 9224 | tf_op jit(solution)/shard_map/ppermute | solution.py:16
  35.4 2.9 %collective-permute-done.4 = f32[3,16,16,1]{3,1,2,0:T(8,128)S(1)} collective-permute-done((f32[3,16,16,1]{3,1,2,0:T(8,128)S(1)}, f32[3,16,16,1]{3,1,2,0:T(8,128)S(1)}, u32[]{:S(2)}, u32[]{:S(2)}) %collective-permute-start.4) | collective-permute-done | bytes 3104 | tf_op jit(solution)/shard_map/ppermute | solution.py:16
  43.8 1.3 slice.1113
  45.1 1.3 slice.1110
  48.7 1.4 collective-permute-start.6
  50.1 2.5 %collective-permute-start.7 = (f32[1,16,1,128]{3,1,2,0:T(8,128)S(1)}, f32[1,16,1,128]{3,1,2,0:T(8,128)S(1)}, u32[]{:S(2)}, u32[]{:S(2)}) collective-permute-start(f32[1,16,1,128]{3,1,2,0:T(8,128)S(1)} %bitcast.706), channel_id=1, source_target_pairs={{0,6},{1,7},{2,0},{3,1},{4,2},{5,3},{6,4},{7,5},{8,14},{9,15},{10,... | collective-permute-start | bytes 24584 | tf_op jit(solution)/shard_map/ppermute | solution.py:16
  52.6 3.1 %collective-permute-start.9 = (f32[1,16,16,1]{3,2,1,0:T(8,128)S(1)}, f32[1,16,16,1]{3,2,1,0:T(8,128)S(1)}, u32[]{:S(2)}, u32[]{:S(2)}) collective-permute-start(f32[1,16,16,1]{3,2,1,0:T(8,128)S(1)} %get-tuple-element.103), channel_id=1, source_target_pairs={{0,7},{1,0},{2,1},{3,2},{4,3},{5,4},{6,5},{7,6},{8,15},{9,8},{10,9... | collective-permute-start | bytes 3080 | tf_op jit(solution)/shard_map/ppermute | solution.py:16
  56.4 1.7 collective-permute-done.9
  58.5 4.9 %collective-permute-done.8 = f32[1,16,16,1]{3,2,1,0:T(8,128)S(1)} collective-permute-done((f32[1,16,16,1]{3,2,1,0:T(8,128)S(1)}, f32[1,16,16,1]{3,2,1,0:T(8,128)S(1)}, u32[]{:S(2)}, u32[]{:S(2)}) %collective-permute-start.8) | collective-permute-done | bytes 1056 | tf_op jit(solution)/shard_map/ppermute | solution.py:16
  64.9 1.5 collective-permute-start.13
  66.4 3.8 %collective-permute-start.12 = (f32[1,16,1,128]{3,1,2,0:T(8,128)S(1)}, f32[1,16,1,128]{3,1,2,0:T(8,128)S(1)}, u32[]{:S(2)}, u32[]{:S(2)}) collective-permute-start(f32[1,16,1,128]{3,1,2,0:T(8,128)S(1)} %bitcast.710), channel_id=1, source_target_pairs={{0,6},{1,7},{2,0},{3,1},{4,2},{5,3},{6,4},{7,5},{8,14},{9,15},{10,... | collective-permute-start | bytes 24584 | tf_op jit(solution)/shard_map/ppermute | solution.py:16
  71.0 1.6 collective-permute-done.13
  76.1 1.4 collective-permute-start.15
  77.5 2.1 %collective-permute-start.16 = (f32[1,8,1,64]{3,2,1,0:T(1,128)S(1)}, f32[1,8,1,64]{3,2,1,0:T(1,128)S(1)}, u32[]{:S(2)}, u32[]{:S(2)}) collective-permute-start(f32[1,8,1,64]{3,2,1,0:T(1,128)S(1)} %get-tuple-element.212), channel_id=1, source_target_pairs={{0,2},{1,3},{2,4},{3,5},{4,6},{5,7},{6,0},{7,1},{8,10},{9,11},{10,... | collective-permute-start | bytes 6152 | tf_op jit(solution)/shard_map/ppermute | solution.py:16
  79.5 1.8 collective-permute-start.17
  81.3 2.0 %collective-permute-start.18 = (f32[1,8,8,1]{3,2,1,0:T(8,128)S(1)}, f32[1,8,8,1]{3,2,1,0:T(8,128)S(1)}, u32[]{:S(2)}, u32[]{:S(2)}) collective-permute-start(f32[1,8,8,1]{3,2,1,0:T(8,128)S(1)} %get-tuple-element.217), channel_id=1, source_target_pairs={{0,1},{1,2},{2,3},{3,4},{4,5},{5,6},{6,7},{7,0},{8,9},{9,10},{10,1... | collective-permute-start | bytes 776 | tf_op jit(solution)/shard_map/ppermute | solution.py:16
  83.3 1.9 collective-permute-done.19
  85.2 2.7 %collective-permute-done.18 = f32[1,8,8,1]{3,2,1,0:T(8,128)S(1)} collective-permute-done((f32[1,8,8,1]{3,2,1,0:T(8,128)S(1)}, f32[1,8,8,1]{3,2,1,0:T(8,128)S(1)}, u32[]{:S(2)}, u32[]{:S(2)}) %collective-permute-start.18) | collective-permute-done | bytes 288 | tf_op jit(solution)/shard_map/ppermute | solution.py:16
  88.4 2.4 %collective-permute-start.22 = (f32[1,8,1,64]{3,2,1,0:T(1,128)S(1)}, f32[1,8,1,64]{3,2,1,0:T(1,128)S(1)}, u32[]{:S(2)}, u32[]{:S(2)}) collective-permute-start(f32[1,8,1,64]{3,2,1,0:T(1,128)S(1)} %get-tuple-element.198), channel_id=1, source_target_pairs={{0,6},{1,7},{2,0},{3,1},{4,2},{5,3},{6,4},{7,5},{8,14},{9,15},{10,... | collective-permute-start | bytes 6152 | tf_op jit(solution)/shard_map/ppermute | solution.py:16
  90.8 2.9 %collective-permute-start.24 = (f32[1,8,8,1]{3,2,1,0:T(8,128)S(1)}, f32[1,8,8,1]{3,2,1,0:T(8,128)S(1)}, u32[]{:S(2)}, u32[]{:S(2)}) collective-permute-start(f32[1,8,8,1]{3,2,1,0:T(8,128)S(1)} %get-tuple-element.188), channel_id=1, source_target_pairs={{0,7},{1,0},{2,1},{3,2},{4,3},{5,4},{6,5},{7,6},{8,15},{9,8},{10,9... | collective-permute-start | bytes 776 | tf_op jit(solution)/shard_map/ppermute | solution.py:16
  93.7 1.8 collective-permute-done.24
  95.5 5.1 %collective-permute-done.23 = f32[1,8,8,1]{3,2,1,0:T(8,128)S(1)} collective-permute-done((f32[1,8,8,1]{3,2,1,0:T(8,128)S(1)}, f32[1,8,8,1]{3,2,1,0:T(8,128)S(1)}, u32[]{:S(2)}, u32[]{:S(2)}) %collective-permute-start.23) | collective-permute-done | bytes 288 | tf_op jit(solution)/shard_map/ppermute | solution.py:16
  102.1 2.9 %collective-permute-start.28 = (f32[2,4,4,32]{3,2,1,0:T(4,128)S(1)}, f32[2,4,4,32]{3,2,1,0:T(4,128)S(1)}, u32[]{:S(2)}, u32[]{:S(2)}) collective-permute-start(f32[2,4,4,32]{3,2,1,0:T(4,128)S(1)} %pad_maximum_fusion.24), channel_id=1, source_target_pairs={{0,4},{1,5},{2,6},{3,7},{4,0},{5,1},{6,2},{7,3},{8,12},{9,13},{10,... | collective-permute-start | bytes 12296 | tf_op jit(solution)/shard_map/ppermute | solution.py:16
  105.0 1.9 collective-permute-start.25
  107.0 4.5 %collective-permute-done.25 = f32[2,4,4,32]{3,2,1,0:T(4,128)S(1)} collective-permute-done((f32[2,4,4,32]{3,2,1,0:T(4,128)S(1)}, f32[2,4,4,32]{3,2,1,0:T(4,128)S(1)}, u32[]{:S(2)}, u32[]{:S(2)}) %collective-permute-start.25) | collective-permute-done | bytes 4128 | tf_op jit(solution)/shard_map/ppermute | solution.py:16
  111.6 5.4 %collective-permute-done.26 = f32[2,4,4,32]{3,2,1,0:T(4,128)S(1)} collective-permute-done((f32[2,4,4,32]{3,2,1,0:T(4,128)S(1)}, f32[2,4,4,32]{3,2,1,0:T(4,128)S(1)}, u32[]{:S(2)}, u32[]{:S(2)}) %collective-permute-start.26) | collective-permute-done | bytes 4128 | tf_op jit(solution)/shard_map/ppermute | solution.py:16
  117.2 3.5 %collective-permute-done.31 = f32[2,4,4,32]{3,2,1,0:T(4,128)S(1)} collective-permute-done((f32[2,4,4,32]{3,2,1,0:T(4,128)S(1)}, f32[2,4,4,32]{3,2,1,0:T(4,128)S(1)}, u32[]{:S(2)}, u32[]{:S(2)}) %collective-permute-start.31) | collective-permute-done | bytes 4128 | tf_op jit(solution)/shard_map/ppermute | solution.py:16
  146.3 2.1 %collective-permute-start.33 = (f32[1,8,1,64]{3,1,2,0:T(8,128)S(1)}, f32[1,8,1,64]{3,1,2,0:T(8,128)S(1)}, u32[]{:S(2)}, u32[]{:S(2)}) collective-permute-start(f32[1,8,1,64]{3,1,2,0:T(8,128)S(1)} %bitcast.714), channel_id=1, source_target_pairs={{0,2},{1,3},{2,4},{3,5},{4,6},{5,7},{6,0},{7,1},{8,10},{9,11},{10,... | collective-permute-start | bytes 6152 | tf_op jit(solution)/shard_map/ppermute | solution.py:16
  148.4 1.7 collective-permute-start.34
  150.2 1.0 collective-permute-start.36
  151.2 1.0 collective-permute-start.35
  152.2 1.9 collective-permute-done.36
  154.1 3.7 %collective-permute-done.35 = f32[1,8,8,1]{3,2,1,0:T(8,128)S(1)} collective-permute-done((f32[1,8,8,1]{3,2,1,0:T(8,128)S(1)}, f32[1,8,8,1]{3,2,1,0:T(8,128)S(1)}, u32[]{:S(2)}, u32[]{:S(2)}) %collective-permute-start.35) | collective-permute-done | bytes 288 | tf_op jit(solution)/shard_map/ppermute | solution.py:16
  159.3 2.0 %collective-permute-start.38 = (f32[1,8,1,64]{3,2,1,0:T(1,128)S(1)}, f32[1,8,1,64]{3,2,1,0:T(1,128)S(1)}, u32[]{:S(2)}, u32[]{:S(2)}) collective-permute-start(f32[1,8,1,64]{3,2,1,0:T(1,128)S(1)} %get-tuple-element.143), channel_id=1, source_target_pairs={{0,2},{1,3},{2,4},{3,5},{4,6},{5,7},{6,0},{7,1},{8,10},{9,11},{10,... | collective-permute-start | bytes 6152 | tf_op jit(solution)/shard_map/ppermute | solution.py:16
  161.3 1.8 collective-permute-start.41
  163.5 1.7 collective-permute-done.41
  165.4 4.4 %collective-permute-done.40 = f32[1,8,8,1]{3,2,1,0:T(8,128)S(1)} collective-permute-done((f32[1,8,8,1]{3,2,1,0:T(8,128)S(1)}, f32[1,8,8,1]{3,2,1,0:T(8,128)S(1)}, u32[]{:S(2)}, u32[]{:S(2)}) %collective-permute-start.40) | collective-permute-done | bytes 288 | tf_op jit(solution)/shard_map/ppermute | solution.py:16
  171.8 1.1 collective-permute-start.42
  173.5 1.4 collective-permute-start.45
  175.0 3.8 %collective-permute-start.44 = (f32[1,16,1,128]{3,1,2,0:T(8,128)S(1)}, f32[1,16,1,128]{3,1,2,0:T(8,128)S(1)}, u32[]{:S(2)}, u32[]{:S(2)}) collective-permute-start(f32[1,16,1,128]{3,1,2,0:T(8,128)S(1)} %bitcast.708), channel_id=1, source_target_pairs={{0,6},{1,7},{2,0},{3,1},{4,2},{5,3},{6,4},{7,5},{8,14},{9,15},{10,... | collective-permute-start | bytes 24584 | tf_op jit(solution)/shard_map/ppermute | solution.py:16
  179.1 2.1 %collective-permute-done.45 = f32[1,16,16,1]{3,2,1,0:T(8,128)S(1)} collective-permute-done((f32[1,16,16,1]{3,2,1,0:T(8,128)S(1)}, f32[1,16,16,1]{3,2,1,0:T(8,128)S(1)}, u32[]{:S(2)}, u32[]{:S(2)}) %collective-permute-start.45) | collective-permute-done | bytes 1056 | tf_op jit(solution)/shard_map/ppermute | solution.py:16
  182.4 2.4 %collective-permute-start.51 = (f32[1,16,16,1]{3,1,2,0:T(8,128)S(1)}, f32[1,16,16,1]{3,1,2,0:T(8,128)S(1)}, u32[]{:S(2)}, u32[]{:S(2)}) collective-permute-start(f32[1,16,16,1]{3,1,2,0:T(8,128)S(1)} %get-tuple-element.59), channel_id=1, source_target_pairs={{0,7},{1,0},{2,1},{3,2},{4,3},{5,4},{6,5},{7,6},{8,15},{9,8},{10,9... | collective-permute-start | bytes 3080 | tf_op jit(solution)/shard_map/ppermute | solution.py:16
  185.5 2.1 %collective-permute-start.49 = (f32[1,16,1,128]{3,1,2,0:T(8,128)S(1)}, f32[1,16,1,128]{3,1,2,0:T(8,128)S(1)}, u32[]{:S(2)}, u32[]{:S(2)}) collective-permute-start(f32[1,16,1,128]{3,1,2,0:T(8,128)S(1)} %get-tuple-element.63), channel_id=1, source_target_pairs={{0,6},{1,7},{2,0},{3,1},{4,2},{5,3},{6,4},{7,5},{8,14},{9,15},{10,... | collective-permute-start | bytes 24584 | tf_op jit(solution)/shard_map/ppermute | solution.py:16
  188.6 4.0 %collective-permute-done.50 = f32[1,16,16,1]{3,1,2,0:T(8,128)S(1)} collective-permute-done((f32[1,16,16,1]{3,1,2,0:T(8,128)S(1)}, f32[1,16,16,1]{3,1,2,0:T(8,128)S(1)}, u32[]{:S(2)}, u32[]{:S(2)}) %collective-permute-start.50) | collective-permute-done | bytes 1056 | tf_op jit(solution)/shard_map/ppermute | solution.py:16
  (509 shorter events, 67.8 us)
Async XLA Ops:
  9.5 32.8 %collective-permute-start.2 = (f32[3,16,1,128]{3,1,2,0:T(8,128)}, f32[3,16,1,128]{3,1,2,0:T(8,128)}, u32[]{:S(2)}, u32[]{:S(2)}) collective-permute-start(f32[3,16,1,128]{3,1,2,0:T(8,128)} %get-tuple-element.55), channel_id=1, source_target_pairs={{0,6},{1,7},{2,0},{3,1},{4,2},{5,3},{6,4},{7,5},{8,14},{9,15},{10,... | collective-permute-start | bytes 73736 | tf_op jit(solution)/shard_map/ppermute | solution.py:16
  14.6 28.5 %collective-permute-start.1 = (f32[3,16,1,128]{3,1,2,0:T(8,128)}, f32[3,16,1,128]{3,1,2,0:T(8,128)}, u32[]{:S(2)}, u32[]{:S(2)}) collective-permute-start(f32[3,16,1,128]{3,1,2,0:T(8,128)} %get-tuple-element.56), channel_id=1, source_target_pairs={{0,2},{1,3},{2,4},{3,5},{4,6},{5,7},{6,0},{7,1},{8,10},{9,11},{10,... | collective-permute-start | bytes 73736 | tf_op jit(solution)/shard_map/ppermute | solution.py:16
  15.3 31.1 %collective-permute-start = (f32[3,2,16,128]{3,1,2,0:T(2,128)}, f32[3,2,16,128]{3,1,2,0:T(2,128)}, u32[]{:S(2)}, u32[]{:S(2)}) collective-permute-start(f32[3,2,16,128]{3,1,2,0:T(2,128)} %fusion.247), channel_id=1, source_target_pairs={{0,4},{1,5},{2,6},{3,7},{4,0},{5,1},{6,2},{7,3},{8,12},{9,13},{10,... | collective-permute-start | bytes 147464 | tf_op jit(solution)/shard_map/ppermute | solution.py:16
  16.8 17.5 %collective-permute-start.3 = (f32[3,16,16,1]{3,1,2,0:T(8,128)S(1)}, f32[3,16,16,1]{3,1,2,0:T(8,128)}, u32[]{:S(2)}, u32[]{:S(2)}) collective-permute-start(f32[3,16,16,1]{3,1,2,0:T(8,128)S(1)} %pad_maximum_fusion.1), channel_id=1, source_target_pairs={{0,1},{1,2},{2,3},{3,4},{4,5},{5,6},{6,7},{7,0},{8,9},{9,10},{10,1... | collective-permute-start | bytes 9224 | tf_op jit(solution)/shard_map/ppermute | solution.py:16
  18.7 19.5 %collective-permute-start.4 = (f32[3,16,16,1]{3,1,2,0:T(8,128)S(1)}, f32[3,16,16,1]{3,1,2,0:T(8,128)S(1)}, u32[]{:S(2)}, u32[]{:S(2)}) collective-permute-start(f32[3,16,16,1]{3,1,2,0:T(8,128)S(1)} %fusion.114), channel_id=1, source_target_pairs={{0,7},{1,0},{2,1},{3,2},{4,3},{5,4},{6,5},{7,6},{8,15},{9,8},{10,9... | collective-permute-start | bytes 9224 | tf_op jit(solution)/shard_map/ppermute | solution.py:16
  48.7 14.9 %collective-permute-start.6 = (f32[1,16,1,128]{3,1,2,0:T(8,128)S(1)}, f32[1,16,1,128]{3,1,2,0:T(8,128)S(1)}, u32[]{:S(2)}, u32[]{:S(2)}) collective-permute-start(f32[1,16,1,128]{3,1,2,0:T(8,128)S(1)} %bitcast.707), channel_id=1, source_target_pairs={{0,2},{1,3},{2,4},{3,5},{4,6},{5,7},{6,0},{7,1},{8,10},{9,11},{10,... | collective-permute-start | bytes 24584 | tf_op jit(solution)/shard_map/ppermute | solution.py:16
  50.1 13.6 %collective-permute-start.7 = (f32[1,16,1,128]{3,1,2,0:T(8,128)S(1)}, f32[1,16,1,128]{3,1,2,0:T(8,128)S(1)}, u32[]{:S(2)}, u32[]{:S(2)}) collective-permute-start(f32[1,16,1,128]{3,1,2,0:T(8,128)S(1)} %bitcast.706), channel_id=1, source_target_pairs={{0,6},{1,7},{2,0},{3,1},{4,2},{5,3},{6,4},{7,5},{8,14},{9,15},{10,... | collective-permute-start | bytes 24584 | tf_op jit(solution)/shard_map/ppermute | solution.py:16
  52.6 11.0 %collective-permute-start.5 = (f32[1,2,16,128]{3,2,1,0:T(8,128)S(1)}, f32[1,2,16,128]{3,2,1,0:T(8,128)S(1)}, u32[]{:S(2)}, u32[]{:S(2)}) collective-permute-start(f32[1,2,16,128]{3,2,1,0:T(8,128)S(1)} %pad_maximum_fusion.22), channel_id=1, source_target_pairs={{0,4},{1,5},{2,6},{3,7},{4,0},{5,1},{6,2},{7,3},{8,12},{9,13},{10,... | collective-permute-start | bytes 49160 | tf_op jit(solution)/shard_map/ppermute | solution.py:16
  52.6 5.6 %collective-permute-start.9 = (f32[1,16,16,1]{3,2,1,0:T(8,128)S(1)}, f32[1,16,16,1]{3,2,1,0:T(8,128)S(1)}, u32[]{:S(2)}, u32[]{:S(2)}) collective-permute-start(f32[1,16,16,1]{3,2,1,0:T(8,128)S(1)} %get-tuple-element.103), channel_id=1, source_target_pairs={{0,7},{1,0},{2,1},{3,2},{4,3},{5,4},{6,5},{7,6},{8,15},{9,8},{10,9... | collective-permute-start | bytes 3080 | tf_op jit(solution)/shard_map/ppermute | solution.py:16
  55.7 7.7 %collective-permute-start.8 = (f32[1,16,16,1]{3,2,1,0:T(8,128)S(1)}, f32[1,16,16,1]{3,2,1,0:T(8,128)S(1)}, u32[]{:S(2)}, u32[]{:S(2)}) collective-permute-start(f32[1,16,16,1]{3,2,1,0:T(8,128)S(1)} %get-tuple-element.104), channel_id=1, source_target_pairs={{0,1},{1,2},{2,3},{3,4},{4,5},{5,6},{6,7},{7,0},{8,9},{9,10},{10,1... | collective-permute-start | bytes 3080 | tf_op jit(solution)/shard_map/ppermute | solution.py:16
  64.2 8.6 %collective-permute-start.10 = (f32[1,2,16,128]{3,2,1,0:T(8,128)S(1)}, f32[1,2,16,128]{3,2,1,0:T(8,128)S(1)}, u32[]{:S(2)}, u32[]{:S(2)}) collective-permute-start(f32[1,2,16,128]{3,2,1,0:T(8,128)S(1)} %pad_maximum_fusion.23), channel_id=1, source_target_pairs={{0,4},{1,5},{2,6},{3,7},{4,0},{5,1},{6,2},{7,3},{8,12},{9,13},{10,... | collective-permute-start | bytes 49160 | tf_op jit(solution)/shard_map/ppermute | solution.py:16
  64.3 6.4 %collective-permute-start.14 = (f32[1,16,16,1]{3,2,1,0:T(8,128)S(1)}, f32[1,16,16,1]{3,2,1,0:T(8,128)S(1)}, u32[]{:S(2)}, u32[]{:S(2)}) collective-permute-start(f32[1,16,16,1]{3,2,1,0:T(8,128)S(1)} %get-tuple-element.91), channel_id=1, source_target_pairs={{0,7},{1,0},{2,1},{3,2},{4,3},{5,4},{6,5},{7,6},{8,15},{9,8},{10,9... | collective-permute-start | bytes 3080 | tf_op jit(solution)/shard_map/ppermute | solution.py:16
  64.9 7.7 %collective-permute-start.13 = (f32[1,16,16,1]{3,2,1,0:T(8,128)S(1)}, f32[1,16,16,1]{3,2,1,0:T(8,128)S(1)}, u32[]{:S(2)}, u32[]{:S(2)}) collective-permute-start(f32[1,16,16,1]{3,2,1,0:T(8,128)S(1)} %get-tuple-element.92), channel_id=1, source_target_pairs={{0,1},{1,2},{2,3},{3,4},{4,5},{5,6},{6,7},{7,0},{8,9},{9,10},{10,1... | collective-permute-start | bytes 3080 | tf_op jit(solution)/shard_map/ppermute | solution.py:16
  66.4 6.5 %collective-permute-start.11 = (f32[1,16,1,128]{3,1,2,0:T(8,128)S(1)}, f32[1,16,1,128]{3,1,2,0:T(8,128)S(1)}, u32[]{:S(2)}, u32[]{:S(2)}) collective-permute-start(f32[1,16,1,128]{3,1,2,0:T(8,128)S(1)} %bitcast.711), channel_id=1, source_target_pairs={{0,2},{1,3},{2,4},{3,5},{4,6},{5,7},{6,0},{7,1},{8,10},{9,11},{10,... | collective-permute-start | bytes 24584 | tf_op jit(solution)/shard_map/ppermute | solution.py:16
  66.4 6.4 %collective-permute-start.12 = (f32[1,16,1,128]{3,1,2,0:T(8,128)S(1)}, f32[1,16,1,128]{3,1,2,0:T(8,128)S(1)}, u32[]{:S(2)}, u32[]{:S(2)}) collective-permute-start(f32[1,16,1,128]{3,1,2,0:T(8,128)S(1)} %bitcast.710), channel_id=1, source_target_pairs={{0,6},{1,7},{2,0},{3,1},{4,2},{5,3},{6,4},{7,5},{8,14},{9,15},{10,... | collective-permute-start | bytes 24584 | tf_op jit(solution)/shard_map/ppermute | solution.py:16
  76.1 7.2 %collective-permute-start.15 = (f32[1,2,8,64]{3,2,1,0:T(8,128)S(1)}, f32[1,2,8,64]{3,2,1,0:T(8,128)S(1)}, u32[]{:S(2)}, u32[]{:S(2)}) collective-permute-start(f32[1,2,8,64]{3,2,1,0:T(8,128)S(1)} %pad_maximum_fusion.27), channel_id=1, source_target_pairs={{0,4},{1,5},{2,6},{3,7},{4,0},{5,1},{6,2},{7,3},{8,12},{9,13},{10,... | collective-permute-start | bytes 12296 | tf_op jit(solution)/shard_map/ppermute | solution.py:16
  77.5 10.4 %collective-permute-start.16 = (f32[1,8,1,64]{3,2,1,0:T(1,128)S(1)}, f32[1,8,1,64]{3,2,1,0:T(1,128)S(1)}, u32[]{:S(2)}, u32[]{:S(2)}) collective-permute-start(f32[1,8,1,64]{3,2,1,0:T(1,128)S(1)} %get-tuple-element.212), channel_id=1, source_target_pairs={{0,2},{1,3},{2,4},{3,5},{4,6},{5,7},{6,0},{7,1},{8,10},{9,11},{10,... | collective-permute-start | bytes 6152 | tf_op jit(solution)/shard_map/ppermute | solution.py:16
  79.5 8.4 %collective-permute-start.17 = (f32[1,8,1,64]{3,2,1,0:T(1,128)S(1)}, f32[1,8,1,64]{3,2,1,0:T(1,128)S(1)}, u32[]{:S(2)}, u32[]{:S(2)}) collective-permute-start(f32[1,8,1,64]{3,2,1,0:T(1,128)S(1)} %get-tuple-element.213), channel_id=1, source_target_pairs={{0,6},{1,7},{2,0},{3,1},{4,2},{5,3},{6,4},{7,5},{8,14},{9,15},{10,... | collective-permute-start | bytes 6152 | tf_op jit(solution)/shard_map/ppermute | solution.py:16
  81.3 6.6 %collective-permute-start.18 = (f32[1,8,8,1]{3,2,1,0:T(8,128)S(1)}, f32[1,8,8,1]{3,2,1,0:T(8,128)S(1)}, u32[]{:S(2)}, u32[]{:S(2)}) collective-permute-start(f32[1,8,8,1]{3,2,1,0:T(8,128)S(1)} %get-tuple-element.217), channel_id=1, source_target_pairs={{0,1},{1,2},{2,3},{3,4},{4,5},{5,6},{6,7},{7,0},{8,9},{9,10},{10,1... | collective-permute-start | bytes 776 | tf_op jit(solution)/shard_map/ppermute | solution.py:16
  88.4 5.3 %collective-permute-start.20 = (f32[1,2,8,64]{3,2,1,0:T(8,128)S(1)}, f32[1,2,8,64]{3,2,1,0:T(8,128)S(1)}, u32[]{:S(2)}, u32[]{:S(2)}) collective-permute-start(f32[1,2,8,64]{3,2,1,0:T(8,128)S(1)} %pad_maximum_fusion.28), channel_id=1, source_target_pairs={{0,4},{1,5},{2,6},{3,7},{4,0},{5,1},{6,2},{7,3},{8,12},{9,13},{10,... | collective-permute-start | bytes 12296 | tf_op jit(solution)/shard_map/ppermute | solution.py:16
  88.4 12.1 %collective-permute-start.22 = (f32[1,8,1,64]{3,2,1,0:T(1,128)S(1)}, f32[1,8,1,64]{3,2,1,0:T(1,128)S(1)}, u32[]{:S(2)}, u32[]{:S(2)}) collective-permute-start(f32[1,8,1,64]{3,2,1,0:T(1,128)S(1)} %get-tuple-element.198), channel_id=1, source_target_pairs={{0,6},{1,7},{2,0},{3,1},{4,2},{5,3},{6,4},{7,5},{8,14},{9,15},{10,... | collective-permute-start | bytes 6152 | tf_op jit(solution)/shard_map/ppermute | solution.py:16
  90.8 9.8 %collective-permute-start.21 = (f32[1,8,1,64]{3,2,1,0:T(1,128)S(1)}, f32[1,8,1,64]{3,2,1,0:T(1,128)S(1)}, u32[]{:S(2)}, u32[]{:S(2)}) collective-permute-start(f32[1,8,1,64]{3,2,1,0:T(1,128)S(1)} %get-tuple-element.199), channel_id=1, source_target_pairs={{0,2},{1,3},{2,4},{3,5},{4,6},{5,7},{6,0},{7,1},{8,10},{9,11},{10,... | collective-permute-start | bytes 6152 | tf_op jit(solution)/shard_map/ppermute | solution.py:16
  90.8 4.6 %collective-permute-start.24 = (f32[1,8,8,1]{3,2,1,0:T(8,128)S(1)}, f32[1,8,8,1]{3,2,1,0:T(8,128)S(1)}, u32[]{:S(2)}, u32[]{:S(2)}) collective-permute-start(f32[1,8,8,1]{3,2,1,0:T(8,128)S(1)} %get-tuple-element.188), channel_id=1, source_target_pairs={{0,7},{1,0},{2,1},{3,2},{4,3},{5,4},{6,5},{7,6},{8,15},{9,8},{10,9... | collective-permute-start | bytes 776 | tf_op jit(solution)/shard_map/ppermute | solution.py:16
  93.7 6.9 %collective-permute-start.23 = (f32[1,8,8,1]{3,2,1,0:T(8,128)S(1)}, f32[1,8,8,1]{3,2,1,0:T(8,128)S(1)}, u32[]{:S(2)}, u32[]{:S(2)}) collective-permute-start(f32[1,8,8,1]{3,2,1,0:T(8,128)S(1)} %get-tuple-element.189), channel_id=1, source_target_pairs={{0,1},{1,2},{2,3},{3,4},{4,5},{5,6},{6,7},{7,0},{8,9},{9,10},{10,1... | collective-permute-start | bytes 776 | tf_op jit(solution)/shard_map/ppermute | solution.py:16
  102.0 15.2 %collective-permute-start.30 = (f32[2,4,4,32]{3,2,1,0:T(4,128)S(1)}, f32[2,4,4,32]{3,2,1,0:T(4,128)S(1)}, u32[]{:S(2)}, u32[]{:S(2)}) collective-permute-start(f32[2,4,4,32]{3,2,1,0:T(4,128)S(1)} %pad_maximum_fusion.24), channel_id=1, source_target_pairs={{0,6},{1,7},{2,0},{3,1},{4,2},{5,3},{6,4},{7,5},{8,14},{9,15},{10,... | collective-permute-start | bytes 12296 | tf_op jit(solution)/shard_map/ppermute | solution.py:16
  102.0 15.2 %collective-permute-start.29 = (f32[2,4,4,32]{3,2,1,0:T(4,128)S(1)}, f32[2,4,4,32]{3,2,1,0:T(4,128)S(1)}, u32[]{:S(2)}, u32[]{:S(2)}) collective-permute-start(f32[2,4,4,32]{3,2,1,0:T(4,128)S(1)} %pad_maximum_fusion.24), channel_id=1, source_target_pairs={{0,5},{1,6},{2,7},{3,0},{4,1},{5,2},{6,3},{7,4},{8,13},{9,14},{10,... | collective-permute-start | bytes 12296 | tf_op jit(solution)/shard_map/ppermute | solution.py:16
  102.1 15.1 %collective-permute-start.28 = (f32[2,4,4,32]{3,2,1,0:T(4,128)S(1)}, f32[2,4,4,32]{3,2,1,0:T(4,128)S(1)}, u32[]{:S(2)}, u32[]{:S(2)}) collective-permute-start(f32[2,4,4,32]{3,2,1,0:T(4,128)S(1)} %pad_maximum_fusion.24), channel_id=1, source_target_pairs={{0,4},{1,5},{2,6},{3,7},{4,0},{5,1},{6,2},{7,3},{8,12},{9,13},{10,... | collective-permute-start | bytes 12296 | tf_op jit(solution)/shard_map/ppermute | solution.py:16
  105.0 12.1 %collective-permute-start.27 = (f32[2,4,4,32]{3,2,1,0:T(4,128)S(1)}, f32[2,4,4,32]{3,2,1,0:T(4,128)S(1)}, u32[]{:S(2)}, u32[]{:S(2)}) collective-permute-start(f32[2,4,4,32]{3,2,1,0:T(4,128)S(1)} %pad_maximum_fusion.24), channel_id=1, source_target_pairs={{0,3},{1,4},{2,5},{3,6},{4,7},{5,0},{6,1},{7,2},{8,11},{9,12},{10,... | collective-permute-start | bytes 12296 | tf_op jit(solution)/shard_map/ppermute | solution.py:16
  105.0 6.4 %collective-permute-start.25 = (f32[2,4,4,32]{3,2,1,0:T(4,128)S(1)}, f32[2,4,4,32]{3,2,1,0:T(4,128)S(1)}, u32[]{:S(2)}, u32[]{:S(2)}) collective-permute-start(f32[2,4,4,32]{3,2,1,0:T(4,128)S(1)} %pad_maximum_fusion.24), channel_id=1, source_target_pairs={{0,1},{1,2},{2,3},{3,4},{4,5},{5,6},{6,7},{7,0},{8,9},{9,10},{10,1... | collective-permute-start | bytes 12296 | tf_op jit(solution)/shard_map/ppermute | solution.py:16
  111.5 5.5 %collective-permute-start.26 = (f32[2,4,4,32]{3,2,1,0:T(4,128)S(1)}, f32[2,4,4,32]{3,2,1,0:T(4,128)S(1)}, u32[]{:S(2)}, u32[]{:S(2)}) collective-permute-start(f32[2,4,4,32]{3,2,1,0:T(4,128)S(1)} %pad_maximum_fusion.24), channel_id=1, source_target_pairs={{0,2},{1,3},{2,4},{3,5},{4,6},{5,7},{6,0},{7,1},{8,10},{9,11},{10,... | collective-permute-start | bytes 12296 | tf_op jit(solution)/shard_map/ppermute | solution.py:16
  146.2 6.0 %collective-permute-start.32 = (f32[1,2,8,64]{3,2,1,0:T(8,128)S(1)}, f32[1,2,8,64]{3,2,1,0:T(8,128)S(1)}, u32[]{:S(2)}, u32[]{:S(2)}) collective-permute-start(f32[1,2,8,64]{3,2,1,0:T(8,128)S(1)} %pad_maximum_fusion.29), channel_id=1, source_target_pairs={{0,4},{1,5},{2,6},{3,7},{4,0},{5,1},{6,2},{7,3},{8,12},{9,13},{10,... | collective-permute-start | bytes 12296 | tf_op jit(solution)/shard_map/ppermute | solution.py:16
  146.3 11.5 %collective-permute-start.33 = (f32[1,8,1,64]{3,1,2,0:T(8,128)S(1)}, f32[1,8,1,64]{3,1,2,0:T(8,128)S(1)}, u32[]{:S(2)}, u32[]{:S(2)}) collective-permute-start(f32[1,8,1,64]{3,1,2,0:T(8,128)S(1)} %bitcast.714), channel_id=1, source_target_pairs={{0,2},{1,3},{2,4},{3,5},{4,6},{5,7},{6,0},{7,1},{8,10},{9,11},{10,... | collective-permute-start | bytes 6152 | tf_op jit(solution)/shard_map/ppermute | solution.py:16
  148.4 9.4 %collective-permute-start.34 = (f32[1,8,1,64]{3,2,1,0:T(1,128)S(1)}, f32[1,8,1,64]{3,2,1,0:T(1,128)S(1)}, u32[]{:S(2)}, u32[]{:S(2)}) collective-permute-start(f32[1,8,1,64]{3,2,1,0:T(1,128)S(1)} %get-tuple-element.160), channel_id=1, source_target_pairs={{0,6},{1,7},{2,0},{3,1},{4,2},{5,3},{6,4},{7,5},{8,14},{9,15},{10,... | collective-permute-start | bytes 6152 | tf_op jit(solution)/shard_map/ppermute | solution.py:16
  151.2 6.6 %collective-permute-start.35 = (f32[1,8,8,1]{3,2,1,0:T(8,128)S(1)}, f32[1,8,8,1]{3,2,1,0:T(8,128)S(1)}, u32[]{:S(2)}, u32[]{:S(2)}) collective-permute-start(f32[1,8,8,1]{3,2,1,0:T(8,128)S(1)} %get-tuple-element.159), channel_id=1, source_target_pairs={{0,1},{1,2},{2,3},{3,4},{4,5},{5,6},{6,7},{7,0},{8,9},{9,10},{10,1... | collective-permute-start | bytes 776 | tf_op jit(solution)/shard_map/ppermute | solution.py:16
  159.2 11.3 %collective-permute-start.39 = (f32[1,8,1,64]{3,2,1,0:T(1,128)S(1)}, f32[1,8,1,64]{3,2,1,0:T(1,128)S(1)}, u32[]{:S(2)}, u32[]{:S(2)}) collective-permute-start(f32[1,8,1,64]{3,2,1,0:T(1,128)S(1)} %get-tuple-element.142), channel_id=1, source_target_pairs={{0,6},{1,7},{2,0},{3,1},{4,2},{5,3},{6,4},{7,5},{8,14},{9,15},{10,... | collective-permute-start | bytes 6152 | tf_op jit(solution)/shard_map/ppermute | solution.py:16
  159.3 11.2 %collective-permute-start.38 = (f32[1,8,1,64]{3,2,1,0:T(1,128)S(1)}, f32[1,8,1,64]{3,2,1,0:T(1,128)S(1)}, u32[]{:S(2)}, u32[]{:S(2)}) collective-permute-start(f32[1,8,1,64]{3,2,1,0:T(1,128)S(1)} %get-tuple-element.143), channel_id=1, source_target_pairs={{0,2},{1,3},{2,4},{3,5},{4,6},{5,7},{6,0},{7,1},{8,10},{9,11},{10,... | collective-permute-start | bytes 6152 | tf_op jit(solution)/shard_map/ppermute | solution.py:16
  163.1 7.7 %collective-permute-start.37 = (f32[1,2,8,64]{3,2,1,0:T(8,128)S(1)}, f32[1,2,8,64]{3,2,1,0:T(8,128)S(1)}, u32[]{:S(2)}, u32[]{:S(2)}) collective-permute-start(f32[1,2,8,64]{3,2,1,0:T(8,128)S(1)} %pad_maximum_fusion.30), channel_id=1, source_target_pairs={{0,4},{1,5},{2,6},{3,7},{4,0},{5,1},{6,2},{7,3},{8,12},{9,13},{10,... | collective-permute-start | bytes 12296 | tf_op jit(solution)/shard_map/ppermute | solution.py:16
  163.1 6.7 %collective-permute-start.40 = (f32[1,8,8,1]{3,2,1,0:T(8,128)S(1)}, f32[1,8,8,1]{3,2,1,0:T(8,128)S(1)}, u32[]{:S(2)}, u32[]{:S(2)}) collective-permute-start(f32[1,8,8,1]{3,2,1,0:T(8,128)S(1)} %get-tuple-element.141), channel_id=1, source_target_pairs={{0,1},{1,2},{2,3},{3,4},{4,5},{5,6},{6,7},{7,0},{8,9},{9,10},{10,1... | collective-permute-start | bytes 776 | tf_op jit(solution)/shard_map/ppermute | solution.py:16
  171.8 9.8 %collective-permute-start.42 = (f32[1,2,16,128]{3,2,1,0:T(8,128)S(1)}, f32[1,2,16,128]{3,2,1,0:T(8,128)S(1)}, u32[]{:S(2)}, u32[]{:S(2)}) collective-permute-start(f32[1,2,16,128]{3,2,1,0:T(8,128)S(1)} %pad_maximum_fusion.25), channel_id=1, source_target_pairs={{0,4},{1,5},{2,6},{3,7},{4,0},{5,1},{6,2},{7,3},{8,12},{9,13},{10,... | collective-permute-start | bytes 49160 | tf_op jit(solution)/shard_map/ppermute | solution.py:16
  172.9 5.9 %collective-permute-start.46 = (f32[1,16,16,1]{3,2,1,0:T(8,128)S(1)}, f32[1,16,16,1]{3,2,1,0:T(8,128)S(1)}, u32[]{:S(2)}, u32[]{:S(2)}) collective-permute-start(f32[1,16,16,1]{3,2,1,0:T(8,128)S(1)} %get-tuple-element.71), channel_id=1, source_target_pairs={{0,7},{1,0},{2,1},{3,2},{4,3},{5,4},{6,5},{7,6},{8,15},{9,8},{10,9... | collective-permute-start | bytes 3080 | tf_op jit(solution)/shard_map/ppermute | solution.py:16
  173.5 7.8 %collective-permute-start.45 = (f32[1,16,16,1]{3,2,1,0:T(8,128)S(1)}, f32[1,16,16,1]{3,2,1,0:T(8,128)S(1)}, u32[]{:S(2)}, u32[]{:S(2)}) collective-permute-start(f32[1,16,16,1]{3,2,1,0:T(8,128)S(1)} %get-tuple-element.72), channel_id=1, source_target_pairs={{0,1},{1,2},{2,3},{3,4},{4,5},{5,6},{6,7},{7,0},{8,9},{9,10},{10,1... | collective-permute-start | bytes 3080 | tf_op jit(solution)/shard_map/ppermute | solution.py:16
  175.0 6.6 %collective-permute-start.43 = (f32[1,16,1,128]{3,1,2,0:T(8,128)S(1)}, f32[1,16,1,128]{3,1,2,0:T(8,128)S(1)}, u32[]{:S(2)}, u32[]{:S(2)}) collective-permute-start(f32[1,16,1,128]{3,1,2,0:T(8,128)S(1)} %bitcast.709), channel_id=1, source_target_pairs={{0,2},{1,3},{2,4},{3,5},{4,6},{5,7},{6,0},{7,1},{8,10},{9,11},{10,... | collective-permute-start | bytes 24584 | tf_op jit(solution)/shard_map/ppermute | solution.py:16
  175.0 6.6 %collective-permute-start.44 = (f32[1,16,1,128]{3,1,2,0:T(8,128)S(1)}, f32[1,16,1,128]{3,1,2,0:T(8,128)S(1)}, u32[]{:S(2)}, u32[]{:S(2)}) collective-permute-start(f32[1,16,1,128]{3,1,2,0:T(8,128)S(1)} %bitcast.708), channel_id=1, source_target_pairs={{0,6},{1,7},{2,0},{3,1},{4,2},{5,3},{6,4},{7,5},{8,14},{9,15},{10,... | collective-permute-start | bytes 24584 | tf_op jit(solution)/shard_map/ppermute | solution.py:16
  182.2 10.8 %collective-permute-start.47 = (f32[1,2,16,128]{3,1,2,0:T(2,128)S(1)}, f32[1,2,16,128]{3,1,2,0:T(2,128)S(1)}, u32[]{:S(2)}, u32[]{:S(2)}) collective-permute-start(f32[1,2,16,128]{3,1,2,0:T(2,128)S(1)} %pad_maximum_fusion.26), channel_id=1, source_target_pairs={{0,4},{1,5},{2,6},{3,7},{4,0},{5,1},{6,2},{7,3},{8,12},{9,13},{10,... | collective-permute-start | bytes 49160 | tf_op jit(solution)/shard_map/ppermute | solution.py:16
  182.4 5.8 %collective-permute-start.51 = (f32[1,16,16,1]{3,1,2,0:T(8,128)S(1)}, f32[1,16,16,1]{3,1,2,0:T(8,128)S(1)}, u32[]{:S(2)}, u32[]{:S(2)}) collective-permute-start(f32[1,16,16,1]{3,1,2,0:T(8,128)S(1)} %get-tuple-element.59), channel_id=1, source_target_pairs={{0,7},{1,0},{2,1},{3,2},{4,3},{5,4},{6,5},{7,6},{8,15},{9,8},{10,9... | collective-permute-start | bytes 3080 | tf_op jit(solution)/shard_map/ppermute | solution.py:16
  184.8 7.7 %collective-permute-start.50 = (f32[1,16,16,1]{3,1,2,0:T(8,128)S(1)}, f32[1,16,16,1]{3,1,2,0:T(8,128)S(1)}, u32[]{:S(2)}, u32[]{:S(2)}) collective-permute-start(f32[1,16,16,1]{3,1,2,0:T(8,128)S(1)} %get-tuple-element.60), channel_id=1, source_target_pairs={{0,1},{1,2},{2,3},{3,4},{4,5},{5,6},{6,7},{7,0},{8,9},{9,10},{10,1... | collective-permute-start | bytes 3080 | tf_op jit(solution)/shard_map/ppermute | solution.py:16
  185.5 7.4 %collective-permute-start.49 = (f32[1,16,1,128]{3,1,2,0:T(8,128)S(1)}, f32[1,16,1,128]{3,1,2,0:T(8,128)S(1)}, u32[]{:S(2)}, u32[]{:S(2)}) collective-permute-start(f32[1,16,1,128]{3,1,2,0:T(8,128)S(1)} %get-tuple-element.63), channel_id=1, source_target_pairs={{0,6},{1,7},{2,0},{3,1},{4,2},{5,3},{6,4},{7,5},{8,14},{9,15},{10,... | collective-permute-start | bytes 24584 | tf_op jit(solution)/shard_map/ppermute | solution.py:16
  187.7 5.4 %collective-permute-start.48 = (f32[1,16,1,128]{3,1,2,0:T(8,128)S(1)}, f32[1,16,1,128]{3,1,2,0:T(8,128)S(1)}, u32[]{:S(2)}, u32[]{:S(2)}) collective-permute-start(f32[1,16,1,128]{3,1,2,0:T(8,128)S(1)} %get-tuple-element.64), channel_id=1, source_target_pairs={{0,2},{1,3},{2,4},{3,5},{4,6},{5,7},{6,0},{7,1},{8,10},{9,11},{10,... | collective-permute-start | bytes 24584 | tf_op jit(solution)/shard_map/ppermute | solution.py:16
  (49 other events, 120.3 us)

commit v5 on v4

--- a/solution.py
+++ b/solution.py
@@ -380,6 +380,34 @@
     )
 
     values = guess[0]
+    if count_dev * (width_x // 2) * (width_y // 2) <= 512:
+        first = exchange(jnp.stack([permeab, values]), per_side)
+        face_coefs, diagonal = coefficients(permeab, with_faces(permeab, pick(first, 0)), 1.0)
+        values = smooth(values, source, face_coefs, diagonal, 1.0, with_faces(values, pick(first, 1)))
+        for sweep_no in range(SWEEPS - 1):
+            faces = pick(exchange(values[None], per_side), 0)
+            values = smooth(values, source, face_coefs, diagonal, 1.0, with_faces(values, faces))
+        stored_faces = pick(exchange(values[None], per_side), 0)
+        leftover = source - operate(values, with_faces(values, stored_faces), face_coefs, 1.0)
+        stored = values
+
+        gathered = gather_rows(jnp.stack([coarsen(permeab), coarsen(leftover)]), per_side)
+        correction_all = global_cycle(gathered[:, 1], gathered[:, 0], 1, per_side)
+
+        correction = lax.dynamic_index_in_dim(correction_all, my_row, 0, keepdims=False)
+        values = stored + refine(correction)
+        faces = [
+            mine + theirs
+            for mine, theirs in zip(stored_faces, refined_faces(correction_all, my_row, per_side))
+        ]
+        values = smooth(values, source, face_coefs, diagonal, 1.0, with_faces(values, faces))
+        for sweep_no in range(SWEEPS - 1):
+            faces = pick(exchange(values[None], per_side), 0)
+            values = smooth(values, source, face_coefs, diagonal, 1.0, with_faces(values, faces))
+        faces = pick(exchange(values[None], per_side), 0)
+        residual = source - operate(values, with_faces(values, faces), face_coefs, 1.0)
+        return (values[None], residual[None])
+
     coarse_perm = coarsen(permeab)
     first, coarse_first = exchange_with_coarse(jnp.stack([permeab, values]), coarse_perm, per_side)
     face_coefs, diagonal = coefficients(permeab, with_faces(permeab, pick(first, 0)), 1.0)

time: 195 us -> 177 us (0.908)
  matrix products: 18.3 us -> 66.4 us
  waiting for transfers between devices: 55.5 us -> 33.1 us
  local copies, waits for them, and re-layouts: 36.2 us -> 14.7 us
  starting transfers between devices: 64.2 us -> 45.4 us
  other arithmetic: 17.1 us -> 14.4 us
    dot_general x11 -> x16, matrix products: 4.73 us -> 43.3 us  [flat_faces(): rows = jnp.dot(picker, values, precision=lax.Precision.HIGHEST)]
    ppermute x52 -> x32, waiting for transfers between devices: 55.5 us -> 33.1 us  [shifted(): lax.ppermute(shard, axis, [(i, (i + by) % peers) for i in range(peers)])]
    ppermute x52 -> x32, starting transfers between devices: 64.2 us -> 45.4 us  [shifted(): lax.ppermute(shard, axis, [(i, (i + by) % peers) for i in range(peers)])]
    unnamed x98 -> x50, local copies, waits for them, and re-layouts: 11.7 us -> 2.54 us
    slice x14 -> x1, local copies, waits for them, and re-layouts: 4.47 us -> 0.04 us  [shards(): correction_all = global_cycle(gathered[:, 1], gathered[:, 0], 1, per_side)]
    dot_general x22 -> x32, matrix products: 5.67 us -> 9.84 us  [along_z(): jnp.dot(wrapped, shift[size_z:], precision=lax.Precision.HIGHEST)]
    concatenate x15 -> x0, local copies, waits for them, and re-layouts: 3.77 us -> none  [the longest x2 1.41 us: with_faces(): jnp.concatenate([lower_z, values[:, :, :-1]], axis=2)]
    dot_general x22 -> x32, matrix products: 4.42 us -> 7.77 us  [along_z(): jnp.dot(values, shift[:size_z], precision=lax.Precision.HIGHEST)]
  transfers between devices with their start and end apart: 52 -> 32, of which waited for: 20 -> 8; matrix products, arithmetic and copies ran while one was open for 13% -> 8% of each run, Pallas kernels for 0% -> 0%
where the time goes in v5:
time: 177 us
  matrix products  66.4 us (38%)
  starting transfers between devices  45.4 us (26%)
  waiting for transfers between devices  33.1 us (19%)
  local copies, waits for them, and re-layouts  14.7 us (8%)
  other arithmetic  14.4 us (8%)
  between operations  2.53 us (1%)
    ppermute x32, starting transfers between devices, shifted(): lax.ppermute(shard, axis, [(i, (i + by) % peers) for i in range(peers)])  45.4 us
    dot_general x16, matrix products, flat_faces(): rows = jnp.dot(picker, values, precision=lax.Precision.HIGHEST)  43.3 us
    ppermute x32, waiting for transfers between devices, shifted(): lax.ppermute(shard, axis, [(i, (i + by) % peers) for i in range(peers)])  33.1 us
    dot_general x32, matrix products, along_z(): jnp.dot(wrapped, shift[size_z:], precision=lax.Precision.HIGHEST)  9.84 us
    dot_general x32, matrix products, along_z(): jnp.dot(values, shift[:size_z], precision=lax.Precision.HIGHEST)  7.77 us
    squeeze x1, other arithmetic, shards(): values = guess[0]  6.02 us
    squeeze x16, local copies, waits for them, and re-layouts, pick(): return [face[number] for face in faces]  3.6 us
  transfers between devices with their start and end apart: 32, of which 8 were waited for; matrix products, arithmetic and copies ran while one was open for 8% of the time, Pallas kernels for 0%

profile of v5, /device:TPU:0, one launch (start us, length us, event | category | flops | bytes accessed | tf_op | source)
XLA Modules:
  0.0 176.5 jit_solution(1644427295152307603)
XLA Ops:
  0.6 1.6 fusion.1255
  2.2 6.0 %copy_bitcast_fusion.3 = (f32[16,16,128]{2,0,1:T(8,128)S(1)}, f32[1,16,16,128]{3,1,2,0:T(8,128)S(1)}, f32[1,16,16,128]{3,1,2,0:T(8,128)S(1)}) fusion(f32[1,16,16,128]{3,2,1,0:T(8,128)} %param.9, f32[]{:T(128)} %bitcast.10, f32[]{:T(128)} %bitcast.9, f32[]{:T(128)} %bitcast.8, f32[]{:T(128)} %bitcast.7, f32[]{:T(128)} %bitcast.6, f32[]{:T(128)} %bitcast.5, ...), kind=kLoop, calls=%fused_computation.1615 | loop fusion | flops 753664 | bytes 655392 | tf_op jit(solution)/shard_map/squeeze | solution.py:382
  8.3 5.1 %collective-permute-start.2 = (f32[2,16,1,128]{3,1,2,0:T(8,128)S(1)}, f32[2,16,1,128]{3,1,2,0:T(8,128)}, u32[]{:S(2)}, u32[]{:S(2)}) collective-permute-start(f32[2,16,1,128]{3,1,2,0:T(8,128)S(1)} %get-tuple-element.51), channel_id=1, source_target_pairs={{0,6},{1,7},{2,0},{3,1},{4,2},{5,3},{6,4},{7,5},{8,14},{9,15},{10,... | collective-permute-start | bytes 49160 | tf_op jit(solution)/shard_map/ppermute | solution.py:16
  13.4 1.1 collective-permute-start
  14.7 3.8 %collective-permute-start.4 = (f32[2,16,16,1]{3,1,2,0:T(8,128)S(1)}, f32[2,16,16,1]{3,1,2,0:T(8,128)S(1)}, u32[]{:S(2)}, u32[]{:S(2)}) collective-permute-start(f32[2,16,16,1]{3,1,2,0:T(8,128)S(1)} %get-tuple-element.49), channel_id=1, source_target_pairs={{0,7},{1,0},{2,1},{3,2},{4,3},{5,4},{6,5},{7,6},{8,15},{9,8},{10,9... | collective-permute-start | bytes 6152 | tf_op jit(solution)/shard_map/ppermute | solution.py:16
  19.0 0.6 iota_add_fusion
  22.4 0.6 and_select_fusion.9
  23.4 0.6 pad_clamp_fusion
  24.2 0.6 constant_dynamic-update-slice_fusion
  24.9 0.6 copy-done.13
  26.7 0.6 concatenate.179
  27.3 1.3 collective-permute-done.3
  30.1 0.7 slice_bitcast_fusion.7
  30.8 0.7 slice_bitcast_fusion.9
  31.6 1.1 fusion.269
  33.0 1.5 collective-permute-start.5
  34.5 4.4 %collective-permute-start.9 = (f32[1,16,16,1]{3,2,1,0:T(8,128)S(1)}, f32[1,16,16,1]{3,2,1,0:T(8,128)S(1)}, u32[]{:S(2)}, u32[]{:S(2)}) collective-permute-start(f32[1,16,16,1]{3,2,1,0:T(8,128)S(1)} %get-tuple-element.97), channel_id=1, source_target_pairs={{0,7},{1,0},{2,1},{3,2},{4,3},{5,4},{6,5},{7,6},{8,15},{9,8},{10,9... | collective-permute-start | bytes 3080 | tf_op jit(solution)/shard_map/ppermute | solution.py:16
  39.0 3.8 %collective-permute-start.7 = (f32[1,16,1,128]{3,1,2,0:T(8,128)S(1)}, f32[1,16,1,128]{3,1,2,0:T(8,128)S(1)}, u32[]{:S(2)}, u32[]{:S(2)}) collective-permute-start(f32[1,16,1,128]{3,1,2,0:T(8,128)S(1)} %bitcast.322), channel_id=1, source_target_pairs={{0,6},{1,7},{2,0},{3,1},{4,2},{5,3},{6,4},{7,5},{8,14},{9,15},{10,... | collective-permute-start | bytes 24584 | tf_op jit(solution)/shard_map/ppermute | solution.py:16
  43.1 3.6 %collective-permute-done.8 = f32[1,16,16,1]{3,2,1,0:T(8,128)S(1)} collective-permute-done((f32[1,16,16,1]{3,2,1,0:T(8,128)S(1)}, f32[1,16,16,1]{3,2,1,0:T(8,128)S(1)}, u32[]{:S(2)}, u32[]{:S(2)}) %collective-permute-start.8) | collective-permute-done | bytes 1056 | tf_op jit(solution)/shard_map/ppermute | solution.py:16
  47.6 2.6 %collective-permute-start.14 = (f32[1,16,16,1]{3,2,1,0:T(8,128)S(1)}, f32[1,16,16,1]{3,2,1,0:T(8,128)S(1)}, u32[]{:S(2)}, u32[]{:S(2)}) collective-permute-start(f32[1,16,16,1]{3,2,1,0:T(8,128)S(1)} %get-tuple-element.85), channel_id=1, source_target_pairs={{0,7},{1,0},{2,1},{3,2},{4,3},{5,4},{6,5},{7,6},{8,15},{9,8},{10,9... | collective-permute-start | bytes 3080 | tf_op jit(solution)/shard_map/ppermute | solution.py:16
  50.3 1.3 collective-permute-start.11
  51.5 2.6 %collective-permute-start.12 = (f32[1,16,1,128]{3,1,2,0:T(8,128)S(1)}, f32[1,16,1,128]{3,1,2,0:T(8,128)S(1)}, u32[]{:S(2)}, u32[]{:S(2)}) collective-permute-start(f32[1,16,1,128]{3,1,2,0:T(8,128)S(1)} %bitcast.325), channel_id=1, source_target_pairs={{0,6},{1,7},{2,0},{3,1},{4,2},{5,3},{6,4},{7,5},{8,14},{9,15},{10,... | collective-permute-start | bytes 24584 | tf_op jit(solution)/shard_map/ppermute | solution.py:16
  54.4 3.6 %collective-permute-done.13 = f32[1,16,16,1]{3,2,1,0:T(8,128)S(1)} collective-permute-done((f32[1,16,16,1]{3,2,1,0:T(8,128)S(1)}, f32[1,16,16,1]{3,2,1,0:T(8,128)S(1)}, u32[]{:S(2)}, u32[]{:S(2)}) %collective-permute-start.13) | collective-permute-done | bytes 1056 | tf_op jit(solution)/shard_map/ppermute | solution.py:16
  59.6 1.3 collective-permute-start.20
  61.3 3.7 %collective-permute-start.18 = (f32[2,8,8,64]{3,2,1,0:T(8,128)S(1)}, f32[2,8,8,64]{3,2,1,0:T(8,128)S(1)}, u32[]{:S(2)}, u32[]{:S(2)}) collective-permute-start(f32[2,8,8,64]{3,2,1,0:T(8,128)S(1)} %pad_maximum_fusion.1), channel_id=1, source_target_pairs={{0,4},{1,5},{2,6},{3,7},{4,0},{5,1},{6,2},{7,3},{8,12},{9,13},{10,... | collective-permute-start | bytes 98312 | tf_op jit(solution)/shard_map/ppermute | solution.py:16
  65.0 1.5 collective-permute-start.15
  66.5 5.5 %collective-permute-done.15 = f32[2,8,8,64]{3,2,1,0:T(8,128)S(1)} collective-permute-done((f32[2,8,8,64]{3,2,1,0:T(8,128)S(1)}, f32[2,8,8,64]{3,2,1,0:T(8,128)S(1)}, u32[]{:S(2)}, u32[]{:S(2)}) %collective-permute-start.15) | collective-permute-done | bytes 32800 | tf_op jit(solution)/shard_map/ppermute | solution.py:16
  72.0 6.1 %collective-permute-done.16 = f32[2,8,8,64]{3,2,1,0:T(8,128)S(1)} collective-permute-done((f32[2,8,8,64]{3,2,1,0:T(8,128)S(1)}, f32[2,8,8,64]{3,2,1,0:T(8,128)S(1)}, u32[]{:S(2)}, u32[]{:S(2)}) %collective-permute-start.16) | collective-permute-done | bytes 32800 | tf_op jit(solution)/shard_map/ppermute | solution.py:16
  78.2 4.2 %collective-permute-done.21 = f32[2,8,8,64]{3,2,1,0:T(8,128)S(1)} collective-permute-done((f32[2,8,8,64]{3,2,1,0:T(8,128)S(1)}, f32[2,8,8,64]{3,2,1,0:T(8,128)S(1)}, u32[]{:S(2)}, u32[]{:S(2)}) %collective-permute-start.21) | collective-permute-done | bytes 32800 | tf_op jit(solution)/shard_map/ppermute | solution.py:16
  82.3 0.7 gather_fusion
  84.3 7.5 %fusion.8 = f32[3072,64]{0,1:T(8,128)S(1)} fusion(f32[512,64]{1,0:T(8,128)S(1)} %bitcast.260, s32[3072]{0:T(1024)S(1)} %copy-done.14), kind=kOutput, calls=%fused_computation.9 | convolution fusion | flops 1211105280 | bytes 929792 | tf_op jit(solution)/shard_map/dot_general | solution.py:262
  93.3 7.6 %fusion.6 = f32[3072,64]{0,1:T(8,128)S(1)} fusion(f32[512,64]{0,1:T(8,128)S(1)} %get-tuple-element.24, s32[3072]{0:T(1024)S(1)} %copy-done.14), kind=kOutput, calls=%fused_computation.7 | convolution fusion | flops 1211105280 | bytes 929792 | tf_op jit(solution)/shard_map/dot_general | solution.py:262
  102.5 7.9 %fusion.4 = f32[3072,64]{0,1:T(8,128)S(1)} fusion(f32[512,64]{0,1:T(8,128)S(1)} %fusion.37, s32[3072]{0:T(1024)S(1)} %copy-done.14), kind=kOutput, calls=%fused_computation.5 | convolution fusion | flops 1211105280 | bytes 929792 | tf_op jit(solution)/shard_map/dot_general | solution.py:262
  114.9 0.6 fusion.180
  116.4 0.6 fusion.178
  126.2 0.6 fusion.176
  130.4 7.6 %fusion.2 = f32[3072,64]{0,1:T(8,128)S(1)} fusion(f32[512,64]{0,1:T(8,128)S(1)} %convolution_add_fusion.10, s32[3072]{0:T(1024)S(1)} %copy-done.14), kind=kOutput, calls=%fused_computation.3 | convolution fusion | flops 1211105280 | bytes 929792 | tf_op jit(solution)/shard_map/dot_general | solution.py:262
  139.6 7.9 %fusion = f32[3072,64]{0,1:T(8,128)S(1)} fusion(f32[512,64]{0,1:T(8,128)S(1)} %fusion.56, s32[3072]{0:T(1024)S(1)} %copy-done.14), kind=kOutput, calls=%fused_computation.1 | convolution fusion | flops 1211105280 | bytes 929792 | tf_op jit(solution)/shard_map/dot_general | solution.py:262
  152.0 2.8 %collective-permute-start.26 = (f32[1,16,16,1]{3,2,1,0:T(8,128)S(1)}, f32[1,16,16,1]{3,2,1,0:T(8,128)S(1)}, u32[]{:S(2)}, u32[]{:S(2)}) collective-permute-start(f32[1,16,16,1]{3,2,1,0:T(8,128)S(1)} %get-tuple-element.67), channel_id=1, source_target_pairs={{0,7},{1,0},{2,1},{3,2},{4,3},{5,4},{6,5},{7,6},{8,15},{9,8},{10,9... | collective-permute-start | bytes 3080 | tf_op jit(solution)/shard_map/ppermute | solution.py:16
  154.8 1.1 collective-permute-start.23
  155.9 2.8 %collective-permute-start.24 = (f32[1,16,1,128]{3,1,2,0:T(8,128)S(1)}, f32[1,16,1,128]{3,1,2,0:T(8,128)S(1)}, u32[]{:S(2)}, u32[]{:S(2)}) collective-permute-start(f32[1,16,1,128]{3,1,2,0:T(8,128)S(1)} %bitcast.321), channel_id=1, source_target_pairs={{0,6},{1,7},{2,0},{3,1},{4,2},{5,3},{6,4},{7,5},{8,14},{9,15},{10,... | collective-permute-start | bytes 24584 | tf_op jit(solution)/shard_map/ppermute | solution.py:16
  158.9 4.4 %collective-permute-done.25 = f32[1,16,16,1]{3,2,1,0:T(8,128)S(1)} collective-permute-done((f32[1,16,16,1]{3,2,1,0:T(8,128)S(1)}, f32[1,16,16,1]{3,2,1,0:T(8,128)S(1)}, u32[]{:S(2)}, u32[]{:S(2)}) %collective-permute-start.25) | collective-permute-done | bytes 1056 | tf_op jit(solution)/shard_map/ppermute | solution.py:16
  164.8 2.8 %collective-permute-start.31 = (f32[1,16,16,1]{3,1,2,0:T(8,128)S(1)}, f32[1,16,16,1]{3,1,2,0:T(8,128)S(1)}, u32[]{:S(2)}, u32[]{:S(2)}) collective-permute-start(f32[1,16,16,1]{3,1,2,0:T(8,128)S(1)} %get-tuple-element.55), channel_id=1, source_target_pairs={{0,7},{1,0},{2,1},{3,2},{4,3},{5,4},{6,5},{7,6},{8,15},{9,8},{10,9... | collective-permute-start | bytes 3080 | tf_op jit(solution)/shard_map/ppermute | solution.py:16
  167.6 0.7 copy.572
  168.3 0.9 collective-permute-start.29
  169.2 1.1 collective-permute-start.28
  170.7 4.6 %collective-permute-done.30 = f32[1,16,16,1]{3,1,2,0:T(8,128)S(1)} collective-permute-done((f32[1,16,16,1]{3,1,2,0:T(8,128)S(1)}, f32[1,16,16,1]{3,1,2,0:T(8,128)S(1)}, u32[]{:S(2)}, u32[]{:S(2)}) %collective-permute-start.30) | collective-permute-done | bytes 1056 | tf_op jit(solution)/shard_map/ppermute | solution.py:16
  175.8 0.7 copy.573
  (337 shorter events, 40.6 us)
Async XLA Ops:
  8.3 21.8 %collective-permute-start.2 = (f32[2,16,1,128]{3,1,2,0:T(8,128)S(1)}, f32[2,16,1,128]{3,1,2,0:T(8,128)}, u32[]{:S(2)}, u32[]{:S(2)}) collective-permute-start(f32[2,16,1,128]{3,1,2,0:T(8,128)S(1)} %get-tuple-element.51), channel_id=1, source_target_pairs={{0,6},{1,7},{2,0},{3,1},{4,2},{5,3},{6,4},{7,5},{8,14},{9,15},{10,... | collective-permute-start | bytes 49160 | tf_op jit(solution)/shard_map/ppermute | solution.py:16
  13.4 17.4 %collective-permute-start.1 = (f32[2,16,1,128]{3,1,2,0:T(8,128)S(1)}, f32[2,16,1,128]{3,1,2,0:T(8,128)}, u32[]{:S(2)}, u32[]{:S(2)}) collective-permute-start(f32[2,16,1,128]{3,1,2,0:T(8,128)S(1)} %get-tuple-element.52), channel_id=1, source_target_pairs={{0,2},{1,3},{2,4},{3,5},{4,6},{5,7},{6,0},{7,1},{8,10},{9,11},{10,... | collective-permute-start | bytes 49160 | tf_op jit(solution)/shard_map/ppermute | solution.py:16
  13.4 18.1 %collective-permute-start = (f32[2,2,16,128]{3,1,2,0:T(2,128)S(1)}, f32[2,2,16,128]{3,1,2,0:T(2,128)S(1)}, u32[]{:S(2)}, u32[]{:S(2)}) collective-permute-start(f32[2,2,16,128]{3,1,2,0:T(2,128)S(1)} %fusion.474), channel_id=1, source_target_pairs={{0,4},{1,5},{2,6},{3,7},{4,0},{5,1},{6,2},{7,3},{8,12},{9,13},{10,... | collective-permute-start | bytes 98312 | tf_op jit(solution)/shard_map/ppermute | solution.py:16
  14.7 12.7 %collective-permute-start.4 = (f32[2,16,16,1]{3,1,2,0:T(8,128)S(1)}, f32[2,16,16,1]{3,1,2,0:T(8,128)S(1)}, u32[]{:S(2)}, u32[]{:S(2)}) collective-permute-start(f32[2,16,16,1]{3,1,2,0:T(8,128)S(1)} %get-tuple-element.49), channel_id=1, source_target_pairs={{0,7},{1,0},{2,1},{3,2},{4,3},{5,4},{6,5},{7,6},{8,15},{9,8},{10,9... | collective-permute-start | bytes 6152 | tf_op jit(solution)/shard_map/ppermute | solution.py:16
  18.5 10.1 %collective-permute-start.3 = (f32[2,16,16,1]{3,1,2,0:T(8,128)S(1)}, f32[2,16,16,1]{3,1,2,0:T(8,128)S(1)}, u32[]{:S(2)}, u32[]{:S(2)}) collective-permute-start(f32[2,16,16,1]{3,1,2,0:T(8,128)S(1)} %get-tuple-element.50), channel_id=1, source_target_pairs={{0,1},{1,2},{2,3},{3,4},{4,5},{5,6},{6,7},{7,0},{8,9},{9,10},{10,1... | collective-permute-start | bytes 6152 | tf_op jit(solution)/shard_map/ppermute | solution.py:16
  22.4 3.5 %copy-start.3 = (s32[256]{0:T(256)}, s32[256]{0:T(256)S(1)}, u32[]{:S(2)}) copy-start(s32[256]{0:T(256)S(1)} %fusion.962) | copy-start | bytes 3076
  23.2 2.8 %copy-start.11 = (s32[16]{0:T(128)S(1)}, s32[16]{0:T(128)}, u32[]{:S(2)}) copy-start(s32[16]{0:T(128)} %param.7) | copy-start | bytes 196
  23.2 3.4 %copy-start.12 = (f32[16]{0:T(128)S(1)}, f32[16]{0:T(128)}, u32[]{:S(2)}) copy-start(f32[16]{0:T(128)} %param.8) | copy-start | bytes 196
  24.0 2.5 %copy-start.6 = (s32[128]{0:T(128)}, s32[128]{0:T(128)S(1)}, u32[]{:S(2)}) copy-start(s32[128]{0:T(128)S(1)} %get-tuple-element.158) | copy-start | bytes 1540
  27.3 4.2 %copy-start = (f32[1,16,16,128]{3,2,1,0:T(8,128)S(1)}, f32[1,16,16,128]{3,2,1,0:T(8,128)}, u32[]{:S(2)}) copy-start(f32[1,16,16,128]{3,2,1,0:T(8,128)} %param.9) | copy-start | bytes 393220
  33.0 13.9 %collective-permute-start.5 = (f32[1,2,16,128]{3,2,1,0:T(8,128)S(1)}, f32[1,2,16,128]{3,2,1,0:T(8,128)S(1)}, u32[]{:S(2)}, u32[]{:S(2)}) collective-permute-start(f32[1,2,16,128]{3,2,1,0:T(8,128)S(1)} %pad_maximum_fusion.6), channel_id=1, source_target_pairs={{0,4},{1,5},{2,6},{3,7},{4,0},{5,1},{6,2},{7,3},{8,12},{9,13},{10,... | collective-permute-start | bytes 49160 | tf_op jit(solution)/shard_map/ppermute | solution.py:16
  34.5 8.3 %collective-permute-start.9 = (f32[1,16,16,1]{3,2,1,0:T(8,128)S(1)}, f32[1,16,16,1]{3,2,1,0:T(8,128)S(1)}, u32[]{:S(2)}, u32[]{:S(2)}) collective-permute-start(f32[1,16,16,1]{3,2,1,0:T(8,128)S(1)} %get-tuple-element.97), channel_id=1, source_target_pairs={{0,7},{1,0},{2,1},{3,2},{4,3},{5,4},{6,5},{7,6},{8,15},{9,8},{10,9... | collective-permute-start | bytes 3080 | tf_op jit(solution)/shard_map/ppermute | solution.py:16
  38.9 7.7 %collective-permute-start.8 = (f32[1,16,16,1]{3,2,1,0:T(8,128)S(1)}, f32[1,16,16,1]{3,2,1,0:T(8,128)S(1)}, u32[]{:S(2)}, u32[]{:S(2)}) collective-permute-start(f32[1,16,16,1]{3,2,1,0:T(8,128)S(1)} %get-tuple-element.98), channel_id=1, source_target_pairs={{0,1},{1,2},{2,3},{3,4},{4,5},{5,6},{6,7},{7,0},{8,9},{9,10},{10,1... | collective-permute-start | bytes 3080 | tf_op jit(solution)/shard_map/ppermute | solution.py:16
  38.9 8.0 %collective-permute-start.6 = (f32[1,16,1,128]{3,1,2,0:T(8,128)S(1)}, f32[1,16,1,128]{3,1,2,0:T(8,128)S(1)}, u32[]{:S(2)}, u32[]{:S(2)}) collective-permute-start(f32[1,16,1,128]{3,1,2,0:T(8,128)S(1)} %bitcast.324), channel_id=1, source_target_pairs={{0,2},{1,3},{2,4},{3,5},{4,6},{5,7},{6,0},{7,1},{8,10},{9,11},{10,... | collective-permute-start | bytes 24584 | tf_op jit(solution)/shard_map/ppermute | solution.py:16
  39.0 8.0 %collective-permute-start.7 = (f32[1,16,1,128]{3,1,2,0:T(8,128)S(1)}, f32[1,16,1,128]{3,1,2,0:T(8,128)S(1)}, u32[]{:S(2)}, u32[]{:S(2)}) collective-permute-start(f32[1,16,1,128]{3,1,2,0:T(8,128)S(1)} %bitcast.322), channel_id=1, source_target_pairs={{0,6},{1,7},{2,0},{3,1},{4,2},{5,3},{6,4},{7,5},{8,14},{9,15},{10,... | collective-permute-start | bytes 24584 | tf_op jit(solution)/shard_map/ppermute | solution.py:16
  47.6 10.7 %collective-permute-start.10 = (f32[1,2,16,128]{3,2,1,0:T(8,128)S(1)}, f32[1,2,16,128]{3,2,1,0:T(8,128)S(1)}, u32[]{:S(2)}, u32[]{:S(2)}) collective-permute-start(f32[1,2,16,128]{3,2,1,0:T(8,128)S(1)} %pad_maximum_fusion.7), channel_id=1, source_target_pairs={{0,4},{1,5},{2,6},{3,7},{4,0},{5,1},{6,2},{7,3},{8,12},{9,13},{10,... | collective-permute-start | bytes 49160 | tf_op jit(solution)/shard_map/ppermute | solution.py:16
  47.6 6.5 %collective-permute-start.14 = (f32[1,16,16,1]{3,2,1,0:T(8,128)S(1)}, f32[1,16,16,1]{3,2,1,0:T(8,128)S(1)}, u32[]{:S(2)}, u32[]{:S(2)}) collective-permute-start(f32[1,16,16,1]{3,2,1,0:T(8,128)S(1)} %get-tuple-element.85), channel_id=1, source_target_pairs={{0,7},{1,0},{2,1},{3,2},{4,3},{5,4},{6,5},{7,6},{8,15},{9,8},{10,9... | collective-permute-start | bytes 3080 | tf_op jit(solution)/shard_map/ppermute | solution.py:16
  50.2 7.8 %collective-permute-start.13 = (f32[1,16,16,1]{3,2,1,0:T(8,128)S(1)}, f32[1,16,16,1]{3,2,1,0:T(8,128)S(1)}, u32[]{:S(2)}, u32[]{:S(2)}) collective-permute-start(f32[1,16,16,1]{3,2,1,0:T(8,128)S(1)} %get-tuple-element.86), channel_id=1, source_target_pairs={{0,1},{1,2},{2,3},{3,4},{4,5},{5,6},{6,7},{7,0},{8,9},{9,10},{10,1... | collective-permute-start | bytes 3080 | tf_op jit(solution)/shard_map/ppermute | solution.py:16
  50.3 8.1 %collective-permute-start.11 = (f32[1,16,1,128]{3,1,2,0:T(8,128)S(1)}, f32[1,16,1,128]{3,1,2,0:T(8,128)S(1)}, u32[]{:S(2)}, u32[]{:S(2)}) collective-permute-start(f32[1,16,1,128]{3,1,2,0:T(8,128)S(1)} %bitcast.326), channel_id=1, source_target_pairs={{0,2},{1,3},{2,4},{3,5},{4,6},{5,7},{6,0},{7,1},{8,10},{9,11},{10,... | collective-permute-start | bytes 24584 | tf_op jit(solution)/shard_map/ppermute | solution.py:16
  51.5 6.8 %collective-permute-start.12 = (f32[1,16,1,128]{3,1,2,0:T(8,128)S(1)}, f32[1,16,1,128]{3,1,2,0:T(8,128)S(1)}, u32[]{:S(2)}, u32[]{:S(2)}) collective-permute-start(f32[1,16,1,128]{3,1,2,0:T(8,128)S(1)} %bitcast.325), channel_id=1, source_target_pairs={{0,6},{1,7},{2,0},{3,1},{4,2},{5,3},{6,4},{7,5},{8,14},{9,15},{10,... | collective-permute-start | bytes 24584 | tf_op jit(solution)/shard_map/ppermute | solution.py:16
  59.6 23.5 %copy-start.10 = (pred[8]{0:T(512)(128)(4,1)S(1)}, pred[8]{0:T(512)(128)(4,1)}, u32[]{:S(2)}) copy-start(pred[8]{0:T(512)(128)(4,1)} %compare_and_fusion) | copy-start | bytes 28
  59.6 18.6 %collective-permute-start.20 = (f32[2,8,8,64]{3,2,1,0:T(8,128)S(1)}, f32[2,8,8,64]{3,2,1,0:T(8,128)S(1)}, u32[]{:S(2)}, u32[]{:S(2)}) collective-permute-start(f32[2,8,8,64]{3,2,1,0:T(8,128)S(1)} %pad_maximum_fusion.1), channel_id=1, source_target_pairs={{0,6},{1,7},{2,0},{3,1},{4,2},{5,3},{6,4},{7,5},{8,14},{9,15},{10,... | collective-permute-start | bytes 98312 | tf_op jit(solution)/shard_map/ppermute | solution.py:16
  60.9 17.2 %collective-permute-start.19 = (f32[2,8,8,64]{3,2,1,0:T(8,128)S(1)}, f32[2,8,8,64]{3,2,1,0:T(8,128)S(1)}, u32[]{:S(2)}, u32[]{:S(2)}) collective-permute-start(f32[2,8,8,64]{3,2,1,0:T(8,128)S(1)} %pad_maximum_fusion.1), channel_id=1, source_target_pairs={{0,5},{1,6},{2,7},{3,0},{4,1},{5,2},{6,3},{7,4},{8,13},{9,14},{10,... | collective-permute-start | bytes 98312 | tf_op jit(solution)/shard_map/ppermute | solution.py:16
  61.3 16.8 %collective-permute-start.18 = (f32[2,8,8,64]{3,2,1,0:T(8,128)S(1)}, f32[2,8,8,64]{3,2,1,0:T(8,128)S(1)}, u32[]{:S(2)}, u32[]{:S(2)}) collective-permute-start(f32[2,8,8,64]{3,2,1,0:T(8,128)S(1)} %pad_maximum_fusion.1), channel_id=1, source_target_pairs={{0,4},{1,5},{2,6},{3,7},{4,0},{5,1},{6,2},{7,3},{8,12},{9,13},{10,... | collective-permute-start | bytes 98312 | tf_op jit(solution)/shard_map/ppermute | solution.py:16
  65.0 13.0 %collective-permute-start.17 = (f32[2,8,8,64]{3,2,1,0:T(8,128)S(1)}, f32[2,8,8,64]{3,2,1,0:T(8,128)S(1)}, u32[]{:S(2)}, u32[]{:S(2)}) collective-permute-start(f32[2,8,8,64]{3,2,1,0:T(8,128)S(1)} %pad_maximum_fusion.1), channel_id=1, source_target_pairs={{0,3},{1,4},{2,5},{3,6},{4,7},{5,0},{6,1},{7,2},{8,11},{9,12},{10,... | collective-permute-start | bytes 98312 | tf_op jit(solution)/shard_map/ppermute | solution.py:16
  65.0 7.0 %collective-permute-start.15 = (f32[2,8,8,64]{3,2,1,0:T(8,128)S(1)}, f32[2,8,8,64]{3,2,1,0:T(8,128)S(1)}, u32[]{:S(2)}, u32[]{:S(2)}) collective-permute-start(f32[2,8,8,64]{3,2,1,0:T(8,128)S(1)} %pad_maximum_fusion.1), channel_id=1, source_target_pairs={{0,1},{1,2},{2,3},{3,4},{4,5},{5,6},{6,7},{7,0},{8,9},{9,10},{10,1... | collective-permute-start | bytes 98312 | tf_op jit(solution)/shard_map/ppermute | solution.py:16
  72.0 6.1 %collective-permute-start.16 = (f32[2,8,8,64]{3,2,1,0:T(8,128)S(1)}, f32[2,8,8,64]{3,2,1,0:T(8,128)S(1)}, u32[]{:S(2)}, u32[]{:S(2)}) collective-permute-start(f32[2,8,8,64]{3,2,1,0:T(8,128)S(1)} %pad_maximum_fusion.1), channel_id=1, source_target_pairs={{0,2},{1,3},{2,4},{3,5},{4,6},{5,7},{6,0},{7,1},{8,10},{9,11},{10,... | collective-permute-start | bytes 98312 | tf_op jit(solution)/shard_map/ppermute | solution.py:16
  78.1 4.3 %collective-permute-start.21 = (f32[2,8,8,64]{3,2,1,0:T(8,128)S(1)}, f32[2,8,8,64]{3,2,1,0:T(8,128)S(1)}, u32[]{:S(2)}, u32[]{:S(2)}) collective-permute-start(f32[2,8,8,64]{3,2,1,0:T(8,128)S(1)} %pad_maximum_fusion.1), channel_id=1, source_target_pairs={{0,7},{1,0},{2,1},{3,2},{4,3},{5,4},{6,5},{7,6},{8,15},{9,8},{10,9... | collective-permute-start | bytes 98312 | tf_op jit(solution)/shard_map/ppermute | solution.py:16
  102.5 7.9 %copy-start.5 = (s32[64]{0:T(128)S(1)}, s32[64]{0:T(128)}, u32[]{:S(2)}) copy-start(s32[64]{0:T(128)} %and_select_fusion.22) | copy-start | bytes 772
  102.5 8.4 %copy-start.1 = (s32[512]{0:T(512)S(1)}, s32[512]{0:T(512)}, u32[]{:S(2)}) copy-start(s32[512]{0:T(512)} %get-tuple-element.156) | copy-start | bytes 6148
  102.5 8.7 %copy-start.17 = (s32[32]{0:T(128)S(1)}, s32[32]{0:T(128)}, u32[]{:S(2)}) copy-start(s32[32]{0:T(128)} %iota_add_fusion.3) | copy-start | bytes 388
  102.5 9.0 %copy-start.18 = (s32[32]{0:T(128)S(1)}, s32[32]{0:T(128)}, u32[]{:S(2)}) copy-start(s32[32]{0:T(128)} %iota_add_fusion.2) | copy-start | bytes 388
  102.5 9.2 %copy-start.16 = (s32[768]{0:T(1024)S(1)}, s32[768]{0:T(1024)}, u32[]{:S(2)}) copy-start(s32[768]{0:T(1024)} %copy-done.15) | copy-start | bytes 9220
  113.1 3.9 %copy-start.2 = (s32[32]{0:T(128)S(1)}, s32[32]{0:T(128)}, u32[]{:S(2)}) copy-start(s32[32]{0:T(128)} %get-tuple-element.159) | copy-start | bytes 388
  113.1 4.1 %copy-start.8 = (s32[128]{0:T(128)S(1)}, s32[128]{0:T(128)}, u32[]{:S(2)}) copy-start(s32[128]{0:T(128)} %fusion.1000) | copy-start | bytes 1540
  113.1 4.2 %copy-start.20 = (s32[16]{0:T(128)S(1)}, s32[16]{0:T(128)}, u32[]{:S(2)}) copy-start(s32[16]{0:T(128)} %iota_add_fusion) | copy-start | bytes 196
  113.1 4.4 %copy-start.19 = (s32[16]{0:T(128)S(1)}, s32[16]{0:T(128)}, u32[]{:S(2)}) copy-start(s32[16]{0:T(128)} %iota_add_fusion.1) | copy-start | bytes 196
  113.2 4.6 %copy-start.9 = (s32[192]{0:T(256)S(1)}, s32[192]{0:T(256)}, u32[]{:S(2)}) copy-start(s32[192]{0:T(256)} %concatenate.179) | copy-start | bytes 2308
  151.9 11.7 %collective-permute-start.22 = (f32[1,2,16,128]{3,2,1,0:T(8,128)S(1)}, f32[1,2,16,128]{3,2,1,0:T(8,128)S(1)}, u32[]{:S(2)}, u32[]{:S(2)}) collective-permute-start(f32[1,2,16,128]{3,2,1,0:T(8,128)S(1)} %pad_maximum_fusion.8), channel_id=1, source_target_pairs={{0,4},{1,5},{2,6},{3,7},{4,0},{5,1},{6,2},{7,3},{8,12},{9,13},{10,... | collective-permute-start | bytes 49160 | tf_op jit(solution)/shard_map/ppermute | solution.py:16
  152.0 6.7 %collective-permute-start.26 = (f32[1,16,16,1]{3,2,1,0:T(8,128)S(1)}, f32[1,16,16,1]{3,2,1,0:T(8,128)S(1)}, u32[]{:S(2)}, u32[]{:S(2)}) collective-permute-start(f32[1,16,16,1]{3,2,1,0:T(8,128)S(1)} %get-tuple-element.67), channel_id=1, source_target_pairs={{0,7},{1,0},{2,1},{3,2},{4,3},{5,4},{6,5},{7,6},{8,15},{9,8},{10,9... | collective-permute-start | bytes 3080 | tf_op jit(solution)/shard_map/ppermute | solution.py:16
  154.8 8.6 %collective-permute-start.25 = (f32[1,16,16,1]{3,2,1,0:T(8,128)S(1)}, f32[1,16,16,1]{3,2,1,0:T(8,128)S(1)}, u32[]{:S(2)}, u32[]{:S(2)}) collective-permute-start(f32[1,16,16,1]{3,2,1,0:T(8,128)S(1)} %get-tuple-element.68), channel_id=1, source_target_pairs={{0,1},{1,2},{2,3},{3,4},{4,5},{5,6},{6,7},{7,0},{8,9},{9,10},{10,1... | collective-permute-start | bytes 3080 | tf_op jit(solution)/shard_map/ppermute | solution.py:16
  154.8 8.9 %collective-permute-start.23 = (f32[1,16,1,128]{3,1,2,0:T(8,128)S(1)}, f32[1,16,1,128]{3,1,2,0:T(8,128)S(1)}, u32[]{:S(2)}, u32[]{:S(2)}) collective-permute-start(f32[1,16,1,128]{3,1,2,0:T(8,128)S(1)} %bitcast.323), channel_id=1, source_target_pairs={{0,2},{1,3},{2,4},{3,5},{4,6},{5,7},{6,0},{7,1},{8,10},{9,11},{10,... | collective-permute-start | bytes 24584 | tf_op jit(solution)/shard_map/ppermute | solution.py:16
  155.9 7.8 %collective-permute-start.24 = (f32[1,16,1,128]{3,1,2,0:T(8,128)S(1)}, f32[1,16,1,128]{3,1,2,0:T(8,128)S(1)}, u32[]{:S(2)}, u32[]{:S(2)}) collective-permute-start(f32[1,16,1,128]{3,1,2,0:T(8,128)S(1)} %bitcast.321), channel_id=1, source_target_pairs={{0,6},{1,7},{2,0},{3,1},{4,2},{5,3},{6,4},{7,5},{8,14},{9,15},{10,... | collective-permute-start | bytes 24584 | tf_op jit(solution)/shard_map/ppermute | solution.py:16
  164.2 11.4 %collective-permute-start.27 = (f32[1,2,16,128]{3,1,2,0:T(2,128)S(1)}, f32[1,2,16,128]{3,1,2,0:T(2,128)S(1)}, u32[]{:S(2)}, u32[]{:S(2)}) collective-permute-start(f32[1,2,16,128]{3,1,2,0:T(2,128)S(1)} %pad_maximum_fusion.9), channel_id=1, source_target_pairs={{0,4},{1,5},{2,6},{3,7},{4,0},{5,1},{6,2},{7,3},{8,12},{9,13},{10,... | collective-permute-start | bytes 49160 | tf_op jit(solution)/shard_map/ppermute | solution.py:16
  164.8 5.6 %collective-permute-start.31 = (f32[1,16,16,1]{3,1,2,0:T(8,128)S(1)}, f32[1,16,16,1]{3,1,2,0:T(8,128)S(1)}, u32[]{:S(2)}, u32[]{:S(2)}) collective-permute-start(f32[1,16,16,1]{3,1,2,0:T(8,128)S(1)} %get-tuple-element.55), channel_id=1, source_target_pairs={{0,7},{1,0},{2,1},{3,2},{4,3},{5,4},{6,5},{7,6},{8,15},{9,8},{10,9... | collective-permute-start | bytes 3080 | tf_op jit(solution)/shard_map/ppermute | solution.py:16
  167.6 7.7 %collective-permute-start.30 = (f32[1,16,16,1]{3,1,2,0:T(8,128)S(1)}, f32[1,16,16,1]{3,1,2,0:T(8,128)S(1)}, u32[]{:S(2)}, u32[]{:S(2)}) collective-permute-start(f32[1,16,16,1]{3,1,2,0:T(8,128)S(1)} %get-tuple-element.56), channel_id=1, source_target_pairs={{0,1},{1,2},{2,3},{3,4},{4,5},{5,6},{6,7},{7,0},{8,9},{9,10},{10,1... | collective-permute-start | bytes 3080 | tf_op jit(solution)/shard_map/ppermute | solution.py:16
  168.3 7.4 %collective-permute-start.29 = (f32[1,16,1,128]{3,1,2,0:T(8,128)S(1)}, f32[1,16,1,128]{3,1,2,0:T(8,128)S(1)}, u32[]{:S(2)}, u32[]{:S(2)}) collective-permute-start(f32[1,16,1,128]{3,1,2,0:T(8,128)S(1)} %get-tuple-element.59), channel_id=1, source_target_pairs={{0,6},{1,7},{2,0},{3,1},{4,2},{5,3},{6,4},{7,5},{8,14},{9,15},{10,... | collective-permute-start | bytes 24584 | tf_op jit(solution)/shard_map/ppermute | solution.py:16
  169.2 6.5 %collective-permute-start.28 = (f32[1,16,1,128]{3,1,2,0:T(8,128)S(1)}, f32[1,16,1,128]{3,1,2,0:T(8,128)S(1)}, u32[]{:S(2)}, u32[]{:S(2)}) collective-permute-start(f32[1,16,1,128]{3,1,2,0:T(8,128)S(1)} %get-tuple-element.60), channel_id=1, source_target_pairs={{0,2},{1,3},{2,4},{3,5},{4,6},{5,7},{6,0},{7,1},{8,10},{9,11},{10,... | collective-permute-start | bytes 24584 | tf_op jit(solution)/shard_map/ppermute | solution.py:16
  (5 other events, 5.8 us)

commit v6 on v5

--- a/solution.py
+++ b/solution.py
@@ -245,7 +245,7 @@
     for sign in (-1, 1):
         picks.append((((row + sign) % count_b) * size_x + at_x) * size_y + at_y)
     target = jnp.concatenate(picks)
-    return jnp.where(target[:, None] == index[None, :], 1.0, 0.0).astype(jnp.float32)
+    return jnp.where(target[:, None] == index[None, :], 1.0, 0.0).astype(jnp.bfloat16)
 
 
 def lane_shift(size_z, sign):
@@ -254,17 +254,39 @@
     inner = jnp.where(lanes_in == lanes_out + sign, 1.0, 0.0)
     edge_in, edge_out = (size_z - 1, 0) if sign < 0 else (0, size_z - 1)
     wrap = jnp.where((lanes_in == edge_in) & (lanes_out == edge_out), 1.0, 0.0)
-    return jnp.concatenate([inner, wrap]).astype(jnp.float32)
+    return jnp.concatenate([inner, wrap]).astype(jnp.bfloat16)
+
+
+def split3(values):
+    pieces = []
+    rest = values
+    for piece_no in range(3):
+        piece = lax.reduce_precision(rest, exponent_bits=8, mantissa_bits=7)
+        pieces.append(piece.astype(jnp.bfloat16))
+        rest = rest - piece
+    return pieces
+
+
+def pick_rows(picker, values):
+    size_z = values.shape[1]
+    joined = jnp.concatenate(split3(values), axis=1)
+    out = jnp.dot(picker, joined, preferred_element_type=jnp.float32)
+    return (out[:, :size_z] + out[:, size_z : 2 * size_z]) + out[:, 2 * size_z :]
+
+
+def pick_lanes(values, shift):
+    count_r = values.shape[0]
+    stacked = jnp.concatenate(split3(values), axis=0)
+    out = jnp.dot(stacked, shift, preferred_element_type=jnp.float32)
+    return (out[:count_r] + out[count_r : 2 * count_r]) + out[2 * count_r :]
 
 
 def flat_faces(values, picker, lower_z, upper_z):
     count_r, size_z = values.shape
-    rows = jnp.dot(picker, values, precision=lax.Precision.HIGHEST)
+    rows = pick_rows(picker, values)
 
     def along_z(shift, wrapped):
-        return jnp.dot(values, shift[:size_z], precision=lax.Precision.HIGHEST) + jnp.dot(
-            wrapped, shift[size_z:], precision=lax.Precision.HIGHEST
-        )
+        return pick_lanes(values, shift[:size_z]) + pick_lanes(wrapped, shift[size_z:])
 
     lower = along_z(lower_z, rows[4 * count_r : 5 * count_r])
     upper = along_z(upper_z, rows[5 * count_r :])

time: 177 us -> 135 us (0.76)
  matrix products: 66.4 us -> 29.7 us
  waiting for transfers between devices: 33.1 us -> 13.3 us
  starting transfers between devices: 45.4 us -> 63.1 us
  local copies, waits for them, and re-layouts: 14.7 us -> 12.4 us
    dot_general x80, matrix products: 60.9 us -> 24.4 us  [the longest x64 15.1 us: pick_lanes(): out = jnp.dot(stacked, shift, preferred_element_type=jnp.float32)]
    ppermute x32, waiting for transfers between devices: 33.1 us -> 13.3 us  [shifted(): lax.ppermute(shard, axis, [(i, (i + by) % peers) for i in range(peers)])]
    ppermute x32, starting transfers between devices: 45.4 us -> 63.1 us  [shifted(): lax.ppermute(shard, axis, [(i, (i + by) % peers) for i in range(peers)])]
    convert_element_type x0 -> x37, other arithmetic: none -> 2.7 us  [split3(): pieces.append(piece.astype(jnp.bfloat16))]
    add x6, other arithmetic: 2.2 us -> 0.02 us  [lane_shift(): inner = jnp.where(lanes_in == lanes_out + sign, 1.0, 0.0)]
  transfers between devices with their start and end apart: 32 -> 32, of which waited for: 8 -> 12; matrix products, arithmetic and copies ran while one was open for 8% -> 6% of each run, Pallas kernels for 0% -> 0%
where the time goes in v6:
time: 135 us; the launch traced here: 134 us
  starting transfers between devices  63.1 us (47%)
  matrix products  29.7 us (22%)
  other arithmetic  13.5 us (10%)
  waiting for transfers between devices  13.3 us (10%)
  local copies, waits for them, and re-layouts  12.4 us (9%)
  between operations  2.44 us (2%)
    ppermute x32, starting transfers between devices, shifted(): lax.ppermute(shard, axis, [(i, (i + by) % peers) for i in range(peers)])  63.1 us
    dot_general x64, matrix products, pick_lanes(): out = jnp.dot(stacked, shift, preferred_element_type=jnp.float32)  15.1 us
    ppermute x32, waiting for transfers between devices, shifted(): lax.ppermute(shard, axis, [(i, (i + by) % peers) for i in range(peers)])  13.3 us
    dot_general x16, matrix products, pick_rows(): out = jnp.dot(picker, joined, preferred_element_type=jnp.float32)  9.34 us
    squeeze x1, other arithmetic, shards(): values = guess[0]  6.17 us
    squeeze x16, local copies, waits for them, and re-layouts, pick(): return [face[number] for face in faces]  2.89 us
  transfers between devices with their start and end apart: 32, of which 12 were waited for; matrix products, arithmetic and copies ran while one was open for 6% of the time, Pallas kernels for 0%

profile of v6, /device:TPU:0, one launch (start us, length us, event | category | flops | bytes accessed | tf_op | source)
XLA Modules:
  0.0 134.4 jit_solution(5187291812937978539)
XLA Ops:
  0.6 1.6 %fusion.1650 = (f32[1]{0:T(128)}, f32[1]{0:T(128)}, f32[1]{0:T(128)}, f32[1]{0:T(128)}, f32[1]{0:T(128)}, /*index=5*/f32[1]{0:T(128)}, f32[1]{0:T(128)}, f32[1]{0:T(128)}) fusion(f32[8]{0:T(128)} %param.6), kind=kLoop, calls=%fused_computation.2357 | loop fusion | bytes 64 | tf_op jit(solution)/shard_map/slice | solution.py:383
  2.3 6.2 %copy_bitcast_fusion.3 = (f32[16,16,128]{2,0,1:T(8,128)S(1)}, f32[1,16,16,128]{3,1,2,0:T(8,128)S(1)}, f32[1,16,16,128]{3,1,2,0:T(8,128)S(1)}) fusion(f32[1,16,16,128]{3,2,1,0:T(8,128)} %param.9, f32[]{:T(128)} %bitcast.10, f32[]{:T(128)} %bitcast.9, f32[]{:T(128)} %bitcast.8, f32[]{:T(128)} %bitcast.7, f32[]{:T(128)} %bitcast.6, f32[]{:T(128)} %bitcast.5, ...), kind=kLoop, calls=%fused_computation.2319 | loop fusion | flops 753664 | bytes 655392 | tf_op jit(solution)/shard_map/squeeze | solution.py:404
  8.5 4.1 %collective-permute-start = (f32[2,2,16,128]{3,1,2,0:T(2,128)S(1)}, f32[2,2,16,128]{3,1,2,0:T(2,128)S(1)}, u32[]{:S(2)}, u32[]{:S(2)}) collective-permute-start(f32[2,2,16,128]{3,1,2,0:T(2,128)S(1)} %fusion.410), channel_id=1, source_target_pairs={{0,4},{1,5},{2,6},{3,7},{4,0},{5,1},{6,2},{7,3},{8,12},{9,13},{10,... | collective-permute-start | bytes 98312 | tf_op jit(solution)/shard_map/ppermute | solution.py:16
  12.6 1.6 %collective-permute-start.1 = (f32[2,16,1,128]{3,1,2,0:T(8,128)S(1)}, f32[2,16,1,128]{3,1,2,0:T(8,128)}, u32[]{:S(2)}, u32[]{:S(2)}) collective-permute-start(f32[2,16,1,128]{3,1,2,0:T(8,128)S(1)} %get-tuple-element.110), channel_id=1, source_target_pairs={{0,2},{1,3},{2,4},{3,5},{4,6},{5,7},{6,0},{7,1},{8,10},{9,11},{10,... | collective-permute-start | bytes 49160 | tf_op jit(solution)/shard_map/ppermute | solution.py:16
  14.2 2.2 %collective-permute-start.2 = (f32[2,16,1,128]{3,1,2,0:T(8,128)S(1)}, f32[2,16,1,128]{3,1,2,0:T(8,128)S(1)}, u32[]{:S(2)}, u32[]{:S(2)}) collective-permute-start(f32[2,16,1,128]{3,1,2,0:T(8,128)S(1)} %get-tuple-element.109), channel_id=1, source_target_pairs={{0,6},{1,7},{2,0},{3,1},{4,2},{5,3},{6,4},{7,5},{8,14},{9,15},{10,... | collective-permute-start | bytes 49160 | tf_op jit(solution)/shard_map/ppermute | solution.py:16
  16.6 1.6 %collective-permute-start.3 = (f32[2,16,16,1]{3,1,2,0:T(8,128)S(1)}, f32[2,16,16,1]{3,1,2,0:T(8,128)S(1)}, u32[]{:S(2)}, u32[]{:S(2)}) collective-permute-start(f32[2,16,16,1]{3,1,2,0:T(8,128)S(1)} %get-tuple-element.108), channel_id=1, source_target_pairs={{0,1},{1,2},{2,3},{3,4},{4,5},{5,6},{6,7},{7,0},{8,9},{9,10},{10,1... | collective-permute-start | bytes 6152 | tf_op jit(solution)/shard_map/ppermute | solution.py:16
  18.1 3.2 %collective-permute-start.4 = (f32[2,16,16,1]{3,1,2,0:T(8,128)S(1)}, f32[2,16,16,1]{3,1,2,0:T(8,128)S(1)}, u32[]{:S(2)}, u32[]{:S(2)}) collective-permute-start(f32[2,16,16,1]{3,1,2,0:T(8,128)S(1)} %get-tuple-element.107), channel_id=1, source_target_pairs={{0,7},{1,0},{2,1},{3,2},{4,3},{5,4},{6,5},{7,6},{8,15},{9,8},{10,9... | collective-permute-start | bytes 6152 | tf_op jit(solution)/shard_map/ppermute | solution.py:16
  21.9 0.5 and_select_fusion.9
  22.7 0.6 pad_clamp_fusion
  24.3 4.2 %collective-permute-done.3 = f32[2,16,16,1]{3,1,2,0:T(8,128)S(1)} collective-permute-done((f32[2,16,16,1]{3,1,2,0:T(8,128)S(1)}, f32[2,16,16,1]{3,1,2,0:T(8,128)S(1)}, u32[]{:S(2)}, u32[]{:S(2)}) %collective-permute-start.3) | collective-permute-done | bytes 2080 | tf_op jit(solution)/shard_map/ppermute | solution.py:16
  28.5 2.2 %collective-permute-done.4 = f32[2,16,16,1]{3,1,2,0:T(8,128)S(1)} collective-permute-done((f32[2,16,16,1]{3,1,2,0:T(8,128)S(1)}, f32[2,16,16,1]{3,1,2,0:T(8,128)S(1)}, u32[]{:S(2)}, u32[]{:S(2)}) %collective-permute-start.4) | collective-permute-done | bytes 2080 | tf_op jit(solution)/shard_map/ppermute | solution.py:16
  32.1 0.7 slice_bitcast_fusion.9
  34.1 4.4 %collective-permute-start.9 = (f32[1,16,16,1]{3,2,1,0:T(8,128)S(1)}, f32[1,16,16,1]{3,2,1,0:T(8,128)S(1)}, u32[]{:S(2)}, u32[]{:S(2)}) collective-permute-start(f32[1,16,16,1]{3,2,1,0:T(8,128)S(1)} %get-tuple-element.164), channel_id=1, source_target_pairs={{0,7},{1,0},{2,1},{3,2},{4,3},{5,4},{6,5},{7,6},{8,15},{9,8},{10,9... | collective-permute-start | bytes 3080 | tf_op jit(solution)/shard_map/ppermute | solution.py:16
  38.6 3.8 %collective-permute-start.7 = (f32[1,16,1,128]{3,1,2,0:T(8,128)S(1)}, f32[1,16,1,128]{3,1,2,0:T(8,128)S(1)}, u32[]{:S(2)}, u32[]{:S(2)}) collective-permute-start(f32[1,16,1,128]{3,1,2,0:T(8,128)S(1)} %bitcast.276), channel_id=1, source_target_pairs={{0,6},{1,7},{2,0},{3,1},{4,2},{5,3},{6,4},{7,5},{8,14},{9,15},{10,... | collective-permute-start | bytes 24584 | tf_op jit(solution)/shard_map/ppermute | solution.py:16
  43.1 1.0 collective-permute-done.6
  44.6 0.7 collective-permute-start.10
  45.4 0.7 collective-permute-start.13
  46.0 4.1 %collective-permute-start.14 = (f32[1,16,16,1]{3,2,1,0:T(8,128)S(1)}, f32[1,16,16,1]{3,2,1,0:T(8,128)S(1)}, u32[]{:S(2)}, u32[]{:S(2)}) collective-permute-start(f32[1,16,16,1]{3,2,1,0:T(8,128)S(1)} %get-tuple-element.152), channel_id=1, source_target_pairs={{0,7},{1,0},{2,1},{3,2},{4,3},{5,4},{6,5},{7,6},{8,15},{9,8},{10,9... | collective-permute-start | bytes 3080 | tf_op jit(solution)/shard_map/ppermute | solution.py:16
  50.1 2.0 %collective-permute-start.11 = (f32[1,16,1,128]{3,1,2,0:T(8,128)S(1)}, f32[1,16,1,128]{3,1,2,0:T(8,128)S(1)}, u32[]{:S(2)}, u32[]{:S(2)}) collective-permute-start(f32[1,16,1,128]{3,1,2,0:T(8,128)S(1)} %bitcast.280), channel_id=1, source_target_pairs={{0,2},{1,3},{2,4},{3,5},{4,6},{5,7},{6,0},{7,1},{8,10},{9,11},{10,... | collective-permute-start | bytes 24584 | tf_op jit(solution)/shard_map/ppermute | solution.py:16
  52.1 1.9 %collective-permute-start.12 = (f32[1,16,1,128]{3,1,2,0:T(8,128)S(1)}, f32[1,16,1,128]{3,1,2,0:T(8,128)S(1)}, u32[]{:S(2)}, u32[]{:S(2)}) collective-permute-start(f32[1,16,1,128]{3,1,2,0:T(8,128)S(1)} %bitcast.279), channel_id=1, source_target_pairs={{0,6},{1,7},{2,0},{3,1},{4,2},{5,3},{6,4},{7,5},{8,14},{9,15},{10,... | collective-permute-start | bytes 24584 | tf_op jit(solution)/shard_map/ppermute | solution.py:16
  54.7 0.9 collective-permute-done.11
  56.6 1.1 collective-permute-start.15
  57.8 4.6 %collective-permute-start.17 = (f32[2,8,8,64]{3,2,1,0:T(8,128)S(1)}, f32[2,8,8,64]{3,2,1,0:T(8,128)S(1)}, u32[]{:S(2)}, u32[]{:S(2)}) collective-permute-start(f32[2,8,8,64]{3,2,1,0:T(8,128)S(1)} %pad_maximum_fusion.16), channel_id=1, source_target_pairs={{0,3},{1,4},{2,5},{3,6},{4,7},{5,0},{6,1},{7,2},{8,11},{9,12},{10,... | collective-permute-start | bytes 98312 | tf_op jit(solution)/shard_map/ppermute | solution.py:16
  62.5 2.9 %collective-permute-start.19 = (f32[2,8,8,64]{3,2,1,0:T(8,128)S(1)}, f32[2,8,8,64]{3,2,1,0:T(8,128)S(1)}, u32[]{:S(2)}, u32[]{:S(2)}) collective-permute-start(f32[2,8,8,64]{3,2,1,0:T(8,128)S(1)} %pad_maximum_fusion.16), channel_id=1, source_target_pairs={{0,5},{1,6},{2,7},{3,0},{4,1},{5,2},{6,3},{7,4},{8,13},{9,14},{10,... | collective-permute-start | bytes 98312 | tf_op jit(solution)/shard_map/ppermute | solution.py:16
  65.4 0.8 collective-permute-start.20
  66.2 1.8 %collective-permute-start.21 = (f32[2,8,8,64]{3,2,1,0:T(8,128)S(1)}, f32[2,8,8,64]{3,2,1,0:T(8,128)S(1)}, u32[]{:S(2)}, u32[]{:S(2)}) collective-permute-start(f32[2,8,8,64]{3,2,1,0:T(8,128)S(1)} %pad_maximum_fusion.16), channel_id=1, source_target_pairs={{0,7},{1,0},{2,1},{3,2},{4,3},{5,4},{6,5},{7,6},{8,15},{9,8},{10,9... | collective-permute-start | bytes 98312 | tf_op jit(solution)/shard_map/ppermute | solution.py:16
  68.0 0.6 collective-permute-done.18
  68.6 1.4 %collective-permute-done.20 = f32[2,8,8,64]{3,2,1,0:T(8,128)S(1)} collective-permute-done((f32[2,8,8,64]{3,2,1,0:T(8,128)S(1)}, f32[2,8,8,64]{3,2,1,0:T(8,128)S(1)}, u32[]{:S(2)}, u32[]{:S(2)}) %collective-permute-start.20) | collective-permute-done | bytes 32800 | tf_op jit(solution)/shard_map/ppermute | solution.py:16
  70.0 0.8 collective-permute-done.21
  70.8 0.7 gather_fusion
  72.0 1.4 %fusion.4 = f32[3072,192]{0,1:T(8,128)S(1)} fusion(s32[3072]{0:T(1024)S(1)} %constant_dynamic-update-slice_fusion.4, bf16[512,64]{1,0:T(8,128)(2,1)S(1)} %get-tuple-element.102, bf16[512,64]{1,0:T(8,128)(2,1)S(1)} %get-tuple-element.101, bf16[512,64]{1,0:T(8,128)(2,1)S(1)} %get-tuple-element.100), kind=kOutput, calls=%fused_computation.7 | convolution fusion | flops 609288192 | bytes 2568192 | tf_op jit(solution)/shard_map/dot_general | solution.py:273
  75.2 1.3 fusion.3
  78.2 1.3 fusion.2
  97.7 0.5 reduce-precision_convert_fusion.13
  98.2 1.3 fusion.1
  101.4 1.3 fusion
  107.9 1.3 collective-permute-start.22
  109.2 1.8 %collective-permute-start.25 = (f32[1,16,16,1]{3,2,1,0:T(8,128)S(1)}, f32[1,16,16,1]{3,2,1,0:T(8,128)S(1)}, u32[]{:S(2)}, u32[]{:S(2)}) collective-permute-start(f32[1,16,16,1]{3,2,1,0:T(8,128)S(1)} %get-tuple-element.126), channel_id=1, source_target_pairs={{0,1},{1,2},{2,3},{3,4},{4,5},{5,6},{6,7},{7,0},{8,9},{9,10},{10,1... | collective-permute-start | bytes 3080 | tf_op jit(solution)/shard_map/ppermute | solution.py:16
  111.0 3.0 %collective-permute-start.26 = (f32[1,16,16,1]{3,2,1,0:T(8,128)S(1)}, f32[1,16,16,1]{3,2,1,0:T(8,128)S(1)}, u32[]{:S(2)}, u32[]{:S(2)}) collective-permute-start(f32[1,16,16,1]{3,2,1,0:T(8,128)S(1)} %get-tuple-element.125), channel_id=1, source_target_pairs={{0,7},{1,0},{2,1},{3,2},{4,3},{5,4},{6,5},{7,6},{8,15},{9,8},{10,9... | collective-permute-start | bytes 3080 | tf_op jit(solution)/shard_map/ppermute | solution.py:16
  114.0 3.8 %collective-permute-start.24 = (f32[1,16,1,128]{3,1,2,0:T(8,128)S(1)}, f32[1,16,1,128]{3,1,2,0:T(8,128)S(1)}, u32[]{:S(2)}, u32[]{:S(2)}) collective-permute-start(f32[1,16,1,128]{3,1,2,0:T(8,128)S(1)} %bitcast.275), channel_id=1, source_target_pairs={{0,6},{1,7},{2,0},{3,1},{4,2},{5,3},{6,4},{7,5},{8,14},{9,15},{10,... | collective-permute-start | bytes 24584 | tf_op jit(solution)/shard_map/ppermute | solution.py:16
  119.0 0.6 collective-permute-done.23
  120.1 2.6 %collective-permute-start.27 = (f32[1,2,16,128]{3,1,2,0:T(2,128)S(1)}, f32[1,2,16,128]{3,1,2,0:T(2,128)S(1)}, u32[]{:S(2)}, u32[]{:S(2)}) collective-permute-start(f32[1,2,16,128]{3,1,2,0:T(2,128)S(1)} %pad_maximum_fusion.29), channel_id=1, source_target_pairs={{0,4},{1,5},{2,6},{3,7},{4,0},{5,1},{6,2},{7,3},{8,12},{9,13},{10,... | collective-permute-start | bytes 49160 | tf_op jit(solution)/shard_map/ppermute | solution.py:16
  122.7 1.3 collective-permute-start.30
  124.0 3.4 %collective-permute-start.31 = (f32[1,16,16,1]{3,1,2,0:T(8,128)S(1)}, f32[1,16,16,1]{3,1,2,0:T(8,128)S(1)}, u32[]{:S(2)}, u32[]{:S(2)}) collective-permute-start(f32[1,16,16,1]{3,1,2,0:T(8,128)S(1)} %get-tuple-element.113), channel_id=1, source_target_pairs={{0,7},{1,0},{2,1},{3,2},{4,3},{5,4},{6,5},{7,6},{8,15},{9,8},{10,9... | collective-permute-start | bytes 3080 | tf_op jit(solution)/shard_map/ppermute | solution.py:16
  127.4 0.7 copy.572
  128.1 3.8 %collective-permute-start.29 = (f32[1,16,1,128]{3,1,2,0:T(8,128)S(1)}, f32[1,16,1,128]{3,1,2,0:T(8,128)S(1)}, u32[]{:S(2)}, u32[]{:S(2)}) collective-permute-start(f32[1,16,1,128]{3,1,2,0:T(8,128)S(1)} %get-tuple-element.117), channel_id=1, source_target_pairs={{0,6},{1,7},{2,0},{3,1},{4,2},{5,3},{6,4},{7,5},{8,14},{9,15},{10,... | collective-permute-start | bytes 24584 | tf_op jit(solution)/shard_map/ppermute | solution.py:16
  132.7 0.9 collective-permute-done.28
  133.7 0.7 copy.573
  (365 shorter events, 38.3 us)
Async XLA Ops:
  8.5 24.4 %collective-permute-start = (f32[2,2,16,128]{3,1,2,0:T(2,128)S(1)}, f32[2,2,16,128]{3,1,2,0:T(2,128)S(1)}, u32[]{:S(2)}, u32[]{:S(2)}) collective-permute-start(f32[2,2,16,128]{3,1,2,0:T(2,128)S(1)} %fusion.410), channel_id=1, source_target_pairs={{0,4},{1,5},{2,6},{3,7},{4,0},{5,1},{6,2},{7,3},{8,12},{9,13},{10,... | collective-permute-start | bytes 98312 | tf_op jit(solution)/shard_map/ppermute | solution.py:16
  12.6 19.5 %collective-permute-start.1 = (f32[2,16,1,128]{3,1,2,0:T(8,128)S(1)}, f32[2,16,1,128]{3,1,2,0:T(8,128)}, u32[]{:S(2)}, u32[]{:S(2)}) collective-permute-start(f32[2,16,1,128]{3,1,2,0:T(8,128)S(1)} %get-tuple-element.110), channel_id=1, source_target_pairs={{0,2},{1,3},{2,4},{3,5},{4,6},{5,7},{6,0},{7,1},{8,10},{9,11},{10,... | collective-permute-start | bytes 49160 | tf_op jit(solution)/shard_map/ppermute | solution.py:16
  14.2 9.9 %copy-start.6 = (s32[16]{0:T(128)S(1)}, s32[16]{0:T(128)}, u32[]{:S(2)}) copy-start(s32[16]{0:T(128)} %param.7) | copy-start | bytes 196
  14.2 10.0 %copy-start.7 = (f32[16]{0:T(128)S(1)}, f32[16]{0:T(128)}, u32[]{:S(2)}) copy-start(f32[16]{0:T(128)} %param.8) | copy-start | bytes 196
  14.2 18.7 %collective-permute-start.2 = (f32[2,16,1,128]{3,1,2,0:T(8,128)S(1)}, f32[2,16,1,128]{3,1,2,0:T(8,128)S(1)}, u32[]{:S(2)}, u32[]{:S(2)}) collective-permute-start(f32[2,16,1,128]{3,1,2,0:T(8,128)S(1)} %get-tuple-element.109), channel_id=1, source_target_pairs={{0,6},{1,7},{2,0},{3,1},{4,2},{5,3},{6,4},{7,5},{8,14},{9,15},{10,... | collective-permute-start | bytes 49160 | tf_op jit(solution)/shard_map/ppermute | solution.py:16
  16.6 11.9 %collective-permute-start.3 = (f32[2,16,16,1]{3,1,2,0:T(8,128)S(1)}, f32[2,16,16,1]{3,1,2,0:T(8,128)S(1)}, u32[]{:S(2)}, u32[]{:S(2)}) collective-permute-start(f32[2,16,16,1]{3,1,2,0:T(8,128)S(1)} %get-tuple-element.108), channel_id=1, source_target_pairs={{0,1},{1,2},{2,3},{3,4},{4,5},{5,6},{6,7},{7,0},{8,9},{9,10},{10,1... | collective-permute-start | bytes 6152 | tf_op jit(solution)/shard_map/ppermute | solution.py:16
  18.1 12.5 %collective-permute-start.4 = (f32[2,16,16,1]{3,1,2,0:T(8,128)S(1)}, f32[2,16,16,1]{3,1,2,0:T(8,128)S(1)}, u32[]{:S(2)}, u32[]{:S(2)}) collective-permute-start(f32[2,16,16,1]{3,1,2,0:T(8,128)S(1)} %get-tuple-element.107), channel_id=1, source_target_pairs={{0,7},{1,0},{2,1},{3,2},{4,3},{5,4},{6,5},{7,6},{8,15},{9,8},{10,9... | collective-permute-start | bytes 6152 | tf_op jit(solution)/shard_map/ppermute | solution.py:16
  21.5 11.4 %copy-start = (f32[1,16,16,128]{3,2,1,0:T(8,128)S(1)}, f32[1,16,16,128]{3,2,1,0:T(8,128)}, u32[]{:S(2)}) copy-start(f32[1,16,16,128]{3,2,1,0:T(8,128)} %param.9) | copy-start | bytes 393220
  21.7 2.4 %copy-start.1 = (s32[256]{0:T(256)}, s32[256]{0:T(256)S(1)}, u32[]{:S(2)}) copy-start(s32[256]{0:T(256)S(1)} %fusion.1266) | copy-start | bytes 3076
  22.7 1.5 %copy-start.3 = (s32[128]{0:T(128)}, s32[128]{0:T(128)S(1)}, u32[]{:S(2)}) copy-start(s32[128]{0:T(128)S(1)} %get-tuple-element.319) | copy-start | bytes 1540
  33.7 9.3 %collective-permute-start.5 = (f32[1,2,16,128]{3,2,1,0:T(8,128)S(1)}, f32[1,2,16,128]{3,2,1,0:T(8,128)S(1)}, u32[]{:S(2)}, u32[]{:S(2)}) collective-permute-start(f32[1,2,16,128]{3,2,1,0:T(8,128)S(1)} %pad_maximum_fusion.26), channel_id=1, source_target_pairs={{0,4},{1,5},{2,6},{3,7},{4,0},{5,1},{6,2},{7,3},{8,12},{9,13},{10,... | collective-permute-start | bytes 49160 | tf_op jit(solution)/shard_map/ppermute | solution.py:16
  33.8 8.7 %collective-permute-start.8 = (f32[1,16,16,1]{3,2,1,0:T(8,128)S(1)}, f32[1,16,16,1]{3,2,1,0:T(8,128)S(1)}, u32[]{:S(2)}, u32[]{:S(2)}) collective-permute-start(f32[1,16,16,1]{3,2,1,0:T(8,128)S(1)} %get-tuple-element.165), channel_id=1, source_target_pairs={{0,1},{1,2},{2,3},{3,4},{4,5},{5,6},{6,7},{7,0},{8,9},{9,10},{10,1... | collective-permute-start | bytes 3080 | tf_op jit(solution)/shard_map/ppermute | solution.py:16
  34.1 8.6 %collective-permute-start.9 = (f32[1,16,16,1]{3,2,1,0:T(8,128)S(1)}, f32[1,16,16,1]{3,2,1,0:T(8,128)S(1)}, u32[]{:S(2)}, u32[]{:S(2)}) collective-permute-start(f32[1,16,16,1]{3,2,1,0:T(8,128)S(1)} %get-tuple-element.164), channel_id=1, source_target_pairs={{0,7},{1,0},{2,1},{3,2},{4,3},{5,4},{6,5},{7,6},{8,15},{9,8},{10,9... | collective-permute-start | bytes 3080 | tf_op jit(solution)/shard_map/ppermute | solution.py:16
  38.6 5.5 %collective-permute-start.6 = (f32[1,16,1,128]{3,1,2,0:T(8,128)S(1)}, f32[1,16,1,128]{3,1,2,0:T(8,128)S(1)}, u32[]{:S(2)}, u32[]{:S(2)}) collective-permute-start(f32[1,16,1,128]{3,1,2,0:T(8,128)S(1)} %bitcast.278), channel_id=1, source_target_pairs={{0,2},{1,3},{2,4},{3,5},{4,6},{5,7},{6,0},{7,1},{8,10},{9,11},{10,... | collective-permute-start | bytes 24584 | tf_op jit(solution)/shard_map/ppermute | solution.py:16
  38.6 5.4 %collective-permute-start.7 = (f32[1,16,1,128]{3,1,2,0:T(8,128)S(1)}, f32[1,16,1,128]{3,1,2,0:T(8,128)S(1)}, u32[]{:S(2)}, u32[]{:S(2)}) collective-permute-start(f32[1,16,1,128]{3,1,2,0:T(8,128)S(1)} %bitcast.276), channel_id=1, source_target_pairs={{0,6},{1,7},{2,0},{3,1},{4,2},{5,3},{6,4},{7,5},{8,14},{9,15},{10,... | collective-permute-start | bytes 24584 | tf_op jit(solution)/shard_map/ppermute | solution.py:16
  44.4 11.6 %copy-start.4 = (s32[128]{0:T(128)S(1)}, s32[128]{0:T(128)}, u32[]{:S(2)}) copy-start(s32[128]{0:T(128)} %copy-done.3) | copy-start | bytes 1540
  44.4 12.0 %copy-start.2 = (s32[256]{0:T(256)S(1)}, s32[256]{0:T(256)}, u32[]{:S(2)}) copy-start(s32[256]{0:T(256)} %copy-done.1) | copy-start | bytes 3076
  44.6 10.1 %collective-permute-start.10 = (f32[1,2,16,128]{3,2,1,0:T(8,128)S(1)}, f32[1,2,16,128]{3,2,1,0:T(8,128)S(1)}, u32[]{:S(2)}, u32[]{:S(2)}) collective-permute-start(f32[1,2,16,128]{3,2,1,0:T(8,128)S(1)} %pad_maximum_fusion.27), channel_id=1, source_target_pairs={{0,4},{1,5},{2,6},{3,7},{4,0},{5,1},{6,2},{7,3},{8,12},{9,13},{10,... | collective-permute-start | bytes 49160 | tf_op jit(solution)/shard_map/ppermute | solution.py:16
  45.4 8.6 %collective-permute-start.13 = (f32[1,16,16,1]{3,2,1,0:T(8,128)S(1)}, f32[1,16,16,1]{3,2,1,0:T(8,128)S(1)}, u32[]{:S(2)}, u32[]{:S(2)}) collective-permute-start(f32[1,16,16,1]{3,2,1,0:T(8,128)S(1)} %get-tuple-element.153), channel_id=1, source_target_pairs={{0,1},{1,2},{2,3},{3,4},{4,5},{5,6},{6,7},{7,0},{8,9},{9,10},{10,1... | collective-permute-start | bytes 3080 | tf_op jit(solution)/shard_map/ppermute | solution.py:16
  46.0 8.4 %collective-permute-start.14 = (f32[1,16,16,1]{3,2,1,0:T(8,128)S(1)}, f32[1,16,16,1]{3,2,1,0:T(8,128)S(1)}, u32[]{:S(2)}, u32[]{:S(2)}) collective-permute-start(f32[1,16,16,1]{3,2,1,0:T(8,128)S(1)} %get-tuple-element.152), channel_id=1, source_target_pairs={{0,7},{1,0},{2,1},{3,2},{4,3},{5,4},{6,5},{7,6},{8,15},{9,8},{10,9... | collective-permute-start | bytes 3080 | tf_op jit(solution)/shard_map/ppermute | solution.py:16
  50.1 5.5 %collective-permute-start.11 = (f32[1,16,1,128]{3,1,2,0:T(8,128)S(1)}, f32[1,16,1,128]{3,1,2,0:T(8,128)S(1)}, u32[]{:S(2)}, u32[]{:S(2)}) collective-permute-start(f32[1,16,1,128]{3,1,2,0:T(8,128)S(1)} %bitcast.280), channel_id=1, source_target_pairs={{0,2},{1,3},{2,4},{3,5},{4,6},{5,7},{6,0},{7,1},{8,10},{9,11},{10,... | collective-permute-start | bytes 24584 | tf_op jit(solution)/shard_map/ppermute | solution.py:16
  52.1 3.7 %collective-permute-start.12 = (f32[1,16,1,128]{3,1,2,0:T(8,128)S(1)}, f32[1,16,1,128]{3,1,2,0:T(8,128)S(1)}, u32[]{:S(2)}, u32[]{:S(2)}) collective-permute-start(f32[1,16,1,128]{3,1,2,0:T(8,128)S(1)} %bitcast.279), channel_id=1, source_target_pairs={{0,6},{1,7},{2,0},{3,1},{4,2},{5,3},{6,4},{7,5},{8,14},{9,15},{10,... | collective-permute-start | bytes 24584 | tf_op jit(solution)/shard_map/ppermute | solution.py:16
  56.6 8.8 %collective-permute-start.15 = (f32[2,8,8,64]{3,2,1,0:T(8,128)S(1)}, f32[2,8,8,64]{3,2,1,0:T(8,128)S(1)}, u32[]{:S(2)}, u32[]{:S(2)}) collective-permute-start(f32[2,8,8,64]{3,2,1,0:T(8,128)S(1)} %pad_maximum_fusion.16), channel_id=1, source_target_pairs={{0,1},{1,2},{2,3},{3,4},{4,5},{5,6},{6,7},{7,0},{8,9},{9,10},{10,1... | collective-permute-start | bytes 98312 | tf_op jit(solution)/shard_map/ppermute | solution.py:16
  57.8 8.4 %collective-permute-start.16 = (f32[2,8,8,64]{3,2,1,0:T(8,128)S(1)}, f32[2,8,8,64]{3,2,1,0:T(8,128)S(1)}, u32[]{:S(2)}, u32[]{:S(2)}) collective-permute-start(f32[2,8,8,64]{3,2,1,0:T(8,128)S(1)} %pad_maximum_fusion.16), channel_id=1, source_target_pairs={{0,2},{1,3},{2,4},{3,5},{4,6},{5,7},{6,0},{7,1},{8,10},{9,11},{10,... | collective-permute-start | bytes 98312 | tf_op jit(solution)/shard_map/ppermute | solution.py:16
  57.8 10.2 %collective-permute-start.17 = (f32[2,8,8,64]{3,2,1,0:T(8,128)S(1)}, f32[2,8,8,64]{3,2,1,0:T(8,128)S(1)}, u32[]{:S(2)}, u32[]{:S(2)}) collective-permute-start(f32[2,8,8,64]{3,2,1,0:T(8,128)S(1)} %pad_maximum_fusion.16), channel_id=1, source_target_pairs={{0,3},{1,4},{2,5},{3,6},{4,7},{5,0},{6,1},{7,2},{8,11},{9,12},{10,... | collective-permute-start | bytes 98312 | tf_op jit(solution)/shard_map/ppermute | solution.py:16
  62.5 6.1 %collective-permute-start.18 = (f32[2,8,8,64]{3,2,1,0:T(8,128)S(1)}, f32[2,8,8,64]{3,2,1,0:T(8,128)S(1)}, u32[]{:S(2)}, u32[]{:S(2)}) collective-permute-start(f32[2,8,8,64]{3,2,1,0:T(8,128)S(1)} %pad_maximum_fusion.16), channel_id=1, source_target_pairs={{0,4},{1,5},{2,6},{3,7},{4,0},{5,1},{6,2},{7,3},{8,12},{9,13},{10,... | collective-permute-start | bytes 98312 | tf_op jit(solution)/shard_map/ppermute | solution.py:16
  62.5 6.1 %collective-permute-start.19 = (f32[2,8,8,64]{3,2,1,0:T(8,128)S(1)}, f32[2,8,8,64]{3,2,1,0:T(8,128)S(1)}, u32[]{:S(2)}, u32[]{:S(2)}) collective-permute-start(f32[2,8,8,64]{3,2,1,0:T(8,128)S(1)} %pad_maximum_fusion.16), channel_id=1, source_target_pairs={{0,5},{1,6},{2,7},{3,0},{4,1},{5,2},{6,3},{7,4},{8,13},{9,14},{10,... | collective-permute-start | bytes 98312 | tf_op jit(solution)/shard_map/ppermute | solution.py:16
  65.4 4.6 %collective-permute-start.20 = (f32[2,8,8,64]{3,2,1,0:T(8,128)S(1)}, f32[2,8,8,64]{3,2,1,0:T(8,128)S(1)}, u32[]{:S(2)}, u32[]{:S(2)}) collective-permute-start(f32[2,8,8,64]{3,2,1,0:T(8,128)S(1)} %pad_maximum_fusion.16), channel_id=1, source_target_pairs={{0,6},{1,7},{2,0},{3,1},{4,2},{5,3},{6,4},{7,5},{8,14},{9,15},{10,... | collective-permute-start | bytes 98312 | tf_op jit(solution)/shard_map/ppermute | solution.py:16
  66.2 4.6 %collective-permute-start.21 = (f32[2,8,8,64]{3,2,1,0:T(8,128)S(1)}, f32[2,8,8,64]{3,2,1,0:T(8,128)S(1)}, u32[]{:S(2)}, u32[]{:S(2)}) collective-permute-start(f32[2,8,8,64]{3,2,1,0:T(8,128)S(1)} %pad_maximum_fusion.16), channel_id=1, source_target_pairs={{0,7},{1,0},{2,1},{3,2},{4,3},{5,4},{6,5},{7,6},{8,15},{9,8},{10,9... | collective-permute-start | bytes 98312 | tf_op jit(solution)/shard_map/ppermute | solution.py:16
  82.9 2.9 %copy-start.5 = (s32[32]{0:T(128)S(1)}, s32[32]{0:T(128)}, u32[]{:S(2)}) copy-start(s32[32]{0:T(128)} %get-tuple-element.320) | copy-start | bytes 388
  107.9 11.0 %collective-permute-start.22 = (f32[1,2,16,128]{3,2,1,0:T(8,128)S(1)}, f32[1,2,16,128]{3,2,1,0:T(8,128)S(1)}, u32[]{:S(2)}, u32[]{:S(2)}) collective-permute-start(f32[1,2,16,128]{3,2,1,0:T(8,128)S(1)} %pad_maximum_fusion.28), channel_id=1, source_target_pairs={{0,4},{1,5},{2,6},{3,7},{4,0},{5,1},{6,2},{7,3},{8,12},{9,13},{10,... | collective-permute-start | bytes 49160 | tf_op jit(solution)/shard_map/ppermute | solution.py:16
  109.2 8.6 %collective-permute-start.25 = (f32[1,16,16,1]{3,2,1,0:T(8,128)S(1)}, f32[1,16,16,1]{3,2,1,0:T(8,128)S(1)}, u32[]{:S(2)}, u32[]{:S(2)}) collective-permute-start(f32[1,16,16,1]{3,2,1,0:T(8,128)S(1)} %get-tuple-element.126), channel_id=1, source_target_pairs={{0,1},{1,2},{2,3},{3,4},{4,5},{5,6},{6,7},{7,0},{8,9},{9,10},{10,1... | collective-permute-start | bytes 3080 | tf_op jit(solution)/shard_map/ppermute | solution.py:16
  111.0 7.7 %collective-permute-start.26 = (f32[1,16,16,1]{3,2,1,0:T(8,128)S(1)}, f32[1,16,16,1]{3,2,1,0:T(8,128)S(1)}, u32[]{:S(2)}, u32[]{:S(2)}) collective-permute-start(f32[1,16,16,1]{3,2,1,0:T(8,128)S(1)} %get-tuple-element.125), channel_id=1, source_target_pairs={{0,7},{1,0},{2,1},{3,2},{4,3},{5,4},{6,5},{7,6},{8,15},{9,8},{10,9... | collective-permute-start | bytes 3080 | tf_op jit(solution)/shard_map/ppermute | solution.py:16
  114.0 5.6 %collective-permute-start.23 = (f32[1,16,1,128]{3,1,2,0:T(8,128)S(1)}, f32[1,16,1,128]{3,1,2,0:T(8,128)S(1)}, u32[]{:S(2)}, u32[]{:S(2)}) collective-permute-start(f32[1,16,1,128]{3,1,2,0:T(8,128)S(1)} %bitcast.277), channel_id=1, source_target_pairs={{0,2},{1,3},{2,4},{3,5},{4,6},{5,7},{6,0},{7,1},{8,10},{9,11},{10,... | collective-permute-start | bytes 24584 | tf_op jit(solution)/shard_map/ppermute | solution.py:16
  114.0 5.5 %collective-permute-start.24 = (f32[1,16,1,128]{3,1,2,0:T(8,128)S(1)}, f32[1,16,1,128]{3,1,2,0:T(8,128)S(1)}, u32[]{:S(2)}, u32[]{:S(2)}) collective-permute-start(f32[1,16,1,128]{3,1,2,0:T(8,128)S(1)} %bitcast.275), channel_id=1, source_target_pairs={{0,6},{1,7},{2,0},{3,1},{4,2},{5,3},{6,4},{7,5},{8,14},{9,15},{10,... | collective-permute-start | bytes 24584 | tf_op jit(solution)/shard_map/ppermute | solution.py:16
  120.1 12.6 %collective-permute-start.27 = (f32[1,2,16,128]{3,1,2,0:T(2,128)S(1)}, f32[1,2,16,128]{3,1,2,0:T(2,128)S(1)}, u32[]{:S(2)}, u32[]{:S(2)}) collective-permute-start(f32[1,2,16,128]{3,1,2,0:T(2,128)S(1)} %pad_maximum_fusion.29), channel_id=1, source_target_pairs={{0,4},{1,5},{2,6},{3,7},{4,0},{5,1},{6,2},{7,3},{8,12},{9,13},{10,... | collective-permute-start | bytes 49160 | tf_op jit(solution)/shard_map/ppermute | solution.py:16
  122.7 9.3 %collective-permute-start.30 = (f32[1,16,16,1]{3,1,2,0:T(8,128)S(1)}, f32[1,16,16,1]{3,1,2,0:T(8,128)S(1)}, u32[]{:S(2)}, u32[]{:S(2)}) collective-permute-start(f32[1,16,16,1]{3,1,2,0:T(8,128)S(1)} %get-tuple-element.114), channel_id=1, source_target_pairs={{0,1},{1,2},{2,3},{3,4},{4,5},{5,6},{6,7},{7,0},{8,9},{9,10},{10,1... | collective-permute-start | bytes 3080 | tf_op jit(solution)/shard_map/ppermute | solution.py:16
  124.0 8.3 %collective-permute-start.31 = (f32[1,16,16,1]{3,1,2,0:T(8,128)S(1)}, f32[1,16,16,1]{3,1,2,0:T(8,128)S(1)}, u32[]{:S(2)}, u32[]{:S(2)}) collective-permute-start(f32[1,16,16,1]{3,1,2,0:T(8,128)S(1)} %get-tuple-element.113), channel_id=1, source_target_pairs={{0,7},{1,0},{2,1},{3,2},{4,3},{5,4},{6,5},{7,6},{8,15},{9,8},{10,9... | collective-permute-start | bytes 3080 | tf_op jit(solution)/shard_map/ppermute | solution.py:16
  128.1 5.4 %collective-permute-start.28 = (f32[1,16,1,128]{3,1,2,0:T(8,128)S(1)}, f32[1,16,1,128]{3,1,2,0:T(8,128)S(1)}, u32[]{:S(2)}, u32[]{:S(2)}) collective-permute-start(f32[1,16,1,128]{3,1,2,0:T(8,128)S(1)} %get-tuple-element.118), channel_id=1, source_target_pairs={{0,2},{1,3},{2,4},{3,5},{4,6},{5,7},{6,0},{7,1},{8,10},{9,11},{10,... | collective-permute-start | bytes 24584 | tf_op jit(solution)/shard_map/ppermute | solution.py:16
  128.1 5.4 %collective-permute-start.29 = (f32[1,16,1,128]{3,1,2,0:T(8,128)S(1)}, f32[1,16,1,128]{3,1,2,0:T(8,128)S(1)}, u32[]{:S(2)}, u32[]{:S(2)}) collective-permute-start(f32[1,16,1,128]{3,1,2,0:T(8,128)S(1)} %get-tuple-element.117), channel_id=1, source_target_pairs={{0,6},{1,7},{2,0},{3,1},{4,2},{5,3},{6,4},{7,5},{8,14},{9,15},{10,... | collective-permute-start | bytes 24584 | tf_op jit(solution)/shard_map/ppermute | solution.py:16

commit v7 on v6

--- a/solution.py
+++ b/solution.py
@@ -19,16 +19,20 @@
 def exchange(fields, per_side):
     count_dev = lax.axis_size("space")
     plane_step = per_side * per_side
+
+    def stack(number):
+        return jnp.stack([own_faces(values)[number] for values in fields])
+
     if (2 * plane_step) % count_dev == 0:
-        both_x = shifted(jnp.concatenate([fields[:, -1:], fields[:, :1]], axis=1), "space", plane_step)
+        both_x = shifted(jnp.concatenate([stack(0), stack(1)], axis=1), "space", plane_step)
         lower_x, upper_x = both_x[:, :1], both_x[:, 1:]
     else:
-        lower_x = shifted(fields[:, -1:], "space", plane_step)
-        upper_x = shifted(fields[:, :1], "space", -plane_step)
-    lower_y = shifted(fields[:, :, -1:], "space", per_side)
-    upper_y = shifted(fields[:, :, :1], "space", -per_side)
-    lower_z = shifted(fields[:, :, :, -1:], "space", 1)
-    upper_z = shifted(fields[:, :, :, :1], "space", -1)
+        lower_x = shifted(stack(0), "space", plane_step)
+        upper_x = shifted(stack(1), "space", -plane_step)
+    lower_y = shifted(stack(2), "space", per_side)
+    upper_y = shifted(stack(3), "space", -per_side)
+    lower_z = shifted(stack(4), "space", 1)
+    upper_z = shifted(stack(5), "space", -1)
     return [lower_x, upper_x, lower_y, upper_y, lower_z, upper_z]
 
 
@@ -284,12 +288,12 @@
 def flat_faces(values, picker, lower_z, upper_z):
     count_r, size_z = values.shape
     rows = pick_rows(picker, values)
-
-    def along_z(shift, wrapped):
-        return pick_lanes(values, shift[:size_z]) + pick_lanes(wrapped, shift[size_z:])
-
-    lower = along_z(lower_z, rows[4 * count_r : 5 * count_r])
-    upper = along_z(upper_z, rows[5 * count_r :])
+    shifts = jnp.concatenate(
+        [lower_z[:size_z], upper_z[:size_z], lower_z[size_z:], upper_z[size_z:]], axis=1
+    )
+    out = pick_lanes(jnp.concatenate([values, rows[4 * count_r :]], axis=0), shifts)
+    lower = out[:count_r, :size_z] + out[count_r : 2 * count_r, 2 * size_z : 3 * size_z]
+    upper = out[:count_r, size_z : 2 * size_z] + out[2 * count_r :, 3 * size_z :]
     return [rows[k * count_r : (k + 1) * count_r] for k in range(4)] + [lower, upper]
 
 
@@ -403,13 +407,13 @@
 
     values = guess[0]
     if count_dev * (width_x // 2) * (width_y // 2) <= 512:
-        first = exchange(jnp.stack([permeab, values]), per_side)
+        first = exchange([permeab, values], per_side)
         face_coefs, diagonal = coefficients(permeab, with_faces(permeab, pick(first, 0)), 1.0)
         values = smooth(values, source, face_coefs, diagonal, 1.0, with_faces(values, pick(first, 1)))
         for sweep_no in range(SWEEPS - 1):
-            faces = pick(exchange(values[None], per_side), 0)
+            faces = pick(exchange([values], per_side), 0)
             values = smooth(values, source, face_coefs, diagonal, 1.0, with_faces(values, faces))
-        stored_faces = pick(exchange(values[None], per_side), 0)
+        stored_faces = pick(exchange([values], per_side), 0)
         leftover = source - operate(values, with_faces(values, stored_faces), face_coefs, 1.0)
         stored = values
 
@@ -424,9 +428,9 @@
         ]
         values = smooth(values, source, face_coefs, diagonal, 1.0, with_faces(values, faces))
         for sweep_no in range(SWEEPS - 1):
-            faces = pick(exchange(values[None], per_side), 0)
+            faces = pick(exchange([values], per_side), 0)
             values = smooth(values, source, face_coefs, diagonal, 1.0, with_faces(values, faces))
-        faces = pick(exchange(values[None], per_side), 0)
+        faces = pick(exchange([values], per_side), 0)
         residual = source - operate(values, with_faces(values, faces), face_coefs, 1.0)
         return (values[None], residual[None])
 
@@ -435,9 +439,9 @@
     face_coefs, diagonal = coefficients(permeab, with_faces(permeab, pick(first, 0)), 1.0)
     values = smooth(values, source, face_coefs, diagonal, 1.0, with_faces(values, pick(first, 1)))
     for sweep_no in range(SWEEPS - 1):
-        faces = pick(exchange(values[None], per_side), 0)
+        faces = pick(exchange([values], per_side), 0)
         values = smooth(values, source, face_coefs, diagonal, 1.0, with_faces(values, faces))
-    stored_faces = pick(exchange(values[None], per_side), 0)
+    stored_faces = pick(exchange([values], per_side), 0)
     leftover = source - operate(values, with_faces(values, stored_faces), face_coefs, 1.0)
     stored = values
 
@@ -446,9 +450,9 @@
     coefs_1, diagonal_1 = coefficients(coarse_perm, with_faces(coarse_perm, coarse_first), scaling)
     values_1 = OMEGA * right_1 / diagonal_1
     for sweep_no in range(SWEEPS - 1):
-        faces = pick(exchange(values_1[None], per_side), 0)
+        faces = pick(exchange([values_1], per_side), 0)
         values_1 = smooth(values_1, right_1, coefs_1, diagonal_1, scaling, with_faces(values_1, faces))
-    stored_faces_1 = pick(exchange(values_1[None], per_side), 0)
+    stored_faces_1 = pick(exchange([values_1], per_side), 0)
     leftover_1 = right_1 - operate(values_1, with_faces(values_1, stored_faces_1), coefs_1, scaling)
     stored_1 = values_1
 
@@ -463,17 +467,17 @@
     ]
     values_1 = smooth(values_1, right_1, coefs_1, diagonal_1, scaling, with_faces(values_1, faces))
     for sweep_no in range(SWEEPS - 1):
-        faces = pick(exchange(values_1[None], per_side), 0)
+        faces = pick(exchange([values_1], per_side), 0)
         values_1 = smooth(values_1, right_1, coefs_1, diagonal_1, scaling, with_faces(values_1, faces))
-    coarse_faces = pick(exchange(values_1[None], per_side), 0)
+    coarse_faces = pick(exchange([values_1], per_side), 0)
 
     values = stored + refine(values_1)
     faces = [mine + refine_face_of(theirs) for mine, theirs in zip(stored_faces, coarse_faces)]
     values = smooth(values, source, face_coefs, diagonal, 1.0, with_faces(values, faces))
     for sweep_no in range(SWEEPS - 1):
-        faces = pick(exchange(values[None], per_side), 0)
+        faces = pick(exchange([values], per_side), 0)
         values = smooth(values, source, face_coefs, diagonal, 1.0, with_faces(values, faces))
-    faces = pick(exchange(values[None], per_side), 0)
+    faces = pick(exchange([values], per_side), 0)
     residual = source - operate(values, with_faces(values, faces), face_coefs, 1.0)
     return (values[None], residual[None])
 

time: 135 us -> 129 us (0.956)
  other arithmetic: 13.5 us -> 22.7 us
  matrix products: 29.7 us -> 21.1 us
  waiting for transfers between devices: 13.3 us -> 7.78 us
  starting transfers between devices: 63.1 us -> 59.5 us
  local copies, waits for them, and re-layouts: 12.4 us -> 14.4 us
    add x0 -> x18, other arithmetic: none -> 15.8 us  [the longest x2 12 us: shards(): permeab = permeab + jnp.where(classes == number, class_values[number], 0.0)]
    dot_general x64 -> x16, matrix products: 15.1 us -> 6.68 us  [pick_lanes(): out = jnp.dot(stacked, shift, preferred_element_type=jnp.float32)]
    squeeze x1 -> x0, other arithmetic: 6.17 us -> none  [shards(): values = guess[0]]
    ppermute x32, waiting for transfers between devices: 13.3 us -> 7.78 us  [shifted(): lax.ppermute(shard, axis, [(i, (i + by) % peers) for i in range(peers)])]
    ppermute x32, starting transfers between devices: 63.1 us -> 59.5 us  [shifted(): lax.ppermute(shard, axis, [(i, (i + by) % peers) for i in range(peers)])]
    slice x19 -> x40, local copies, waits for them, and re-layouts: 1.2 us -> 3.61 us  [the longest x12 1.61 us: own_faces(): values[:, :, :1]]
    squeeze x16 -> x17, local copies, waits for them, and re-layouts: 2.89 us -> 2.15 us  [pick(): return [face[number] for face in faces]]
  transfers between devices with their start and end apart: 32 -> 32, of which waited for: 12 -> 12; matrix products, arithmetic and copies ran while one was open for 6% -> 11% of each run, Pallas kernels for 0% -> 0%
where the time goes in v7:
time: 129 us; the launch traced here: 128 us
  starting transfers between devices  59.5 us (46%)
  other arithmetic  22.7 us (18%)
  matrix products  21.1 us (16%)
  local copies, waits for them, and re-layouts  14.4 us (11%)
  waiting for transfers between devices  7.78 us (6%)
  between operations  2.62 us (2%)
    ppermute x32, starting transfers between devices, shifted(): lax.ppermute(shard, axis, [(i, (i + by) % peers) for i in range(peers)])  59.5 us
    add x2, other arithmetic, shards(): permeab = permeab + jnp.where(classes == number, class_values[number], 0.0)  12 us
    dot_general x16, matrix products, pick_rows(): out = jnp.dot(picker, joined, preferred_element_type=jnp.float32)  9.34 us
    ppermute x32, waiting for transfers between devices, shifted(): lax.ppermute(shard, axis, [(i, (i + by) % peers) for i in range(peers)])  7.78 us
    dot_general x16, matrix products, pick_lanes(): out = jnp.dot(stacked, shift, preferred_element_type=jnp.float32)  6.68 us
    add x16, other arithmetic, pick_lanes(): return out[:count_r] + out[count_r:2 * count_r] + out[2 * count_r:]  3.78 us
    convert_element_type x37, other arithmetic, split3(): pieces.append(piece.astype(jnp.bfloat16))  3.61 us
  transfers between devices with their start and end apart: 32, of which 12 were waited for; matrix products, arithmetic and copies ran while one was open for 11% of the time, Pallas kernels for 0%

profile of v7, /device:TPU:0, one launch (start us, length us, event | category | flops | bytes accessed | tf_op | source)
XLA Modules:
  0.0 128.2 jit_solution(11637233700940537596)
XLA Ops:
  0.6 1.6 %fusion.1060 = (f32[1]{0:T(128)}, f32[1]{0:T(128)}, f32[1]{0:T(128)}, f32[1]{0:T(128)}, f32[1]{0:T(128)}, /*index=5*/f32[1]{0:T(128)}, f32[1]{0:T(128)}, f32[1]{0:T(128)}) fusion(f32[8]{0:T(128)} %param.6), kind=kLoop, calls=%fused_computation.1651 | loop fusion | bytes 64 | tf_op jit(solution)/shard_map/slice | solution.py:387
  2.2 6.0 %add_add_fusion = f32[1,16,16,128]{3,1,2,0:T(8,128)S(1)} fusion(s32[1,16,16,128]{3,2,1,0:T(8,128)} %param.5, f32[]{:T(128)} %bitcast.10, f32[]{:T(128)} %bitcast.9, f32[]{:T(128)} %bitcast.8, f32[]{:T(128)} %bitcast.7, f32[]{:T(128)} %bitcast.6, f32[]{:T(128)} %bitcast.5, f32[]{:T(128)} %bitcast.4, f32[]{:T(128)} %bitcast.3), kind=kLoop, calls=%fused_computation.456 | loop fusion | flops 753664 | bytes 262176 | tf_op jit(solution)/shard_map/add | solution.py:387
  8.3 0.7 fusion.1055
  9.0 4.1 %collective-permute-start = (f32[2,2,16,128]{3,1,2,0:T(2,128)S(1)}, f32[2,2,16,128]{3,1,2,0:T(2,128)S(1)}, u32[]{:S(2)}, u32[]{:S(2)}) collective-permute-start(f32[2,2,16,128]{3,1,2,0:T(2,128)S(1)} %maximum_maximum_fusion), channel_id=1, source_target_pairs={{0,4},{1,5},{2,6},{3,7},{4,0},{5,1},{6,2},{7,3},{8,12},{9,13},{10,... | collective-permute-start | bytes 98312 | tf_op jit(solution)/shard_map/ppermute | solution.py:16
  13.2 6.0 %fusion.1089 = f32[16,16,128]{2,0,1:T(8,128)S(1)} fusion(f32[]{:T(128)} %bitcast.10, f32[]{:T(128)} %bitcast.9, f32[]{:T(128)} %bitcast.8, f32[]{:T(128)} %bitcast.7, f32[]{:T(128)} %bitcast.6, f32[]{:T(128)} %bitcast.5, f32[]{:T(128)} %bitcast.4, f32[]{:T(128)} %bitcast.3, s32[1,16,16,128]{3,2,1,0:T(8,128)} %param.5), kind=kLoop, calls=%fused_computation.1652 | loop fusion | flops 753664 | bytes 262176 | tf_op jit(solution)/shard_map/add | solution.py:387
  19.2 1.0 copy.1059
  20.7 1.6 %collective-permute-start.3 = (f32[2,16,16,1]{2,1,3,0:T(8,128)S(1)}, f32[2,16,16,1]{2,1,3,0:T(8,128)S(1)}, u32[]{:S(2)}, u32[]{:S(2)}) collective-permute-start(f32[2,16,16,1]{2,1,3,0:T(8,128)S(1)} %pad_maximum_fusion.14), channel_id=1, source_target_pairs={{0,1},{1,2},{2,3},{3,4},{4,5},{5,6},{6,7},{7,0},{8,9},{9,10},{10,1... | collective-permute-start | bytes 6152 | tf_op jit(solution)/shard_map/ppermute | solution.py:16
  22.6 3.2 %collective-permute-start.4 = (f32[2,16,16,1]{2,1,3,0:T(8,128)S(1)}, f32[2,16,16,1]{2,1,3,0:T(8,128)S(1)}, u32[]{:S(2)}, u32[]{:S(2)}) collective-permute-start(f32[2,16,16,1]{2,1,3,0:T(8,128)S(1)} %pad_maximum_fusion.15), channel_id=1, source_target_pairs={{0,7},{1,0},{2,1},{3,2},{4,3},{5,4},{6,5},{7,6},{8,15},{9,8},{10,9... | collective-permute-start | bytes 6152 | tf_op jit(solution)/shard_map/ppermute | solution.py:16
  25.9 3.8 %collective-permute-start.2 = (f32[2,16,1,128]{3,1,2,0:T(8,128)S(1)}, f32[2,16,1,128]{3,1,2,0:T(8,128)S(1)}, u32[]{:S(2)}, u32[]{:S(2)}) collective-permute-start(f32[2,16,1,128]{3,1,2,0:T(8,128)S(1)} %pad_maximum_fusion.13), channel_id=1, source_target_pairs={{0,6},{1,7},{2,0},{3,1},{4,2},{5,3},{6,4},{7,5},{8,14},{9,15},{10,... | collective-permute-start | bytes 49160 | tf_op jit(solution)/shard_map/ppermute | solution.py:16
  34.1 4.7 %collective-permute-start.9 = (f32[1,16,16,1]{2,1,3,0:T(8,128)S(1)}, f32[1,16,16,1]{2,1,3,0:T(8,128)S(1)}, u32[]{:S(2)}, u32[]{:S(2)}) collective-permute-start(f32[1,16,16,1]{2,1,3,0:T(8,128)S(1)} %bitcast.333), channel_id=1, source_target_pairs={{0,7},{1,0},{2,1},{3,2},{4,3},{5,4},{6,5},{7,6},{8,15},{9,8},{10,9... | collective-permute-start | bytes 3080 | tf_op jit(solution)/shard_map/ppermute | solution.py:16
  38.8 1.1 collective-permute-start.6
  39.9 2.8 %collective-permute-start.7 = (f32[1,16,1,128]{3,1,2,0:T(8,128)S(1)}, f32[1,16,1,128]{3,1,2,0:T(8,128)S(1)}, u32[]{:S(2)}, u32[]{:S(2)}) collective-permute-start(f32[1,16,1,128]{3,1,2,0:T(8,128)S(1)} %get-tuple-element.155), channel_id=1, source_target_pairs={{0,6},{1,7},{2,0},{3,1},{4,2},{5,3},{6,4},{7,5},{8,14},{9,15},{10,... | collective-permute-start | bytes 24584 | tf_op jit(solution)/shard_map/ppermute | solution.py:16
  43.5 0.9 collective-permute-done.6
  45.2 4.7 %collective-permute-start.14 = (f32[1,16,16,1]{2,1,3,0:T(8,128)S(1)}, f32[1,16,16,1]{2,1,3,0:T(8,128)S(1)}, u32[]{:S(2)}, u32[]{:S(2)}) collective-permute-start(f32[1,16,16,1]{2,1,3,0:T(8,128)S(1)} %bitcast.337), channel_id=1, source_target_pairs={{0,7},{1,0},{2,1},{3,2},{4,3},{5,4},{6,5},{7,6},{8,15},{9,8},{10,9... | collective-permute-start | bytes 3080 | tf_op jit(solution)/shard_map/ppermute | solution.py:16
  50.0 2.6 %collective-permute-start.11 = (f32[1,16,1,128]{3,1,2,0:T(8,128)S(1)}, f32[1,16,1,128]{3,1,2,0:T(8,128)S(1)}, u32[]{:S(2)}, u32[]{:S(2)}) collective-permute-start(f32[1,16,1,128]{3,1,2,0:T(8,128)S(1)} %get-tuple-element.144), channel_id=1, source_target_pairs={{0,2},{1,3},{2,4},{3,5},{4,6},{5,7},{6,0},{7,1},{8,10},{9,11},{10,... | collective-permute-start | bytes 24584 | tf_op jit(solution)/shard_map/ppermute | solution.py:16
  52.5 1.3 %collective-permute-start.12 = (f32[1,16,1,128]{3,1,2,0:T(8,128)S(1)}, f32[1,16,1,128]{3,1,2,0:T(8,128)S(1)}, u32[]{:S(2)}, u32[]{:S(2)}) collective-permute-start(f32[1,16,1,128]{3,1,2,0:T(8,128)S(1)} %get-tuple-element.143), channel_id=1, source_target_pairs={{0,6},{1,7},{2,0},{3,1},{4,2},{5,3},{6,4},{7,5},{8,14},{9,15},{10,... | collective-permute-start | bytes 24584 | tf_op jit(solution)/shard_map/ppermute | solution.py:16
  54.6 0.9 collective-permute-done.11
  55.5 0.7 collective-permute-done.12
  57.5 1.2 collective-permute-start.16
  58.8 3.5 %collective-permute-start.17 = (f32[2,8,8,64]{3,2,1,0:T(8,128)S(1)}, f32[2,8,8,64]{3,2,1,0:T(8,128)S(1)}, u32[]{:S(2)}, u32[]{:S(2)}) collective-permute-start(f32[2,8,8,64]{3,2,1,0:T(8,128)S(1)} %pad_maximum_fusion.5), channel_id=1, source_target_pairs={{0,3},{1,4},{2,5},{3,6},{4,7},{5,0},{6,1},{7,2},{8,11},{9,12},{10,... | collective-permute-start | bytes 98312 | tf_op jit(solution)/shard_map/ppermute | solution.py:16
  62.3 1.8 %collective-permute-start.18 = (f32[2,8,8,64]{3,2,1,0:T(8,128)S(1)}, f32[2,8,8,64]{3,2,1,0:T(8,128)S(1)}, u32[]{:S(2)}, u32[]{:S(2)}) collective-permute-start(f32[2,8,8,64]{3,2,1,0:T(8,128)S(1)} %pad_maximum_fusion.5), channel_id=1, source_target_pairs={{0,4},{1,5},{2,6},{3,7},{4,0},{5,1},{6,2},{7,3},{8,12},{9,13},{10,... | collective-permute-start | bytes 98312 | tf_op jit(solution)/shard_map/ppermute | solution.py:16
  64.0 1.9 %collective-permute-start.19 = (f32[2,8,8,64]{3,2,1,0:T(8,128)S(1)}, f32[2,8,8,64]{3,2,1,0:T(8,128)S(1)}, u32[]{:S(2)}, u32[]{:S(2)}) collective-permute-start(f32[2,8,8,64]{3,2,1,0:T(8,128)S(1)} %pad_maximum_fusion.5), channel_id=1, source_target_pairs={{0,5},{1,6},{2,7},{3,0},{4,1},{5,2},{6,3},{7,4},{8,13},{9,14},{10,... | collective-permute-start | bytes 98312 | tf_op jit(solution)/shard_map/ppermute | solution.py:16
  66.4 1.8 %collective-permute-start.21 = (f32[2,8,8,64]{3,2,1,0:T(8,128)S(1)}, f32[2,8,8,64]{3,2,1,0:T(8,128)S(1)}, u32[]{:S(2)}, u32[]{:S(2)}) collective-permute-start(f32[2,8,8,64]{3,2,1,0:T(8,128)S(1)} %pad_maximum_fusion.5), channel_id=1, source_target_pairs={{0,7},{1,0},{2,1},{3,2},{4,3},{5,4},{6,5},{7,6},{8,15},{9,8},{10,9... | collective-permute-start | bytes 98312 | tf_op jit(solution)/shard_map/ppermute | solution.py:16
  69.2 1.0 collective-permute-done.20
  71.7 1.4 %fusion.4 = f32[3072,192]{0,1:T(8,128)S(1)} fusion(s32[3072]{0:T(1024)S(1)} %constant_dynamic-update-slice_fusion.4, bf16[512,64]{1,0:T(8,128)(2,1)S(1)} %get-tuple-element.97, bf16[512,64]{1,0:T(8,128)(2,1)S(1)} %get-tuple-element.96, bf16[512,64]{1,0:T(8,128)(2,1)S(1)} %get-tuple-element.95), kind=kOutput, calls=%fused_computation.7 | convolution fusion | flops 609288192 | bytes 2568192 | tf_op jit(solution)/shard_map/dot_general | solution.py:277
  73.5 0.8 fusion.20
  74.3 1.6 %slice_add_fusion.8 = f32[1536,256]{0,1:T(8,128)} fusion(f32[4608,256]{0,1:T(8,128)S(1)} %fusion.20), kind=kLoop, calls=%fused_computation.31 | loop fusion | flops 786432 | bytes 6291456 | tf_op jit(solution)/shard_map/add | solution.py:285
  76.0 1.2 reduce-precision_convert_fusion.19
  77.3 1.3 fusion.3
  78.8 0.8 fusion.26
  80.3 1.3 fusion.2
  81.9 0.8 fusion.32
  94.9 1.3 fusion.1
  96.5 0.8 fusion.38
  98.0 1.3 fusion
  99.5 0.8 fusion.44
  104.6 2.6 %collective-permute-start.25 = (f32[1,16,16,1]{2,1,3,0:T(8,128)S(1)}, f32[1,16,16,1]{2,1,3,0:T(8,128)S(1)}, u32[]{:S(2)}, u32[]{:S(2)}) collective-permute-start(f32[1,16,16,1]{2,1,3,0:T(8,128)S(1)} %bitcast.331), channel_id=1, source_target_pairs={{0,1},{1,2},{2,3},{3,4},{4,5},{5,6},{6,7},{7,0},{8,9},{9,10},{10,1... | collective-permute-start | bytes 3080 | tf_op jit(solution)/shard_map/ppermute | solution.py:16
  107.5 2.1 %collective-permute-start.26 = (f32[1,16,16,1]{2,1,3,0:T(8,128)S(1)}, f32[1,16,16,1]{2,1,3,0:T(8,128)S(1)}, u32[]{:S(2)}, u32[]{:S(2)}) collective-permute-start(f32[1,16,16,1]{2,1,3,0:T(8,128)S(1)} %bitcast.335), channel_id=1, source_target_pairs={{0,7},{1,0},{2,1},{3,2},{4,3},{5,4},{6,5},{7,6},{8,15},{9,8},{10,9... | collective-permute-start | bytes 3080 | tf_op jit(solution)/shard_map/ppermute | solution.py:16
  109.6 0.7 collective-permute-start.23
  110.3 3.2 %collective-permute-start.24 = (f32[1,16,1,128]{3,1,2,0:T(8,128)S(1)}, f32[1,16,1,128]{3,1,2,0:T(8,128)S(1)}, u32[]{:S(2)}, u32[]{:S(2)}) collective-permute-start(f32[1,16,1,128]{3,1,2,0:T(8,128)S(1)} %get-tuple-element.116), channel_id=1, source_target_pairs={{0,6},{1,7},{2,0},{3,1},{4,2},{5,3},{6,4},{7,5},{8,14},{9,15},{10,... | collective-permute-start | bytes 24584 | tf_op jit(solution)/shard_map/ppermute | solution.py:16
  114.2 0.9 collective-permute-done.23
  115.6 1.1 collective-permute-start.27
  116.9 0.8 collective-permute-start.30
  117.9 4.0 %collective-permute-start.31 = (f32[1,16,16,1]{2,1,3,0:T(8,128)S(1)}, f32[1,16,16,1]{2,1,3,0:T(8,128)S(1)}, u32[]{:S(2)}, u32[]{:S(2)}) collective-permute-start(f32[1,16,16,1]{2,1,3,0:T(8,128)S(1)} %bitcast.340), channel_id=1, source_target_pairs={{0,7},{1,0},{2,1},{3,2},{4,3},{5,4},{6,5},{7,6},{8,15},{9,8},{10,9... | collective-permute-start | bytes 3080 | tf_op jit(solution)/shard_map/ppermute | solution.py:16
  121.9 1.5 %collective-permute-start.28 = (f32[1,16,1,128]{3,1,2,0:T(8,128)S(1)}, f32[1,16,1,128]{3,1,2,0:T(8,128)S(1)}, u32[]{:S(2)}, u32[]{:S(2)}) collective-permute-start(f32[1,16,1,128]{3,1,2,0:T(8,128)S(1)} %get-tuple-element.105), channel_id=1, source_target_pairs={{0,2},{1,3},{2,4},{3,5},{4,6},{5,7},{6,0},{7,1},{8,10},{9,11},{10,... | collective-permute-start | bytes 24584 | tf_op jit(solution)/shard_map/ppermute | solution.py:16
  123.4 2.3 %collective-permute-start.29 = (f32[1,16,1,128]{3,1,2,0:T(8,128)S(1)}, f32[1,16,1,128]{3,1,2,0:T(8,128)S(1)}, u32[]{:S(2)}, u32[]{:S(2)}) collective-permute-start(f32[1,16,1,128]{3,1,2,0:T(8,128)S(1)} %get-tuple-element.104), channel_id=1, source_target_pairs={{0,6},{1,7},{2,0},{3,1},{4,2},{5,3},{6,4},{7,5},{8,14},{9,15},{10,... | collective-permute-start | bytes 24584 | tf_op jit(solution)/shard_map/ppermute | solution.py:16
  125.7 0.7 copy.1044
  127.5 0.7 copy.1045
  (355 shorter events, 32.7 us)
Async XLA Ops:
  9.0 23.9 %collective-permute-start = (f32[2,2,16,128]{3,1,2,0:T(2,128)S(1)}, f32[2,2,16,128]{3,1,2,0:T(2,128)S(1)}, u32[]{:S(2)}, u32[]{:S(2)}) collective-permute-start(f32[2,2,16,128]{3,1,2,0:T(2,128)S(1)} %maximum_maximum_fusion), channel_id=1, source_target_pairs={{0,4},{1,5},{2,6},{3,7},{4,0},{5,1},{6,2},{7,3},{8,12},{9,13},{10,... | collective-permute-start | bytes 98312 | tf_op jit(solution)/shard_map/ppermute | solution.py:16
  20.7 11.5 %collective-permute-start.3 = (f32[2,16,16,1]{2,1,3,0:T(8,128)S(1)}, f32[2,16,16,1]{2,1,3,0:T(8,128)S(1)}, u32[]{:S(2)}, u32[]{:S(2)}) collective-permute-start(f32[2,16,16,1]{2,1,3,0:T(8,128)S(1)} %pad_maximum_fusion.14), channel_id=1, source_target_pairs={{0,1},{1,2},{2,3},{3,4},{4,5},{5,6},{6,7},{7,0},{8,9},{9,10},{10,1... | collective-permute-start | bytes 6152 | tf_op jit(solution)/shard_map/ppermute | solution.py:16
  22.6 9.5 %collective-permute-start.4 = (f32[2,16,16,1]{2,1,3,0:T(8,128)S(1)}, f32[2,16,16,1]{2,1,3,0:T(8,128)S(1)}, u32[]{:S(2)}, u32[]{:S(2)}) collective-permute-start(f32[2,16,16,1]{2,1,3,0:T(8,128)S(1)} %pad_maximum_fusion.15), channel_id=1, source_target_pairs={{0,7},{1,0},{2,1},{3,2},{4,3},{5,4},{6,5},{7,6},{8,15},{9,8},{10,9... | collective-permute-start | bytes 6152 | tf_op jit(solution)/shard_map/ppermute | solution.py:16
  25.9 7.0 %collective-permute-start.1 = (f32[2,16,1,128]{3,1,2,0:T(8,128)S(1)}, f32[2,16,1,128]{3,1,2,0:T(8,128)S(1)}, u32[]{:S(2)}, u32[]{:S(2)}) collective-permute-start(f32[2,16,1,128]{3,1,2,0:T(8,128)S(1)} %pad_maximum_fusion.12), channel_id=1, source_target_pairs={{0,2},{1,3},{2,4},{3,5},{4,6},{5,7},{6,0},{7,1},{8,10},{9,11},{10,... | collective-permute-start | bytes 49160 | tf_op jit(solution)/shard_map/ppermute | solution.py:16
  25.9 7.0 %collective-permute-start.2 = (f32[2,16,1,128]{3,1,2,0:T(8,128)S(1)}, f32[2,16,1,128]{3,1,2,0:T(8,128)S(1)}, u32[]{:S(2)}, u32[]{:S(2)}) collective-permute-start(f32[2,16,1,128]{3,1,2,0:T(8,128)S(1)} %pad_maximum_fusion.13), channel_id=1, source_target_pairs={{0,6},{1,7},{2,0},{3,1},{4,2},{5,3},{6,4},{7,5},{8,14},{9,15},{10,... | collective-permute-start | bytes 49160 | tf_op jit(solution)/shard_map/ppermute | solution.py:16
  29.9 1.7 %copy-start.1 = (s32[16]{0:T(128)S(1)}, s32[16]{0:T(128)}, u32[]{:S(2)}) copy-start(s32[16]{0:T(128)} %param.7) | copy-start | bytes 196
  29.9 1.7 %copy-start.2 = (f32[16]{0:T(128)S(1)}, f32[16]{0:T(128)}, u32[]{:S(2)}) copy-start(f32[16]{0:T(128)} %param.8) | copy-start | bytes 196
  29.9 3.0 %copy-start = (f32[1,16,16,128]{3,2,1,0:T(8,128)S(1)}, f32[1,16,16,128]{3,2,1,0:T(8,128)}, u32[]{:S(2)}) copy-start(f32[1,16,16,128]{3,2,1,0:T(8,128)} %param.9) | copy-start | bytes 393220
  33.9 8.8 %collective-permute-start.8 = (f32[1,16,16,1]{2,1,3,0:T(8,128)S(1)}, f32[1,16,16,1]{2,1,3,0:T(8,128)S(1)}, u32[]{:S(2)}, u32[]{:S(2)}) collective-permute-start(f32[1,16,16,1]{2,1,3,0:T(8,128)S(1)} %bitcast.328), channel_id=1, source_target_pairs={{0,1},{1,2},{2,3},{3,4},{4,5},{5,6},{6,7},{7,0},{8,9},{9,10},{10,1... | collective-permute-start | bytes 3080 | tf_op jit(solution)/shard_map/ppermute | solution.py:16
  34.1 8.8 %collective-permute-start.9 = (f32[1,16,16,1]{2,1,3,0:T(8,128)S(1)}, f32[1,16,16,1]{2,1,3,0:T(8,128)S(1)}, u32[]{:S(2)}, u32[]{:S(2)}) collective-permute-start(f32[1,16,16,1]{2,1,3,0:T(8,128)S(1)} %bitcast.333), channel_id=1, source_target_pairs={{0,7},{1,0},{2,1},{3,2},{4,3},{5,4},{6,5},{7,6},{8,15},{9,8},{10,9... | collective-permute-start | bytes 3080 | tf_op jit(solution)/shard_map/ppermute | solution.py:16
  38.8 4.6 %collective-permute-start.5 = (f32[1,2,16,128]{3,2,1,0:T(8,128)S(1)}, f32[1,2,16,128]{3,2,1,0:T(8,128)S(1)}, u32[]{:S(2)}, u32[]{:S(2)}) collective-permute-start(f32[1,2,16,128]{3,2,1,0:T(8,128)S(1)} %pad_maximum_fusion.16), channel_id=1, source_target_pairs={{0,4},{1,5},{2,6},{3,7},{4,0},{5,1},{6,2},{7,3},{8,12},{9,13},{10,... | collective-permute-start | bytes 49160 | tf_op jit(solution)/shard_map/ppermute | solution.py:16
  38.8 5.5 %collective-permute-start.6 = (f32[1,16,1,128]{3,1,2,0:T(8,128)S(1)}, f32[1,16,1,128]{3,1,2,0:T(8,128)S(1)}, u32[]{:S(2)}, u32[]{:S(2)}) collective-permute-start(f32[1,16,1,128]{3,1,2,0:T(8,128)S(1)} %get-tuple-element.156), channel_id=1, source_target_pairs={{0,2},{1,3},{2,4},{3,5},{4,6},{5,7},{6,0},{7,1},{8,10},{9,11},{10,... | collective-permute-start | bytes 24584 | tf_op jit(solution)/shard_map/ppermute | solution.py:16
  39.9 4.4 %collective-permute-start.7 = (f32[1,16,1,128]{3,1,2,0:T(8,128)S(1)}, f32[1,16,1,128]{3,1,2,0:T(8,128)S(1)}, u32[]{:S(2)}, u32[]{:S(2)}) collective-permute-start(f32[1,16,1,128]{3,1,2,0:T(8,128)S(1)} %get-tuple-element.155), channel_id=1, source_target_pairs={{0,6},{1,7},{2,0},{3,1},{4,2},{5,3},{6,4},{7,5},{8,14},{9,15},{10,... | collective-permute-start | bytes 24584 | tf_op jit(solution)/shard_map/ppermute | solution.py:16
  45.0 8.8 %collective-permute-start.13 = (f32[1,16,16,1]{2,1,3,0:T(8,128)S(1)}, f32[1,16,16,1]{2,1,3,0:T(8,128)S(1)}, u32[]{:S(2)}, u32[]{:S(2)}) collective-permute-start(f32[1,16,16,1]{2,1,3,0:T(8,128)S(1)} %bitcast.330), channel_id=1, source_target_pairs={{0,1},{1,2},{2,3},{3,4},{4,5},{5,6},{6,7},{7,0},{8,9},{9,10},{10,1... | collective-permute-start | bytes 3080 | tf_op jit(solution)/shard_map/ppermute | solution.py:16
  45.2 8.8 %collective-permute-start.14 = (f32[1,16,16,1]{2,1,3,0:T(8,128)S(1)}, f32[1,16,16,1]{2,1,3,0:T(8,128)S(1)}, u32[]{:S(2)}, u32[]{:S(2)}) collective-permute-start(f32[1,16,16,1]{2,1,3,0:T(8,128)S(1)} %bitcast.337), channel_id=1, source_target_pairs={{0,7},{1,0},{2,1},{3,2},{4,3},{5,4},{6,5},{7,6},{8,15},{9,8},{10,9... | collective-permute-start | bytes 3080 | tf_op jit(solution)/shard_map/ppermute | solution.py:16
  50.0 4.6 %collective-permute-start.10 = (f32[1,2,16,128]{3,2,1,0:T(8,128)S(1)}, f32[1,2,16,128]{3,2,1,0:T(8,128)S(1)}, u32[]{:S(2)}, u32[]{:S(2)}) collective-permute-start(f32[1,2,16,128]{3,2,1,0:T(8,128)S(1)} %pad_maximum_fusion.17), channel_id=1, source_target_pairs={{0,4},{1,5},{2,6},{3,7},{4,0},{5,1},{6,2},{7,3},{8,12},{9,13},{10,... | collective-permute-start | bytes 49160 | tf_op jit(solution)/shard_map/ppermute | solution.py:16
  50.0 5.5 %collective-permute-start.11 = (f32[1,16,1,128]{3,1,2,0:T(8,128)S(1)}, f32[1,16,1,128]{3,1,2,0:T(8,128)S(1)}, u32[]{:S(2)}, u32[]{:S(2)}) collective-permute-start(f32[1,16,1,128]{3,1,2,0:T(8,128)S(1)} %get-tuple-element.144), channel_id=1, source_target_pairs={{0,2},{1,3},{2,4},{3,5},{4,6},{5,7},{6,0},{7,1},{8,10},{9,11},{10,... | collective-permute-start | bytes 24584 | tf_op jit(solution)/shard_map/ppermute | solution.py:16
  52.5 3.7 %collective-permute-start.12 = (f32[1,16,1,128]{3,1,2,0:T(8,128)S(1)}, f32[1,16,1,128]{3,1,2,0:T(8,128)S(1)}, u32[]{:S(2)}, u32[]{:S(2)}) collective-permute-start(f32[1,16,1,128]{3,1,2,0:T(8,128)S(1)} %get-tuple-element.143), channel_id=1, source_target_pairs={{0,6},{1,7},{2,0},{3,1},{4,2},{5,3},{6,4},{7,5},{8,14},{9,15},{10,... | collective-permute-start | bytes 24584 | tf_op jit(solution)/shard_map/ppermute | solution.py:16
  57.0 8.9 %collective-permute-start.15 = (f32[2,8,8,64]{3,2,1,0:T(8,128)S(1)}, f32[2,8,8,64]{3,2,1,0:T(8,128)S(1)}, u32[]{:S(2)}, u32[]{:S(2)}) collective-permute-start(f32[2,8,8,64]{3,2,1,0:T(8,128)S(1)} %pad_maximum_fusion.5), channel_id=1, source_target_pairs={{0,1},{1,2},{2,3},{3,4},{4,5},{5,6},{6,7},{7,0},{8,9},{9,10},{10,1... | collective-permute-start | bytes 98312 | tf_op jit(solution)/shard_map/ppermute | solution.py:16
  57.5 8.9 %collective-permute-start.16 = (f32[2,8,8,64]{3,2,1,0:T(8,128)S(1)}, f32[2,8,8,64]{3,2,1,0:T(8,128)S(1)}, u32[]{:S(2)}, u32[]{:S(2)}) collective-permute-start(f32[2,8,8,64]{3,2,1,0:T(8,128)S(1)} %pad_maximum_fusion.5), channel_id=1, source_target_pairs={{0,2},{1,3},{2,4},{3,5},{4,6},{5,7},{6,0},{7,1},{8,10},{9,11},{10,... | collective-permute-start | bytes 98312 | tf_op jit(solution)/shard_map/ppermute | solution.py:16
  58.8 9.4 %collective-permute-start.17 = (f32[2,8,8,64]{3,2,1,0:T(8,128)S(1)}, f32[2,8,8,64]{3,2,1,0:T(8,128)S(1)}, u32[]{:S(2)}, u32[]{:S(2)}) collective-permute-start(f32[2,8,8,64]{3,2,1,0:T(8,128)S(1)} %pad_maximum_fusion.5), channel_id=1, source_target_pairs={{0,3},{1,4},{2,5},{3,6},{4,7},{5,0},{6,1},{7,2},{8,11},{9,12},{10,... | collective-permute-start | bytes 98312 | tf_op jit(solution)/shard_map/ppermute | solution.py:16
  62.3 6.6 %collective-permute-start.18 = (f32[2,8,8,64]{3,2,1,0:T(8,128)S(1)}, f32[2,8,8,64]{3,2,1,0:T(8,128)S(1)}, u32[]{:S(2)}, u32[]{:S(2)}) collective-permute-start(f32[2,8,8,64]{3,2,1,0:T(8,128)S(1)} %pad_maximum_fusion.5), channel_id=1, source_target_pairs={{0,4},{1,5},{2,6},{3,7},{4,0},{5,1},{6,2},{7,3},{8,12},{9,13},{10,... | collective-permute-start | bytes 98312 | tf_op jit(solution)/shard_map/ppermute | solution.py:16
  64.0 5.2 %collective-permute-start.19 = (f32[2,8,8,64]{3,2,1,0:T(8,128)S(1)}, f32[2,8,8,64]{3,2,1,0:T(8,128)S(1)}, u32[]{:S(2)}, u32[]{:S(2)}) collective-permute-start(f32[2,8,8,64]{3,2,1,0:T(8,128)S(1)} %pad_maximum_fusion.5), channel_id=1, source_target_pairs={{0,5},{1,6},{2,7},{3,0},{4,1},{5,2},{6,3},{7,4},{8,13},{9,14},{10,... | collective-permute-start | bytes 98312 | tf_op jit(solution)/shard_map/ppermute | solution.py:16
  65.9 4.4 %collective-permute-start.20 = (f32[2,8,8,64]{3,2,1,0:T(8,128)S(1)}, f32[2,8,8,64]{3,2,1,0:T(8,128)S(1)}, u32[]{:S(2)}, u32[]{:S(2)}) collective-permute-start(f32[2,8,8,64]{3,2,1,0:T(8,128)S(1)} %pad_maximum_fusion.5), channel_id=1, source_target_pairs={{0,6},{1,7},{2,0},{3,1},{4,2},{5,3},{6,4},{7,5},{8,14},{9,15},{10,... | collective-permute-start | bytes 98312 | tf_op jit(solution)/shard_map/ppermute | solution.py:16
  66.4 4.5 %collective-permute-start.21 = (f32[2,8,8,64]{3,2,1,0:T(8,128)S(1)}, f32[2,8,8,64]{3,2,1,0:T(8,128)S(1)}, u32[]{:S(2)}, u32[]{:S(2)}) collective-permute-start(f32[2,8,8,64]{3,2,1,0:T(8,128)S(1)} %pad_maximum_fusion.5), channel_id=1, source_target_pairs={{0,7},{1,0},{2,1},{3,2},{4,3},{5,4},{6,5},{7,6},{8,15},{9,8},{10,9... | collective-permute-start | bytes 98312 | tf_op jit(solution)/shard_map/ppermute | solution.py:16
  104.6 8.8 %collective-permute-start.25 = (f32[1,16,16,1]{2,1,3,0:T(8,128)S(1)}, f32[1,16,16,1]{2,1,3,0:T(8,128)S(1)}, u32[]{:S(2)}, u32[]{:S(2)}) collective-permute-start(f32[1,16,16,1]{2,1,3,0:T(8,128)S(1)} %bitcast.331), channel_id=1, source_target_pairs={{0,1},{1,2},{2,3},{3,4},{4,5},{5,6},{6,7},{7,0},{8,9},{9,10},{10,1... | collective-permute-start | bytes 3080 | tf_op jit(solution)/shard_map/ppermute | solution.py:16
  107.5 6.2 %collective-permute-start.26 = (f32[1,16,16,1]{2,1,3,0:T(8,128)S(1)}, f32[1,16,16,1]{2,1,3,0:T(8,128)S(1)}, u32[]{:S(2)}, u32[]{:S(2)}) collective-permute-start(f32[1,16,16,1]{2,1,3,0:T(8,128)S(1)} %bitcast.335), channel_id=1, source_target_pairs={{0,7},{1,0},{2,1},{3,2},{4,3},{5,4},{6,5},{7,6},{8,15},{9,8},{10,9... | collective-permute-start | bytes 3080 | tf_op jit(solution)/shard_map/ppermute | solution.py:16
  109.6 4.6 %collective-permute-start.22 = (f32[1,2,16,128]{3,2,1,0:T(8,128)S(1)}, f32[1,2,16,128]{3,2,1,0:T(8,128)S(1)}, u32[]{:S(2)}, u32[]{:S(2)}) collective-permute-start(f32[1,2,16,128]{3,2,1,0:T(8,128)S(1)} %pad_maximum_fusion.18), channel_id=1, source_target_pairs={{0,4},{1,5},{2,6},{3,7},{4,0},{5,1},{6,2},{7,3},{8,12},{9,13},{10,... | collective-permute-start | bytes 49160 | tf_op jit(solution)/shard_map/ppermute | solution.py:16
  109.6 5.5 %collective-permute-start.23 = (f32[1,16,1,128]{3,1,2,0:T(8,128)S(1)}, f32[1,16,1,128]{3,1,2,0:T(8,128)S(1)}, u32[]{:S(2)}, u32[]{:S(2)}) collective-permute-start(f32[1,16,1,128]{3,1,2,0:T(8,128)S(1)} %get-tuple-element.117), channel_id=1, source_target_pairs={{0,2},{1,3},{2,4},{3,5},{4,6},{5,7},{6,0},{7,1},{8,10},{9,11},{10,... | collective-permute-start | bytes 24584 | tf_op jit(solution)/shard_map/ppermute | solution.py:16
  110.3 4.8 %collective-permute-start.24 = (f32[1,16,1,128]{3,1,2,0:T(8,128)S(1)}, f32[1,16,1,128]{3,1,2,0:T(8,128)S(1)}, u32[]{:S(2)}, u32[]{:S(2)}) collective-permute-start(f32[1,16,1,128]{3,1,2,0:T(8,128)S(1)} %get-tuple-element.116), channel_id=1, source_target_pairs={{0,6},{1,7},{2,0},{3,1},{4,2},{5,3},{6,4},{7,5},{8,14},{9,15},{10,... | collective-permute-start | bytes 24584 | tf_op jit(solution)/shard_map/ppermute | solution.py:16
  115.6 11.1 %collective-permute-start.27 = (f32[1,2,16,128]{3,2,1,0:T(8,128)S(1)}, f32[1,2,16,128]{3,2,1,0:T(8,128)S(1)}, u32[]{:S(2)}, u32[]{:S(2)}) collective-permute-start(f32[1,2,16,128]{3,2,1,0:T(8,128)S(1)} %pad_maximum_fusion.19), channel_id=1, source_target_pairs={{0,4},{1,5},{2,6},{3,7},{4,0},{5,1},{6,2},{7,3},{8,12},{9,13},{10,... | collective-permute-start | bytes 49160 | tf_op jit(solution)/shard_map/ppermute | solution.py:16
  116.9 9.5 %collective-permute-start.30 = (f32[1,16,16,1]{2,1,3,0:T(8,128)S(1)}, f32[1,16,16,1]{2,1,3,0:T(8,128)S(1)}, u32[]{:S(2)}, u32[]{:S(2)}) collective-permute-start(f32[1,16,16,1]{2,1,3,0:T(8,128)S(1)} %bitcast.338), channel_id=1, source_target_pairs={{0,1},{1,2},{2,3},{3,4},{4,5},{5,6},{6,7},{7,0},{8,9},{9,10},{10,1... | collective-permute-start | bytes 3080 | tf_op jit(solution)/shard_map/ppermute | solution.py:16
  117.9 8.7 %collective-permute-start.31 = (f32[1,16,16,1]{2,1,3,0:T(8,128)S(1)}, f32[1,16,16,1]{2,1,3,0:T(8,128)S(1)}, u32[]{:S(2)}, u32[]{:S(2)}) collective-permute-start(f32[1,16,16,1]{2,1,3,0:T(8,128)S(1)} %bitcast.340), channel_id=1, source_target_pairs={{0,7},{1,0},{2,1},{3,2},{4,3},{5,4},{6,5},{7,6},{8,15},{9,8},{10,9... | collective-permute-start | bytes 3080 | tf_op jit(solution)/shard_map/ppermute | solution.py:16
  121.9 5.4 %collective-permute-start.28 = (f32[1,16,1,128]{3,1,2,0:T(8,128)S(1)}, f32[1,16,1,128]{3,1,2,0:T(8,128)S(1)}, u32[]{:S(2)}, u32[]{:S(2)}) collective-permute-start(f32[1,16,1,128]{3,1,2,0:T(8,128)S(1)} %get-tuple-element.105), channel_id=1, source_target_pairs={{0,2},{1,3},{2,4},{3,5},{4,6},{5,7},{6,0},{7,1},{8,10},{9,11},{10,... | collective-permute-start | bytes 24584 | tf_op jit(solution)/shard_map/ppermute | solution.py:16
  123.4 3.9 %collective-permute-start.29 = (f32[1,16,1,128]{3,1,2,0:T(8,128)S(1)}, f32[1,16,1,128]{3,1,2,0:T(8,128)S(1)}, u32[]{:S(2)}, u32[]{:S(2)}) collective-permute-start(f32[1,16,1,128]{3,1,2,0:T(8,128)S(1)} %get-tuple-element.104), channel_id=1, source_target_pairs={{0,6},{1,7},{2,0},{3,1},{4,2},{5,3},{6,4},{7,5},{8,14},{9,15},{10,... | collective-permute-start | bytes 24584 | tf_op jit(solution)/shard_map/ppermute | solution.py:16

commit v8 on v7

--- a/solution.py
+++ b/solution.py
@@ -102,9 +102,8 @@
     count_dev = lax.axis_size("space")
     if count_dev > 16:
         return lax.all_gather(block[None], "space", axis=0, tiled=True)
-    my_row = lax.axis_index("space")
-    by_offset = jnp.stack([block] + [shifted(block, "space", k) for k in range(1, count_dev)])
-    return jnp.take(by_offset, (my_row - jnp.arange(count_dev)) % count_dev, axis=0)
+    copies = jnp.broadcast_to(block[None], (count_dev,) + block.shape)
+    return lax.all_to_all(copies, "space", 0, 0, tiled=True)
 
 
 def pick(faces, number):

time: 129 us -> 135 us (1.047)
  starting transfers between devices: 59.5 us -> 53.3 us
  other arithmetic: 22.7 us -> 27.7 us
  waiting for transfers between devices: 7.78 us -> 12.7 us
  local copies, waits for them, and re-layouts: 14.4 us -> 16 us
    ppermute x32 -> x25, starting transfers between devices: 59.5 us -> 48.4 us  [shifted(): lax.ppermute(shard, axis, [(i, (i + by) % peers) for i in range(peers)])]
    all_to_all x0 -> x1, waiting for transfers between devices: none -> 7.64 us  [gather_rows(): return lax.all_to_all(copies, 'space', 0, 0, tiled=True)]
    all_to_all x0 -> x1, starting transfers between devices: none -> 4.96 us  [gather_rows(): return lax.all_to_all(copies, 'space', 0, 0, tiled=True)]
    ppermute x32 -> x25, waiting for transfers between devices: 7.78 us -> 5.08 us  [shifted(): lax.ppermute(shard, axis, [(i, (i + by) % peers) for i in range(peers)])]
    unnamed x15 -> x41, local copies, waits for them, and re-layouts: 2.4 us -> 3.92 us
  transfers between devices with their start and end apart: 32 -> 26, of which waited for: 12 -> 9; matrix products, arithmetic and copies ran while one was open for 11% -> 13% of each run, Pallas kernels for 0% -> 0%
where the time goes in v8:
time: 135 us
  starting transfers between devices  53.3 us (39%)
  other arithmetic  27.7 us (21%)
  matrix products  22 us (16%)
  local copies, waits for them, and re-layouts  16 us (12%)
  waiting for transfers between devices  12.7 us (9%)
  between operations  2.78 us (2%)
    ppermute x25, starting transfers between devices, shifted(): lax.ppermute(shard, axis, [(i, (i + by) % peers) for i in range(peers)])  48.4 us
    add x2, other arithmetic, shards(): permeab = permeab + jnp.where(classes == number, class_values[number], 0.0)  12.1 us
    dot_general x16, matrix products, pick_rows(): out = jnp.dot(picker, joined, preferred_element_type=jnp.float32)  9.45 us
    all_to_all x1, waiting for transfers between devices, gather_rows(): return lax.all_to_all(copies, 'space', 0, 0, tiled=True)  7.64 us
    dot_general x16, matrix products, pick_lanes(): out = jnp.dot(stacked, shift, preferred_element_type=jnp.float32)  6.68 us
    ppermute x25, waiting for transfers between devices, shifted(): lax.ppermute(shard, axis, [(i, (i + by) % peers) for i in range(peers)])  5.08 us
    all_to_all x1, starting transfers between devices, gather_rows(): return lax.all_to_all(copies, 'space', 0, 0, tiled=True)  4.96 us
    unnamed x41, local copies, waits for them, and re-layouts  3.92 us
  transfers between devices with their start and end apart: 26, of which 9 were waited for; matrix products, arithmetic and copies ran while one was open for 13% of the time, Pallas kernels for 0%

profile of v8, /device:TPU:0, one launch (start us, length us, event | category | flops | bytes accessed | tf_op | source)
XLA Modules:
  0.0 134.6 jit_solution(12102606978118987255)
XLA Ops:
  0.6 1.6 %fusion.1057 = (f32[1]{0:T(128)}, f32[1]{0:T(128)}, f32[1]{0:T(128)}, f32[1]{0:T(128)}, f32[1]{0:T(128)}, /*index=5*/f32[1]{0:T(128)}, f32[1]{0:T(128)}, f32[1]{0:T(128)}) fusion(f32[8]{0:T(128)} %param.6), kind=kLoop, calls=%fused_computation.1628 | loop fusion | bytes 64 | tf_op jit(solution)/shard_map/slice | solution.py:386
  2.3 6.0 %add_add_fusion = f32[1,16,16,128]{3,1,2,0:T(8,128)S(1)} fusion(s32[1,16,16,128]{3,2,1,0:T(8,128)} %param.5, f32[]{:T(128)} %bitcast.10, f32[]{:T(128)} %bitcast.9, f32[]{:T(128)} %bitcast.8, f32[]{:T(128)} %bitcast.7, f32[]{:T(128)} %bitcast.6, f32[]{:T(128)} %bitcast.5, f32[]{:T(128)} %bitcast.4, f32[]{:T(128)} %bitcast.3), kind=kLoop, calls=%fused_computation.454 | loop fusion | flops 753664 | bytes 262176 | tf_op jit(solution)/shard_map/add | solution.py:386
  8.3 0.7 fusion.1052
  9.1 4.1 %collective-permute-start = (f32[2,2,16,128]{3,1,2,0:T(2,128)S(1)}, f32[2,2,16,128]{3,1,2,0:T(2,128)S(1)}, u32[]{:S(2)}, u32[]{:S(2)}) collective-permute-start(f32[2,2,16,128]{3,1,2,0:T(2,128)S(1)} %maximum_maximum_fusion), channel_id=1, source_target_pairs={{0,4},{1,5},{2,6},{3,7},{4,0},{5,1},{6,2},{7,3},{8,12},{9,13},{10,... | collective-permute-start | bytes 98312 | tf_op jit(solution)/shard_map/ppermute | solution.py:16
  13.2 6.0 %fusion.1086 = f32[16,16,128]{2,0,1:T(8,128)S(1)} fusion(f32[]{:T(128)} %bitcast.10, f32[]{:T(128)} %bitcast.9, f32[]{:T(128)} %bitcast.8, f32[]{:T(128)} %bitcast.7, f32[]{:T(128)} %bitcast.6, f32[]{:T(128)} %bitcast.5, f32[]{:T(128)} %bitcast.4, f32[]{:T(128)} %bitcast.3, s32[1,16,16,128]{3,2,1,0:T(8,128)} %param.5), kind=kLoop, calls=%fused_computation.1629 | loop fusion | flops 753664 | bytes 262176 | tf_op jit(solution)/shard_map/add | solution.py:386
  19.2 1.0 copy.1058
  20.8 1.6 %collective-permute-start.3 = (f32[2,16,16,1]{2,1,3,0:T(8,128)S(1)}, f32[2,16,16,1]{2,1,3,0:T(8,128)S(1)}, u32[]{:S(2)}, u32[]{:S(2)}) collective-permute-start(f32[2,16,16,1]{2,1,3,0:T(8,128)S(1)} %pad_maximum_fusion.14), channel_id=1, source_target_pairs={{0,1},{1,2},{2,3},{3,4},{4,5},{5,6},{6,7},{7,0},{8,9},{9,10},{10,1... | collective-permute-start | bytes 6152 | tf_op jit(solution)/shard_map/ppermute | solution.py:16
  22.7 3.2 %collective-permute-start.4 = (f32[2,16,16,1]{2,1,3,0:T(8,128)S(1)}, f32[2,16,16,1]{2,1,3,0:T(8,128)S(1)}, u32[]{:S(2)}, u32[]{:S(2)}) collective-permute-start(f32[2,16,16,1]{2,1,3,0:T(8,128)S(1)} %pad_maximum_fusion.15), channel_id=1, source_target_pairs={{0,7},{1,0},{2,1},{3,2},{4,3},{5,4},{6,5},{7,6},{8,15},{9,8},{10,9... | collective-permute-start | bytes 6152 | tf_op jit(solution)/shard_map/ppermute | solution.py:16
  26.0 3.8 %collective-permute-start.2 = (f32[2,16,1,128]{3,1,2,0:T(8,128)S(1)}, f32[2,16,1,128]{3,1,2,0:T(8,128)S(1)}, u32[]{:S(2)}, u32[]{:S(2)}) collective-permute-start(f32[2,16,1,128]{3,1,2,0:T(8,128)S(1)} %pad_maximum_fusion.13), channel_id=1, source_target_pairs={{0,6},{1,7},{2,0},{3,1},{4,2},{5,3},{6,4},{7,5},{8,14},{9,15},{10,... | collective-permute-start | bytes 49160 | tf_op jit(solution)/shard_map/ppermute | solution.py:16
  30.8 0.6 and_select_fusion.9
  31.4 0.6 fusion.850
  32.0 0.6 multiply_add_fusion.1
  32.8 0.6 constant_dynamic-update-slice_fusion
  34.3 0.6 fusion.852
  36.6 1.2 fusion.217
  38.4 4.7 %collective-permute-start.9 = (f32[1,16,16,1]{2,1,3,0:T(8,128)S(1)}, f32[1,16,16,1]{2,1,3,0:T(8,128)S(1)}, u32[]{:S(2)}, u32[]{:S(2)}) collective-permute-start(f32[1,16,16,1]{2,1,3,0:T(8,128)S(1)} %bitcast.315), channel_id=1, source_target_pairs={{0,7},{1,0},{2,1},{3,2},{4,3},{5,4},{6,5},{7,6},{8,15},{9,8},{10,9... | collective-permute-start | bytes 3080 | tf_op jit(solution)/shard_map/ppermute | solution.py:16
  43.2 3.8 %collective-permute-start.7 = (f32[1,16,1,128]{3,1,2,0:T(8,128)S(1)}, f32[1,16,1,128]{3,1,2,0:T(8,128)S(1)}, u32[]{:S(2)}, u32[]{:S(2)}) collective-permute-start(f32[1,16,1,128]{3,1,2,0:T(8,128)S(1)} %get-tuple-element.155), channel_id=1, source_target_pairs={{0,6},{1,7},{2,0},{3,1},{4,2},{5,3},{6,4},{7,5},{8,14},{9,15},{10,... | collective-permute-start | bytes 24584 | tf_op jit(solution)/shard_map/ppermute | solution.py:16
  47.8 0.9 collective-permute-done.6
  49.5 4.7 %collective-permute-start.14 = (f32[1,16,16,1]{2,1,3,0:T(8,128)S(1)}, f32[1,16,16,1]{2,1,3,0:T(8,128)S(1)}, u32[]{:S(2)}, u32[]{:S(2)}) collective-permute-start(f32[1,16,16,1]{2,1,3,0:T(8,128)S(1)} %bitcast.319), channel_id=1, source_target_pairs={{0,7},{1,0},{2,1},{3,2},{4,3},{5,4},{6,5},{7,6},{8,15},{9,8},{10,9... | collective-permute-start | bytes 3080 | tf_op jit(solution)/shard_map/ppermute | solution.py:16
  54.3 2.6 %collective-permute-start.11 = (f32[1,16,1,128]{3,1,2,0:T(8,128)S(1)}, f32[1,16,1,128]{3,1,2,0:T(8,128)S(1)}, u32[]{:S(2)}, u32[]{:S(2)}) collective-permute-start(f32[1,16,1,128]{3,1,2,0:T(8,128)S(1)} %get-tuple-element.144), channel_id=1, source_target_pairs={{0,2},{1,3},{2,4},{3,5},{4,6},{5,7},{6,0},{7,1},{8,10},{9,11},{10,... | collective-permute-start | bytes 24584 | tf_op jit(solution)/shard_map/ppermute | solution.py:16
  56.8 1.3 collective-permute-start.12
  58.9 0.9 collective-permute-done.11
  59.8 0.7 collective-permute-done.12
  61.5 1.0 reshape.690
  62.5 5.0 %all-to-all-start = ((f32[8,1,8192]{2,1,0:T(1,128)}), f32[8,1,8192]{2,1,0:T(1,128)S(1)}, u32[]{:S(2)}, u32[]{:S(2)}) async-start(f32[8,1,8192]{2,1,0:T(1,128)} %reshape.690), calls=%async_computation | async-start | bytes 524288 | tf_op jit(solution)/shard_map/all_to_all | solution.py:106
  68.1 7.6 %all-to-all-done = f32[8,1,8192]{2,1,0:T(1,128)S(1)} async-done(((f32[8,1,8192]{2,1,0:T(1,128)}), f32[8,1,8192]{2,1,0:T(1,128)S(1)}, u32[]{:S(2)}, u32[]{:S(2)}) %all-to-all-start) | async-done | bytes 262176 | tf_op jit(solution)/shard_map/all_to_all | solution.py:106
  76.3 1.3 reduce.4
  78.0 1.4 %fusion.4 = f32[3072,192]{0,1:T(8,128)S(1)} fusion(s32[3072]{0:T(1024)S(1)} %copy-done.13, bf16[512,64]{1,0:T(8,128)(2,1)S(1)} %get-tuple-element.97, bf16[512,64]{1,0:T(8,128)(2,1)S(1)} %get-tuple-element.96, bf16[512,64]{1,0:T(8,128)(2,1)S(1)} %get-tuple-element.95), kind=kOutput, calls=%fused_computation.6 | convolution fusion | flops 609288192 | bytes 2568192 | tf_op jit(solution)/shard_map/dot_general | solution.py:276
  79.8 0.8 fusion.20
  80.6 1.5 %slice_add_fusion.8 = f32[1536,256]{0,1:T(8,128)} fusion(f32[4608,256]{0,1:T(8,128)S(1)} %fusion.20), kind=kLoop, calls=%fused_computation.30 | loop fusion | flops 786432 | bytes 6291456 | tf_op jit(solution)/shard_map/add | solution.py:284
  82.2 1.2 reduce-precision_convert_fusion.19
  83.5 1.3 fusion.3
  85.0 0.8 fusion.26
  86.5 1.3 fusion.2
  88.1 0.8 fusion.32
  101.3 1.3 fusion.1
  102.8 0.8 fusion.38
  104.3 1.3 fusion
  105.8 0.8 fusion.44
  111.2 4.7 %collective-permute-start.19 = (f32[1,16,16,1]{2,1,3,0:T(8,128)S(1)}, f32[1,16,16,1]{2,1,3,0:T(8,128)S(1)}, u32[]{:S(2)}, u32[]{:S(2)}) collective-permute-start(f32[1,16,16,1]{2,1,3,0:T(8,128)S(1)} %bitcast.317), channel_id=1, source_target_pairs={{0,7},{1,0},{2,1},{3,2},{4,3},{5,4},{6,5},{7,6},{8,15},{9,8},{10,9... | collective-permute-start | bytes 3080 | tf_op jit(solution)/shard_map/ppermute | solution.py:16
  116.0 3.8 %collective-permute-start.17 = (f32[1,16,1,128]{3,1,2,0:T(8,128)S(1)}, f32[1,16,1,128]{3,1,2,0:T(8,128)S(1)}, u32[]{:S(2)}, u32[]{:S(2)}) collective-permute-start(f32[1,16,1,128]{3,1,2,0:T(8,128)S(1)} %get-tuple-element.116), channel_id=1, source_target_pairs={{0,6},{1,7},{2,0},{3,1},{4,2},{5,3},{6,4},{7,5},{8,14},{9,15},{10,... | collective-permute-start | bytes 24584 | tf_op jit(solution)/shard_map/ppermute | solution.py:16
  120.6 0.9 collective-permute-done.16
  122.0 1.1 collective-permute-start.20
  123.5 4.7 %collective-permute-start.24 = (f32[1,16,16,1]{2,1,3,0:T(8,128)S(1)}, f32[1,16,16,1]{2,1,3,0:T(8,128)S(1)}, u32[]{:S(2)}, u32[]{:S(2)}) collective-permute-start(f32[1,16,16,1]{2,1,3,0:T(8,128)S(1)} %bitcast.322), channel_id=1, source_target_pairs={{0,7},{1,0},{2,1},{3,2},{4,3},{5,4},{6,5},{7,6},{8,15},{9,8},{10,9... | collective-permute-start | bytes 3080 | tf_op jit(solution)/shard_map/ppermute | solution.py:16
  128.2 1.5 %collective-permute-start.21 = (f32[1,16,1,128]{3,1,2,0:T(8,128)S(1)}, f32[1,16,1,128]{3,1,2,0:T(8,128)S(1)}, u32[]{:S(2)}, u32[]{:S(2)}) collective-permute-start(f32[1,16,1,128]{3,1,2,0:T(8,128)S(1)} %get-tuple-element.105), channel_id=1, source_target_pairs={{0,2},{1,3},{2,4},{3,5},{4,6},{5,7},{6,0},{7,1},{8,10},{9,11},{10,... | collective-permute-start | bytes 24584 | tf_op jit(solution)/shard_map/ppermute | solution.py:16
  129.7 2.3 %collective-permute-start.22 = (f32[1,16,1,128]{3,1,2,0:T(8,128)S(1)}, f32[1,16,1,128]{3,1,2,0:T(8,128)S(1)}, u32[]{:S(2)}, u32[]{:S(2)}) collective-permute-start(f32[1,16,1,128]{3,1,2,0:T(8,128)S(1)} %get-tuple-element.104), channel_id=1, source_target_pairs={{0,6},{1,7},{2,0},{3,1},{4,2},{5,3},{6,4},{7,5},{8,14},{9,15},{10,... | collective-permute-start | bytes 24584 | tf_op jit(solution)/shard_map/ppermute | solution.py:16
  132.1 0.7 copy.1043
  133.9 0.7 copy.1044
  (365 shorter events, 31.1 us)
Async XLA Ops:
  9.1 27.4 %collective-permute-start = (f32[2,2,16,128]{3,1,2,0:T(2,128)S(1)}, f32[2,2,16,128]{3,1,2,0:T(2,128)S(1)}, u32[]{:S(2)}, u32[]{:S(2)}) collective-permute-start(f32[2,2,16,128]{3,1,2,0:T(2,128)S(1)} %maximum_maximum_fusion), channel_id=1, source_target_pairs={{0,4},{1,5},{2,6},{3,7},{4,0},{5,1},{6,2},{7,3},{8,12},{9,13},{10,... | collective-permute-start | bytes 98312 | tf_op jit(solution)/shard_map/ppermute | solution.py:16
  20.8 15.0 %collective-permute-start.3 = (f32[2,16,16,1]{2,1,3,0:T(8,128)S(1)}, f32[2,16,16,1]{2,1,3,0:T(8,128)S(1)}, u32[]{:S(2)}, u32[]{:S(2)}) collective-permute-start(f32[2,16,16,1]{2,1,3,0:T(8,128)S(1)} %pad_maximum_fusion.14), channel_id=1, source_target_pairs={{0,1},{1,2},{2,3},{3,4},{4,5},{5,6},{6,7},{7,0},{8,9},{9,10},{10,1... | collective-permute-start | bytes 6152 | tf_op jit(solution)/shard_map/ppermute | solution.py:16
  22.7 13.0 %collective-permute-start.4 = (f32[2,16,16,1]{2,1,3,0:T(8,128)S(1)}, f32[2,16,16,1]{2,1,3,0:T(8,128)S(1)}, u32[]{:S(2)}, u32[]{:S(2)}) collective-permute-start(f32[2,16,16,1]{2,1,3,0:T(8,128)S(1)} %pad_maximum_fusion.15), channel_id=1, source_target_pairs={{0,7},{1,0},{2,1},{3,2},{4,3},{5,4},{6,5},{7,6},{8,15},{9,8},{10,9... | collective-permute-start | bytes 6152 | tf_op jit(solution)/shard_map/ppermute | solution.py:16
  25.9 10.5 %collective-permute-start.1 = (f32[2,16,1,128]{3,1,2,0:T(8,128)S(1)}, f32[2,16,1,128]{3,1,2,0:T(8,128)S(1)}, u32[]{:S(2)}, u32[]{:S(2)}) collective-permute-start(f32[2,16,1,128]{3,1,2,0:T(8,128)S(1)} %pad_maximum_fusion.12), channel_id=1, source_target_pairs={{0,2},{1,3},{2,4},{3,5},{4,6},{5,7},{6,0},{7,1},{8,10},{9,11},{10,... | collective-permute-start | bytes 49160 | tf_op jit(solution)/shard_map/ppermute | solution.py:16
  26.0 10.5 %collective-permute-start.2 = (f32[2,16,1,128]{3,1,2,0:T(8,128)S(1)}, f32[2,16,1,128]{3,1,2,0:T(8,128)S(1)}, u32[]{:S(2)}, u32[]{:S(2)}) collective-permute-start(f32[2,16,1,128]{3,1,2,0:T(8,128)S(1)} %pad_maximum_fusion.13), channel_id=1, source_target_pairs={{0,6},{1,7},{2,0},{3,1},{4,2},{5,3},{6,4},{7,5},{8,14},{9,15},{10,... | collective-permute-start | bytes 49160 | tf_op jit(solution)/shard_map/ppermute | solution.py:16
  29.9 4.3 %copy-start.4 = (s32[16]{0:T(128)S(1)}, s32[16]{0:T(128)}, u32[]{:S(2)}) copy-start(s32[16]{0:T(128)} %param.7) | copy-start | bytes 196
  30.0 4.9 %copy-start.5 = (f32[16]{0:T(128)S(1)}, f32[16]{0:T(128)}, u32[]{:S(2)}) copy-start(f32[16]{0:T(128)} %param.8) | copy-start | bytes 196
  30.0 6.5 %copy-start = (f32[1,16,16,128]{3,2,1,0:T(8,128)S(1)}, f32[1,16,16,128]{3,2,1,0:T(8,128)}, u32[]{:S(2)}) copy-start(f32[1,16,16,128]{3,2,1,0:T(8,128)} %param.9) | copy-start | bytes 393220
  32.8 0.7 copy-start.14
  33.5 3.1 %copy-start.12 = (s32[3072]{0:T(1024)}, s32[3072]{0:T(1024)S(1)}, u32[]{:S(2)}) copy-start(s32[3072]{0:T(1024)S(1)} %constant_dynamic-update-slice_fusion.4) | copy-start | bytes 36868
  38.2 8.8 %collective-permute-start.8 = (f32[1,16,16,1]{2,1,3,0:T(8,128)S(1)}, f32[1,16,16,1]{2,1,3,0:T(8,128)S(1)}, u32[]{:S(2)}, u32[]{:S(2)}) collective-permute-start(f32[1,16,16,1]{2,1,3,0:T(8,128)S(1)} %bitcast.310), channel_id=1, source_target_pairs={{0,1},{1,2},{2,3},{3,4},{4,5},{5,6},{6,7},{7,0},{8,9},{9,10},{10,1... | collective-permute-start | bytes 3080 | tf_op jit(solution)/shard_map/ppermute | solution.py:16
  38.4 8.8 %collective-permute-start.9 = (f32[1,16,16,1]{2,1,3,0:T(8,128)S(1)}, f32[1,16,16,1]{2,1,3,0:T(8,128)S(1)}, u32[]{:S(2)}, u32[]{:S(2)}) collective-permute-start(f32[1,16,16,1]{2,1,3,0:T(8,128)S(1)} %bitcast.315), channel_id=1, source_target_pairs={{0,7},{1,0},{2,1},{3,2},{4,3},{5,4},{6,5},{7,6},{8,15},{9,8},{10,9... | collective-permute-start | bytes 3080 | tf_op jit(solution)/shard_map/ppermute | solution.py:16
  43.1 4.6 %collective-permute-start.5 = (f32[1,2,16,128]{3,2,1,0:T(8,128)S(1)}, f32[1,2,16,128]{3,2,1,0:T(8,128)S(1)}, u32[]{:S(2)}, u32[]{:S(2)}) collective-permute-start(f32[1,2,16,128]{3,2,1,0:T(8,128)S(1)} %pad_maximum_fusion.16), channel_id=1, source_target_pairs={{0,4},{1,5},{2,6},{3,7},{4,0},{5,1},{6,2},{7,3},{8,12},{9,13},{10,... | collective-permute-start | bytes 49160 | tf_op jit(solution)/shard_map/ppermute | solution.py:16
  43.1 5.5 %collective-permute-start.6 = (f32[1,16,1,128]{3,1,2,0:T(8,128)S(1)}, f32[1,16,1,128]{3,1,2,0:T(8,128)S(1)}, u32[]{:S(2)}, u32[]{:S(2)}) collective-permute-start(f32[1,16,1,128]{3,1,2,0:T(8,128)S(1)} %get-tuple-element.156), channel_id=1, source_target_pairs={{0,2},{1,3},{2,4},{3,5},{4,6},{5,7},{6,0},{7,1},{8,10},{9,11},{10,... | collective-permute-start | bytes 24584 | tf_op jit(solution)/shard_map/ppermute | solution.py:16
  43.2 5.4 %collective-permute-start.7 = (f32[1,16,1,128]{3,1,2,0:T(8,128)S(1)}, f32[1,16,1,128]{3,1,2,0:T(8,128)S(1)}, u32[]{:S(2)}, u32[]{:S(2)}) collective-permute-start(f32[1,16,1,128]{3,1,2,0:T(8,128)S(1)} %get-tuple-element.155), channel_id=1, source_target_pairs={{0,6},{1,7},{2,0},{3,1},{4,2},{5,3},{6,4},{7,5},{8,14},{9,15},{10,... | collective-permute-start | bytes 24584 | tf_op jit(solution)/shard_map/ppermute | solution.py:16
  49.3 8.8 %collective-permute-start.13 = (f32[1,16,16,1]{2,1,3,0:T(8,128)S(1)}, f32[1,16,16,1]{2,1,3,0:T(8,128)S(1)}, u32[]{:S(2)}, u32[]{:S(2)}) collective-permute-start(f32[1,16,16,1]{2,1,3,0:T(8,128)S(1)} %bitcast.312), channel_id=1, source_target_pairs={{0,1},{1,2},{2,3},{3,4},{4,5},{5,6},{6,7},{7,0},{8,9},{9,10},{10,1... | collective-permute-start | bytes 3080 | tf_op jit(solution)/shard_map/ppermute | solution.py:16
  49.5 8.8 %collective-permute-start.14 = (f32[1,16,16,1]{2,1,3,0:T(8,128)S(1)}, f32[1,16,16,1]{2,1,3,0:T(8,128)S(1)}, u32[]{:S(2)}, u32[]{:S(2)}) collective-permute-start(f32[1,16,16,1]{2,1,3,0:T(8,128)S(1)} %bitcast.319), channel_id=1, source_target_pairs={{0,7},{1,0},{2,1},{3,2},{4,3},{5,4},{6,5},{7,6},{8,15},{9,8},{10,9... | collective-permute-start | bytes 3080 | tf_op jit(solution)/shard_map/ppermute | solution.py:16
  54.3 4.6 %collective-permute-start.10 = (f32[1,2,16,128]{3,2,1,0:T(8,128)S(1)}, f32[1,2,16,128]{3,2,1,0:T(8,128)S(1)}, u32[]{:S(2)}, u32[]{:S(2)}) collective-permute-start(f32[1,2,16,128]{3,2,1,0:T(8,128)S(1)} %pad_maximum_fusion.17), channel_id=1, source_target_pairs={{0,4},{1,5},{2,6},{3,7},{4,0},{5,1},{6,2},{7,3},{8,12},{9,13},{10,... | collective-permute-start | bytes 49160 | tf_op jit(solution)/shard_map/ppermute | solution.py:16
  54.3 5.5 %collective-permute-start.11 = (f32[1,16,1,128]{3,1,2,0:T(8,128)S(1)}, f32[1,16,1,128]{3,1,2,0:T(8,128)S(1)}, u32[]{:S(2)}, u32[]{:S(2)}) collective-permute-start(f32[1,16,1,128]{3,1,2,0:T(8,128)S(1)} %get-tuple-element.144), channel_id=1, source_target_pairs={{0,2},{1,3},{2,4},{3,5},{4,6},{5,7},{6,0},{7,1},{8,10},{9,11},{10,... | collective-permute-start | bytes 24584 | tf_op jit(solution)/shard_map/ppermute | solution.py:16
  56.8 3.7 %collective-permute-start.12 = (f32[1,16,1,128]{3,1,2,0:T(8,128)S(1)}, f32[1,16,1,128]{3,1,2,0:T(8,128)S(1)}, u32[]{:S(2)}, u32[]{:S(2)}) collective-permute-start(f32[1,16,1,128]{3,1,2,0:T(8,128)S(1)} %get-tuple-element.143), channel_id=1, source_target_pairs={{0,6},{1,7},{2,0},{3,1},{4,2},{5,3},{6,4},{7,5},{8,14},{9,15},{10,... | collective-permute-start | bytes 24584 | tf_op jit(solution)/shard_map/ppermute | solution.py:16
  60.7 6.8 %copy-start.15 = (s32[768]{0:T(1024)S(1)}, s32[768]{0:T(1024)}, u32[]{:S(2)}) copy-start(s32[768]{0:T(1024)} %copy-done.14) | copy-start | bytes 9220
  60.7 6.9 %copy-start.6 = (s32[32]{0:T(128)S(1)}, s32[32]{0:T(128)}, u32[]{:S(2)}) copy-start(s32[32]{0:T(128)} %get-tuple-element.294) | copy-start | bytes 388
  60.7 6.9 %copy-start.7 = (s32[32]{0:T(128)S(1)}, s32[32]{0:T(128)}, u32[]{:S(2)}) copy-start(s32[32]{0:T(128)} %get-tuple-element.295) | copy-start | bytes 388
  60.7 6.9 %copy-start.8 = (s32[32]{0:T(128)S(1)}, s32[32]{0:T(128)}, u32[]{:S(2)}) copy-start(s32[32]{0:T(128)} %get-tuple-element.296) | copy-start | bytes 388
  60.7 6.9 %copy-start.9 = (s32[32]{0:T(128)S(1)}, s32[32]{0:T(128)}, u32[]{:S(2)}) copy-start(s32[32]{0:T(128)} %get-tuple-element.297) | copy-start | bytes 388
  60.7 6.9 %copy-start.10 = (s32[32]{0:T(128)S(1)}, s32[32]{0:T(128)}, u32[]{:S(2)}) copy-start(s32[32]{0:T(128)} %get-tuple-element.298) | copy-start | bytes 388
  60.7 6.9 %copy-start.11 = (s32[32]{0:T(128)S(1)}, s32[32]{0:T(128)}, u32[]{:S(2)}) copy-start(s32[32]{0:T(128)} %multiply_add_fusion.3) | copy-start | bytes 388
  60.8 7.1 %copy-start.1 = (pred[64]{0:T(512)(128)(4,1)S(1)}, pred[64]{0:T(512)(128)(4,1)}, u32[]{:S(2)}) copy-start(pred[64]{0:T(512)(128)(4,1)} %get-tuple-element.307) | copy-start | bytes 196
  60.8 7.1 %copy-start.2 = (pred[64]{0:T(512)(128)(4,1)S(1)}, pred[64]{0:T(512)(128)(4,1)}, u32[]{:S(2)}) copy-start(pred[64]{0:T(512)(128)(4,1)} %get-tuple-element.308) | copy-start | bytes 196
  62.5 13.2 %all-to-all-start = ((f32[8,1,8192]{2,1,0:T(1,128)}), f32[8,1,8192]{2,1,0:T(1,128)S(1)}, u32[]{:S(2)}, u32[]{:S(2)}) async-start(f32[8,1,8192]{2,1,0:T(1,128)} %reshape.690), calls=%async_computation | async-start | bytes 524288 | tf_op jit(solution)/shard_map/all_to_all | solution.py:106
  67.5 24.1 %copy-start.16 = (s32[768]{0:T(1024)}, s32[768]{0:T(1024)S(1)}, u32[]{:S(2)}) copy-start(s32[768]{0:T(1024)S(1)} %constant_dynamic-update-slice_fusion.8) | copy-start | bytes 9220
  68.0 10.0 %copy-start.13 = (s32[3072]{0:T(1024)S(1)}, s32[3072]{0:T(1024)}, u32[]{:S(2)}) copy-start(s32[3072]{0:T(1024)} %copy-done.12) | copy-start | bytes 36868
  89.3 0.9 copy-start.3
  91.9 0.7 copy-start.17
  111.0 8.8 %collective-permute-start.18 = (f32[1,16,16,1]{2,1,3,0:T(8,128)S(1)}, f32[1,16,16,1]{2,1,3,0:T(8,128)S(1)}, u32[]{:S(2)}, u32[]{:S(2)}) collective-permute-start(f32[1,16,16,1]{2,1,3,0:T(8,128)S(1)} %bitcast.313), channel_id=1, source_target_pairs={{0,1},{1,2},{2,3},{3,4},{4,5},{5,6},{6,7},{7,0},{8,9},{9,10},{10,1... | collective-permute-start | bytes 3080 | tf_op jit(solution)/shard_map/ppermute | solution.py:16
  111.2 8.8 %collective-permute-start.19 = (f32[1,16,16,1]{2,1,3,0:T(8,128)S(1)}, f32[1,16,16,1]{2,1,3,0:T(8,128)S(1)}, u32[]{:S(2)}, u32[]{:S(2)}) collective-permute-start(f32[1,16,16,1]{2,1,3,0:T(8,128)S(1)} %bitcast.317), channel_id=1, source_target_pairs={{0,7},{1,0},{2,1},{3,2},{4,3},{5,4},{6,5},{7,6},{8,15},{9,8},{10,9... | collective-permute-start | bytes 3080 | tf_op jit(solution)/shard_map/ppermute | solution.py:16
  116.0 4.6 %collective-permute-start.15 = (f32[1,2,16,128]{3,2,1,0:T(8,128)S(1)}, f32[1,2,16,128]{3,2,1,0:T(8,128)S(1)}, u32[]{:S(2)}, u32[]{:S(2)}) collective-permute-start(f32[1,2,16,128]{3,2,1,0:T(8,128)S(1)} %pad_maximum_fusion.18), channel_id=1, source_target_pairs={{0,4},{1,5},{2,6},{3,7},{4,0},{5,1},{6,2},{7,3},{8,12},{9,13},{10,... | collective-permute-start | bytes 49160 | tf_op jit(solution)/shard_map/ppermute | solution.py:16
  116.0 5.5 %collective-permute-start.16 = (f32[1,16,1,128]{3,1,2,0:T(8,128)S(1)}, f32[1,16,1,128]{3,1,2,0:T(8,128)S(1)}, u32[]{:S(2)}, u32[]{:S(2)}) collective-permute-start(f32[1,16,1,128]{3,1,2,0:T(8,128)S(1)} %get-tuple-element.117), channel_id=1, source_target_pairs={{0,2},{1,3},{2,4},{3,5},{4,6},{5,7},{6,0},{7,1},{8,10},{9,11},{10,... | collective-permute-start | bytes 24584 | tf_op jit(solution)/shard_map/ppermute | solution.py:16
  116.0 5.4 %collective-permute-start.17 = (f32[1,16,1,128]{3,1,2,0:T(8,128)S(1)}, f32[1,16,1,128]{3,1,2,0:T(8,128)S(1)}, u32[]{:S(2)}, u32[]{:S(2)}) collective-permute-start(f32[1,16,1,128]{3,1,2,0:T(8,128)S(1)} %get-tuple-element.116), channel_id=1, source_target_pairs={{0,6},{1,7},{2,0},{3,1},{4,2},{5,3},{6,4},{7,5},{8,14},{9,15},{10,... | collective-permute-start | bytes 24584 | tf_op jit(solution)/shard_map/ppermute | solution.py:16
  122.0 11.1 %collective-permute-start.20 = (f32[1,2,16,128]{3,2,1,0:T(8,128)S(1)}, f32[1,2,16,128]{3,2,1,0:T(8,128)S(1)}, u32[]{:S(2)}, u32[]{:S(2)}) collective-permute-start(f32[1,2,16,128]{3,2,1,0:T(8,128)S(1)} %pad_maximum_fusion.19), channel_id=1, source_target_pairs={{0,4},{1,5},{2,6},{3,7},{4,0},{5,1},{6,2},{7,3},{8,12},{9,13},{10,... | collective-permute-start | bytes 49160 | tf_op jit(solution)/shard_map/ppermute | solution.py:16
  123.3 9.5 %collective-permute-start.23 = (f32[1,16,16,1]{2,1,3,0:T(8,128)S(1)}, f32[1,16,16,1]{2,1,3,0:T(8,128)S(1)}, u32[]{:S(2)}, u32[]{:S(2)}) collective-permute-start(f32[1,16,16,1]{2,1,3,0:T(8,128)S(1)} %bitcast.320), channel_id=1, source_target_pairs={{0,1},{1,2},{2,3},{3,4},{4,5},{5,6},{6,7},{7,0},{8,9},{9,10},{10,1... | collective-permute-start | bytes 3080 | tf_op jit(solution)/shard_map/ppermute | solution.py:16
  123.5 9.4 %collective-permute-start.24 = (f32[1,16,16,1]{2,1,3,0:T(8,128)S(1)}, f32[1,16,16,1]{2,1,3,0:T(8,128)S(1)}, u32[]{:S(2)}, u32[]{:S(2)}) collective-permute-start(f32[1,16,16,1]{2,1,3,0:T(8,128)S(1)} %bitcast.322), channel_id=1, source_target_pairs={{0,7},{1,0},{2,1},{3,2},{4,3},{5,4},{6,5},{7,6},{8,15},{9,8},{10,9... | collective-permute-start | bytes 3080 | tf_op jit(solution)/shard_map/ppermute | solution.py:16
  128.2 5.4 %collective-permute-start.21 = (f32[1,16,1,128]{3,1,2,0:T(8,128)S(1)}, f32[1,16,1,128]{3,1,2,0:T(8,128)S(1)}, u32[]{:S(2)}, u32[]{:S(2)}) collective-permute-start(f32[1,16,1,128]{3,1,2,0:T(8,128)S(1)} %get-tuple-element.105), channel_id=1, source_target_pairs={{0,2},{1,3},{2,4},{3,5},{4,6},{5,7},{6,0},{7,1},{8,10},{9,11},{10,... | collective-permute-start | bytes 24584 | tf_op jit(solution)/shard_map/ppermute | solution.py:16
  129.7 3.9 %collective-permute-start.22 = (f32[1,16,1,128]{3,1,2,0:T(8,128)S(1)}, f32[1,16,1,128]{3,1,2,0:T(8,128)S(1)}, u32[]{:S(2)}, u32[]{:S(2)}) collective-permute-start(f32[1,16,1,128]{3,1,2,0:T(8,128)S(1)} %get-tuple-element.104), channel_id=1, source_target_pairs={{0,6},{1,7},{2,0},{3,1},{4,2},{5,3},{6,4},{7,5},{8,14},{9,15},{10,... | collective-permute-start | bytes 24584 | tf_op jit(solution)/shard_map/ppermute | solution.py:16

commit v9 on v7

--- a/solution.py
+++ b/solution.py
@@ -271,11 +271,18 @@
     return pieces
 
 
+def lane_tile(size):
+    return -(-size // 128) * 128
+
+
 def pick_rows(picker, values):
     size_z = values.shape[1]
-    joined = jnp.concatenate(split3(values), axis=1)
+    width = lane_tile(size_z)
+    joined = jnp.concatenate(
+        [jnp.pad(piece, ((0, 0), (0, width - size_z))) for piece in split3(values)], axis=1
+    )
     out = jnp.dot(picker, joined, preferred_element_type=jnp.float32)
-    return (out[:, :size_z] + out[:, size_z : 2 * size_z]) + out[:, 2 * size_z :]
+    return (out[:, :size_z] + out[:, width : width + size_z]) + out[:, 2 * width : 2 * width + size_z]
 
 
 def pick_lanes(values, shift):

time: 129 us -> 133 us (1.031)
  matrix products: 21.1 us -> 23.7 us
  local copies, waits for them, and re-layouts: 14.4 us -> 16.5 us
    dot_general x16, matrix products: 9.34 us -> 11.9 us  [pick_rows(): out = jnp.dot(picker, joined, preferred_element_type=jnp.float32)]
    unnamed x15 -> x39, local copies, waits for them, and re-layouts: 2.4 us -> 4.44 us
  transfers between devices with their start and end apart: 32 -> 32, of which waited for: 12 -> 12; matrix products, arithmetic and copies ran while one was open for 11% -> 10% of each run, Pallas kernels for 0% -> 0%
where the time goes in v9:
time: 133 us
  starting transfers between devices  59.5 us (45%)
  matrix products  23.7 us (18%)
  other arithmetic  22.3 us (17%)
  local copies, waits for them, and re-layouts  16.5 us (12%)
  waiting for transfers between devices  7.78 us (6%)
  between operations  2.77 us (2%)
    ppermute x32, starting transfers between devices, shifted(): lax.ppermute(shard, axis, [(i, (i + by) % peers) for i in range(peers)])  59.5 us
    add x2, other arithmetic, shards(): permeab = permeab + jnp.where(classes == number, class_values[number], 0.0)  12 us
    dot_general x16, matrix products, pick_rows(): out = jnp.dot(picker, joined, preferred_element_type=jnp.float32)  11.9 us
    ppermute x32, waiting for transfers between devices, shifted(): lax.ppermute(shard, axis, [(i, (i + by) % peers) for i in range(peers)])  7.78 us
    dot_general x16, matrix products, pick_lanes(): out = jnp.dot(stacked, shift, preferred_element_type=jnp.float32)  6.68 us
    unnamed x39, local copies, waits for them, and re-layouts  4.44 us
    add x16, other arithmetic, pick_lanes(): return out[:count_r] + out[count_r:2 * count_r] + out[2 * count_r:]  3.78 us
    convert_element_type x37, other arithmetic, split3(): pieces.append(piece.astype(jnp.bfloat16))  3.39 us
  transfers between devices with their start and end apart: 32, of which 12 were waited for; matrix products, arithmetic and copies ran while one was open for 10% of the time, Pallas kernels for 0%

profile of v9, /device:TPU:0, one launch (start us, length us, event | category | flops | bytes accessed | tf_op | source)
XLA Modules:
  0.0 132.6 jit_solution(14140602000528028799)
XLA Ops:
  0.6 1.6 %fusion.1256 = (f32[1]{0:T(128)}, f32[1]{0:T(128)}, f32[1]{0:T(128)}, f32[1]{0:T(128)}, f32[1]{0:T(128)}, /*index=5*/f32[1]{0:T(128)}, f32[1]{0:T(128)}, f32[1]{0:T(128)}) fusion(f32[8]{0:T(128)} %param.6), kind=kLoop, calls=%fused_computation.1815 | loop fusion | bytes 64 | tf_op jit(solution)/shard_map/slice | solution.py:394
  2.3 6.0 %add_add_fusion = f32[1,16,16,128]{3,1,2,0:T(8,128)S(1)} fusion(s32[1,16,16,128]{3,2,1,0:T(8,128)} %param.5, f32[]{:T(128)} %bitcast.10, f32[]{:T(128)} %bitcast.9, f32[]{:T(128)} %bitcast.8, f32[]{:T(128)} %bitcast.7, f32[]{:T(128)} %bitcast.6, f32[]{:T(128)} %bitcast.5, f32[]{:T(128)} %bitcast.4, f32[]{:T(128)} %bitcast.3), kind=kLoop, calls=%fused_computation.511 | loop fusion | flops 753664 | bytes 262176 | tf_op jit(solution)/shard_map/add | solution.py:394
  8.3 0.7 fusion.1251
  9.0 4.1 %collective-permute-start = (f32[2,2,16,128]{3,1,2,0:T(2,128)S(1)}, f32[2,2,16,128]{3,1,2,0:T(2,128)S(1)}, u32[]{:S(2)}, u32[]{:S(2)}) collective-permute-start(f32[2,2,16,128]{3,1,2,0:T(2,128)S(1)} %maximum_maximum_fusion), channel_id=1, source_target_pairs={{0,4},{1,5},{2,6},{3,7},{4,0},{5,1},{6,2},{7,3},{8,12},{9,13},{10,... | collective-permute-start | bytes 98312 | tf_op jit(solution)/shard_map/ppermute | solution.py:16
  13.1 6.0 %fusion.1285 = f32[16,16,128]{2,0,1:T(8,128)S(1)} fusion(f32[]{:T(128)} %bitcast.10, f32[]{:T(128)} %bitcast.9, f32[]{:T(128)} %bitcast.8, f32[]{:T(128)} %bitcast.7, f32[]{:T(128)} %bitcast.6, f32[]{:T(128)} %bitcast.5, f32[]{:T(128)} %bitcast.4, f32[]{:T(128)} %bitcast.3, s32[1,16,16,128]{3,2,1,0:T(8,128)} %param.5), kind=kLoop, calls=%fused_computation.1816 | loop fusion | flops 753664 | bytes 262176 | tf_op jit(solution)/shard_map/add | solution.py:394
  19.1 1.0 copy.1317
  20.6 1.6 %collective-permute-start.3 = (f32[2,16,16,1]{2,1,3,0:T(8,128)S(1)}, f32[2,16,16,1]{2,1,3,0:T(8,128)S(1)}, u32[]{:S(2)}, u32[]{:S(2)}) collective-permute-start(f32[2,16,16,1]{2,1,3,0:T(8,128)S(1)} %pad_maximum_fusion.14), channel_id=1, source_target_pairs={{0,1},{1,2},{2,3},{3,4},{4,5},{5,6},{6,7},{7,0},{8,9},{9,10},{10,1... | collective-permute-start | bytes 6152 | tf_op jit(solution)/shard_map/ppermute | solution.py:16
  22.6 3.2 %collective-permute-start.4 = (f32[2,16,16,1]{2,1,3,0:T(8,128)S(1)}, f32[2,16,16,1]{2,1,3,0:T(8,128)S(1)}, u32[]{:S(2)}, u32[]{:S(2)}) collective-permute-start(f32[2,16,16,1]{2,1,3,0:T(8,128)S(1)} %pad_maximum_fusion.15), channel_id=1, source_target_pairs={{0,7},{1,0},{2,1},{3,2},{4,3},{5,4},{6,5},{7,6},{8,15},{9,8},{10,9... | collective-permute-start | bytes 6152 | tf_op jit(solution)/shard_map/ppermute | solution.py:16
  25.9 3.8 %collective-permute-start.2 = (f32[2,16,1,128]{3,1,2,0:T(8,128)S(1)}, f32[2,16,1,128]{3,1,2,0:T(8,128)S(1)}, u32[]{:S(2)}, u32[]{:S(2)}) collective-permute-start(f32[2,16,1,128]{3,1,2,0:T(8,128)S(1)} %pad_maximum_fusion.13), channel_id=1, source_target_pairs={{0,6},{1,7},{2,0},{3,1},{4,2},{5,3},{6,4},{7,5},{8,14},{9,15},{10,... | collective-permute-start | bytes 49160 | tf_op jit(solution)/shard_map/ppermute | solution.py:16
  34.1 4.7 %collective-permute-start.9 = (f32[1,16,16,1]{2,1,3,0:T(8,128)S(1)}, f32[1,16,16,1]{2,1,3,0:T(8,128)S(1)}, u32[]{:S(2)}, u32[]{:S(2)}) collective-permute-start(f32[1,16,16,1]{2,1,3,0:T(8,128)S(1)} %bitcast.333), channel_id=1, source_target_pairs={{0,7},{1,0},{2,1},{3,2},{4,3},{5,4},{6,5},{7,6},{8,15},{9,8},{10,9... | collective-permute-start | bytes 3080 | tf_op jit(solution)/shard_map/ppermute | solution.py:16
  38.8 1.1 collective-permute-start.6
  39.9 2.8 %collective-permute-start.7 = (f32[1,16,1,128]{3,1,2,0:T(8,128)S(1)}, f32[1,16,1,128]{3,1,2,0:T(8,128)S(1)}, u32[]{:S(2)}, u32[]{:S(2)}) collective-permute-start(f32[1,16,1,128]{3,1,2,0:T(8,128)S(1)} %get-tuple-element.155), channel_id=1, source_target_pairs={{0,6},{1,7},{2,0},{3,1},{4,2},{5,3},{6,4},{7,5},{8,14},{9,15},{10,... | collective-permute-start | bytes 24584 | tf_op jit(solution)/shard_map/ppermute | solution.py:16
  43.5 0.9 collective-permute-done.6
  45.2 4.7 %collective-permute-start.14 = (f32[1,16,16,1]{2,1,3,0:T(8,128)S(1)}, f32[1,16,16,1]{2,1,3,0:T(8,128)S(1)}, u32[]{:S(2)}, u32[]{:S(2)}) collective-permute-start(f32[1,16,16,1]{2,1,3,0:T(8,128)S(1)} %bitcast.337), channel_id=1, source_target_pairs={{0,7},{1,0},{2,1},{3,2},{4,3},{5,4},{6,5},{7,6},{8,15},{9,8},{10,9... | collective-permute-start | bytes 3080 | tf_op jit(solution)/shard_map/ppermute | solution.py:16
  50.0 2.6 %collective-permute-start.11 = (f32[1,16,1,128]{3,1,2,0:T(8,128)S(1)}, f32[1,16,1,128]{3,1,2,0:T(8,128)S(1)}, u32[]{:S(2)}, u32[]{:S(2)}) collective-permute-start(f32[1,16,1,128]{3,1,2,0:T(8,128)S(1)} %get-tuple-element.144), channel_id=1, source_target_pairs={{0,2},{1,3},{2,4},{3,5},{4,6},{5,7},{6,0},{7,1},{8,10},{9,11},{10,... | collective-permute-start | bytes 24584 | tf_op jit(solution)/shard_map/ppermute | solution.py:16
  52.5 1.3 collective-permute-start.12
  54.6 0.9 collective-permute-done.11
  55.5 0.7 collective-permute-done.12
  57.5 1.2 collective-permute-start.16
  58.7 3.5 %collective-permute-start.17 = (f32[2,8,8,64]{3,2,1,0:T(8,128)S(1)}, f32[2,8,8,64]{3,2,1,0:T(8,128)S(1)}, u32[]{:S(2)}, u32[]{:S(2)}) collective-permute-start(f32[2,8,8,64]{3,2,1,0:T(8,128)S(1)} %pad_maximum_fusion.5), channel_id=1, source_target_pairs={{0,3},{1,4},{2,5},{3,6},{4,7},{5,0},{6,1},{7,2},{8,11},{9,12},{10,... | collective-permute-start | bytes 98312 | tf_op jit(solution)/shard_map/ppermute | solution.py:16
  62.3 1.8 %collective-permute-start.18 = (f32[2,8,8,64]{3,2,1,0:T(8,128)S(1)}, f32[2,8,8,64]{3,2,1,0:T(8,128)S(1)}, u32[]{:S(2)}, u32[]{:S(2)}) collective-permute-start(f32[2,8,8,64]{3,2,1,0:T(8,128)S(1)} %pad_maximum_fusion.5), channel_id=1, source_target_pairs={{0,4},{1,5},{2,6},{3,7},{4,0},{5,1},{6,2},{7,3},{8,12},{9,13},{10,... | collective-permute-start | bytes 98312 | tf_op jit(solution)/shard_map/ppermute | solution.py:16
  64.0 1.9 %collective-permute-start.19 = (f32[2,8,8,64]{3,2,1,0:T(8,128)S(1)}, f32[2,8,8,64]{3,2,1,0:T(8,128)S(1)}, u32[]{:S(2)}, u32[]{:S(2)}) collective-permute-start(f32[2,8,8,64]{3,2,1,0:T(8,128)S(1)} %pad_maximum_fusion.5), channel_id=1, source_target_pairs={{0,5},{1,6},{2,7},{3,0},{4,1},{5,2},{6,3},{7,4},{8,13},{9,14},{10,... | collective-permute-start | bytes 98312 | tf_op jit(solution)/shard_map/ppermute | solution.py:16
  66.4 1.8 %collective-permute-start.21 = (f32[2,8,8,64]{3,2,1,0:T(8,128)S(1)}, f32[2,8,8,64]{3,2,1,0:T(8,128)S(1)}, u32[]{:S(2)}, u32[]{:S(2)}) collective-permute-start(f32[2,8,8,64]{3,2,1,0:T(8,128)S(1)} %pad_maximum_fusion.5), channel_id=1, source_target_pairs={{0,7},{1,0},{2,1},{3,2},{4,3},{5,4},{6,5},{7,6},{8,15},{9,8},{10,9... | collective-permute-start | bytes 98312 | tf_op jit(solution)/shard_map/ppermute | solution.py:16
  69.2 1.0 collective-permute-done.20
  72.2 1.6 %fusion.4 = f32[3072,384]{0,1:T(8,128)S(1)} fusion(s32[3072]{0:T(1024)S(1)} %copy-done.4, bf16[512,64]{1,0:T(8,128)(2,1)S(1)} %get-tuple-element.97, bf16[512,64]{1,0:T(8,128)(2,1)S(1)} %get-tuple-element.96, bf16[512,64]{1,0:T(8,128)(2,1)S(1)} %get-tuple-element.95), kind=kOutput, calls=%fused_computation.7 | convolution fusion | flops 1215430656 | bytes 4927488 | tf_op jit(solution)/shard_map/dot_general | solution.py:284
  74.2 0.8 fusion.33
  75.0 1.6 %slice_add_fusion.8 = f32[1536,256]{0,1:T(8,128)} fusion(f32[4608,256]{0,1:T(8,128)S(1)} %fusion.33), kind=kLoop, calls=%fused_computation.31 | loop fusion | flops 786432 | bytes 6291456 | tf_op jit(solution)/shard_map/add | solution.py:292
  76.7 1.3 reduce-precision_convert_fusion.19
  78.0 1.5 %fusion.3 = f32[3072,384]{0,1:T(8,128)S(1)} fusion(s32[3072]{0:T(1024)S(1)} %copy-done.4, bf16[512,64]{0,1:T(8,128)(2,1)S(1)} %get-tuple-element.136, bf16[512,64]{0,1:T(8,128)(2,1)S(1)} %get-tuple-element.135, bf16[512,64]{0,1:T(8,128)(2,1)S(1)} %get-tuple-element.56), kind=kOutput, calls=%fused_computation.6 | convolution fusion | flops 1215430656 | bytes 4927488 | tf_op jit(solution)/shard_map/dot_general | solution.py:284
  79.7 0.8 fusion.39
  81.2 1.5 %fusion.2 = f32[3072,384]{0,1:T(8,128)S(1)} fusion(s32[3072]{0:T(1024)S(1)} %copy-done.4, bf16[512,64]{0,1:T(8,128)(2,1)S(1)} %get-tuple-element.134, bf16[512,64]{0,1:T(8,128)(2,1)S(1)} %get-tuple-element.133, bf16[512,64]{0,1:T(8,128)(2,1)S(1)} %get-tuple-element.54), kind=kOutput, calls=%fused_computation.5 | convolution fusion | flops 1215430656 | bytes 4927488 | tf_op jit(solution)/shard_map/dot_general | solution.py:284
  83.0 0.8 fusion.45
  98.8 1.5 %fusion.1 = f32[3072,384]{0,1:T(8,128)S(1)} fusion(s32[3072]{0:T(1024)S(1)} %copy-done.5, bf16[512,64]{0,1:T(8,128)(2,1)S(1)} %get-tuple-element.131, bf16[512,64]{0,1:T(8,128)(2,1)S(1)} %get-tuple-element.132, bf16[512,64]{0,1:T(8,128)(2,1)S(1)} %get-tuple-element.130), kind=kOutput, calls=%fused_computation.4 | convolution fusion | flops 1215430656 | bytes 4927488 | tf_op jit(solution)/shard_map/dot_general | solution.py:284
  100.6 0.8 fusion.51
  102.1 1.5 %fusion = f32[3072,384]{0,1:T(8,128)S(1)} fusion(s32[3072]{0:T(1024)S(1)} %copy-done.5, bf16[512,64]{0,1:T(8,128)(2,1)S(1)} %get-tuple-element.129, bf16[512,64]{0,1:T(8,128)(2,1)S(1)} %get-tuple-element.128, bf16[512,64]{0,1:T(8,128)(2,1)S(1)} %get-tuple-element.24), kind=kOutput, calls=%fused_computation.3 | convolution fusion | flops 1215430656 | bytes 4927488 | tf_op jit(solution)/shard_map/dot_general | solution.py:284
  103.8 0.8 fusion.57
  109.0 2.7 %collective-permute-start.25 = (f32[1,16,16,1]{2,1,3,0:T(8,128)S(1)}, f32[1,16,16,1]{2,1,3,0:T(8,128)S(1)}, u32[]{:S(2)}, u32[]{:S(2)}) collective-permute-start(f32[1,16,16,1]{2,1,3,0:T(8,128)S(1)} %bitcast.331), channel_id=1, source_target_pairs={{0,1},{1,2},{2,3},{3,4},{4,5},{5,6},{6,7},{7,0},{8,9},{9,10},{10,1... | collective-permute-start | bytes 3080 | tf_op jit(solution)/shard_map/ppermute | solution.py:16
  111.8 2.1 %collective-permute-start.26 = (f32[1,16,16,1]{2,1,3,0:T(8,128)S(1)}, f32[1,16,16,1]{2,1,3,0:T(8,128)S(1)}, u32[]{:S(2)}, u32[]{:S(2)}) collective-permute-start(f32[1,16,16,1]{2,1,3,0:T(8,128)S(1)} %bitcast.335), channel_id=1, source_target_pairs={{0,7},{1,0},{2,1},{3,2},{4,3},{5,4},{6,5},{7,6},{8,15},{9,8},{10,9... | collective-permute-start | bytes 3080 | tf_op jit(solution)/shard_map/ppermute | solution.py:16
  114.0 0.7 collective-permute-start.23
  114.7 3.2 %collective-permute-start.24 = (f32[1,16,1,128]{3,1,2,0:T(8,128)S(1)}, f32[1,16,1,128]{3,1,2,0:T(8,128)S(1)}, u32[]{:S(2)}, u32[]{:S(2)}) collective-permute-start(f32[1,16,1,128]{3,1,2,0:T(8,128)S(1)} %get-tuple-element.116), channel_id=1, source_target_pairs={{0,6},{1,7},{2,0},{3,1},{4,2},{5,3},{6,4},{7,5},{8,14},{9,15},{10,... | collective-permute-start | bytes 24584 | tf_op jit(solution)/shard_map/ppermute | solution.py:16
  118.6 0.9 collective-permute-done.23
  120.0 1.1 collective-permute-start.27
  121.3 0.8 collective-permute-start.30
  122.2 4.0 %collective-permute-start.31 = (f32[1,16,16,1]{2,1,3,0:T(8,128)S(1)}, f32[1,16,16,1]{2,1,3,0:T(8,128)S(1)}, u32[]{:S(2)}, u32[]{:S(2)}) collective-permute-start(f32[1,16,16,1]{2,1,3,0:T(8,128)S(1)} %bitcast.340), channel_id=1, source_target_pairs={{0,7},{1,0},{2,1},{3,2},{4,3},{5,4},{6,5},{7,6},{8,15},{9,8},{10,9... | collective-permute-start | bytes 3080 | tf_op jit(solution)/shard_map/ppermute | solution.py:16
  126.2 1.5 %collective-permute-start.28 = (f32[1,16,1,128]{3,1,2,0:T(8,128)S(1)}, f32[1,16,1,128]{3,1,2,0:T(8,128)S(1)}, u32[]{:S(2)}, u32[]{:S(2)}) collective-permute-start(f32[1,16,1,128]{3,1,2,0:T(8,128)S(1)} %get-tuple-element.105), channel_id=1, source_target_pairs={{0,2},{1,3},{2,4},{3,5},{4,6},{5,7},{6,0},{7,1},{8,10},{9,11},{10,... | collective-permute-start | bytes 24584 | tf_op jit(solution)/shard_map/ppermute | solution.py:16
  127.7 2.3 %collective-permute-start.29 = (f32[1,16,1,128]{3,1,2,0:T(8,128)S(1)}, f32[1,16,1,128]{3,1,2,0:T(8,128)S(1)}, u32[]{:S(2)}, u32[]{:S(2)}) collective-permute-start(f32[1,16,1,128]{3,1,2,0:T(8,128)S(1)} %get-tuple-element.104), channel_id=1, source_target_pairs={{0,6},{1,7},{2,0},{3,1},{4,2},{5,3},{6,4},{7,5},{8,14},{9,15},{10,... | collective-permute-start | bytes 24584 | tf_op jit(solution)/shard_map/ppermute | solution.py:16
  130.1 0.7 copy.1278
  131.9 0.7 copy.1279
  (379 shorter events, 35.9 us)
Async XLA Ops:
  9.0 23.9 %collective-permute-start = (f32[2,2,16,128]{3,1,2,0:T(2,128)S(1)}, f32[2,2,16,128]{3,1,2,0:T(2,128)S(1)}, u32[]{:S(2)}, u32[]{:S(2)}) collective-permute-start(f32[2,2,16,128]{3,1,2,0:T(2,128)S(1)} %maximum_maximum_fusion), channel_id=1, source_target_pairs={{0,4},{1,5},{2,6},{3,7},{4,0},{5,1},{6,2},{7,3},{8,12},{9,13},{10,... | collective-permute-start | bytes 98312 | tf_op jit(solution)/shard_map/ppermute | solution.py:16
  20.6 11.5 %collective-permute-start.3 = (f32[2,16,16,1]{2,1,3,0:T(8,128)S(1)}, f32[2,16,16,1]{2,1,3,0:T(8,128)S(1)}, u32[]{:S(2)}, u32[]{:S(2)}) collective-permute-start(f32[2,16,16,1]{2,1,3,0:T(8,128)S(1)} %pad_maximum_fusion.14), channel_id=1, source_target_pairs={{0,1},{1,2},{2,3},{3,4},{4,5},{5,6},{6,7},{7,0},{8,9},{9,10},{10,1... | collective-permute-start | bytes 6152 | tf_op jit(solution)/shard_map/ppermute | solution.py:16
  22.6 9.6 %collective-permute-start.4 = (f32[2,16,16,1]{2,1,3,0:T(8,128)S(1)}, f32[2,16,16,1]{2,1,3,0:T(8,128)S(1)}, u32[]{:S(2)}, u32[]{:S(2)}) collective-permute-start(f32[2,16,16,1]{2,1,3,0:T(8,128)S(1)} %pad_maximum_fusion.15), channel_id=1, source_target_pairs={{0,7},{1,0},{2,1},{3,2},{4,3},{5,4},{6,5},{7,6},{8,15},{9,8},{10,9... | collective-permute-start | bytes 6152 | tf_op jit(solution)/shard_map/ppermute | solution.py:16
  25.8 7.0 %collective-permute-start.1 = (f32[2,16,1,128]{3,1,2,0:T(8,128)S(1)}, f32[2,16,1,128]{3,1,2,0:T(8,128)S(1)}, u32[]{:S(2)}, u32[]{:S(2)}) collective-permute-start(f32[2,16,1,128]{3,1,2,0:T(8,128)S(1)} %pad_maximum_fusion.12), channel_id=1, source_target_pairs={{0,2},{1,3},{2,4},{3,5},{4,6},{5,7},{6,0},{7,1},{8,10},{9,11},{10,... | collective-permute-start | bytes 49160 | tf_op jit(solution)/shard_map/ppermute | solution.py:16
  25.9 7.0 %collective-permute-start.2 = (f32[2,16,1,128]{3,1,2,0:T(8,128)S(1)}, f32[2,16,1,128]{3,1,2,0:T(8,128)S(1)}, u32[]{:S(2)}, u32[]{:S(2)}) collective-permute-start(f32[2,16,1,128]{3,1,2,0:T(8,128)S(1)} %pad_maximum_fusion.13), channel_id=1, source_target_pairs={{0,6},{1,7},{2,0},{3,1},{4,2},{5,3},{6,4},{7,5},{8,14},{9,15},{10,... | collective-permute-start | bytes 49160 | tf_op jit(solution)/shard_map/ppermute | solution.py:16
  29.8 1.7 %copy-start.1 = (s32[16]{0:T(128)S(1)}, s32[16]{0:T(128)}, u32[]{:S(2)}) copy-start(s32[16]{0:T(128)} %param.7) | copy-start | bytes 196
  29.8 1.7 %copy-start.2 = (f32[16]{0:T(128)S(1)}, f32[16]{0:T(128)}, u32[]{:S(2)}) copy-start(f32[16]{0:T(128)} %param.8) | copy-start | bytes 196
  29.9 3.1 %copy-start = (f32[1,16,16,128]{3,2,1,0:T(8,128)S(1)}, f32[1,16,16,128]{3,2,1,0:T(8,128)}, u32[]{:S(2)}) copy-start(f32[1,16,16,128]{3,2,1,0:T(8,128)} %param.9) | copy-start | bytes 393220
  30.5 2.9 %copy-start.3 = (s32[3072]{0:T(1024)}, s32[3072]{0:T(1024)S(1)}, u32[]{:S(2)}) copy-start(s32[3072]{0:T(1024)S(1)} %constant_dynamic-update-slice_fusion.4) | copy-start | bytes 36868
  33.9 8.8 %collective-permute-start.8 = (f32[1,16,16,1]{2,1,3,0:T(8,128)S(1)}, f32[1,16,16,1]{2,1,3,0:T(8,128)S(1)}, u32[]{:S(2)}, u32[]{:S(2)}) collective-permute-start(f32[1,16,16,1]{2,1,3,0:T(8,128)S(1)} %bitcast.328), channel_id=1, source_target_pairs={{0,1},{1,2},{2,3},{3,4},{4,5},{5,6},{6,7},{7,0},{8,9},{9,10},{10,1... | collective-permute-start | bytes 3080 | tf_op jit(solution)/shard_map/ppermute | solution.py:16
  34.1 8.8 %collective-permute-start.9 = (f32[1,16,16,1]{2,1,3,0:T(8,128)S(1)}, f32[1,16,16,1]{2,1,3,0:T(8,128)S(1)}, u32[]{:S(2)}, u32[]{:S(2)}) collective-permute-start(f32[1,16,16,1]{2,1,3,0:T(8,128)S(1)} %bitcast.333), channel_id=1, source_target_pairs={{0,7},{1,0},{2,1},{3,2},{4,3},{5,4},{6,5},{7,6},{8,15},{9,8},{10,9... | collective-permute-start | bytes 3080 | tf_op jit(solution)/shard_map/ppermute | solution.py:16
  38.8 4.6 %collective-permute-start.5 = (f32[1,2,16,128]{3,2,1,0:T(8,128)S(1)}, f32[1,2,16,128]{3,2,1,0:T(8,128)S(1)}, u32[]{:S(2)}, u32[]{:S(2)}) collective-permute-start(f32[1,2,16,128]{3,2,1,0:T(8,128)S(1)} %pad_maximum_fusion.16), channel_id=1, source_target_pairs={{0,4},{1,5},{2,6},{3,7},{4,0},{5,1},{6,2},{7,3},{8,12},{9,13},{10,... | collective-permute-start | bytes 49160 | tf_op jit(solution)/shard_map/ppermute | solution.py:16
  38.8 5.5 %collective-permute-start.6 = (f32[1,16,1,128]{3,1,2,0:T(8,128)S(1)}, f32[1,16,1,128]{3,1,2,0:T(8,128)S(1)}, u32[]{:S(2)}, u32[]{:S(2)}) collective-permute-start(f32[1,16,1,128]{3,1,2,0:T(8,128)S(1)} %get-tuple-element.156), channel_id=1, source_target_pairs={{0,2},{1,3},{2,4},{3,5},{4,6},{5,7},{6,0},{7,1},{8,10},{9,11},{10,... | collective-permute-start | bytes 24584 | tf_op jit(solution)/shard_map/ppermute | solution.py:16
  39.9 4.4 %collective-permute-start.7 = (f32[1,16,1,128]{3,1,2,0:T(8,128)S(1)}, f32[1,16,1,128]{3,1,2,0:T(8,128)S(1)}, u32[]{:S(2)}, u32[]{:S(2)}) collective-permute-start(f32[1,16,1,128]{3,1,2,0:T(8,128)S(1)} %get-tuple-element.155), channel_id=1, source_target_pairs={{0,6},{1,7},{2,0},{3,1},{4,2},{5,3},{6,4},{7,5},{8,14},{9,15},{10,... | collective-permute-start | bytes 24584 | tf_op jit(solution)/shard_map/ppermute | solution.py:16
  45.0 8.8 %collective-permute-start.13 = (f32[1,16,16,1]{2,1,3,0:T(8,128)S(1)}, f32[1,16,16,1]{2,1,3,0:T(8,128)S(1)}, u32[]{:S(2)}, u32[]{:S(2)}) collective-permute-start(f32[1,16,16,1]{2,1,3,0:T(8,128)S(1)} %bitcast.330), channel_id=1, source_target_pairs={{0,1},{1,2},{2,3},{3,4},{4,5},{5,6},{6,7},{7,0},{8,9},{9,10},{10,1... | collective-permute-start | bytes 3080 | tf_op jit(solution)/shard_map/ppermute | solution.py:16
  45.2 8.8 %collective-permute-start.14 = (f32[1,16,16,1]{2,1,3,0:T(8,128)S(1)}, f32[1,16,16,1]{2,1,3,0:T(8,128)S(1)}, u32[]{:S(2)}, u32[]{:S(2)}) collective-permute-start(f32[1,16,16,1]{2,1,3,0:T(8,128)S(1)} %bitcast.337), channel_id=1, source_target_pairs={{0,7},{1,0},{2,1},{3,2},{4,3},{5,4},{6,5},{7,6},{8,15},{9,8},{10,9... | collective-permute-start | bytes 3080 | tf_op jit(solution)/shard_map/ppermute | solution.py:16
  49.9 4.6 %collective-permute-start.10 = (f32[1,2,16,128]{3,2,1,0:T(8,128)S(1)}, f32[1,2,16,128]{3,2,1,0:T(8,128)S(1)}, u32[]{:S(2)}, u32[]{:S(2)}) collective-permute-start(f32[1,2,16,128]{3,2,1,0:T(8,128)S(1)} %pad_maximum_fusion.17), channel_id=1, source_target_pairs={{0,4},{1,5},{2,6},{3,7},{4,0},{5,1},{6,2},{7,3},{8,12},{9,13},{10,... | collective-permute-start | bytes 49160 | tf_op jit(solution)/shard_map/ppermute | solution.py:16
  50.0 5.5 %collective-permute-start.11 = (f32[1,16,1,128]{3,1,2,0:T(8,128)S(1)}, f32[1,16,1,128]{3,1,2,0:T(8,128)S(1)}, u32[]{:S(2)}, u32[]{:S(2)}) collective-permute-start(f32[1,16,1,128]{3,1,2,0:T(8,128)S(1)} %get-tuple-element.144), channel_id=1, source_target_pairs={{0,2},{1,3},{2,4},{3,5},{4,6},{5,7},{6,0},{7,1},{8,10},{9,11},{10,... | collective-permute-start | bytes 24584 | tf_op jit(solution)/shard_map/ppermute | solution.py:16
  52.5 3.7 %collective-permute-start.12 = (f32[1,16,1,128]{3,1,2,0:T(8,128)S(1)}, f32[1,16,1,128]{3,1,2,0:T(8,128)S(1)}, u32[]{:S(2)}, u32[]{:S(2)}) collective-permute-start(f32[1,16,1,128]{3,1,2,0:T(8,128)S(1)} %get-tuple-element.143), channel_id=1, source_target_pairs={{0,6},{1,7},{2,0},{3,1},{4,2},{5,3},{6,4},{7,5},{8,14},{9,15},{10,... | collective-permute-start | bytes 24584 | tf_op jit(solution)/shard_map/ppermute | solution.py:16
  57.0 8.9 %collective-permute-start.15 = (f32[2,8,8,64]{3,2,1,0:T(8,128)S(1)}, f32[2,8,8,64]{3,2,1,0:T(8,128)S(1)}, u32[]{:S(2)}, u32[]{:S(2)}) collective-permute-start(f32[2,8,8,64]{3,2,1,0:T(8,128)S(1)} %pad_maximum_fusion.5), channel_id=1, source_target_pairs={{0,1},{1,2},{2,3},{3,4},{4,5},{5,6},{6,7},{7,0},{8,9},{9,10},{10,1... | collective-permute-start | bytes 98312 | tf_op jit(solution)/shard_map/ppermute | solution.py:16
  57.5 8.9 %collective-permute-start.16 = (f32[2,8,8,64]{3,2,1,0:T(8,128)S(1)}, f32[2,8,8,64]{3,2,1,0:T(8,128)S(1)}, u32[]{:S(2)}, u32[]{:S(2)}) collective-permute-start(f32[2,8,8,64]{3,2,1,0:T(8,128)S(1)} %pad_maximum_fusion.5), channel_id=1, source_target_pairs={{0,2},{1,3},{2,4},{3,5},{4,6},{5,7},{6,0},{7,1},{8,10},{9,11},{10,... | collective-permute-start | bytes 98312 | tf_op jit(solution)/shard_map/ppermute | solution.py:16
  58.7 9.4 %collective-permute-start.17 = (f32[2,8,8,64]{3,2,1,0:T(8,128)S(1)}, f32[2,8,8,64]{3,2,1,0:T(8,128)S(1)}, u32[]{:S(2)}, u32[]{:S(2)}) collective-permute-start(f32[2,8,8,64]{3,2,1,0:T(8,128)S(1)} %pad_maximum_fusion.5), channel_id=1, source_target_pairs={{0,3},{1,4},{2,5},{3,6},{4,7},{5,0},{6,1},{7,2},{8,11},{9,12},{10,... | collective-permute-start | bytes 98312 | tf_op jit(solution)/shard_map/ppermute | solution.py:16
  62.3 6.6 %collective-permute-start.18 = (f32[2,8,8,64]{3,2,1,0:T(8,128)S(1)}, f32[2,8,8,64]{3,2,1,0:T(8,128)S(1)}, u32[]{:S(2)}, u32[]{:S(2)}) collective-permute-start(f32[2,8,8,64]{3,2,1,0:T(8,128)S(1)} %pad_maximum_fusion.5), channel_id=1, source_target_pairs={{0,4},{1,5},{2,6},{3,7},{4,0},{5,1},{6,2},{7,3},{8,12},{9,13},{10,... | collective-permute-start | bytes 98312 | tf_op jit(solution)/shard_map/ppermute | solution.py:16
  64.0 5.2 %collective-permute-start.19 = (f32[2,8,8,64]{3,2,1,0:T(8,128)S(1)}, f32[2,8,8,64]{3,2,1,0:T(8,128)S(1)}, u32[]{:S(2)}, u32[]{:S(2)}) collective-permute-start(f32[2,8,8,64]{3,2,1,0:T(8,128)S(1)} %pad_maximum_fusion.5), channel_id=1, source_target_pairs={{0,5},{1,6},{2,7},{3,0},{4,1},{5,2},{6,3},{7,4},{8,13},{9,14},{10,... | collective-permute-start | bytes 98312 | tf_op jit(solution)/shard_map/ppermute | solution.py:16
  65.9 4.4 %collective-permute-start.20 = (f32[2,8,8,64]{3,2,1,0:T(8,128)S(1)}, f32[2,8,8,64]{3,2,1,0:T(8,128)S(1)}, u32[]{:S(2)}, u32[]{:S(2)}) collective-permute-start(f32[2,8,8,64]{3,2,1,0:T(8,128)S(1)} %pad_maximum_fusion.5), channel_id=1, source_target_pairs={{0,6},{1,7},{2,0},{3,1},{4,2},{5,3},{6,4},{7,5},{8,14},{9,15},{10,... | collective-permute-start | bytes 98312 | tf_op jit(solution)/shard_map/ppermute | solution.py:16
  66.4 4.5 %collective-permute-start.21 = (f32[2,8,8,64]{3,2,1,0:T(8,128)S(1)}, f32[2,8,8,64]{3,2,1,0:T(8,128)S(1)}, u32[]{:S(2)}, u32[]{:S(2)}) collective-permute-start(f32[2,8,8,64]{3,2,1,0:T(8,128)S(1)} %pad_maximum_fusion.5), channel_id=1, source_target_pairs={{0,7},{1,0},{2,1},{3,2},{4,3},{5,4},{6,5},{7,6},{8,15},{9,8},{10,9... | collective-permute-start | bytes 98312 | tf_op jit(solution)/shard_map/ppermute | solution.py:16
  71.5 0.7 copy-start.4
  97.6 1.2 copy-start.5
  109.0 8.8 %collective-permute-start.25 = (f32[1,16,16,1]{2,1,3,0:T(8,128)S(1)}, f32[1,16,16,1]{2,1,3,0:T(8,128)S(1)}, u32[]{:S(2)}, u32[]{:S(2)}) collective-permute-start(f32[1,16,16,1]{2,1,3,0:T(8,128)S(1)} %bitcast.331), channel_id=1, source_target_pairs={{0,1},{1,2},{2,3},{3,4},{4,5},{5,6},{6,7},{7,0},{8,9},{9,10},{10,1... | collective-permute-start | bytes 3080 | tf_op jit(solution)/shard_map/ppermute | solution.py:16
  111.8 6.2 %collective-permute-start.26 = (f32[1,16,16,1]{2,1,3,0:T(8,128)S(1)}, f32[1,16,16,1]{2,1,3,0:T(8,128)S(1)}, u32[]{:S(2)}, u32[]{:S(2)}) collective-permute-start(f32[1,16,16,1]{2,1,3,0:T(8,128)S(1)} %bitcast.335), channel_id=1, source_target_pairs={{0,7},{1,0},{2,1},{3,2},{4,3},{5,4},{6,5},{7,6},{8,15},{9,8},{10,9... | collective-permute-start | bytes 3080 | tf_op jit(solution)/shard_map/ppermute | solution.py:16
  114.0 4.6 %collective-permute-start.22 = (f32[1,2,16,128]{3,2,1,0:T(8,128)S(1)}, f32[1,2,16,128]{3,2,1,0:T(8,128)S(1)}, u32[]{:S(2)}, u32[]{:S(2)}) collective-permute-start(f32[1,2,16,128]{3,2,1,0:T(8,128)S(1)} %pad_maximum_fusion.18), channel_id=1, source_target_pairs={{0,4},{1,5},{2,6},{3,7},{4,0},{5,1},{6,2},{7,3},{8,12},{9,13},{10,... | collective-permute-start | bytes 49160 | tf_op jit(solution)/shard_map/ppermute | solution.py:16
  114.0 5.5 %collective-permute-start.23 = (f32[1,16,1,128]{3,1,2,0:T(8,128)S(1)}, f32[1,16,1,128]{3,1,2,0:T(8,128)S(1)}, u32[]{:S(2)}, u32[]{:S(2)}) collective-permute-start(f32[1,16,1,128]{3,1,2,0:T(8,128)S(1)} %get-tuple-element.117), channel_id=1, source_target_pairs={{0,2},{1,3},{2,4},{3,5},{4,6},{5,7},{6,0},{7,1},{8,10},{9,11},{10,... | collective-permute-start | bytes 24584 | tf_op jit(solution)/shard_map/ppermute | solution.py:16
  114.7 4.8 %collective-permute-start.24 = (f32[1,16,1,128]{3,1,2,0:T(8,128)S(1)}, f32[1,16,1,128]{3,1,2,0:T(8,128)S(1)}, u32[]{:S(2)}, u32[]{:S(2)}) collective-permute-start(f32[1,16,1,128]{3,1,2,0:T(8,128)S(1)} %get-tuple-element.116), channel_id=1, source_target_pairs={{0,6},{1,7},{2,0},{3,1},{4,2},{5,3},{6,4},{7,5},{8,14},{9,15},{10,... | collective-permute-start | bytes 24584 | tf_op jit(solution)/shard_map/ppermute | solution.py:16
  120.0 11.1 %collective-permute-start.27 = (f32[1,2,16,128]{3,2,1,0:T(8,128)S(1)}, f32[1,2,16,128]{3,2,1,0:T(8,128)S(1)}, u32[]{:S(2)}, u32[]{:S(2)}) collective-permute-start(f32[1,2,16,128]{3,2,1,0:T(8,128)S(1)} %pad_maximum_fusion.19), channel_id=1, source_target_pairs={{0,4},{1,5},{2,6},{3,7},{4,0},{5,1},{6,2},{7,3},{8,12},{9,13},{10,... | collective-permute-start | bytes 49160 | tf_op jit(solution)/shard_map/ppermute | solution.py:16
  121.3 9.5 %collective-permute-start.30 = (f32[1,16,16,1]{2,1,3,0:T(8,128)S(1)}, f32[1,16,16,1]{2,1,3,0:T(8,128)S(1)}, u32[]{:S(2)}, u32[]{:S(2)}) collective-permute-start(f32[1,16,16,1]{2,1,3,0:T(8,128)S(1)} %bitcast.338), channel_id=1, source_target_pairs={{0,1},{1,2},{2,3},{3,4},{4,5},{5,6},{6,7},{7,0},{8,9},{9,10},{10,1... | collective-permute-start | bytes 3080 | tf_op jit(solution)/shard_map/ppermute | solution.py:16
  122.2 8.7 %collective-permute-start.31 = (f32[1,16,16,1]{2,1,3,0:T(8,128)S(1)}, f32[1,16,16,1]{2,1,3,0:T(8,128)S(1)}, u32[]{:S(2)}, u32[]{:S(2)}) collective-permute-start(f32[1,16,16,1]{2,1,3,0:T(8,128)S(1)} %bitcast.340), channel_id=1, source_target_pairs={{0,7},{1,0},{2,1},{3,2},{4,3},{5,4},{6,5},{7,6},{8,15},{9,8},{10,9... | collective-permute-start | bytes 3080 | tf_op jit(solution)/shard_map/ppermute | solution.py:16
  126.2 5.4 %collective-permute-start.28 = (f32[1,16,1,128]{3,1,2,0:T(8,128)S(1)}, f32[1,16,1,128]{3,1,2,0:T(8,128)S(1)}, u32[]{:S(2)}, u32[]{:S(2)}) collective-permute-start(f32[1,16,1,128]{3,1,2,0:T(8,128)S(1)} %get-tuple-element.105), channel_id=1, source_target_pairs={{0,2},{1,3},{2,4},{3,5},{4,6},{5,7},{6,0},{7,1},{8,10},{9,11},{10,... | collective-permute-start | bytes 24584 | tf_op jit(solution)/shard_map/ppermute | solution.py:16
  127.7 3.9 %collective-permute-start.29 = (f32[1,16,1,128]{3,1,2,0:T(8,128)S(1)}, f32[1,16,1,128]{3,1,2,0:T(8,128)S(1)}, u32[]{:S(2)}, u32[]{:S(2)}) collective-permute-start(f32[1,16,1,128]{3,1,2,0:T(8,128)S(1)} %get-tuple-element.104), channel_id=1, source_target_pairs={{0,6},{1,7},{2,0},{3,1},{4,2},{5,3},{6,4},{7,5},{8,14},{9,15},{10,... | collective-permute-start | bytes 24584 | tf_op jit(solution)/shard_map/ppermute | solution.py:16

commit v10 on v7

--- a/solution.py
+++ b/solution.py
@@ -382,9 +382,17 @@
     block_z = block_no % per_side
     classes = perm_class[0]
     width_x, width_y, width_z = classes.shape
-    permeab = jnp.zeros(classes.shape, jnp.float32)
-    for number in range(class_values.shape[0]):
-        permeab = permeab + jnp.where(classes == number, class_values[number], 0.0)
+    count_c = class_values.shape[0]
+    if count_c == 8:
+        low = jnp.where(classes < 2, jnp.where(classes < 1, class_values[0], class_values[1]),
+                        jnp.where(classes < 3, class_values[2], class_values[3]))
+        high = jnp.where(classes < 6, jnp.where(classes < 5, class_values[4], class_values[5]),
+                         jnp.where(classes < 7, class_values[6], class_values[7]))
+        permeab = jnp.where(classes < 4, low, high).astype(jnp.float32)
+    else:
+        permeab = jnp.zeros(classes.shape, jnp.float32)
+        for number in range(count_c):
+            permeab = permeab + jnp.where(classes == number, class_values[number], 0.0)
     row_len = per_side * width_z
     plane = per_side * width_y * row_len
     glob_x = well_cells // plane

time: 129 us -> 129 us (level)
    add x2 -> x0, other arithmetic: 12 us -> none  [shards(): permeab = permeab + jnp.where(classes == number, class_values[number], 0.0)]
    select_n x0 -> x2, other arithmetic: none -> 11.9 us  [shards(): permeab = jnp.where(classes < 4, low, high).astype(jnp.float32)]
where the time goes in v10:
time: 129 us; the launch traced here: 128 us
  starting transfers between devices  59.5 us (46%)
  other arithmetic  22.7 us (18%)
  matrix products  21.1 us (16%)
  local copies, waits for them, and re-layouts  14.4 us (11%)
  waiting for transfers between devices  7.78 us (6%)
  between operations  2.63 us (2%)
    ppermute x32, starting transfers between devices, shifted(): lax.ppermute(shard, axis, [(i, (i + by) % peers) for i in range(peers)])  59.5 us
    select_n x2, other arithmetic, shards(): permeab = jnp.where(classes < 4, low, high).astype(jnp.float32)  11.9 us
    dot_general x16, matrix products, pick_rows(): out = jnp.dot(picker, joined, preferred_element_type=jnp.float32)  9.34 us
    ppermute x32, waiting for transfers between devices, shifted(): lax.ppermute(shard, axis, [(i, (i + by) % peers) for i in range(peers)])  7.78 us
    dot_general x16, matrix products, pick_lanes(): out = jnp.dot(stacked, shift, preferred_element_type=jnp.float32)  6.68 us
    add x16, other arithmetic, pick_lanes(): return out[:count_r] + out[count_r:2 * count_r] + out[2 * count_r:]  3.78 us
    convert_element_type x37, other arithmetic, split3(): pieces.append(piece.astype(jnp.bfloat16))  3.61 us
  transfers between devices with their start and end apart: 32, of which 12 were waited for; matrix products, arithmetic and copies ran while one was open for 11% of the time, Pallas kernels for 0%

profile of v10, /device:TPU:0, one launch (start us, length us, event | category | flops | bytes accessed | tf_op | source)
XLA Modules:
  0.0 128.1 jit_solution(4141898678001377553)
XLA Ops:
  0.6 1.6 %fusion.1060 = (f32[1]{0:T(128)}, f32[1]{0:T(128)}, f32[1]{0:T(128)}, f32[1]{0:T(128)}, f32[1]{0:T(128)}, /*index=5*/f32[1]{0:T(128)}, f32[1]{0:T(128)}, f32[1]{0:T(128)}) fusion(f32[8]{0:T(128)} %param.6), kind=kLoop, calls=%fused_computation.1651 | loop fusion | bytes 64 | tf_op jit(solution)/shard_map/slice | solution.py:387
  2.2 6.0 %select_select_fusion = f32[1,16,16,128]{3,1,2,0:T(8,128)S(1)} fusion(s32[1,16,16,128]{3,2,1,0:T(8,128)} %param.5, f32[]{:T(128)} %bitcast.10, f32[]{:T(128)} %bitcast.9, f32[]{:T(128)} %bitcast.8, f32[]{:T(128)} %bitcast.7, f32[]{:T(128)} %bitcast.6, f32[]{:T(128)} %bitcast.5, f32[]{:T(128)} %bitcast.4, f32[]{:T(128)} %bitcast.3), kind=kLoop, calls=%fused_computation.469 | loop fusion | flops 458752 | bytes 262176 | tf_op jit(solution)/shard_map/jit(_where)/select_n | solution.py:391
  8.2 0.7 fusion.1055
  9.0 4.1 %collective-permute-start = (f32[2,2,16,128]{3,1,2,0:T(2,128)S(1)}, f32[2,2,16,128]{3,1,2,0:T(2,128)S(1)}, u32[]{:S(2)}, u32[]{:S(2)}) collective-permute-start(f32[2,2,16,128]{3,1,2,0:T(2,128)S(1)} %maximum_maximum_fusion), channel_id=1, source_target_pairs={{0,4},{1,5},{2,6},{3,7},{4,0},{5,1},{6,2},{7,3},{8,12},{9,13},{10,... | collective-permute-start | bytes 98312 | tf_op jit(solution)/shard_map/ppermute | solution.py:16
  13.1 6.0 %fusion.1089 = f32[16,16,128]{2,0,1:T(8,128)S(1)} fusion(f32[]{:T(128)} %bitcast.10, f32[]{:T(128)} %bitcast.9, f32[]{:T(128)} %bitcast.8, f32[]{:T(128)} %bitcast.7, f32[]{:T(128)} %bitcast.6, f32[]{:T(128)} %bitcast.5, f32[]{:T(128)} %bitcast.4, f32[]{:T(128)} %bitcast.3, s32[1,16,16,128]{3,2,1,0:T(8,128)} %param.5), kind=kLoop, calls=%fused_computation.1652 | loop fusion | flops 458752 | bytes 262176 | tf_op jit(solution)/shard_map/jit(_where)/select_n | solution.py:391
  19.1 1.0 copy.1022
  20.6 1.6 %collective-permute-start.3 = (f32[2,16,16,1]{2,1,3,0:T(8,128)S(1)}, f32[2,16,16,1]{2,1,3,0:T(8,128)S(1)}, u32[]{:S(2)}, u32[]{:S(2)}) collective-permute-start(f32[2,16,16,1]{2,1,3,0:T(8,128)S(1)} %pad_maximum_fusion.14), channel_id=1, source_target_pairs={{0,1},{1,2},{2,3},{3,4},{4,5},{5,6},{6,7},{7,0},{8,9},{9,10},{10,1... | collective-permute-start | bytes 6152 | tf_op jit(solution)/shard_map/ppermute | solution.py:16
  22.5 3.2 %collective-permute-start.4 = (f32[2,16,16,1]{2,1,3,0:T(8,128)S(1)}, f32[2,16,16,1]{2,1,3,0:T(8,128)S(1)}, u32[]{:S(2)}, u32[]{:S(2)}) collective-permute-start(f32[2,16,16,1]{2,1,3,0:T(8,128)S(1)} %pad_maximum_fusion.15), channel_id=1, source_target_pairs={{0,7},{1,0},{2,1},{3,2},{4,3},{5,4},{6,5},{7,6},{8,15},{9,8},{10,9... | collective-permute-start | bytes 6152 | tf_op jit(solution)/shard_map/ppermute | solution.py:16
  25.8 3.8 %collective-permute-start.2 = (f32[2,16,1,128]{3,1,2,0:T(8,128)S(1)}, f32[2,16,1,128]{3,1,2,0:T(8,128)S(1)}, u32[]{:S(2)}, u32[]{:S(2)}) collective-permute-start(f32[2,16,1,128]{3,1,2,0:T(8,128)S(1)} %pad_maximum_fusion.13), channel_id=1, source_target_pairs={{0,6},{1,7},{2,0},{3,1},{4,2},{5,3},{6,4},{7,5},{8,14},{9,15},{10,... | collective-permute-start | bytes 49160 | tf_op jit(solution)/shard_map/ppermute | solution.py:16
  34.0 4.7 %collective-permute-start.9 = (f32[1,16,16,1]{2,1,3,0:T(8,128)S(1)}, f32[1,16,16,1]{2,1,3,0:T(8,128)S(1)}, u32[]{:S(2)}, u32[]{:S(2)}) collective-permute-start(f32[1,16,16,1]{2,1,3,0:T(8,128)S(1)} %bitcast.333), channel_id=1, source_target_pairs={{0,7},{1,0},{2,1},{3,2},{4,3},{5,4},{6,5},{7,6},{8,15},{9,8},{10,9... | collective-permute-start | bytes 3080 | tf_op jit(solution)/shard_map/ppermute | solution.py:16
  38.8 1.1 collective-permute-start.6
  39.8 2.8 %collective-permute-start.7 = (f32[1,16,1,128]{3,1,2,0:T(8,128)S(1)}, f32[1,16,1,128]{3,1,2,0:T(8,128)S(1)}, u32[]{:S(2)}, u32[]{:S(2)}) collective-permute-start(f32[1,16,1,128]{3,1,2,0:T(8,128)S(1)} %get-tuple-element.155), channel_id=1, source_target_pairs={{0,6},{1,7},{2,0},{3,1},{4,2},{5,3},{6,4},{7,5},{8,14},{9,15},{10,... | collective-permute-start | bytes 24584 | tf_op jit(solution)/shard_map/ppermute | solution.py:16
  43.4 0.9 collective-permute-done.6
  45.2 4.7 %collective-permute-start.14 = (f32[1,16,16,1]{2,1,3,0:T(8,128)S(1)}, f32[1,16,16,1]{2,1,3,0:T(8,128)S(1)}, u32[]{:S(2)}, u32[]{:S(2)}) collective-permute-start(f32[1,16,16,1]{2,1,3,0:T(8,128)S(1)} %bitcast.337), channel_id=1, source_target_pairs={{0,7},{1,0},{2,1},{3,2},{4,3},{5,4},{6,5},{7,6},{8,15},{9,8},{10,9... | collective-permute-start | bytes 3080 | tf_op jit(solution)/shard_map/ppermute | solution.py:16
  49.9 2.6 %collective-permute-start.11 = (f32[1,16,1,128]{3,1,2,0:T(8,128)S(1)}, f32[1,16,1,128]{3,1,2,0:T(8,128)S(1)}, u32[]{:S(2)}, u32[]{:S(2)}) collective-permute-start(f32[1,16,1,128]{3,1,2,0:T(8,128)S(1)} %get-tuple-element.144), channel_id=1, source_target_pairs={{0,2},{1,3},{2,4},{3,5},{4,6},{5,7},{6,0},{7,1},{8,10},{9,11},{10,... | collective-permute-start | bytes 24584 | tf_op jit(solution)/shard_map/ppermute | solution.py:16
  52.5 1.3 %collective-permute-start.12 = (f32[1,16,1,128]{3,1,2,0:T(8,128)S(1)}, f32[1,16,1,128]{3,1,2,0:T(8,128)S(1)}, u32[]{:S(2)}, u32[]{:S(2)}) collective-permute-start(f32[1,16,1,128]{3,1,2,0:T(8,128)S(1)} %get-tuple-element.143), channel_id=1, source_target_pairs={{0,6},{1,7},{2,0},{3,1},{4,2},{5,3},{6,4},{7,5},{8,14},{9,15},{10,... | collective-permute-start | bytes 24584 | tf_op jit(solution)/shard_map/ppermute | solution.py:16
  54.5 0.9 collective-permute-done.11
  55.4 0.7 collective-permute-done.12
  57.5 1.2 collective-permute-start.16
  58.7 3.5 %collective-permute-start.17 = (f32[2,8,8,64]{3,2,1,0:T(8,128)S(1)}, f32[2,8,8,64]{3,2,1,0:T(8,128)S(1)}, u32[]{:S(2)}, u32[]{:S(2)}) collective-permute-start(f32[2,8,8,64]{3,2,1,0:T(8,128)S(1)} %pad_maximum_fusion.5), channel_id=1, source_target_pairs={{0,3},{1,4},{2,5},{3,6},{4,7},{5,0},{6,1},{7,2},{8,11},{9,12},{10,... | collective-permute-start | bytes 98312 | tf_op jit(solution)/shard_map/ppermute | solution.py:16
  62.2 1.8 %collective-permute-start.18 = (f32[2,8,8,64]{3,2,1,0:T(8,128)S(1)}, f32[2,8,8,64]{3,2,1,0:T(8,128)S(1)}, u32[]{:S(2)}, u32[]{:S(2)}) collective-permute-start(f32[2,8,8,64]{3,2,1,0:T(8,128)S(1)} %pad_maximum_fusion.5), channel_id=1, source_target_pairs={{0,4},{1,5},{2,6},{3,7},{4,0},{5,1},{6,2},{7,3},{8,12},{9,13},{10,... | collective-permute-start | bytes 98312 | tf_op jit(solution)/shard_map/ppermute | solution.py:16
  64.0 1.9 %collective-permute-start.19 = (f32[2,8,8,64]{3,2,1,0:T(8,128)S(1)}, f32[2,8,8,64]{3,2,1,0:T(8,128)S(1)}, u32[]{:S(2)}, u32[]{:S(2)}) collective-permute-start(f32[2,8,8,64]{3,2,1,0:T(8,128)S(1)} %pad_maximum_fusion.5), channel_id=1, source_target_pairs={{0,5},{1,6},{2,7},{3,0},{4,1},{5,2},{6,3},{7,4},{8,13},{9,14},{10,... | collective-permute-start | bytes 98312 | tf_op jit(solution)/shard_map/ppermute | solution.py:16
  66.3 1.8 %collective-permute-start.21 = (f32[2,8,8,64]{3,2,1,0:T(8,128)S(1)}, f32[2,8,8,64]{3,2,1,0:T(8,128)S(1)}, u32[]{:S(2)}, u32[]{:S(2)}) collective-permute-start(f32[2,8,8,64]{3,2,1,0:T(8,128)S(1)} %pad_maximum_fusion.5), channel_id=1, source_target_pairs={{0,7},{1,0},{2,1},{3,2},{4,3},{5,4},{6,5},{7,6},{8,15},{9,8},{10,9... | collective-permute-start | bytes 98312 | tf_op jit(solution)/shard_map/ppermute | solution.py:16
  69.1 1.0 collective-permute-done.20
  71.7 1.4 %fusion.4 = f32[3072,192]{0,1:T(8,128)S(1)} fusion(s32[3072]{0:T(1024)S(1)} %constant_dynamic-update-slice_fusion.4, bf16[512,64]{1,0:T(8,128)(2,1)S(1)} %get-tuple-element.97, bf16[512,64]{1,0:T(8,128)(2,1)S(1)} %get-tuple-element.96, bf16[512,64]{1,0:T(8,128)(2,1)S(1)} %get-tuple-element.95), kind=kOutput, calls=%fused_computation.7 | convolution fusion | flops 609288192 | bytes 2568192 | tf_op jit(solution)/shard_map/dot_general | solution.py:277
  73.5 0.8 fusion.20
  74.3 1.6 %slice_add_fusion.8 = f32[1536,256]{0,1:T(8,128)} fusion(f32[4608,256]{0,1:T(8,128)S(1)} %fusion.20), kind=kLoop, calls=%fused_computation.31 | loop fusion | flops 786432 | bytes 6291456 | tf_op jit(solution)/shard_map/add | solution.py:285
  75.9 1.2 reduce-precision_convert_fusion.19
  77.2 1.3 fusion.3
  78.8 0.8 fusion.26
  80.3 1.3 fusion.2
  81.8 0.8 fusion.32
  94.9 1.3 fusion.1
  96.4 0.8 fusion.38
  97.9 1.3 fusion
  99.4 0.8 fusion.44
  104.6 2.6 %collective-permute-start.25 = (f32[1,16,16,1]{2,1,3,0:T(8,128)S(1)}, f32[1,16,16,1]{2,1,3,0:T(8,128)S(1)}, u32[]{:S(2)}, u32[]{:S(2)}) collective-permute-start(f32[1,16,16,1]{2,1,3,0:T(8,128)S(1)} %bitcast.331), channel_id=1, source_target_pairs={{0,1},{1,2},{2,3},{3,4},{4,5},{5,6},{6,7},{7,0},{8,9},{9,10},{10,1... | collective-permute-start | bytes 3080 | tf_op jit(solution)/shard_map/ppermute | solution.py:16
  107.4 2.1 %collective-permute-start.26 = (f32[1,16,16,1]{2,1,3,0:T(8,128)S(1)}, f32[1,16,16,1]{2,1,3,0:T(8,128)S(1)}, u32[]{:S(2)}, u32[]{:S(2)}) collective-permute-start(f32[1,16,16,1]{2,1,3,0:T(8,128)S(1)} %bitcast.335), channel_id=1, source_target_pairs={{0,7},{1,0},{2,1},{3,2},{4,3},{5,4},{6,5},{7,6},{8,15},{9,8},{10,9... | collective-permute-start | bytes 3080 | tf_op jit(solution)/shard_map/ppermute | solution.py:16
  109.5 0.7 collective-permute-start.23
  110.2 3.2 %collective-permute-start.24 = (f32[1,16,1,128]{3,1,2,0:T(8,128)S(1)}, f32[1,16,1,128]{3,1,2,0:T(8,128)S(1)}, u32[]{:S(2)}, u32[]{:S(2)}) collective-permute-start(f32[1,16,1,128]{3,1,2,0:T(8,128)S(1)} %get-tuple-element.116), channel_id=1, source_target_pairs={{0,6},{1,7},{2,0},{3,1},{4,2},{5,3},{6,4},{7,5},{8,14},{9,15},{10,... | collective-permute-start | bytes 24584 | tf_op jit(solution)/shard_map/ppermute | solution.py:16
  114.1 0.9 collective-permute-done.23
  115.5 1.1 collective-permute-start.27
  116.8 0.8 collective-permute-start.30
  117.8 4.0 %collective-permute-start.31 = (f32[1,16,16,1]{2,1,3,0:T(8,128)S(1)}, f32[1,16,16,1]{2,1,3,0:T(8,128)S(1)}, u32[]{:S(2)}, u32[]{:S(2)}) collective-permute-start(f32[1,16,16,1]{2,1,3,0:T(8,128)S(1)} %bitcast.340), channel_id=1, source_target_pairs={{0,7},{1,0},{2,1},{3,2},{4,3},{5,4},{6,5},{7,6},{8,15},{9,8},{10,9... | collective-permute-start | bytes 3080 | tf_op jit(solution)/shard_map/ppermute | solution.py:16
  121.8 1.5 %collective-permute-start.28 = (f32[1,16,1,128]{3,1,2,0:T(8,128)S(1)}, f32[1,16,1,128]{3,1,2,0:T(8,128)S(1)}, u32[]{:S(2)}, u32[]{:S(2)}) collective-permute-start(f32[1,16,1,128]{3,1,2,0:T(8,128)S(1)} %get-tuple-element.105), channel_id=1, source_target_pairs={{0,2},{1,3},{2,4},{3,5},{4,6},{5,7},{6,0},{7,1},{8,10},{9,11},{10,... | collective-permute-start | bytes 24584 | tf_op jit(solution)/shard_map/ppermute | solution.py:16
  123.3 2.3 %collective-permute-start.29 = (f32[1,16,1,128]{3,1,2,0:T(8,128)S(1)}, f32[1,16,1,128]{3,1,2,0:T(8,128)S(1)}, u32[]{:S(2)}, u32[]{:S(2)}) collective-permute-start(f32[1,16,1,128]{3,1,2,0:T(8,128)S(1)} %get-tuple-element.104), channel_id=1, source_target_pairs={{0,6},{1,7},{2,0},{3,1},{4,2},{5,3},{6,4},{7,5},{8,14},{9,15},{10,... | collective-permute-start | bytes 24584 | tf_op jit(solution)/shard_map/ppermute | solution.py:16
  125.6 0.7 copy.1007
  127.4 0.7 copy.1008
  (355 shorter events, 32.7 us)
Async XLA Ops:
  9.0 23.9 %collective-permute-start = (f32[2,2,16,128]{3,1,2,0:T(2,128)S(1)}, f32[2,2,16,128]{3,1,2,0:T(2,128)S(1)}, u32[]{:S(2)}, u32[]{:S(2)}) collective-permute-start(f32[2,2,16,128]{3,1,2,0:T(2,128)S(1)} %maximum_maximum_fusion), channel_id=1, source_target_pairs={{0,4},{1,5},{2,6},{3,7},{4,0},{5,1},{6,2},{7,3},{8,12},{9,13},{10,... | collective-permute-start | bytes 98312 | tf_op jit(solution)/shard_map/ppermute | solution.py:16
  20.6 11.5 %collective-permute-start.3 = (f32[2,16,16,1]{2,1,3,0:T(8,128)S(1)}, f32[2,16,16,1]{2,1,3,0:T(8,128)S(1)}, u32[]{:S(2)}, u32[]{:S(2)}) collective-permute-start(f32[2,16,16,1]{2,1,3,0:T(8,128)S(1)} %pad_maximum_fusion.14), channel_id=1, source_target_pairs={{0,1},{1,2},{2,3},{3,4},{4,5},{5,6},{6,7},{7,0},{8,9},{9,10},{10,1... | collective-permute-start | bytes 6152 | tf_op jit(solution)/shard_map/ppermute | solution.py:16
  22.5 9.5 %collective-permute-start.4 = (f32[2,16,16,1]{2,1,3,0:T(8,128)S(1)}, f32[2,16,16,1]{2,1,3,0:T(8,128)S(1)}, u32[]{:S(2)}, u32[]{:S(2)}) collective-permute-start(f32[2,16,16,1]{2,1,3,0:T(8,128)S(1)} %pad_maximum_fusion.15), channel_id=1, source_target_pairs={{0,7},{1,0},{2,1},{3,2},{4,3},{5,4},{6,5},{7,6},{8,15},{9,8},{10,9... | collective-permute-start | bytes 6152 | tf_op jit(solution)/shard_map/ppermute | solution.py:16
  25.8 7.0 %collective-permute-start.1 = (f32[2,16,1,128]{3,1,2,0:T(8,128)S(1)}, f32[2,16,1,128]{3,1,2,0:T(8,128)S(1)}, u32[]{:S(2)}, u32[]{:S(2)}) collective-permute-start(f32[2,16,1,128]{3,1,2,0:T(8,128)S(1)} %pad_maximum_fusion.12), channel_id=1, source_target_pairs={{0,2},{1,3},{2,4},{3,5},{4,6},{5,7},{6,0},{7,1},{8,10},{9,11},{10,... | collective-permute-start | bytes 49160 | tf_op jit(solution)/shard_map/ppermute | solution.py:16
  25.8 7.0 %collective-permute-start.2 = (f32[2,16,1,128]{3,1,2,0:T(8,128)S(1)}, f32[2,16,1,128]{3,1,2,0:T(8,128)S(1)}, u32[]{:S(2)}, u32[]{:S(2)}) collective-permute-start(f32[2,16,1,128]{3,1,2,0:T(8,128)S(1)} %pad_maximum_fusion.13), channel_id=1, source_target_pairs={{0,6},{1,7},{2,0},{3,1},{4,2},{5,3},{6,4},{7,5},{8,14},{9,15},{10,... | collective-permute-start | bytes 49160 | tf_op jit(solution)/shard_map/ppermute | solution.py:16
  29.8 1.7 %copy-start.1 = (s32[16]{0:T(128)S(1)}, s32[16]{0:T(128)}, u32[]{:S(2)}) copy-start(s32[16]{0:T(128)} %param.7) | copy-start | bytes 196
  29.8 1.7 %copy-start.2 = (f32[16]{0:T(128)S(1)}, f32[16]{0:T(128)}, u32[]{:S(2)}) copy-start(f32[16]{0:T(128)} %param.8) | copy-start | bytes 196
  29.8 3.0 %copy-start = (f32[1,16,16,128]{3,2,1,0:T(8,128)S(1)}, f32[1,16,16,128]{3,2,1,0:T(8,128)}, u32[]{:S(2)}) copy-start(f32[1,16,16,128]{3,2,1,0:T(8,128)} %param.9) | copy-start | bytes 393220
  33.8 8.8 %collective-permute-start.8 = (f32[1,16,16,1]{2,1,3,0:T(8,128)S(1)}, f32[1,16,16,1]{2,1,3,0:T(8,128)S(1)}, u32[]{:S(2)}, u32[]{:S(2)}) collective-permute-start(f32[1,16,16,1]{2,1,3,0:T(8,128)S(1)} %bitcast.328), channel_id=1, source_target_pairs={{0,1},{1,2},{2,3},{3,4},{4,5},{5,6},{6,7},{7,0},{8,9},{9,10},{10,1... | collective-permute-start | bytes 3080 | tf_op jit(solution)/shard_map/ppermute | solution.py:16
  34.0 8.8 %collective-permute-start.9 = (f32[1,16,16,1]{2,1,3,0:T(8,128)S(1)}, f32[1,16,16,1]{2,1,3,0:T(8,128)S(1)}, u32[]{:S(2)}, u32[]{:S(2)}) collective-permute-start(f32[1,16,16,1]{2,1,3,0:T(8,128)S(1)} %bitcast.333), channel_id=1, source_target_pairs={{0,7},{1,0},{2,1},{3,2},{4,3},{5,4},{6,5},{7,6},{8,15},{9,8},{10,9... | collective-permute-start | bytes 3080 | tf_op jit(solution)/shard_map/ppermute | solution.py:16
  38.8 4.6 %collective-permute-start.5 = (f32[1,2,16,128]{3,2,1,0:T(8,128)S(1)}, f32[1,2,16,128]{3,2,1,0:T(8,128)S(1)}, u32[]{:S(2)}, u32[]{:S(2)}) collective-permute-start(f32[1,2,16,128]{3,2,1,0:T(8,128)S(1)} %pad_maximum_fusion.16), channel_id=1, source_target_pairs={{0,4},{1,5},{2,6},{3,7},{4,0},{5,1},{6,2},{7,3},{8,12},{9,13},{10,... | collective-permute-start | bytes 49160 | tf_op jit(solution)/shard_map/ppermute | solution.py:16
  38.8 5.5 %collective-permute-start.6 = (f32[1,16,1,128]{3,1,2,0:T(8,128)S(1)}, f32[1,16,1,128]{3,1,2,0:T(8,128)S(1)}, u32[]{:S(2)}, u32[]{:S(2)}) collective-permute-start(f32[1,16,1,128]{3,1,2,0:T(8,128)S(1)} %get-tuple-element.156), channel_id=1, source_target_pairs={{0,2},{1,3},{2,4},{3,5},{4,6},{5,7},{6,0},{7,1},{8,10},{9,11},{10,... | collective-permute-start | bytes 24584 | tf_op jit(solution)/shard_map/ppermute | solution.py:16
  39.8 4.4 %collective-permute-start.7 = (f32[1,16,1,128]{3,1,2,0:T(8,128)S(1)}, f32[1,16,1,128]{3,1,2,0:T(8,128)S(1)}, u32[]{:S(2)}, u32[]{:S(2)}) collective-permute-start(f32[1,16,1,128]{3,1,2,0:T(8,128)S(1)} %get-tuple-element.155), channel_id=1, source_target_pairs={{0,6},{1,7},{2,0},{3,1},{4,2},{5,3},{6,4},{7,5},{8,14},{9,15},{10,... | collective-permute-start | bytes 24584 | tf_op jit(solution)/shard_map/ppermute | solution.py:16
  44.9 8.8 %collective-permute-start.13 = (f32[1,16,16,1]{2,1,3,0:T(8,128)S(1)}, f32[1,16,16,1]{2,1,3,0:T(8,128)S(1)}, u32[]{:S(2)}, u32[]{:S(2)}) collective-permute-start(f32[1,16,16,1]{2,1,3,0:T(8,128)S(1)} %bitcast.330), channel_id=1, source_target_pairs={{0,1},{1,2},{2,3},{3,4},{4,5},{5,6},{6,7},{7,0},{8,9},{9,10},{10,1... | collective-permute-start | bytes 3080 | tf_op jit(solution)/shard_map/ppermute | solution.py:16
  45.2 8.8 %collective-permute-start.14 = (f32[1,16,16,1]{2,1,3,0:T(8,128)S(1)}, f32[1,16,16,1]{2,1,3,0:T(8,128)S(1)}, u32[]{:S(2)}, u32[]{:S(2)}) collective-permute-start(f32[1,16,16,1]{2,1,3,0:T(8,128)S(1)} %bitcast.337), channel_id=1, source_target_pairs={{0,7},{1,0},{2,1},{3,2},{4,3},{5,4},{6,5},{7,6},{8,15},{9,8},{10,9... | collective-permute-start | bytes 3080 | tf_op jit(solution)/shard_map/ppermute | solution.py:16
  49.9 4.6 %collective-permute-start.10 = (f32[1,2,16,128]{3,2,1,0:T(8,128)S(1)}, f32[1,2,16,128]{3,2,1,0:T(8,128)S(1)}, u32[]{:S(2)}, u32[]{:S(2)}) collective-permute-start(f32[1,2,16,128]{3,2,1,0:T(8,128)S(1)} %pad_maximum_fusion.17), channel_id=1, source_target_pairs={{0,4},{1,5},{2,6},{3,7},{4,0},{5,1},{6,2},{7,3},{8,12},{9,13},{10,... | collective-permute-start | bytes 49160 | tf_op jit(solution)/shard_map/ppermute | solution.py:16
  49.9 5.5 %collective-permute-start.11 = (f32[1,16,1,128]{3,1,2,0:T(8,128)S(1)}, f32[1,16,1,128]{3,1,2,0:T(8,128)S(1)}, u32[]{:S(2)}, u32[]{:S(2)}) collective-permute-start(f32[1,16,1,128]{3,1,2,0:T(8,128)S(1)} %get-tuple-element.144), channel_id=1, source_target_pairs={{0,2},{1,3},{2,4},{3,5},{4,6},{5,7},{6,0},{7,1},{8,10},{9,11},{10,... | collective-permute-start | bytes 24584 | tf_op jit(solution)/shard_map/ppermute | solution.py:16
  52.5 3.7 %collective-permute-start.12 = (f32[1,16,1,128]{3,1,2,0:T(8,128)S(1)}, f32[1,16,1,128]{3,1,2,0:T(8,128)S(1)}, u32[]{:S(2)}, u32[]{:S(2)}) collective-permute-start(f32[1,16,1,128]{3,1,2,0:T(8,128)S(1)} %get-tuple-element.143), channel_id=1, source_target_pairs={{0,6},{1,7},{2,0},{3,1},{4,2},{5,3},{6,4},{7,5},{8,14},{9,15},{10,... | collective-permute-start | bytes 24584 | tf_op jit(solution)/shard_map/ppermute | solution.py:16
  57.0 8.9 %collective-permute-start.15 = (f32[2,8,8,64]{3,2,1,0:T(8,128)S(1)}, f32[2,8,8,64]{3,2,1,0:T(8,128)S(1)}, u32[]{:S(2)}, u32[]{:S(2)}) collective-permute-start(f32[2,8,8,64]{3,2,1,0:T(8,128)S(1)} %pad_maximum_fusion.5), channel_id=1, source_target_pairs={{0,1},{1,2},{2,3},{3,4},{4,5},{5,6},{6,7},{7,0},{8,9},{9,10},{10,1... | collective-permute-start | bytes 98312 | tf_op jit(solution)/shard_map/ppermute | solution.py:16
  57.5 8.9 %collective-permute-start.16 = (f32[2,8,8,64]{3,2,1,0:T(8,128)S(1)}, f32[2,8,8,64]{3,2,1,0:T(8,128)S(1)}, u32[]{:S(2)}, u32[]{:S(2)}) collective-permute-start(f32[2,8,8,64]{3,2,1,0:T(8,128)S(1)} %pad_maximum_fusion.5), channel_id=1, source_target_pairs={{0,2},{1,3},{2,4},{3,5},{4,6},{5,7},{6,0},{7,1},{8,10},{9,11},{10,... | collective-permute-start | bytes 98312 | tf_op jit(solution)/shard_map/ppermute | solution.py:16
  58.7 9.4 %collective-permute-start.17 = (f32[2,8,8,64]{3,2,1,0:T(8,128)S(1)}, f32[2,8,8,64]{3,2,1,0:T(8,128)S(1)}, u32[]{:S(2)}, u32[]{:S(2)}) collective-permute-start(f32[2,8,8,64]{3,2,1,0:T(8,128)S(1)} %pad_maximum_fusion.5), channel_id=1, source_target_pairs={{0,3},{1,4},{2,5},{3,6},{4,7},{5,0},{6,1},{7,2},{8,11},{9,12},{10,... | collective-permute-start | bytes 98312 | tf_op jit(solution)/shard_map/ppermute | solution.py:16
  62.2 6.6 %collective-permute-start.18 = (f32[2,8,8,64]{3,2,1,0:T(8,128)S(1)}, f32[2,8,8,64]{3,2,1,0:T(8,128)S(1)}, u32[]{:S(2)}, u32[]{:S(2)}) collective-permute-start(f32[2,8,8,64]{3,2,1,0:T(8,128)S(1)} %pad_maximum_fusion.5), channel_id=1, source_target_pairs={{0,4},{1,5},{2,6},{3,7},{4,0},{5,1},{6,2},{7,3},{8,12},{9,13},{10,... | collective-permute-start | bytes 98312 | tf_op jit(solution)/shard_map/ppermute | solution.py:16
  64.0 5.2 %collective-permute-start.19 = (f32[2,8,8,64]{3,2,1,0:T(8,128)S(1)}, f32[2,8,8,64]{3,2,1,0:T(8,128)S(1)}, u32[]{:S(2)}, u32[]{:S(2)}) collective-permute-start(f32[2,8,8,64]{3,2,1,0:T(8,128)S(1)} %pad_maximum_fusion.5), channel_id=1, source_target_pairs={{0,5},{1,6},{2,7},{3,0},{4,1},{5,2},{6,3},{7,4},{8,13},{9,14},{10,... | collective-permute-start | bytes 98312 | tf_op jit(solution)/shard_map/ppermute | solution.py:16
  65.8 4.4 %collective-permute-start.20 = (f32[2,8,8,64]{3,2,1,0:T(8,128)S(1)}, f32[2,8,8,64]{3,2,1,0:T(8,128)S(1)}, u32[]{:S(2)}, u32[]{:S(2)}) collective-permute-start(f32[2,8,8,64]{3,2,1,0:T(8,128)S(1)} %pad_maximum_fusion.5), channel_id=1, source_target_pairs={{0,6},{1,7},{2,0},{3,1},{4,2},{5,3},{6,4},{7,5},{8,14},{9,15},{10,... | collective-permute-start | bytes 98312 | tf_op jit(solution)/shard_map/ppermute | solution.py:16
  66.3 4.5 %collective-permute-start.21 = (f32[2,8,8,64]{3,2,1,0:T(8,128)S(1)}, f32[2,8,8,64]{3,2,1,0:T(8,128)S(1)}, u32[]{:S(2)}, u32[]{:S(2)}) collective-permute-start(f32[2,8,8,64]{3,2,1,0:T(8,128)S(1)} %pad_maximum_fusion.5), channel_id=1, source_target_pairs={{0,7},{1,0},{2,1},{3,2},{4,3},{5,4},{6,5},{7,6},{8,15},{9,8},{10,9... | collective-permute-start | bytes 98312 | tf_op jit(solution)/shard_map/ppermute | solution.py:16
  104.6 8.8 %collective-permute-start.25 = (f32[1,16,16,1]{2,1,3,0:T(8,128)S(1)}, f32[1,16,16,1]{2,1,3,0:T(8,128)S(1)}, u32[]{:S(2)}, u32[]{:S(2)}) collective-permute-start(f32[1,16,16,1]{2,1,3,0:T(8,128)S(1)} %bitcast.331), channel_id=1, source_target_pairs={{0,1},{1,2},{2,3},{3,4},{4,5},{5,6},{6,7},{7,0},{8,9},{9,10},{10,1... | collective-permute-start | bytes 3080 | tf_op jit(solution)/shard_map/ppermute | solution.py:16
  107.4 6.2 %collective-permute-start.26 = (f32[1,16,16,1]{2,1,3,0:T(8,128)S(1)}, f32[1,16,16,1]{2,1,3,0:T(8,128)S(1)}, u32[]{:S(2)}, u32[]{:S(2)}) collective-permute-start(f32[1,16,16,1]{2,1,3,0:T(8,128)S(1)} %bitcast.335), channel_id=1, source_target_pairs={{0,7},{1,0},{2,1},{3,2},{4,3},{5,4},{6,5},{7,6},{8,15},{9,8},{10,9... | collective-permute-start | bytes 3080 | tf_op jit(solution)/shard_map/ppermute | solution.py:16
  109.5 4.6 %collective-permute-start.22 = (f32[1,2,16,128]{3,2,1,0:T(8,128)S(1)}, f32[1,2,16,128]{3,2,1,0:T(8,128)S(1)}, u32[]{:S(2)}, u32[]{:S(2)}) collective-permute-start(f32[1,2,16,128]{3,2,1,0:T(8,128)S(1)} %pad_maximum_fusion.18), channel_id=1, source_target_pairs={{0,4},{1,5},{2,6},{3,7},{4,0},{5,1},{6,2},{7,3},{8,12},{9,13},{10,... | collective-permute-start | bytes 49160 | tf_op jit(solution)/shard_map/ppermute | solution.py:16
  109.5 5.5 %collective-permute-start.23 = (f32[1,16,1,128]{3,1,2,0:T(8,128)S(1)}, f32[1,16,1,128]{3,1,2,0:T(8,128)S(1)}, u32[]{:S(2)}, u32[]{:S(2)}) collective-permute-start(f32[1,16,1,128]{3,1,2,0:T(8,128)S(1)} %get-tuple-element.117), channel_id=1, source_target_pairs={{0,2},{1,3},{2,4},{3,5},{4,6},{5,7},{6,0},{7,1},{8,10},{9,11},{10,... | collective-permute-start | bytes 24584 | tf_op jit(solution)/shard_map/ppermute | solution.py:16
  110.2 4.8 %collective-permute-start.24 = (f32[1,16,1,128]{3,1,2,0:T(8,128)S(1)}, f32[1,16,1,128]{3,1,2,0:T(8,128)S(1)}, u32[]{:S(2)}, u32[]{:S(2)}) collective-permute-start(f32[1,16,1,128]{3,1,2,0:T(8,128)S(1)} %get-tuple-element.116), channel_id=1, source_target_pairs={{0,6},{1,7},{2,0},{3,1},{4,2},{5,3},{6,4},{7,5},{8,14},{9,15},{10,... | collective-permute-start | bytes 24584 | tf_op jit(solution)/shard_map/ppermute | solution.py:16
  115.5 11.1 %collective-permute-start.27 = (f32[1,2,16,128]{3,2,1,0:T(8,128)S(1)}, f32[1,2,16,128]{3,2,1,0:T(8,128)S(1)}, u32[]{:S(2)}, u32[]{:S(2)}) collective-permute-start(f32[1,2,16,128]{3,2,1,0:T(8,128)S(1)} %pad_maximum_fusion.19), channel_id=1, source_target_pairs={{0,4},{1,5},{2,6},{3,7},{4,0},{5,1},{6,2},{7,3},{8,12},{9,13},{10,... | collective-permute-start | bytes 49160 | tf_op jit(solution)/shard_map/ppermute | solution.py:16
  116.8 9.5 %collective-permute-start.30 = (f32[1,16,16,1]{2,1,3,0:T(8,128)S(1)}, f32[1,16,16,1]{2,1,3,0:T(8,128)S(1)}, u32[]{:S(2)}, u32[]{:S(2)}) collective-permute-start(f32[1,16,16,1]{2,1,3,0:T(8,128)S(1)} %bitcast.338), channel_id=1, source_target_pairs={{0,1},{1,2},{2,3},{3,4},{4,5},{5,6},{6,7},{7,0},{8,9},{9,10},{10,1... | collective-permute-start | bytes 3080 | tf_op jit(solution)/shard_map/ppermute | solution.py:16
  117.8 8.7 %collective-permute-start.31 = (f32[1,16,16,1]{2,1,3,0:T(8,128)S(1)}, f32[1,16,16,1]{2,1,3,0:T(8,128)S(1)}, u32[]{:S(2)}, u32[]{:S(2)}) collective-permute-start(f32[1,16,16,1]{2,1,3,0:T(8,128)S(1)} %bitcast.340), channel_id=1, source_target_pairs={{0,7},{1,0},{2,1},{3,2},{4,3},{5,4},{6,5},{7,6},{8,15},{9,8},{10,9... | collective-permute-start | bytes 3080 | tf_op jit(solution)/shard_map/ppermute | solution.py:16
  121.8 5.4 %collective-permute-start.28 = (f32[1,16,1,128]{3,1,2,0:T(8,128)S(1)}, f32[1,16,1,128]{3,1,2,0:T(8,128)S(1)}, u32[]{:S(2)}, u32[]{:S(2)}) collective-permute-start(f32[1,16,1,128]{3,1,2,0:T(8,128)S(1)} %get-tuple-element.105), channel_id=1, source_target_pairs={{0,2},{1,3},{2,4},{3,5},{4,6},{5,7},{6,0},{7,1},{8,10},{9,11},{10,... | collective-permute-start | bytes 24584 | tf_op jit(solution)/shard_map/ppermute | solution.py:16
  123.3 3.9 %collective-permute-start.29 = (f32[1,16,1,128]{3,1,2,0:T(8,128)S(1)}, f32[1,16,1,128]{3,1,2,0:T(8,128)S(1)}, u32[]{:S(2)}, u32[]{:S(2)}) collective-permute-start(f32[1,16,1,128]{3,1,2,0:T(8,128)S(1)} %get-tuple-element.104), channel_id=1, source_target_pairs={{0,6},{1,7},{2,0},{3,1},{4,2},{5,3},{6,4},{7,5},{8,14},{9,15},{10,... | collective-permute-start | bytes 24584 | tf_op jit(solution)/shard_map/ppermute | solution.py:16
